TPU v7x, 256 devices: a whole 4x4x8 slice. The times are simulated.
256 devices in a mesh: zone: 8 (over x, z_lo), brick: 32 (over z_hi, y, core).
Axes of the slice: x: 4, y: 4, z: 8 (z_hi: 4, z_lo: 2; z = z_hi * 2 + z_lo), core: 2. Of those that a mesh axis runs over, the one named last changes fastest.
Arguments:
- velocity: float32 [3, 2048, 64, 256], P(None, ('zone', 'brick')), may hold values from -3 to 3
- enthalpy: float32 [2048, 64, 256], P(('zone', 'brick')), may hold values from -6 to 6
- solvent: float32 [2048, 64, 256], P(('zone', 'brick')), may hold values from 0 to 1
- pressure: float32 [2048, 64, 256], P(('zone', 'brick')), may hold values from -6 to 6
- porosity: float32 [2048, 64, 256], P(('zone', 'brick')), may hold values from 0.1 to 1
- solid_mask: int32 [2048, 64, 256], P(('zone', 'brick')), may hold values 0 or 1
- nozzle_mask: int32 [2048, 256], P(('zone', 'brick')), may hold values 0 or 1
- zone_sizes: int32 [8], replicated, may hold values from 16 to 64, as said below
- zone_setpoint: float32 [8], replicated, may hold values from 0.5 to 2
- duct_source: int32 [256], P(('zone', 'brick')), may hold values from 0 to 7
- duct_span: int32 [256, 2], P(('zone', 'brick')), may hold values from 0 to 256, as said below
Outputs:
- velocity_new: float32 [3, 2048, 64, 256], P(None, ('zone', 'brick'))
- enthalpy_new: float32 [2048, 64, 256], P(('zone', 'brick'))
- solvent_new: float32 [2048, 64, 256], P(('zone', 'brick'))
- pressure_new: float32 [2048, 64, 256], P(('zone', 'brick'))
Inputs may be any that keep to these rules, and one draw needn't show every extreme that they name: `zone_sizes`: each zone's group holds a multiple of one thirty-second of all devices; the groups cover all devices, zone 0 first. duct_span[d,0] + duct_span[d,1] <= 256; duct_span[d,1] >= 64.
All inputs are finite; a program needn't handle non-finite values. No bound on the sum of `solid_mask` or of `nozzle_mask` on one device may be relied on, other than what follows from the above.
Results may differ from a plain program's by a relative error of at most 0.0003.
Values sent between devices are 32-bit elements; how exact they have to be, the bound alone decides.
No kernel may reach another device: no remote copies, remote signals or barrier semaphores. Data moves between devices by JAX's collectives and lax.ppermute only.
A program may use at most 128 MiB of HBM per device.

v0:
```python
import jax
import jax.numpy as jnp
from jax import lax
from jax.sharding import PartitionSpec as P

ITERS = 4


time_step = 0.2
viscosity = 0.1
diffusivity = 0.1
buoyancy = 0.5
evaporation = 0.5
latent_heat = 0.8
solvent_limit = 0.2


def extended(cells, sides, width):
    for axis, dim in sides:
        count = lax.axis_size(axis)
        ends = count - 1
        head = lax.slice_in_dim(cells, 0, width, axis=dim)
        tail = lax.slice_in_dim(cells, cells.shape[dim] - width, cells.shape[dim], axis=dim)
        cells = jnp.concatenate(
            [
                lax.ppermute(tail, axis, [(i, (i + 1) % count) for i in range(ends)]),
                cells,
                lax.ppermute(head, axis, [((i + 1) % count, i) for i in range(ends)]),
            ],
            axis=dim,
        )
    return cells


def shifted_down(values, axis):
    border = jnp.zeros_like(lax.slice_in_dim(values, 0, 1, axis=axis))
    inner = lax.slice_in_dim(values, 0, values.shape[axis] - 1, axis=axis)
    return jnp.concatenate([border, inner], axis=axis)


def shifted_up(values, axis):
    border = jnp.zeros_like(lax.slice_in_dim(values, 0, 1, axis=axis))
    inner = lax.slice_in_dim(values, 1, values.shape[axis], axis=axis)
    return jnp.concatenate([inner, border], axis=axis)


def momentum(vel_ext, pres_ext, heat_ext, poro_ext, components):
    open_here = poro_ext[1:-1]
    pressure_mid = pres_ext[1:-1]
    parts = []
    for component in components:
        values = vel_ext[component]
        centre = values[1:-1]
        laplacian = values[:-2] + values[2:] + shifted_down(centre, 1) + shifted_up(centre, 1)
        laplacian = laplacian + shifted_down(centre, 2) + shifted_up(centre, 2) - 6.0 * centre
        if component == 0:
            gradient = 0.5 * (pres_ext[2:] - pres_ext[:-2])
        else:
            gradient = 0.5 * (
                shifted_up(pressure_mid, component) - shifted_down(pressure_mid, component)
            )
        forcing = viscosity * laplacian - gradient
        if component == 1:
            forcing = forcing + buoyancy * heat_ext[1:-1]
        parts.append(open_here * (centre + time_step * forcing))
    return jnp.stack(parts)


def divergence_parts(first_ext, vel_star):
    result = 0.5 * (first_ext[2:] - first_ext[:-2])
    middle = vel_star[1]
    result = result + 0.5 * (shifted_up(middle, 1) - shifted_down(middle, 1))
    across = vel_star[2]
    return result + 0.5 * (shifted_up(across, 2) - shifted_down(across, 2))


def transport(scalar_ext, vel_star):
    centre = scalar_ext[1:-1]
    laplacian = scalar_ext[:-2] + scalar_ext[2:] + shifted_down(centre, 1) + shifted_up(centre, 1)
    laplacian = laplacian + shifted_down(centre, 2) + shifted_up(centre, 2) - 6.0 * centre
    advect = jnp.maximum(vel_star[0], 0.0) * (centre - scalar_ext[:-2]) + jnp.minimum(
        vel_star[0], 0.0
    ) * (scalar_ext[2:] - centre)
    for component in (1, 2):
        advect = advect + jnp.maximum(vel_star[component], 0.0) * (
            centre - shifted_down(centre, component)
        )
        advect = advect + jnp.minimum(vel_star[component], 0.0) * (
            shifted_up(centre, component) - centre
        )
    return centre + time_step * (diffusivity * laplacian - advect)


def sweep(pres_ext, open_ext, source):
    open_here = open_ext[1:-1]
    pressure_mid = pres_ext[1:-1]
    face_back = 0.5 * (open_here + open_ext[:-2])
    face_front = 0.5 * (open_here + open_ext[2:])
    numerator = face_back * pres_ext[:-2] + face_front * pres_ext[2:] - source
    denominator = face_back + face_front
    for component in (1, 2):
        face_low = 0.5 * (open_here + shifted_down(open_here, component))
        face_high = 0.5 * (open_here + shifted_up(open_here, component))
        numerator = (
            numerator
            + face_low * shifted_down(pressure_mid, component)
            + face_high * shifted_up(pressure_mid, component)
        )
        denominator = denominator + face_low + face_high
    inside = open_here > 0.0
    return jnp.where(inside, numerator / jnp.where(inside, denominator, 1.0), 0.0)


def on_device(
    velocity,
    enthalpy,
    solvent,
    pressure,
    porosity,
    solid_mask,
    nozzle_mask,
    zone_sizes,
    zone_setpoint,
    duct_source,
    duct_span,
):
    stacked = jnp.concatenate(
        [velocity, jnp.stack([enthalpy, solvent, pressure, porosity])], axis=0
    )
    padded = extended(stacked, ((("zone", "brick"), 1),), 1)
    heat_ext = padded[3]
    solv_ext = padded[4]
    poro_ext = padded[6]
    vel_star = momentum(padded[0:3], padded[5], padded[3], padded[6], (0, 1, 2))
    first_ext = extended(vel_star[0], ((("zone", "brick"), 0),), 1)
    source = divergence_parts(first_ext, vel_star) / time_step
    heat_new = transport(heat_ext, vel_star)
    solv_new = transport(solv_ext, vel_star)
    drying = time_step * evaporation * solid_mask.astype(jnp.float32) * solvent
    heat_new = heat_new - latent_heat * drying
    solv_new = solv_new - drying
    device = lax.axis_index(("zone", "brick"))
    starts = jnp.cumsum(zone_sizes) - zone_sizes
    zone_here = jnp.sum((device >= starts).astype(jnp.int32)) - 1
    choose = (jnp.arange(zone_sizes.shape[0], dtype=jnp.int32) == zone_here).astype(jnp.float32)
    totals = lax.psum(choose * jnp.sum(solvent[:, -1, :]), ("zone", "brick"))
    counts = zone_sizes.astype(jnp.float32) * (enthalpy.shape[0] * enthalpy.shape[2])
    means = totals / counts
    fresh_all = means / (means + solvent_limit)
    fresh = jnp.sum(choose * fresh_all)
    target = jnp.sum(choose * zone_setpoint)
    planes = jnp.stack([enthalpy[:, -1, :], solvent[:, -1, :]])[None]
    gathered = lax.all_gather(planes, "zone", axis=0, tiled=True)
    pick = (jnp.arange(gathered.shape[0], dtype=jnp.int32) == duct_source[0]).astype(jnp.float32)
    arrived = jnp.sum(pick[:, None, None, None] * gathered, axis=0)
    supply_heat = (1.0 - fresh) * arrived[0] + fresh * target
    supply_solv = (1.0 - fresh) * arrived[1]
    column = jnp.arange(enthalpy.shape[2], dtype=jnp.int32)
    inside_box = (column >= duct_span[0, 0]) & (column < duct_span[0, 0] + duct_span[0, 1])
    jets = (nozzle_mask > 0) & inside_box[None, :]
    heat_layer = jnp.where(jets, supply_heat, heat_new[:, 0, :])
    solv_layer = jnp.where(jets, supply_solv, solv_new[:, 0, :])
    enthalpy_new = jnp.concatenate([heat_layer[:, None, :], heat_new[:, 1:, :]], axis=1)
    solvent_new = jnp.concatenate([solv_layer[:, None, :], solv_new[:, 1:, :]], axis=1)
    iterate = pressure
    for iteration in range(ITERS):
        pres_ext = extended(iterate, ((("zone", "brick"), 0),), 1)
        iterate = sweep(pres_ext, poro_ext, source)
    pres_ext = extended(iterate, ((("zone", "brick"), 0),), 1)
    gradients = jnp.stack(
        [
            0.5 * (pres_ext[2:] - pres_ext[:-2]),
            0.5 * (shifted_up(iterate, 1) - shifted_down(iterate, 1)),
            0.5 * (shifted_up(iterate, 2) - shifted_down(iterate, 2)),
        ]
    )
    velocity_new = vel_star - time_step * porosity[None] * gradients
    return (velocity_new, enthalpy_new, solvent_new, iterate)


def solution(mesh):
    placed = (
        P(None, ("zone", "brick"), None, None),
        P(("zone", "brick"), None, None),
        P(("zone", "brick"), None, None),
        P(("zone", "brick"), None, None),
        P(("zone", "brick"), None, None),
        P(("zone", "brick"), None, None),
        P(("zone", "brick"), None),
        P(),
        P(),
        P(("zone", "brick")),
        P(("zone", "brick"), None),
    )
    return jax.shard_map(
        on_device,
        mesh=mesh,
        in_specs=placed,
        out_specs=(
            P(None, ("zone", "brick"), None, None),
            P(("zone", "brick"), None, None),
            P(("zone", "brick"), None, None),
            P(("zone", "brick"), None, None),
        ),
        check_vma=False,
    )
```

profile of v0, /device:TPU:32, one launch (start us, length us, event | category | flops | bytes accessed | tf_op | source)
XLA Modules:
  0.0 256.3 jit_solution(2717288666460999411)
XLA Ops:
  0.7 2.4 fusion.106
  6.7 1.9 collective-permute-start
  8.6 9.6 %collective-permute-start.1 = (f32[7,1,64,256]{3,1,2,0:T(1,128)}, f32[7,1,64,256]{3,1,2,0:T(1,128)}, u32[]{:S(2)}, u32[]{:S(2)}) collective-permute-start(f32[7,1,64,256]{3,1,2,0:T(1,128)} %get-tuple-element.31), channel_id=1, source_target_pairs={{1,0},{2,1},{3,2},{4,3},{5,4},{6,5},{7,6},{8,7},{9,8},{10,9},{11,1... | collective-permute-start | bytes 1376264 | tf_op jit(solution)/shard_map/ppermute | solution.py:28
  18.3 1.9 collective-permute-start.2
  20.3 8.8 %collective-permute-start.3 = (f32[1,64,256]{2,0,1:T(1,128)S(1)}, f32[1,64,256]{2,0,1:T(1,128)S(1)}, u32[]{:S(2)}, u32[]{:S(2)}) collective-permute-start(f32[1,64,256]{2,0,1:T(1,128)S(1)} %copy.188), channel_id=1, source_target_pairs={{1,0},{2,1},{3,2},{4,3},{5,4},{6,5},{7,6},{8,7},{9,8},{10,9},{11,1... | collective-permute-start | bytes 196616 | tf_op jit(solution)/shard_map/ppermute | solution.py:28
  45.2 74.0 %psum.7 = f32[8]{0:T(128)S(1)} all-reduce(f32[8]{0:T(128)S(1)} %fusion.98), channel_id=1, replica_groups=mesh['zone'=8,'brick'=32] {'zone','brick'}, use_global_device_ids=true, to_apply=%region_3.4 | all-reduce | flops 8 | bytes 64 | tf_op jit(solution)/shard_map/psum | solution.py:146
  119.9 26.4 %all-gather = f32[16,8,256]{2,1,0:T(8,128)S(1)} all-gather(f32[2,8,256]{2,1,0:T(8,128)S(1)} %pad_maximum_fusion.16), channel_id=2, replica_groups=mesh['zone'=8,'brick'=32] {'zone'}, dimensions={0}, use_global_device_ids=true | all-gather | bytes 147456 | tf_op jit(solution)/shard_map/all_gather | solution.py:153
  153.0 2.2 copy.269
  155.2 2.2 copy.270
  164.2 6.4 %add_subtract_fusion = (f32[8,64,256]{2,0,1:T(8,128)S(1)}, f32[8,64,256]{2,0,1:T(8,128)S(1)}, f32[8,64,256]{2,0,1:T(8,128)S(1)}, f32[8,64,256]{2,0,1:T(8,128)S(1)}) fusion(f32[8,64,255]{2,0,1:T(8,128)S(1)} %get-tuple-element.108, f32[8,64,255]{2,0,1:T(8,128)S(1)} %get-tuple-element.109, f32[8,63,256]{2,0,1:T(8,128)} %get-tuple-element.106, ...), kind=kLoop, calls=%fused_computation.125 | loop fusion | flops 12058624 | bytes 20738048 | tf_op jit(solution)/shard_map/sub | solution.py:141
  173.6 2.6 %multiply_subtract_fusion = f32[8,64,256]{2,0,1:T(8,128)S(1)} fusion(f32[8,64,255]{2,0,1:T(8,128)S(1)} %copy-done.18, f32[8,64,255]{2,0,1:T(8,128)S(1)} %copy-done.17, f32[8,63,256]{2,0,1:T(8,128)S(1)} %copy-done.22, f32[8,63,256]{2,0,1:T(8,128)S(1)} %copy-done.21, f32[7,8,64,256]{3,1,2,0:T(8,128)S(1)} %copy-done.1, ...), kind=kLoop, calls=%fused_computation.126 | loop fusion | flops 5373952 | bytes 10334208 | tf_op jit(solution)/shard_map/sub | solution.py:140
  176.3 2.2 collective-permute-start.4
  178.5 2.4 collective-permute-start.5
  181.9 8.0 %collective-permute-done.5 = f32[1,64,256]{2,0,1:T(1,128)S(1)} collective-permute-done((f32[1,64,256]{2,0,1:T(1,128)S(1)}, f32[1,64,256]{2,0,1:T(1,128)S(1)}, u32[]{:S(2)}, u32[]{:S(2)}) %collective-permute-start.5) | collective-permute-done | bytes 65568 | tf_op jit(solution)/shard_map/ppermute | solution.py:26
  189.9 2.5 fusion.47
  192.8 1.9 collective-permute-start.6
  194.7 8.8 %collective-permute-start.7 = (f32[1,64,256]{2,0,1:T(1,128)S(1)}, f32[1,64,256]{2,0,1:T(1,128)S(1)}, u32[]{:S(2)}, u32[]{:S(2)}) collective-permute-start(f32[1,64,256]{2,0,1:T(1,128)S(1)} %get-tuple-element.67), channel_id=1, source_target_pairs={{1,0},{2,1},{3,2},{4,3},{5,4},{6,5},{7,6},{8,7},{9,8},{10,9},{11,1... | collective-permute-start | bytes 196616 | tf_op jit(solution)/shard_map/ppermute | solution.py:28
  206.3 1.9 collective-permute-start.8
  208.2 8.8 %collective-permute-start.9 = (f32[1,64,256]{2,0,1:T(1,128)S(1)}, f32[1,64,256]{2,0,1:T(1,128)S(1)}, u32[]{:S(2)}, u32[]{:S(2)}) collective-permute-start(f32[1,64,256]{2,0,1:T(1,128)S(1)} %get-tuple-element.61), channel_id=1, source_target_pairs={{1,0},{2,1},{3,2},{4,3},{5,4},{6,5},{7,6},{8,7},{9,8},{10,9},{11,1... | collective-permute-start | bytes 196616 | tf_op jit(solution)/shard_map/ppermute | solution.py:28
  219.9 1.9 collective-permute-start.10
  221.8 9.0 %collective-permute-start.11 = (f32[1,64,256]{2,0,1:T(1,128)S(1)}, f32[1,64,256]{2,0,1:T(1,128)S(1)}, u32[]{:S(2)}, u32[]{:S(2)}) collective-permute-start(f32[1,64,256]{2,0,1:T(1,128)S(1)} %get-tuple-element.55), channel_id=1, source_target_pairs={{1,0},{2,1},{3,2},{4,3},{5,4},{6,5},{7,6},{8,7},{9,8},{10,9},{11,1... | collective-permute-start | bytes 196616 | tf_op jit(solution)/shard_map/ppermute | solution.py:28
  234.6 8.8 %collective-permute-start.12 = (f32[1,64,256]{2,0,1:T(1,128)S(1)}, f32[1,64,256]{2,0,1:T(1,128)S(1)}, u32[]{:S(2)}, u32[]{:S(2)}) collective-permute-start(f32[1,64,256]{2,0,1:T(1,128)S(1)} %get-tuple-element.44), channel_id=1, source_target_pairs={{1,0},{2,1},{3,2},{4,3},{5,4},{6,5},{7,6},{8,7},{9,8},{10,9},{11,1... | collective-permute-start | bytes 196616 | tf_op jit(solution)/shard_map/ppermute | solution.py:28
  243.4 1.9 collective-permute-start.13
  245.6 8.5 %collective-permute-done.13 = f32[1,64,256]{2,0,1:T(1,128)S(1)} collective-permute-done((f32[1,64,256]{2,0,1:T(1,128)S(1)}, f32[1,64,256]{2,0,1:T(1,128)S(1)}, u32[]{:S(2)}, u32[]{:S(2)}) %collective-permute-start.13) | collective-permute-done | bytes 65568 | tf_op jit(solution)/shard_map/ppermute | solution.py:26
  (136 shorter events, 45.3 us)
Async XLA Ops:
  4.7 24.5 %copy-start = (f32[7,8,64,256]{3,1,2,0:T(8,128)}, f32[7,8,64,256]{3,1,2,0:T(8,128)S(1)}, u32[]{:S(2)}) copy-start(f32[7,8,64,256]{3,1,2,0:T(8,128)S(1)} %bitcast_dynamic-update-slice_fusion) | copy-start | bytes 11010052
  6.7 156.8 %collective-permute-start = (f32[7,1,64,256]{3,1,2,0:T(1,128)}, f32[7,1,64,256]{3,1,2,0:T(1,128)}, u32[]{:S(2)}, u32[]{:S(2)}) collective-permute-start(f32[7,1,64,256]{3,1,2,0:T(1,128)} %get-tuple-element.32), channel_id=1, source_target_pairs={{0,1},{1,2},{2,3},{3,4},{4,5},{5,6},{6,7},{7,8},{8,9},{9,10},{10,1... | collective-permute-start | bytes 1376264 | tf_op jit(solution)/shard_map/ppermute | solution.py:26
  8.6 154.8 %collective-permute-start.1 = (f32[7,1,64,256]{3,1,2,0:T(1,128)}, f32[7,1,64,256]{3,1,2,0:T(1,128)}, u32[]{:S(2)}, u32[]{:S(2)}) collective-permute-start(f32[7,1,64,256]{3,1,2,0:T(1,128)} %get-tuple-element.31), channel_id=1, source_target_pairs={{1,0},{2,1},{3,2},{4,3},{5,4},{6,5},{7,6},{8,7},{9,8},{10,9},{11,1... | collective-permute-start | bytes 1376264 | tf_op jit(solution)/shard_map/ppermute | solution.py:28
  18.3 163.6 %collective-permute-start.2 = (f32[1,64,256]{2,0,1:T(1,128)S(1)}, f32[1,64,256]{2,0,1:T(1,128)S(1)}, u32[]{:S(2)}, u32[]{:S(2)}) collective-permute-start(f32[1,64,256]{2,0,1:T(1,128)S(1)} %copy.185), channel_id=1, source_target_pairs={{0,1},{1,2},{2,3},{3,4},{4,5},{5,6},{6,7},{7,8},{8,9},{9,10},{10,1... | collective-permute-start | bytes 196616 | tf_op jit(solution)/shard_map/ppermute | solution.py:26
  20.3 161.6 %collective-permute-start.3 = (f32[1,64,256]{2,0,1:T(1,128)S(1)}, f32[1,64,256]{2,0,1:T(1,128)S(1)}, u32[]{:S(2)}, u32[]{:S(2)}) collective-permute-start(f32[1,64,256]{2,0,1:T(1,128)S(1)} %copy.188), channel_id=1, source_target_pairs={{1,0},{2,1},{3,2},{4,3},{5,4},{6,5},{7,6},{8,7},{9,8},{10,9},{11,1... | collective-permute-start | bytes 196616 | tf_op jit(solution)/shard_map/ppermute | solution.py:28
  29.2 11.4 %copy-start.3 = (f32[8,64,256]{2,0,1:T(8,128)}, f32[8,64,256]{2,0,1:T(8,128)S(1)}, u32[]{:S(2)}) copy-start(f32[8,64,256]{2,0,1:T(8,128)S(1)} %get-tuple-element.35) | copy-start | bytes 1572868
  173.6 16.3 %copy-start.23 = (f32[8,63,256]{2,0,1:T(8,128)S(1)}, f32[8,63,256]{2,0,1:T(8,128)}, u32[]{:S(2)}) copy-start(f32[8,63,256]{2,0,1:T(8,128)} %copy.271) | copy-start | bytes 1548292
  173.6 16.3 %copy-start.24 = (f32[8,63,256]{2,0,1:T(8,128)S(1)}, f32[8,63,256]{2,0,1:T(8,128)}, u32[]{:S(2)}) copy-start(f32[8,63,256]{2,0,1:T(8,128)} %copy.272) | copy-start | bytes 1548292
  176.2 13.7 %copy-start.8 = (f32[8,64,255]{2,0,1:T(8,128)S(1)}, f32[8,64,255]{2,0,1:T(8,128)}, u32[]{:S(2)}) copy-start(f32[8,64,255]{2,0,1:T(8,128)} %get-tuple-element.84) | copy-start | bytes 1566724
  176.2 13.7 %copy-start.9 = (f32[8,64,255]{2,0,1:T(8,128)S(1)}, f32[8,64,255]{2,0,1:T(8,128)}, u32[]{:S(2)}) copy-start(f32[8,64,255]{2,0,1:T(8,128)} %get-tuple-element.85) | copy-start | bytes 1566724
  176.2 13.7 %copy-start.10 = (f32[8,63,256]{2,0,1:T(8,128)S(1)}, f32[8,63,256]{2,0,1:T(8,128)}, u32[]{:S(2)}) copy-start(f32[8,63,256]{2,0,1:T(8,128)} %get-tuple-element.90) | copy-start | bytes 1548292
  176.2 13.7 %copy-start.11 = (f32[8,63,256]{2,0,1:T(8,128)S(1)}, f32[8,63,256]{2,0,1:T(8,128)}, u32[]{:S(2)}) copy-start(f32[8,63,256]{2,0,1:T(8,128)} %get-tuple-element.91) | copy-start | bytes 1548292
  176.2 13.7 %copy-start.15 = (f32[8,64,255]{2,0,1:T(8,128)S(1)}, f32[8,64,255]{2,0,1:T(8,128)}, u32[]{:S(2)}) copy-start(f32[8,64,255]{2,0,1:T(8,128)} %copy.269) | copy-start | bytes 1566724
  176.2 13.7 %copy-start.16 = (f32[8,64,255]{2,0,1:T(8,128)S(1)}, f32[8,64,255]{2,0,1:T(8,128)}, u32[]{:S(2)}) copy-start(f32[8,64,255]{2,0,1:T(8,128)} %copy.270) | copy-start | bytes 1566724
  176.3 5.6 %collective-permute-start.4 = (f32[1,64,256]{2,0,1:T(1,128)S(1)}, f32[1,64,256]{2,0,1:T(1,128)S(1)}, u32[]{:S(2)}, u32[]{:S(2)}) collective-permute-start(f32[1,64,256]{2,0,1:T(1,128)S(1)} %get-tuple-element.68), channel_id=1, source_target_pairs={{1,0},{2,1},{3,2},{4,3},{5,4},{6,5},{7,6},{8,7},{9,8},{10,9},{11,1... | collective-permute-start | bytes 196616 | tf_op jit(solution)/shard_map/ppermute | solution.py:28
  178.5 11.4 %collective-permute-start.5 = (f32[1,64,256]{2,0,1:T(1,128)S(1)}, f32[1,64,256]{2,0,1:T(1,128)S(1)}, u32[]{:S(2)}, u32[]{:S(2)}) collective-permute-start(f32[1,64,256]{2,0,1:T(1,128)S(1)} %get-tuple-element.69), channel_id=1, source_target_pairs={{0,1},{1,2},{2,3},{3,4},{4,5},{5,6},{6,7},{7,8},{8,9},{9,10},{10,1... | collective-permute-start | bytes 196616 | tf_op jit(solution)/shard_map/ppermute | solution.py:26
  192.8 10.8 %collective-permute-start.6 = (f32[1,64,256]{2,0,1:T(1,128)S(1)}, f32[1,64,256]{2,0,1:T(1,128)S(1)}, u32[]{:S(2)}, u32[]{:S(2)}) collective-permute-start(f32[1,64,256]{2,0,1:T(1,128)S(1)} %get-tuple-element.66), channel_id=1, source_target_pairs={{0,1},{1,2},{2,3},{3,4},{4,5},{5,6},{6,7},{7,8},{8,9},{9,10},{10,1... | collective-permute-start | bytes 196616 | tf_op jit(solution)/shard_map/ppermute | solution.py:26
  194.7 10.7 %collective-permute-start.7 = (f32[1,64,256]{2,0,1:T(1,128)S(1)}, f32[1,64,256]{2,0,1:T(1,128)S(1)}, u32[]{:S(2)}, u32[]{:S(2)}) collective-permute-start(f32[1,64,256]{2,0,1:T(1,128)S(1)} %get-tuple-element.67), channel_id=1, source_target_pairs={{1,0},{2,1},{3,2},{4,3},{5,4},{6,5},{7,6},{8,7},{9,8},{10,9},{11,1... | collective-permute-start | bytes 196616 | tf_op jit(solution)/shard_map/ppermute | solution.py:28
  206.3 10.8 %collective-permute-start.8 = (f32[1,64,256]{2,0,1:T(1,128)S(1)}, f32[1,64,256]{2,0,1:T(1,128)S(1)}, u32[]{:S(2)}, u32[]{:S(2)}) collective-permute-start(f32[1,64,256]{2,0,1:T(1,128)S(1)} %get-tuple-element.60), channel_id=1, source_target_pairs={{0,1},{1,2},{2,3},{3,4},{4,5},{5,6},{6,7},{7,8},{8,9},{9,10},{10,1... | collective-permute-start | bytes 196616 | tf_op jit(solution)/shard_map/ppermute | solution.py:26
  208.2 10.7 %collective-permute-start.9 = (f32[1,64,256]{2,0,1:T(1,128)S(1)}, f32[1,64,256]{2,0,1:T(1,128)S(1)}, u32[]{:S(2)}, u32[]{:S(2)}) collective-permute-start(f32[1,64,256]{2,0,1:T(1,128)S(1)} %get-tuple-element.61), channel_id=1, source_target_pairs={{1,0},{2,1},{3,2},{4,3},{5,4},{6,5},{7,6},{8,7},{9,8},{10,9},{11,1... | collective-permute-start | bytes 196616 | tf_op jit(solution)/shard_map/ppermute | solution.py:28
  219.9 11.0 %collective-permute-start.10 = (f32[1,64,256]{2,0,1:T(1,128)S(1)}, f32[1,64,256]{2,0,1:T(1,128)S(1)}, u32[]{:S(2)}, u32[]{:S(2)}) collective-permute-start(f32[1,64,256]{2,0,1:T(1,128)S(1)} %get-tuple-element.54), channel_id=1, source_target_pairs={{0,1},{1,2},{2,3},{3,4},{4,5},{5,6},{6,7},{7,8},{8,9},{9,10},{10,1... | collective-permute-start | bytes 196616 | tf_op jit(solution)/shard_map/ppermute | solution.py:26
  221.8 10.7 %collective-permute-start.11 = (f32[1,64,256]{2,0,1:T(1,128)S(1)}, f32[1,64,256]{2,0,1:T(1,128)S(1)}, u32[]{:S(2)}, u32[]{:S(2)}) collective-permute-start(f32[1,64,256]{2,0,1:T(1,128)S(1)} %get-tuple-element.55), channel_id=1, source_target_pairs={{1,0},{2,1},{3,2},{4,3},{5,4},{6,5},{7,6},{8,7},{9,8},{10,9},{11,1... | collective-permute-start | bytes 196616 | tf_op jit(solution)/shard_map/ppermute | solution.py:28
  234.6 11.1 %collective-permute-start.12 = (f32[1,64,256]{2,0,1:T(1,128)S(1)}, f32[1,64,256]{2,0,1:T(1,128)S(1)}, u32[]{:S(2)}, u32[]{:S(2)}) collective-permute-start(f32[1,64,256]{2,0,1:T(1,128)S(1)} %get-tuple-element.44), channel_id=1, source_target_pairs={{1,0},{2,1},{3,2},{4,3},{5,4},{6,5},{7,6},{8,7},{9,8},{10,9},{11,1... | collective-permute-start | bytes 196616 | tf_op jit(solution)/shard_map/ppermute | solution.py:28
  243.4 10.7 %collective-permute-start.13 = (f32[1,64,256]{2,0,1:T(1,128)S(1)}, f32[1,64,256]{2,0,1:T(1,128)S(1)}, u32[]{:S(2)}, u32[]{:S(2)}) collective-permute-start(f32[1,64,256]{2,0,1:T(1,128)S(1)} %get-tuple-element.45), channel_id=1, source_target_pairs={{0,1},{1,2},{2,3},{3,4},{4,5},{5,6},{6,7},{7,8},{8,9},{9,10},{10,1... | collective-permute-start | bytes 196616 | tf_op jit(solution)/shard_map/ppermute | solution.py:26
  (17 other events, 47.6 us)
where the time goes:
time: 257 us; the launch traced here: 256 us
  blocking collectives  100 us (39%)
  starting transfers between devices  69.9 us (27%)
  local copies, waits for them, and re-layouts  36.6 us (14%)
  other arithmetic  21.9 us (9%)
  waiting for transfers between devices  21.6 us (8%)
  between operations  5.9 us (2%)
    psum x1, blocking collectives, on_device(): totals = lax.psum(choose * jnp.sum(solvent[:, -1, :]), ('zone', 'brick'))  74 us
    ppermute x7, starting transfers between devices, extended(): lax.ppermute(head, axis, [((i + 1) % count, i) for i in range(ends)])  56 us
    all_gather x1, blocking collectives, on_device(): gathered = lax.all_gather(planes, 'zone', axis=0, tiled=True)  26.4 us
    unnamed x70, local copies, waits for them, and re-layouts  18.1 us
    ppermute x7, waiting for transfers between devices, extended(): lax.ppermute(tail, axis, [(i, (i + 1) % count) for i in range(ends)])  16.4 us
    ppermute x7, starting transfers between devices, extended(): lax.ppermute(tail, axis, [(i, (i + 1) % count) for i in range(ends)])  13.9 us
    slice x12, local copies, waits for them, and re-layouts, shifted_down(): inner = lax.slice_in_dim(values, 0, values.shape[axis] - 1, axis=axis)  9.19 us
    sub x1, other arithmetic, on_device(): solv_new = solv_new - drying  6.42 us
  transfers between devices with their start and end apart: 14, of which 5 were waited for; matrix products, arithmetic and copies ran while one was open for 16% of the time, Pallas kernels for 0%

commit v1 on v0

v1 whole, which is shorter than its diff:
```python
import jax
import jax.numpy as jnp
from jax import lax
from jax.sharding import PartitionSpec as P

ITERS = 4
ALL = ("zone", "brick")
REDUCE_SLOTS = 16384


time_step = 0.2
viscosity = 0.1
diffusivity = 0.1
buoyancy = 0.5
evaporation = 0.5
latent_heat = 0.8
solvent_limit = 0.2


def neighbours(head, tail):
    count = lax.axis_size(ALL)
    from_left = lax.ppermute(tail, ALL, [(i, i + 1) for i in range(count - 1)])
    from_right = lax.ppermute(head, ALL, [(i + 1, i) for i in range(count - 1)])
    return from_left, from_right


def shifted_down(values, axis):
    border = jnp.zeros_like(lax.slice_in_dim(values, 0, 1, axis=axis))
    inner = lax.slice_in_dim(values, 0, values.shape[axis] - 1, axis=axis)
    return jnp.concatenate([border, inner], axis=axis)


def shifted_up(values, axis):
    border = jnp.zeros_like(lax.slice_in_dim(values, 0, 1, axis=axis))
    inner = lax.slice_in_dim(values, 1, values.shape[axis], axis=axis)
    return jnp.concatenate([inner, border], axis=axis)


def momentum(vel2, pres5, heat1, poro5):
    open_here = poro5[4:14]
    pressure_mid = pres5[4:14]
    parts = []
    for component in range(3):
        values = vel2[component]
        centre = values[1:-1]
        laplacian = values[:-2] + values[2:] + shifted_down(centre, 1) + shifted_up(centre, 1)
        laplacian = laplacian + shifted_down(centre, 2) + shifted_up(centre, 2) - 6.0 * centre
        if component == 0:
            gradient = 0.5 * (pres5[5:15] - pres5[3:13])
        else:
            gradient = 0.5 * (
                shifted_up(pressure_mid, component) - shifted_down(pressure_mid, component)
            )
        forcing = viscosity * laplacian - gradient
        if component == 1:
            forcing = forcing + buoyancy * heat1
        parts.append(open_here * (centre + time_step * forcing))
    return parts


def divergence(star):
    result = 0.5 * (star[0][2:] - star[0][:-2])
    middle = star[1][1:-1]
    result = result + 0.5 * (shifted_up(middle, 1) - shifted_down(middle, 1))
    across = star[2][1:-1]
    return result + 0.5 * (shifted_up(across, 2) - shifted_down(across, 2))


def transport(scalar_ext, vel_star):
    centre = scalar_ext[1:-1]
    laplacian = scalar_ext[:-2] + scalar_ext[2:] + shifted_down(centre, 1) + shifted_up(centre, 1)
    laplacian = laplacian + shifted_down(centre, 2) + shifted_up(centre, 2) - 6.0 * centre
    advect = jnp.maximum(vel_star[0], 0.0) * (centre - scalar_ext[:-2]) + jnp.minimum(
        vel_star[0], 0.0
    ) * (scalar_ext[2:] - centre)
    for component in (1, 2):
        advect = advect + jnp.maximum(vel_star[component], 0.0) * (
            centre - shifted_down(centre, component)
        )
        advect = advect + jnp.minimum(vel_star[component], 0.0) * (
            shifted_up(centre, component) - centre
        )
    return centre + time_step * (diffusivity * laplacian - advect)


def sweep(pres_ext, open_ext, source):
    open_here = open_ext[1:-1]
    pressure_mid = pres_ext[1:-1]
    face_back = 0.5 * (open_here + open_ext[:-2])
    face_front = 0.5 * (open_here + open_ext[2:])
    numerator = face_back * pres_ext[:-2] + face_front * pres_ext[2:] - source
    denominator = face_back + face_front
    for component in (1, 2):
        face_low = 0.5 * (open_here + shifted_down(open_here, component))
        face_high = 0.5 * (open_here + shifted_up(open_here, component))
        numerator = (
            numerator
            + face_low * shifted_down(pressure_mid, component)
            + face_high * shifted_up(pressure_mid, component)
        )
        denominator = denominator + face_low + face_high
    inside = open_here > 0.0
    return jnp.where(inside, numerator / jnp.where(inside, denominator, 1.0), 0.0)


def on_device_body(
    velocity,
    enthalpy,
    solvent,
    pressure,
    porosity,
    solid_mask,
    nozzle_mask,
    zone_sizes,
    zone_setpoint,
    duct_source,
    duct_span,
):
    cx = enthalpy.shape[0]
    device = lax.axis_index(ALL)

    starts = jnp.cumsum(zone_sizes) - zone_sizes
    zone_here = jnp.sum((device >= starts).astype(jnp.int32)) - 1
    nzones = zone_sizes.shape[0]
    choose = (jnp.arange(nzones, dtype=jnp.int32) == zone_here).astype(jnp.float32)
    mine = choose * jnp.sum(solvent[:, -1, :])
    slots = jnp.zeros((REDUCE_SLOTS,), jnp.float32).at[:nzones].set(mine)
    totals = lax.psum(slots, ALL)[:nzones]

    planes = jnp.stack([enthalpy[:, -1, :], solvent[:, -1, :]])
    rows = lax.axis_size("zone")
    buffer = jnp.zeros((rows,) + planes.shape, jnp.float32)
    buffer = lax.dynamic_update_slice(
        buffer, planes[None], (lax.axis_index("zone"), 0, 0, 0)
    )
    gathered = lax.psum(buffer, "zone")

    narrow_head = jnp.concatenate(
        [velocity[:, 0:2].reshape((6,) + enthalpy.shape[1:]), pressure[0:2],
         enthalpy[0:1], solvent[0:1]], axis=0)
    narrow_tail = jnp.concatenate(
        [velocity[:, cx - 2:].reshape((6,) + enthalpy.shape[1:]), pressure[cx - 2:],
         enthalpy[cx - 1:], solvent[cx - 1:]], axis=0)
    wide_head = jnp.concatenate([pressure[0:5], porosity[0:5]], axis=0)
    wide_tail = jnp.concatenate([pressure[cx - 5:], porosity[cx - 5:]], axis=0)
    n_left, n_right = neighbours(narrow_head, narrow_tail)
    w_left, w_right = neighbours(wide_head, wide_tail)

    vel2 = jnp.concatenate(
        [n_left[0:6].reshape((3, 2) + enthalpy.shape[1:]), velocity,
         n_right[0:6].reshape((3, 2) + enthalpy.shape[1:])], axis=1)
    pres5 = jnp.concatenate([w_left[0:5], pressure, w_right[0:5]], axis=0)
    poro5 = jnp.concatenate([w_left[5:10], porosity, w_right[5:10]], axis=0)
    heat1 = jnp.concatenate([n_left[8:9], enthalpy, n_right[8:9]], axis=0)
    solv1 = jnp.concatenate([n_left[9:10], solvent, n_right[9:10]], axis=0)

    star = momentum(vel2, pres5, heat1, poro5)
    source = divergence(star) / time_step
    vel_star = jnp.stack([part[1:-1] for part in star])

    s_left, s_right = neighbours(source[0:4], source[cx - 4:])
    source4 = jnp.concatenate([s_left, source, s_right], axis=0)

    heat_new = transport(heat1, vel_star)
    solv_new = transport(solv1, vel_star)
    drying = time_step * evaporation * solid_mask.astype(jnp.float32) * solvent
    heat_new = heat_new - latent_heat * drying
    solv_new = solv_new - drying

    iterate = pres5
    for iteration in range(ITERS):
        lo = iteration
        hi = poro5.shape[0] - iteration
        iterate = sweep(iterate, poro5[lo:hi], source4[lo:hi - 2])
    iterate, heat_new, solv_new, totals, gathered = lax.optimization_barrier(
        (iterate, heat_new, solv_new, totals, gathered))

    counts = zone_sizes.astype(jnp.float32) * (cx * enthalpy.shape[2])
    means = totals / counts
    fresh_all = means / (means + solvent_limit)
    fresh = jnp.sum(choose * fresh_all)
    target = jnp.sum(choose * zone_setpoint)
    arrived = lax.dynamic_index_in_dim(gathered, duct_source[0], axis=0, keepdims=False)
    supply_heat = (1.0 - fresh) * arrived[0] + fresh * target
    supply_solv = (1.0 - fresh) * arrived[1]
    column = jnp.arange(enthalpy.shape[2], dtype=jnp.int32)
    inside_box = (column >= duct_span[0, 0]) & (column < duct_span[0, 0] + duct_span[0, 1])
    jets = (nozzle_mask > 0) & inside_box[None, :]
    heat_layer = jnp.where(jets, supply_heat, heat_new[:, 0, :])
    solv_layer = jnp.where(jets, supply_solv, solv_new[:, 0, :])
    enthalpy_new = jnp.concatenate([heat_layer[:, None, :], heat_new[:, 1:, :]], axis=1)
    solvent_new = jnp.concatenate([solv_layer[:, None, :], solv_new[:, 1:, :]], axis=1)

    final = iterate[1:-1]
    gradients = jnp.stack(
        [
            0.5 * (iterate[2:] - iterate[:-2]),
            0.5 * (shifted_up(final, 1) - shifted_down(final, 1)),
            0.5 * (shifted_up(final, 2) - shifted_down(final, 2)),
        ]
    )
    velocity_new = vel_star - time_step * porosity[None] * gradients
    return (velocity_new, enthalpy_new, solvent_new, final)


def solution(mesh):
    placed = (
        P(None, ALL, None, None),
        P(ALL, None, None),
        P(ALL, None, None),
        P(ALL, None, None),
        P(ALL, None, None),
        P(ALL, None, None),
        P(ALL, None),
        P(),
        P(),
        P(ALL),
        P(ALL, None),
    )
    return jax.shard_map(
        on_device_body,
        mesh=mesh,
        in_specs=placed,
        out_specs=(
            P(None, ALL, None, None),
            P(ALL, None, None),
            P(ALL, None, None),
            P(ALL, None, None),
        ),
        check_vma=False,
    )
```

time: 257 us -> 377 us (1.47)
  waiting for transfers between devices: 21.6 us -> 222 us
  blocking collectives: 100 us -> 0 us
  starting transfers between devices: 69.9 us -> 33.2 us
  local copies, waits for them, and re-layouts: 36.6 us -> 63.7 us
  other arithmetic: 21.9 us -> 36.5 us
  between operations: 5.9 us -> 19.4 us
    psum x0 -> x2, waiting for transfers between devices: none -> 222 us  [the longest x1 222 us: on_device_body(): totals = lax.psum(slots, ALL)[:nzones]]
    psum x1 -> x0, blocking collectives: 74 us -> none  [on_device(): totals = lax.psum(choose * jnp.sum(solvent[:, -1, :]), ('zone', 'brick'))]
    ppermute x14 -> x6, starting transfers between devices: 69.9 us -> 33.1 us  [the longest x3 25.5 us: neighbours(): from_right = lax.ppermute(head, ALL, [(i + 1, i) for i in range(count - 1)])]
    all_gather x1 -> x0, blocking collectives: 26.4 us -> none  [on_device(): gathered = lax.all_gather(planes, 'zone', axis=0, tiled=True)]
    ppermute x14 -> x6, waiting for transfers between devices: 21.6 us -> 0.11 us  [the longest x3 0.1 us: neighbours(): from_right = lax.ppermute(head, ALL, [(i + 1, i) for i in range(count - 1)])]
    slice x12 -> x24, local copies, waits for them, and re-layouts: 9.19 us -> 25 us  [shifted_down(): inner = lax.slice_in_dim(values, 0, values.shape[axis] - 1, axis=axis)]
    mul x3 -> x5, other arithmetic: 1.83 us -> 8.97 us  [the longest x3 7.19 us: momentum(): parts.append(open_here * (centre + time_step * forcing))]
    slice x12 -> x27, local copies, waits for them, and re-layouts: 3.87 us -> 10.2 us  [the longest x4 2.65 us: on_device_body(): poro5 = jnp.concatenate([w_left[5:10], porosity, w_right[5:10]], axis=0)]
  transfers between devices with their start and end apart: 14 -> 8, of which waited for: 5 -> 2; matrix products, arithmetic and copies ran while one was open for 16% -> 20% of each run, Pallas kernels for 0% -> 0%
where the time goes in v1:
time: 377 us; the launch traced here: 375 us
  waiting for transfers between devices  222 us (59%)
  local copies, waits for them, and re-layouts  63.7 us (17%)
  other arithmetic  36.5 us (10%)
  starting transfers between devices  33.2 us (9%)
  between operations  19.4 us (5%)
    psum x1, waiting for transfers between devices, on_device_body(): totals = lax.psum(slots, ALL)[:nzones]  222 us
    ppermute x3, starting transfers between devices, neighbours(): from_right = lax.ppermute(head, ALL, [(i + 1, i) for i in range(count - 1)])  25.5 us
    slice x24, local copies, waits for them, and re-layouts, shifted_down(): inner = lax.slice_in_dim(values, 0, values.shape[axis] - 1, axis=axis)  25 us
    unnamed x99, local copies, waits for them, and re-layouts  18.3 us
    ppermute x3, starting transfers between devices, neighbours(): from_left = lax.ppermute(tail, ALL, [(i, i + 1) for i in range(count - 1)])  7.64 us
  transfers between devices with their start and end apart: 8, of which 2 were waited for; matrix products, arithmetic and copies ran while one was open for 20% of the time, Pallas kernels for 0%

profile of v1, /device:TPU:32, one launch (start us, length us, event | category | flops | bytes accessed | tf_op | source)
XLA Modules:
  0.0 375.0 jit_solution(15690611356648640355)
XLA Ops:
  9.7 2.0 collective-permute-start.2
  12.7 9.6 %collective-permute-start.3 = (f32[10,64,256]{2,1,0:T(8,128)}, f32[10,64,256]{2,1,0:T(8,128)}, u32[]{:S(2)}, u32[]{:S(2)}) collective-permute-start(f32[10,64,256]{2,1,0:T(8,128)} %pad_maximum_fusion.12), channel_id=1, source_target_pairs={{1,0},{2,1},{3,2},{4,3},{5,4},{6,5},{7,6},{8,7},{9,8},{10,9},{11,1... | collective-permute-start | bytes 1966088 | tf_op jit(solution)/shard_map/ppermute | solution.py:23
  23.4 1.9 collective-permute-start
  26.2 8.7 %collective-permute-start.1 = (f32[10,64,256]{2,1,0:T(8,128)}, f32[10,64,256]{2,1,0:T(8,128)}, u32[]{:S(2)}, u32[]{:S(2)}) collective-permute-start(f32[10,64,256]{2,1,0:T(8,128)} %pad_maximum_fusion.10), channel_id=1, source_target_pairs={{1,0},{2,1},{3,2},{4,3},{5,4},{6,5},{7,6},{8,7},{9,8},{10,9},{11,1... | collective-permute-start | bytes 1966088 | tf_op jit(solution)/shard_map/ppermute | solution.py:23
  51.2 3.5 fusion.143
  54.7 222.0 %all-reduce.68.cloned.1.call-done = f32[16384]{0:T(1024)} async-done(((f32[16384]{0:T(1024)}), f32[16384]{0:T(1024)}) %all-reduce.68.cloned.1.call-update) | async-done | bytes 65552 | tf_op jit(solution)/shard_map/psum | solution.py:128
  282.7 2.1 fusion.154
  284.8 1.7 fusion.155
  289.2 1.6 fusion.140
  295.8 1.6 fusion.137
  297.4 1.8 fusion.135
  299.2 1.6 fusion.134
  300.8 1.7 fusion.133
  304.1 1.8 fusion.131
  306.8 3.1 fusion.75
  313.1 2.9 fusion.13
  319.1 3.7 collective-permute-start.4
  322.8 7.1 %collective-permute-start.5 = (f32[4,64,256]{2,0,1:T(4,128)S(1)}, f32[4,64,256]{2,0,1:T(4,128)S(1)}, u32[]{:S(2)}, u32[]{:S(2)}) collective-permute-start(f32[4,64,256]{2,0,1:T(4,128)S(1)} %get-tuple-element.139), channel_id=1, source_target_pairs={{1,0},{2,1},{3,2},{4,3},{5,4},{6,5},{7,6},{8,7},{9,8},{10,9},{11,1... | collective-permute-start | bytes 786440 | tf_op jit(solution)/shard_map/ppermute | solution.py:23
  330.4 2.6 fusion.104
  335.1 1.6 copy_subtract_fusion
  338.9 2.0 fusion.58
  343.3 2.1 fusion.48
  347.7 2.1 fusion.40
  351.7 2.3 fusion.31
  (196 shorter events, 64.2 us)
Async XLA Ops:
  7.2 269.5 %all-reduce.68.cloned.1.call-start = ((), (), s32[]{:S(2)}) async-start(), calls=%async_computation | async-start | bytes 131072 | tf_op jit(solution)/shard_map/psum | solution.py:128
  9.7 12.6 %copy-start.24 = (f32[8,64,256]{2,1,0:T(8,128)S(1)}, f32[8,64,256]{2,1,0:T(8,128)}, u32[]{:S(2)}) copy-start(f32[8,64,256]{2,1,0:T(8,128)} %param.17) | copy-start | bytes 1572868
  9.7 267.0 %collective-permute-start.2 = (f32[10,64,256]{2,1,0:T(8,128)}, f32[10,64,256]{2,1,0:T(8,128)}, u32[]{:S(2)}, u32[]{:S(2)}) collective-permute-start(f32[10,64,256]{2,1,0:T(8,128)} %pad_maximum_fusion.11), channel_id=1, source_target_pairs={{0,1},{1,2},{2,3},{3,4},{4,5},{5,6},{6,7},{7,8},{8,9},{9,10},{10,1... | collective-permute-start | bytes 1966088 | tf_op jit(solution)/shard_map/ppermute | solution.py:22
  12.7 265.4 %collective-permute-start.3 = (f32[10,64,256]{2,1,0:T(8,128)}, f32[10,64,256]{2,1,0:T(8,128)}, u32[]{:S(2)}, u32[]{:S(2)}) collective-permute-start(f32[10,64,256]{2,1,0:T(8,128)} %pad_maximum_fusion.12), channel_id=1, source_target_pairs={{1,0},{2,1},{3,2},{4,3},{5,4},{6,5},{7,6},{8,7},{9,8},{10,9},{11,1... | collective-permute-start | bytes 1966088 | tf_op jit(solution)/shard_map/ppermute | solution.py:23
  23.4 258.0 %collective-permute-start = (f32[10,64,256]{2,1,0:T(8,128)}, f32[10,64,256]{2,1,0:T(8,128)}, u32[]{:S(2)}, u32[]{:S(2)}) collective-permute-start(f32[10,64,256]{2,1,0:T(8,128)} %pad_maximum_fusion.9), channel_id=1, source_target_pairs={{0,1},{1,2},{2,3},{3,4},{4,5},{5,6},{6,7},{7,8},{8,9},{9,10},{10,1... | collective-permute-start | bytes 1966088 | tf_op jit(solution)/shard_map/ppermute | solution.py:22
  25.3 10.9 %copy-start.45 = (s32[8]{0:T(128)S(1)}, s32[8]{0:T(128)}, u32[]{:S(2)}) copy-start(s32[8]{0:T(128)} %param.20) | copy-start | bytes 100
  26.2 260.2 %collective-permute-start.1 = (f32[10,64,256]{2,1,0:T(8,128)}, f32[10,64,256]{2,1,0:T(8,128)}, u32[]{:S(2)}, u32[]{:S(2)}) collective-permute-start(f32[10,64,256]{2,1,0:T(8,128)} %pad_maximum_fusion.10), channel_id=1, source_target_pairs={{1,0},{2,1},{3,2},{4,3},{5,4},{6,5},{7,6},{8,7},{9,8},{10,9},{11,1... | collective-permute-start | bytes 1966088 | tf_op jit(solution)/shard_map/ppermute | solution.py:23
  39.0 315.5 %all-reduce.70.cloned.1.call-start = ((), (), s32[]{:S(2)}) async-start(), calls=%async_computation.1 | async-start | bytes 262144 | tf_op jit(solution)/shard_map/psum | solution.py:136
  42.1 2.1 copy-start.44
  42.1 2.7 copy-start.46
  304.1 2.7 copy-start
  309.9 3.2 copy-start.21
  309.9 3.2 copy-start.22
  318.7 11.6 %copy-start.37 = (f32[8,63,256]{2,0,1:T(8,128)S(1)}, f32[8,63,256]{2,0,1:T(8,128)}, u32[]{:S(2)}) copy-start(f32[8,63,256]{2,0,1:T(8,128)} %get-tuple-element.135) | copy-start | bytes 1548292
  318.7 11.6 %copy-start.41 = (s32[8,64,256]{2,1,0:T(8,128)S(1)}, s32[8,64,256]{2,1,0:T(8,128)}, u32[]{:S(2)}) copy-start(s32[8,64,256]{2,1,0:T(8,128)} %param.18) | copy-start | bytes 1572868
  319.0 11.3 %copy-start.3 = (f32[8,64,255]{2,0,1:T(8,128)S(1)}, f32[8,64,255]{2,0,1:T(8,128)}, u32[]{:S(2)}) copy-start(f32[8,64,255]{2,0,1:T(8,128)} %get-tuple-element.131) | copy-start | bytes 1566724
  319.0 11.3 %copy-start.27 = (f32[8,64,255]{2,0,1:T(8,128)S(1)}, f32[8,64,255]{2,0,1:T(8,128)}, u32[]{:S(2)}) copy-start(f32[8,64,255]{2,0,1:T(8,128)} %get-tuple-element.136) | copy-start | bytes 1566724
  319.0 11.3 %copy-start.28 = (f32[8,64,255]{2,0,1:T(8,128)S(1)}, f32[8,64,255]{2,0,1:T(8,128)}, u32[]{:S(2)}) copy-start(f32[8,64,255]{2,0,1:T(8,128)} %get-tuple-element.137) | copy-start | bytes 1566724
  319.0 11.3 %copy-start.36 = (f32[8,63,256]{2,0,1:T(8,128)S(1)}, f32[8,63,256]{2,0,1:T(8,128)}, u32[]{:S(2)}) copy-start(f32[8,63,256]{2,0,1:T(8,128)} %get-tuple-element.134) | copy-start | bytes 1548292
  319.1 17.9 %collective-permute-start.4 = (f32[4,64,256]{2,0,1:T(4,128)S(1)}, f32[4,64,256]{2,0,1:T(4,128)S(1)}, u32[]{:S(2)}, u32[]{:S(2)}) collective-permute-start(f32[4,64,256]{2,0,1:T(4,128)S(1)} %get-tuple-element.138), channel_id=1, source_target_pairs={{0,1},{1,2},{2,3},{3,4},{4,5},{5,6},{6,7},{7,8},{8,9},{9,10},{10,1... | collective-permute-start | bytes 786440 | tf_op jit(solution)/shard_map/ppermute | solution.py:22
  322.8 14.3 %collective-permute-start.5 = (f32[4,64,256]{2,0,1:T(4,128)S(1)}, f32[4,64,256]{2,0,1:T(4,128)S(1)}, u32[]{:S(2)}, u32[]{:S(2)}) collective-permute-start(f32[4,64,256]{2,0,1:T(4,128)S(1)} %get-tuple-element.139), channel_id=1, source_target_pairs={{1,0},{2,1},{3,2},{4,3},{5,4},{6,5},{7,6},{8,7},{9,8},{10,9},{11,1... | collective-permute-start | bytes 786440 | tf_op jit(solution)/shard_map/ppermute | solution.py:23
  336.7 2.1 copy-start.18
  358.5 2.2 copy-start.43
  358.5 4.2 %copy-start.26 = (f32[8,64,256]{2,0,1:T(8,128)S(1)}, f32[8,64,256]{2,0,1:T(8,128)}, u32[]{:S(2)}) copy-start(f32[8,64,256]{2,0,1:T(8,128)} %get-tuple-element.24) | copy-start | bytes 1572868
  (32 other events, 43.8 us)
Sparse Core Ops, SparseCore 0:
  39.1 237.6 all-reduce.67
  279.3 73.4 all-reduce.69

commit v2 on v1

--- a/solution.py
+++ b/solution.py
@@ -5,7 +5,6 @@
 
 ITERS = 4
 ALL = ("zone", "brick")
-REDUCE_SLOTS = 16384
 
 
 time_step = 0.2
@@ -123,9 +122,12 @@
     zone_here = jnp.sum((device >= starts).astype(jnp.int32)) - 1
     nzones = zone_sizes.shape[0]
     choose = (jnp.arange(nzones, dtype=jnp.int32) == zone_here).astype(jnp.float32)
-    mine = choose * jnp.sum(solvent[:, -1, :])
-    slots = jnp.zeros((REDUCE_SLOTS,), jnp.float32).at[:nzones].set(mine)
-    totals = lax.psum(slots, ALL)[:nzones]
+    totals = choose * jnp.sum(solvent[:, -1, :])
+    count = lax.axis_size(ALL)
+    bit = 1
+    while bit < count:
+        totals = totals + lax.ppermute(totals, ALL, [(i, i ^ bit) for i in range(count)])
+        bit *= 2
 
     planes = jnp.stack([enthalpy[:, -1, :], solvent[:, -1, :]])
     rows = lax.axis_size("zone")
@@ -133,7 +135,11 @@
     buffer = lax.dynamic_update_slice(
         buffer, planes[None], (lax.axis_index("zone"), 0, 0, 0)
     )
-    gathered = lax.psum(buffer, "zone")
+    bit = 1
+    while bit < rows:
+        buffer = buffer + lax.ppermute(buffer, "zone", [(i, i ^ bit) for i in range(rows)])
+        bit *= 2
+    gathered = buffer
 
     narrow_head = jnp.concatenate(
         [velocity[:, 0:2].reshape((6,) + enthalpy.shape[1:]), pressure[0:2],

time: 377 us -> 182 us (0.48)
  waiting for transfers between devices: 222 us -> 33 us
  between operations: 19.4 us -> 6.13 us
  starting transfers between devices: 33.2 us -> 38.2 us
    psum x2 -> x0, waiting for transfers between devices: 222 us -> none  [the longest x1 222 us: on_device_body(): totals = lax.psum(slots, ALL)[:nzones]]
    ppermute x0 -> x11, waiting for transfers between devices: none -> 27.2 us  [the longest x8 23.9 us: on_device_body(): lax.ppermute(totals, ALL, [(i, i ^ bit) for i in range(count)])]
    ppermute x0 -> x11, starting transfers between devices: none -> 11.1 us  [the longest x8 5.62 us: on_device_body(): lax.ppermute(totals, ALL, [(i, i ^ bit) for i in range(count)])]
    ppermute x3, waiting for transfers between devices: 0.1 us -> 5.76 us  [neighbours(): from_right = lax.ppermute(head, ALL, [(i + 1, i) for i in range(count - 1)])]
    ppermute x3, starting transfers between devices: 25.5 us -> 20.7 us  [neighbours(): from_right = lax.ppermute(head, ALL, [(i + 1, i) for i in range(count - 1)])]
    unnamed x99 -> x97, local copies, waits for them, and re-layouts: 18.3 us -> 18.9 us
  transfers between devices with their start and end apart: 8 -> 17, of which waited for: 2 -> 8; matrix products, arithmetic and copies ran while one was open for 20% -> 22% of each run, Pallas kernels for 0% -> 0%
where the time goes in v2:
time: 182 us; the launch traced here: 181 us
  local copies, waits for them, and re-layouts  64.3 us (35%)
  other arithmetic  39.1 us (21%)
  starting transfers between devices  38.2 us (21%)
  waiting for transfers between devices  33 us (18%)
  between operations  6.13 us (3%)
    slice x24, local copies, waits for them, and re-layouts, shifted_down(): inner = lax.slice_in_dim(values, 0, values.shape[axis] - 1, axis=axis)  25 us
    ppermute x8, waiting for transfers between devices, on_device_body(): lax.ppermute(totals, ALL, [(i, i ^ bit) for i in range(count)])  23.9 us
    ppermute x3, starting transfers between devices, neighbours(): from_right = lax.ppermute(head, ALL, [(i + 1, i) for i in range(count - 1)])  20.7 us
    unnamed x97, local copies, waits for them, and re-layouts  18.9 us
    mul x3, other arithmetic, momentum(): parts.append(open_here * (centre + time_step * forcing))  7.39 us
    select_n x4, other arithmetic, sweep(): jnp.where(inside, numerator / jnp.where(inside, denominator, 1.0), 0.0)  6.5 us
    ppermute x3, starting transfers between devices, neighbours(): from_left = lax.ppermute(tail, ALL, [(i, i + 1) for i in range(count - 1)])  6.48 us
    ppermute x3, waiting for transfers between devices, neighbours(): from_right = lax.ppermute(head, ALL, [(i + 1, i) for i in range(count - 1)])  5.76 us
  transfers between devices with their start and end apart: 17, of which 8 were waited for; matrix products, arithmetic and copies ran while one was open for 22% of the time, Pallas kernels for 0%

profile of v2, /device:TPU:32, one launch (start us, length us, event | category | flops | bytes accessed | tf_op | source)
XLA Modules:
  0.0 180.7 jit_solution(16276356062420417936)
XLA Ops:
  9.4 2.5 %collective-permute-start.2 = (f32[10,64,256]{2,1,0:T(8,128)}, f32[10,64,256]{2,1,0:T(8,128)}, u32[]{:S(2)}, u32[]{:S(2)}) collective-permute-start(f32[10,64,256]{2,1,0:T(8,128)} %pad_maximum_fusion.11), channel_id=1, source_target_pairs={{0,1},{1,2},{2,3},{3,4},{4,5},{5,6},{6,7},{7,8},{8,9},{9,10},{10,1... | collective-permute-start | bytes 1966088 | tf_op jit(solution)/shard_map/ppermute | solution.py:21
  12.8 9.8 %collective-permute-start.3 = (f32[10,64,256]{2,1,0:T(8,128)}, f32[10,64,256]{2,1,0:T(8,128)}, u32[]{:S(2)}, u32[]{:S(2)}) collective-permute-start(f32[10,64,256]{2,1,0:T(8,128)} %pad_maximum_fusion.12), channel_id=1, source_target_pairs={{1,0},{2,1},{3,2},{4,3},{5,4},{6,5},{7,6},{8,7},{9,8},{10,9},{11,1... | collective-permute-start | bytes 1966088 | tf_op jit(solution)/shard_map/ppermute | solution.py:22
  27.6 3.6 %fusion.143 = (f32[3,8,64,256]{3,1,2,0:T(8,128)S(1)}, f32[3,10,64,256]{3,1,2,0:T(8,128)}) fusion(f32[3,8,64,256]{3,2,1,0:T(8,128)} %param.11), kind=kLoop, calls=%fused_computation.225 | loop fusion | bytes 4718592 | tf_op args[0]
  40.8 2.0 %copy.183 = f32[8,64,256]{2,1,0:T(8,128)} copy(f32[8,64,256]{2,0,1:T(8,128)} %get-tuple-element.111) | data formatting | bytes 1048576 | tf_op jit(solution)/shard_map/mul | solution.py:208
  48.5 3.4 %collective-permute-done.15 = f32[8,2,8,256]{3,2,1,0:T(8,128)S(1)} collective-permute-done((f32[8,2,8,256]{3,2,1,0:T(8,128)}, f32[8,2,8,256]{3,2,1,0:T(8,128)S(1)}, u32[]{:S(2)}, u32[]{:S(2)}) %collective-permute-start.15) | collective-permute-done | bytes 131104 | tf_op jit(solution)/shard_map/ppermute | solution.py:140
  52.8 3.9 %collective-permute-start.16 = (f32[8,2,8,256]{3,2,1,0:T(8,128)S(1)}, f32[8,2,8,256]{3,2,1,0:T(8,128)S(1)}, u32[]{:S(2)}, u32[]{:S(2)}) collective-permute-start(f32[8,2,8,256]{3,2,1,0:T(8,128)S(1)} %add.638), channel_id=1, source_target_pairs={{0,128},{32,160},{64,192},{96,224},{128,0},{160,32},{192,64},{224,... | collective-permute-start | bytes 393224 | tf_op jit(solution)/shard_map/ppermute | solution.py:140
  57.4 5.1 %collective-permute-done.8 = f32[8]{0:T(128)S(1)} collective-permute-done((f32[8]{0:T(128)S(1)}, f32[8]{0:T(128)S(1)}, u32[]{:S(2)}, u32[]{:S(2)}) %collective-permute-start.8) | collective-permute-done | bytes 64 | tf_op jit(solution)/shard_map/ppermute | solution.py:129
  62.4 4.5 %collective-permute-done.9 = f32[8]{0:T(128)S(1)} collective-permute-done((f32[8]{0:T(128)S(1)}, f32[8]{0:T(128)S(1)}, u32[]{:S(2)}, u32[]{:S(2)}) %collective-permute-start.9) | collective-permute-done | bytes 64 | tf_op jit(solution)/shard_map/ppermute | solution.py:129
  66.9 3.5 %collective-permute-start.10 = (f32[8]{0:T(128)S(1)}, f32[8]{0:T(128)S(1)}, u32[]{:S(2)}, u32[]{:S(2)}) collective-permute-start(f32[8]{0:T(128)S(1)} %add.631), channel_id=1, source_target_pairs={{0,16},{1,17},{2,18},{3,19},{4,20},{5,21},{6,22},{7,23},{8,24},{9,... | collective-permute-start | bytes 104 | tf_op jit(solution)/shard_map/ppermute | solution.py:129
  70.5 3.9 %collective-permute-done.10 = f32[8]{0:T(128)S(1)} collective-permute-done((f32[8]{0:T(128)S(1)}, f32[8]{0:T(128)S(1)}, u32[]{:S(2)}, u32[]{:S(2)}) %collective-permute-start.10) | collective-permute-done | bytes 64 | tf_op jit(solution)/shard_map/ppermute | solution.py:129
  75.7 2.3 %collective-permute-done.11 = f32[8]{0:T(128)S(1)} collective-permute-done((f32[8]{0:T(128)S(1)}, f32[8]{0:T(128)S(1)}, u32[]{:S(2)}, u32[]{:S(2)}) %collective-permute-start.11) | collective-permute-done | bytes 64 | tf_op jit(solution)/shard_map/ppermute | solution.py:129
  78.0 3.6 %collective-permute-done.12 = f32[8]{0:T(128)S(1)} collective-permute-done((f32[8]{0:T(128)S(1)}, f32[8]{0:T(128)S(1)}, u32[]{:S(2)}, u32[]{:S(2)}) %collective-permute-start.12) | collective-permute-done | bytes 64 | tf_op jit(solution)/shard_map/ppermute | solution.py:129
  82.1 4.6 %collective-permute-done.13 = f32[8]{0:T(128)S(1)} collective-permute-done((f32[8]{0:T(128)S(1)}, f32[8]{0:T(128)S(1)}, u32[]{:S(2)}, u32[]{:S(2)}) %collective-permute-start.13) | collective-permute-done | bytes 64 | tf_op jit(solution)/shard_map/ppermute | solution.py:129
  86.6 2.1 %collective-permute-start.1 = (f32[10,64,256]{2,1,0:T(8,128)}, f32[10,64,256]{2,1,0:T(8,128)S(1)}, u32[]{:S(2)}, u32[]{:S(2)}) collective-permute-start(f32[10,64,256]{2,1,0:T(8,128)} %pad_maximum_fusion.10), channel_id=1, source_target_pairs={{1,0},{2,1},{3,2},{4,3},{5,4},{6,5},{7,6},{8,7},{9,8},{10,9},{11,1... | collective-permute-start | bytes 1966088 | tf_op jit(solution)/shard_map/ppermute | solution.py:22
  94.1 2.2 %fusion.154 = (f32[10,63,256]{2,0,1:T(8,128)}, f32[10,63,256]{2,0,1:T(8,128)}, f32[10,63,256]{2,0,1:T(8,128)}, f32[10,63,256]{2,0,1:T(8,128)}) fusion(f32[10,64,256]{2,0,1:T(8,128)S(1)} %get-tuple-element.34, f32[10,64,256]{2,0,1:T(8,128)S(1)} %get-tuple-element.33), kind=kLoop, calls=%fused_computation.236 | loop fusion | bytes 5160960 | tf_op jit(solution)/shard_map/slice | solution.py:28
  97.9 5.8 %collective-permute-done.1 = f32[10,64,256]{2,1,0:T(8,128)S(1)} collective-permute-done((f32[10,64,256]{2,1,0:T(8,128)}, f32[10,64,256]{2,1,0:T(8,128)S(1)}, u32[]{:S(2)}, u32[]{:S(2)}) %collective-permute-start.1) | collective-permute-done | bytes 655392 | tf_op jit(solution)/shard_map/ppermute | solution.py:22
  122.0 3.1 %fusion.75 = f32[10,64,256]{2,0,1:T(8,128)S(1)} fusion(f32[3,10,64,256]{3,1,2,0:T(8,128)S(1)} %get-tuple-element.139, f32[3,8,64,256]{3,1,2,0:T(8,128)S(1)} %get-tuple-element.63, f32[3,2,64,256]{3,1,2,0:T(2,128)S(1)} %copy.162, f32[10,64,255]{2,0,1:T(8,128)S(1)} %get-tuple-element.60, f32[10,64,255]{2,0,1:T(8,128)S(1)} %get-tuple-element.59, ...), kind=kLoop, calls=%fused_computation.104 | loop fusion | flops 2457600 | bytes 8488960 | tf_op jit(solution)/shard_map/mul | solution.py:56
  128.2 2.9 %fusion.13 = f32[10,64,256]{2,0,1:T(8,128)S(1)} fusion(f32[3,8,64,256]{3,1,2,0:T(8,128)S(1)} %get-tuple-element.63, f32[3,2,64,256]{3,1,2,0:T(2,128)S(1)} %copy.162, f32[3,10,64,256]{3,1,2,0:T(8,128)S(1)} %get-tuple-element.139, f32[1,64,256]{2,0,1:T(1,128)S(1)} %copy.178, f32[8,64,256]{2,0,1:T(8,128)S(1)} %copy.177, f32[1,64,256]{2,0,1:T(1,128)S(1)} %copy.176, ...), kind=kLoop, calls=%fused_computation.22 | loop fusion | flops 3112960 | bytes 9128960 | tf_op jit(solution)/shard_map/mul | solution.py:56
  134.4 2.1 %collective-permute-start.4 = (f32[4,64,256]{2,0,1:T(4,128)S(1)}, f32[4,64,256]{2,0,1:T(4,128)S(1)}, u32[]{:S(2)}, u32[]{:S(2)}) collective-permute-start(f32[4,64,256]{2,0,1:T(4,128)S(1)} %get-tuple-element.126), channel_id=1, source_target_pairs={{0,1},{1,2},{2,3},{3,4},{4,5},{5,6},{6,7},{7,8},{8,9},{9,10},{10,1... | collective-permute-start | bytes 786440 | tf_op jit(solution)/shard_map/ppermute | solution.py:21
  136.5 8.8 %collective-permute-start.5 = (f32[4,64,256]{2,0,1:T(4,128)S(1)}, f32[4,64,256]{2,0,1:T(4,128)S(1)}, u32[]{:S(2)}, u32[]{:S(2)}) collective-permute-start(f32[4,64,256]{2,0,1:T(4,128)S(1)} %get-tuple-element.127), channel_id=1, source_target_pairs={{1,0},{2,1},{3,2},{4,3},{5,4},{6,5},{7,6},{8,7},{9,8},{10,9},{11,1... | collective-permute-start | bytes 786440 | tf_op jit(solution)/shard_map/ppermute | solution.py:22
  153.4 2.0 %fusion.58 = (f32[16,64,256]{2,0,1:T(8,128)S(1)}, f32[16,64,256]{2,0,1:T(8,128)S(1)}) fusion(f32[18,64,256]{2,0,1:T(8,128)S(1)} %get-tuple-element.147, f32[18,64,256]{2,0,1:T(8,128)S(1)} %get-tuple-element.146, f32[16,64,255]{2,0,1:T(8,128)S(1)} %get-tuple-element.56, f32[16,64,255]{2,0,1:T(8,128)S(1)} %get-tuple-element.54, ...), kind=kLoop, calls=%fused_computation.80 | loop fusion | flops 9175040 | bytes 16695296 | tf_op jit(solution)/shard_map/jit(_where)/select_n | solution.py:102
  157.8 2.0 %fusion.48 = f32[14,64,256]{2,0,1:T(8,128)S(1)} fusion(f32[16,64,256]{2,0,1:T(8,128)S(1)} %get-tuple-element.80, f32[16,64,256]{2,0,1:T(8,128)S(1)} %get-tuple-element.79, f32[18,64,256]{2,0,1:T(8,128)S(1)} %get-tuple-element.146, f32[14,64,255]{2,0,1:T(8,128)S(1)} %get-tuple-element.78, f32[14,64,255]{2,0,1:T(8,128)S(1)} %copy-done.10, ...), kind=kLoop, calls=%fused_computation.66 | loop fusion | flops 7569408 | bytes 13690880 | tf_op jit(solution)/shard_map/jit(_where)/select_n | solution.py:102
  162.2 2.0 %fusion.40 = f32[12,64,256]{2,0,1:T(8,128)S(1)} fusion(f32[16,64,256]{2,0,1:T(8,128)S(1)} %get-tuple-element.80, f32[14,64,256]{2,0,1:T(8,128)S(1)} %fusion.48, f32[18,64,256]{2,0,1:T(8,128)S(1)} %get-tuple-element.146, f32[12,64,255]{2,0,1:T(8,128)S(1)} %get-tuple-element.74, f32[12,64,255]{2,0,1:T(8,128)S(1)} %copy-done.8, ...), kind=kLoop, calls=%fused_computation.54 | loop fusion | flops 6488064 | bytes 11735040 | tf_op jit(solution)/shard_map/jit(_where)/select_n | solution.py:102
  166.2 2.1 %fusion.31 = (f32[10,64,256]{2,0,1:T(8,128)S(1)}, pred[10,64,256]{2,0,1:T(8,128)(4,1)S(1)}) fusion(f32[16,64,256]{2,0,1:T(8,128)S(1)} %get-tuple-element.80, f32[12,64,256]{2,0,1:T(8,128)S(1)} %fusion.40, f32[8,64,256]{2,0,1:T(8,128)S(1)} %copy-done.4, f32[5,64,256]{2,0,1:T(8,128)S(1)} %copy.159, f32[5,64,256]{2,0,1:T(8,128)S(1)} %copy.161, ...), kind=kLoop, calls=%fused_computation.41 | loop fusion | flops 5570560 | bytes 9811968 | tf_op jit(solution)/shard_map/div | solution.py:102
  (218 shorter events, 86.9 us)
Async XLA Ops:
  6.2 41.5 %collective-permute-start.6 = (f32[8]{0:T(128)S(1)}, f32[8]{0:T(128)S(1)}, u32[]{:S(2)}, u32[]{:S(2)}) collective-permute-start(f32[8]{0:T(128)S(1)} %fusion.128), channel_id=1, source_target_pairs={{0,1},{1,0},{2,3},{3,2},{4,5},{5,4},{6,7},{7,6},{8,9},{9,8},{10,11... | collective-permute-start | bytes 104 | tf_op jit(solution)/shard_map/ppermute | solution.py:129
  9.4 13.3 %copy-start.25 = (f32[8,64,256]{2,1,0:T(8,128)S(1)}, f32[8,64,256]{2,1,0:T(8,128)}, u32[]{:S(2)}) copy-start(f32[8,64,256]{2,1,0:T(8,128)} %param.15) | copy-start | bytes 1572868
  9.4 79.4 %collective-permute-start.2 = (f32[10,64,256]{2,1,0:T(8,128)}, f32[10,64,256]{2,1,0:T(8,128)}, u32[]{:S(2)}, u32[]{:S(2)}) collective-permute-start(f32[10,64,256]{2,1,0:T(8,128)} %pad_maximum_fusion.11), channel_id=1, source_target_pairs={{0,1},{1,2},{2,3},{3,4},{4,5},{5,6},{6,7},{7,8},{8,9},{9,10},{10,1... | collective-permute-start | bytes 1966088 | tf_op jit(solution)/shard_map/ppermute | solution.py:21
  12.8 77.3 %collective-permute-start.3 = (f32[10,64,256]{2,1,0:T(8,128)}, f32[10,64,256]{2,1,0:T(8,128)}, u32[]{:S(2)}, u32[]{:S(2)}) collective-permute-start(f32[10,64,256]{2,1,0:T(8,128)} %pad_maximum_fusion.12), channel_id=1, source_target_pairs={{1,0},{2,1},{3,2},{4,3},{5,4},{6,5},{7,6},{8,7},{9,8},{10,9},{11,1... | collective-permute-start | bytes 1966088 | tf_op jit(solution)/shard_map/ppermute | solution.py:22
  24.4 68.3 %collective-permute-start = (f32[10,64,256]{2,1,0:T(8,128)}, f32[10,64,256]{2,1,0:T(8,128)}, u32[]{:S(2)}, u32[]{:S(2)}) collective-permute-start(f32[10,64,256]{2,1,0:T(8,128)} %pad_maximum_fusion.9), channel_id=1, source_target_pairs={{0,1},{1,2},{2,3},{3,4},{4,5},{5,6},{6,7},{7,8},{8,9},{9,10},{10,1... | collective-permute-start | bytes 1966088 | tf_op jit(solution)/shard_map/ppermute | solution.py:21
  27.6 17.3 %collective-permute-start.14 = (f32[8,2,8,256]{3,2,1,0:T(8,128)}, f32[8,2,8,256]{3,2,1,0:T(8,128)}, u32[]{:S(2)}, u32[]{:S(2)}) collective-permute-start(f32[8,2,8,256]{3,2,1,0:T(8,128)} %fusion.120), channel_id=1, source_target_pairs={{0,32},{32,0},{64,96},{96,64},{128,160},{160,128},{192,224},{224,1... | collective-permute-start | bytes 393224 | tf_op jit(solution)/shard_map/ppermute | solution.py:140
  46.1 5.7 %collective-permute-start.15 = (f32[8,2,8,256]{3,2,1,0:T(8,128)}, f32[8,2,8,256]{3,2,1,0:T(8,128)S(1)}, u32[]{:S(2)}, u32[]{:S(2)}) collective-permute-start(f32[8,2,8,256]{3,2,1,0:T(8,128)} %add_dynamic-update-slice_fusion), channel_id=1, source_target_pairs={{0,64},{32,96},{64,0},{96,32},{128,192},{160,224},{192,128},{224,1... | collective-permute-start | bytes 393224 | tf_op jit(solution)/shard_map/ppermute | solution.py:140
  48.4 42.8 %copy-start = (f32[3,10,64,256]{3,1,2,0:T(8,128)S(1)}, f32[3,10,64,256]{3,1,2,0:T(8,128)}, u32[]{:S(2)}) copy-start(f32[3,10,64,256]{3,1,2,0:T(8,128)} %get-tuple-element.64) | copy-start | bytes 5898244
  48.4 8.3 %collective-permute-start.7 = (f32[8]{0:T(128)S(1)}, f32[8]{0:T(128)S(1)}, u32[]{:S(2)}, u32[]{:S(2)}) collective-permute-start(f32[8]{0:T(128)S(1)} %fusion.177), channel_id=1, source_target_pairs={{0,2},{1,3},{2,0},{3,1},{4,6},{5,7},{6,4},{7,5},{8,10},{9,11},{10,... | collective-permute-start | bytes 104 | tf_op jit(solution)/shard_map/ppermute | solution.py:129
  52.8 36.0 %collective-permute-start.16 = (f32[8,2,8,256]{3,2,1,0:T(8,128)S(1)}, f32[8,2,8,256]{3,2,1,0:T(8,128)S(1)}, u32[]{:S(2)}, u32[]{:S(2)}) collective-permute-start(f32[8,2,8,256]{3,2,1,0:T(8,128)S(1)} %add.638), channel_id=1, source_target_pairs={{0,128},{32,160},{64,192},{96,224},{128,0},{160,32},{192,64},{224,... | collective-permute-start | bytes 393224 | tf_op jit(solution)/shard_map/ppermute | solution.py:140
  57.3 5.2 %collective-permute-start.8 = (f32[8]{0:T(128)S(1)}, f32[8]{0:T(128)S(1)}, u32[]{:S(2)}, u32[]{:S(2)}) collective-permute-start(f32[8]{0:T(128)S(1)} %fusion.178), channel_id=1, source_target_pairs={{0,4},{1,5},{2,6},{3,7},{4,0},{5,1},{6,2},{7,3},{8,12},{9,13},{10,... | collective-permute-start | bytes 104 | tf_op jit(solution)/shard_map/ppermute | solution.py:129
  62.4 4.5 %collective-permute-start.9 = (f32[8]{0:T(128)S(1)}, f32[8]{0:T(128)S(1)}, u32[]{:S(2)}, u32[]{:S(2)}) collective-permute-start(f32[8]{0:T(128)S(1)} %add.630), channel_id=1, source_target_pairs={{0,8},{1,9},{2,10},{3,11},{4,12},{5,13},{6,14},{7,15},{8,0},{9,1},... | collective-permute-start | bytes 104 | tf_op jit(solution)/shard_map/ppermute | solution.py:129
  66.9 7.5 %collective-permute-start.10 = (f32[8]{0:T(128)S(1)}, f32[8]{0:T(128)S(1)}, u32[]{:S(2)}, u32[]{:S(2)}) collective-permute-start(f32[8]{0:T(128)S(1)} %add.631), channel_id=1, source_target_pairs={{0,16},{1,17},{2,18},{3,19},{4,20},{5,21},{6,22},{7,23},{8,24},{9,... | collective-permute-start | bytes 104 | tf_op jit(solution)/shard_map/ppermute | solution.py:129
  74.4 3.6 %collective-permute-start.11 = (f32[8]{0:T(128)S(1)}, f32[8]{0:T(128)S(1)}, u32[]{:S(2)}, u32[]{:S(2)}) collective-permute-start(f32[8]{0:T(128)S(1)} %add.632), channel_id=1, source_target_pairs={{0,32},{1,33},{2,34},{3,35},{4,36},{5,37},{6,38},{7,39},{8,40},{9,... | collective-permute-start | bytes 104 | tf_op jit(solution)/shard_map/ppermute | solution.py:129
  78.0 3.6 %collective-permute-start.12 = (f32[8]{0:T(128)S(1)}, f32[8]{0:T(128)S(1)}, u32[]{:S(2)}, u32[]{:S(2)}) collective-permute-start(f32[8]{0:T(128)S(1)} %add.633), channel_id=1, source_target_pairs={{0,64},{1,65},{2,66},{3,67},{4,68},{5,69},{6,70},{7,71},{8,72},{9,... | collective-permute-start | bytes 104 | tf_op jit(solution)/shard_map/ppermute | solution.py:129
  81.5 5.1 %collective-permute-start.13 = (f32[8]{0:T(128)S(1)}, f32[8]{0:T(128)S(1)}, u32[]{:S(2)}, u32[]{:S(2)}) collective-permute-start(f32[8]{0:T(128)S(1)} %add.634), channel_id=1, source_target_pairs={{0,128},{1,129},{2,130},{3,131},{4,132},{5,133},{6,134},{7,135},{8... | collective-permute-start | bytes 104 | tf_op jit(solution)/shard_map/ppermute | solution.py:129
  86.6 17.1 %collective-permute-start.1 = (f32[10,64,256]{2,1,0:T(8,128)}, f32[10,64,256]{2,1,0:T(8,128)S(1)}, u32[]{:S(2)}, u32[]{:S(2)}) collective-permute-start(f32[10,64,256]{2,1,0:T(8,128)} %pad_maximum_fusion.10), channel_id=1, source_target_pairs={{1,0},{2,1},{3,2},{4,3},{5,4},{6,5},{7,6},{8,7},{9,8},{10,9},{11,1... | collective-permute-start | bytes 1966088 | tf_op jit(solution)/shard_map/ppermute | solution.py:22
  134.0 11.6 %copy-start.37 = (f32[8,63,256]{2,0,1:T(8,128)S(1)}, f32[8,63,256]{2,0,1:T(8,128)}, u32[]{:S(2)}) copy-start(f32[8,63,256]{2,0,1:T(8,128)} %get-tuple-element.123) | copy-start | bytes 1548292
  134.0 11.6 %copy-start.41 = (s32[8,64,256]{2,1,0:T(8,128)S(1)}, s32[8,64,256]{2,1,0:T(8,128)}, u32[]{:S(2)}) copy-start(s32[8,64,256]{2,1,0:T(8,128)} %param.16) | copy-start | bytes 1572868
  134.3 11.4 %copy-start.3 = (f32[8,64,255]{2,0,1:T(8,128)S(1)}, f32[8,64,255]{2,0,1:T(8,128)}, u32[]{:S(2)}) copy-start(f32[8,64,255]{2,0,1:T(8,128)} %get-tuple-element.119) | copy-start | bytes 1566724
  134.3 11.4 %copy-start.28 = (f32[8,64,255]{2,0,1:T(8,128)S(1)}, f32[8,64,255]{2,0,1:T(8,128)}, u32[]{:S(2)}) copy-start(f32[8,64,255]{2,0,1:T(8,128)} %get-tuple-element.124) | copy-start | bytes 1566724
  134.3 11.4 %copy-start.29 = (f32[8,64,255]{2,0,1:T(8,128)S(1)}, f32[8,64,255]{2,0,1:T(8,128)}, u32[]{:S(2)}) copy-start(f32[8,64,255]{2,0,1:T(8,128)} %get-tuple-element.125) | copy-start | bytes 1566724
  134.4 17.2 %collective-permute-start.4 = (f32[4,64,256]{2,0,1:T(4,128)S(1)}, f32[4,64,256]{2,0,1:T(4,128)S(1)}, u32[]{:S(2)}, u32[]{:S(2)}) collective-permute-start(f32[4,64,256]{2,0,1:T(4,128)S(1)} %get-tuple-element.126), channel_id=1, source_target_pairs={{0,1},{1,2},{2,3},{3,4},{4,5},{5,6},{6,7},{7,8},{8,9},{9,10},{10,1... | collective-permute-start | bytes 786440 | tf_op jit(solution)/shard_map/ppermute | solution.py:21
  136.5 15.1 %collective-permute-start.5 = (f32[4,64,256]{2,0,1:T(4,128)S(1)}, f32[4,64,256]{2,0,1:T(4,128)S(1)}, u32[]{:S(2)}, u32[]{:S(2)}) collective-permute-start(f32[4,64,256]{2,0,1:T(4,128)S(1)} %get-tuple-element.127), channel_id=1, source_target_pairs={{1,0},{2,1},{3,2},{4,3},{5,4},{6,5},{7,6},{8,7},{9,8},{10,9},{11,1... | collective-permute-start | bytes 786440 | tf_op jit(solution)/shard_map/ppermute | solution.py:22
  (39 other events, 89.3 us)

commit v3 on v2

--- a/solution.py
+++ b/solution.py
@@ -124,9 +124,10 @@
     choose = (jnp.arange(nzones, dtype=jnp.int32) == zone_here).astype(jnp.float32)
     totals = choose * jnp.sum(solvent[:, -1, :])
     count = lax.axis_size(ALL)
+    zone_bits = []
     bit = 1
     while bit < count:
-        totals = totals + lax.ppermute(totals, ALL, [(i, i ^ bit) for i in range(count)])
+        zone_bits.append(bit)
         bit *= 2
 
     planes = jnp.stack([enthalpy[:, -1, :], solvent[:, -1, :]])
@@ -135,11 +136,28 @@
     buffer = lax.dynamic_update_slice(
         buffer, planes[None], (lax.axis_index("zone"), 0, 0, 0)
     )
+    duct_bits = []
     bit = 1
     while bit < rows:
-        buffer = buffer + lax.ppermute(buffer, "zone", [(i, i ^ bit) for i in range(rows)])
+        duct_bits.append(bit)
         bit *= 2
-    gathered = buffer
+    state = {"totals": totals, "buffer": buffer}
+
+    def advance(anchor):
+        sent = {}
+        if zone_bits:
+            b = zone_bits.pop(0)
+            sent["totals"] = lax.ppermute(
+                state["totals"], ALL, [(i, i ^ b) for i in range(count)])
+        if duct_bits:
+            b = duct_bits.pop(0)
+            sent["buffer"] = lax.ppermute(
+                state["buffer"], "zone", [(i, i ^ b) for i in range(rows)])
+        if sent and anchor is not None:
+            sent, _ = lax.optimization_barrier((sent, anchor))
+        if sent:
+            for key, value in sent.items():
+                state[key] = state[key] + value
 
     narrow_head = jnp.concatenate(
         [velocity[:, 0:2].reshape((6,) + enthalpy.shape[1:]), pressure[0:2],
@@ -160,12 +178,18 @@
     heat1 = jnp.concatenate([n_left[8:9], enthalpy, n_right[8:9]], axis=0)
     solv1 = jnp.concatenate([n_left[9:10], solvent, n_right[9:10]], axis=0)
 
+    advance(None)
+    advance(None)
+    advance(None)
+    advance(None)
     star = momentum(vel2, pres5, heat1, poro5)
+    advance(star[1])
     source = divergence(star) / time_step
     vel_star = jnp.stack([part[1:-1] for part in star])
 
     s_left, s_right = neighbours(source[0:4], source[cx - 4:])
     source4 = jnp.concatenate([s_left, source, s_right], axis=0)
+    advance(source4)
 
     heat_new = transport(heat1, vel_star)
     solv_new = transport(solv1, vel_star)
@@ -178,6 +202,12 @@
         lo = iteration
         hi = poro5.shape[0] - iteration
         iterate = sweep(iterate, poro5[lo:hi], source4[lo:hi - 2])
+        if iteration in (1, 2):
+            advance(iterate)
+    while zone_bits or duct_bits:
+        advance(iterate)
+    totals = state["totals"]
+    gathered = state["buffer"]
     iterate, heat_new, solv_new, totals, gathered = lax.optimization_barrier(
         (iterate, heat_new, solv_new, totals, gathered))
 

time: 182 us -> 183 us (level)
  the two profiles are of different devices: /device:TPU:32 before, /device:TPU:2 now
where the time goes in v3:
time: 183 us; the launch traced here: 182 us
  local copies, waits for them, and re-layouts  57.8 us (32%)
  other arithmetic  43.2 us (24%)
  waiting for transfers between devices  41.6 us (23%)
  starting transfers between devices  33.1 us (18%)
  between operations  6.01 us (3%)
    ppermute x3, waiting for transfers between devices, neighbours(): from_left = lax.ppermute(tail, ALL, [(i, i + 1) for i in range(count - 1)])  22 us
    slice x22, local copies, waits for them, and re-layouts, shifted_down(): inner = lax.slice_in_dim(values, 0, values.shape[axis] - 1, axis=axis)  21.6 us
    ppermute x3, starting transfers between devices, neighbours(): from_right = lax.ppermute(head, ALL, [(i + 1, i) for i in range(count - 1)])  19.6 us
    ppermute x8, waiting for transfers between devices, advance(): lax.ppermute(state['totals'], ALL, [(i, i ^ b) for i in range(count)])  14.9 us
    unnamed x89, local copies, waits for them, and re-layouts  12.9 us
    mul x3, other arithmetic, momentum(): parts.append(open_here * (centre + time_step * forcing))  7.52 us
    select_n x4, other arithmetic, sweep(): jnp.where(inside, numerator / jnp.where(inside, denominator, 1.0), 0.0)  6.62 us
    ppermute x3, starting transfers between devices, neighbours(): from_left = lax.ppermute(tail, ALL, [(i, i + 1) for i in range(count - 1)])  6.22 us
  transfers between devices with their start and end apart: 17, of which 8 were waited for; matrix products, arithmetic and copies ran while one was open for 43% of the time, Pallas kernels for 0%

profile of v3, /device:TPU:2, one launch (start us, length us, event | category | flops | bytes accessed | tf_op | source)
XLA Modules:
  0.0 181.7 jit_solution(3877259674474093314)
XLA Ops:
  5.5 9.7 %collective-permute-start.3 = (f32[10,64,256]{2,1,0:T(8,128)}, f32[10,64,256]{2,1,0:T(8,128)}, u32[]{:S(2)}, u32[]{:S(2)}) collective-permute-start(f32[10,64,256]{2,1,0:T(8,128)} %pad_maximum_fusion.12), channel_id=1, source_target_pairs={{1,0},{2,1},{3,2},{4,3},{5,4},{6,5},{7,6},{8,7},{9,8},{10,9},{11,1... | collective-permute-start | bytes 1966088 | tf_op jit(solution)/shard_map/ppermute | solution.py:22
  16.1 1.9 %collective-permute-start.2 = (f32[10,64,256]{2,1,0:T(8,128)}, f32[10,64,256]{2,1,0:T(8,128)}, u32[]{:S(2)}, u32[]{:S(2)}) collective-permute-start(f32[10,64,256]{2,1,0:T(8,128)} %pad_maximum_fusion.11), channel_id=1, source_target_pairs={{0,1},{1,2},{2,3},{3,4},{4,5},{5,6},{6,7},{7,8},{8,9},{9,10},{10,1... | collective-permute-start | bytes 1966088 | tf_op jit(solution)/shard_map/ppermute | solution.py:21
  19.8 7.8 %collective-permute-start.1 = (f32[10,64,256]{2,1,0:T(8,128)}, f32[10,64,256]{2,1,0:T(8,128)}, u32[]{:S(2)}, u32[]{:S(2)}) collective-permute-start(f32[10,64,256]{2,1,0:T(8,128)} %pad_maximum_fusion.10), channel_id=1, source_target_pairs={{1,0},{2,1},{3,2},{4,3},{5,4},{6,5},{7,6},{8,7},{9,8},{10,9},{11,1... | collective-permute-start | bytes 1966088 | tf_op jit(solution)/shard_map/ppermute | solution.py:22
  32.3 2.8 %collective-permute-start.14 = (f32[8,2,8,256]{3,2,1,0:T(8,128)}, f32[8,2,8,256]{3,2,1,0:T(8,128)}, u32[]{:S(2)}, u32[]{:S(2)}) collective-permute-start(f32[8,2,8,256]{3,2,1,0:T(8,128)} %fusion.120), channel_id=1, source_target_pairs={{0,32},{32,0},{64,96},{96,64},{128,160},{160,128},{192,224},{224,1... | collective-permute-start | bytes 393224 | tf_op jit(solution)/shard_map/ppermute | solution.py:154
  35.2 3.5 %fusion.143 = (f32[3,8,64,256]{3,1,2,0:T(8,128)S(1)}, f32[3,10,64,256]{3,1,2,0:T(8,128)}) fusion(f32[3,8,64,256]{3,2,1,0:T(8,128)} %param.11), kind=kLoop, calls=%fused_computation.225 | loop fusion | bytes 4718592 | tf_op args[0]
  53.5 4.6 %collective-permute-done.15 = f32[8,2,8,256]{3,2,1,0:T(8,128)S(1)} collective-permute-done((f32[8,2,8,256]{3,2,1,0:T(8,128)}, f32[8,2,8,256]{3,2,1,0:T(8,128)S(1)}, u32[]{:S(2)}, u32[]{:S(2)}) %collective-permute-start.15) | collective-permute-done | bytes 131104 | tf_op jit(solution)/shard_map/ppermute | solution.py:154
  59.0 2.2 %collective-permute-start.16 = (f32[8,2,8,256]{3,2,1,0:T(8,128)S(1)}, f32[8,2,8,256]{3,2,1,0:T(8,128)S(1)}, u32[]{:S(2)}, u32[]{:S(2)}) collective-permute-start(f32[8,2,8,256]{3,2,1,0:T(8,128)S(1)} %add.638), channel_id=1, source_target_pairs={{0,128},{32,160},{64,192},{96,224},{128,0},{160,32},{192,64},{224,... | collective-permute-start | bytes 393224 | tf_op jit(solution)/shard_map/ppermute | solution.py:154
  61.9 5.1 %collective-permute-done.8 = f32[8]{0:T(128)S(1)} collective-permute-done((f32[8]{0:T(128)S(1)}, f32[8]{0:T(128)S(1)}, u32[]{:S(2)}, u32[]{:S(2)}) %collective-permute-start.8) | collective-permute-done | bytes 64 | tf_op jit(solution)/shard_map/ppermute | solution.py:150
  67.0 4.5 %collective-permute-done.9 = f32[8]{0:T(128)S(1)} collective-permute-done((f32[8]{0:T(128)S(1)}, f32[8]{0:T(128)S(1)}, u32[]{:S(2)}, u32[]{:S(2)}) %collective-permute-start.9) | collective-permute-done | bytes 64 | tf_op jit(solution)/shard_map/ppermute | solution.py:150
  71.5 1.9 %collective-permute-start = (f32[10,64,256]{2,1,0:T(8,128)}, f32[10,64,256]{2,1,0:T(8,128)S(1)}, u32[]{:S(2)}, u32[]{:S(2)}) collective-permute-start(f32[10,64,256]{2,1,0:T(8,128)} %pad_maximum_fusion.9), channel_id=1, source_target_pairs={{0,1},{1,2},{2,3},{3,4},{4,5},{5,6},{6,7},{7,8},{8,9},{9,10},{10,1... | collective-permute-start | bytes 1966088 | tf_op jit(solution)/shard_map/ppermute | solution.py:21
  79.3 2.2 %fusion.154 = (f32[10,63,256]{2,0,1:T(8,128)}, f32[10,63,256]{2,0,1:T(8,128)}, f32[10,63,256]{2,0,1:T(8,128)}, f32[10,63,256]{2,0,1:T(8,128)}) fusion(f32[10,64,256]{2,0,1:T(8,128)S(1)} %get-tuple-element.42, f32[10,64,256]{2,0,1:T(8,128)S(1)} %get-tuple-element.41), kind=kLoop, calls=%fused_computation.236 | loop fusion | bytes 5160960 | tf_op jit(solution)/shard_map/slice | solution.py:28
  82.1 12.7 %collective-permute-done = f32[10,64,256]{2,1,0:T(8,128)S(1)} collective-permute-done((f32[10,64,256]{2,1,0:T(8,128)}, f32[10,64,256]{2,1,0:T(8,128)S(1)}, u32[]{:S(2)}, u32[]{:S(2)}) %collective-permute-start) | collective-permute-done | bytes 655392 | tf_op jit(solution)/shard_map/ppermute | solution.py:21
  101.5 2.2 %fusion.136 = (f32[16,63,256]{2,0,1:T(8,128)}, f32[16,63,256]{2,0,1:T(8,128)}, f32[16,63,256]{2,0,1:T(8,128)}, f32[16,63,256]{2,0,1:T(8,128)}) fusion(f32[18,64,256]{2,0,1:T(8,128)S(1)} %pad_maximum_fusion.1, f32[18,64,256]{2,0,1:T(8,128)S(1)} %pad_maximum_fusion.2), kind=kLoop, calls=%fused_computation.218 | loop fusion | bytes 8257536 | tf_op jit(solution)/shard_map/slice | solution.py:28
  103.7 2.8 %fusion.75 = f32[10,64,256]{2,0,1:T(8,128)S(1)} fusion(f32[3,10,64,256]{3,1,2,0:T(8,128)S(1)} %get-tuple-element.147, f32[3,8,64,256]{3,1,2,0:T(8,128)S(1)} %get-tuple-element.71, f32[3,2,64,256]{3,1,2,0:T(2,128)S(1)} %copy.162, f32[10,64,255]{2,0,1:T(8,128)S(1)} %get-tuple-element.68, f32[10,64,255]{2,0,1:T(8,128)S(1)} %get-tuple-element.67, ...), kind=kLoop, calls=%fused_computation.104 | loop fusion | flops 2457600 | bytes 8488960 | tf_op jit(solution)/shard_map/mul | solution.py:56
  118.0 3.6 %fusion.13 = f32[10,64,256]{2,0,1:T(8,128)S(1)} fusion(f32[3,8,64,256]{3,1,2,0:T(8,128)S(1)} %get-tuple-element.71, f32[3,2,64,256]{3,1,2,0:T(2,128)S(1)} %copy.162, f32[3,10,64,256]{3,1,2,0:T(8,128)S(1)} %get-tuple-element.147, f32[1,64,256]{2,0,1:T(1,128)S(1)} %copy.178, f32[8,64,256]{2,0,1:T(8,128)S(1)} %copy.177, f32[1,64,256]{2,0,1:T(1,128)S(1)} %copy.176, ...), kind=kLoop, calls=%fused_computation.22 | loop fusion | flops 3112960 | bytes 9128960 | tf_op jit(solution)/shard_map/mul | solution.py:56
  124.7 3.4 %fusion.104 = (f32[8,64,256]{2,0,1:T(8,128)S(1)}, f32[8,64,256]{2,0,1:T(8,128)S(1)}, f32[1,8,64,256]{3,1,2,0:T(8,128)S(1)}, f32[1,8,64,256]{3,1,2,0:T(8,128)S(1)}, f32[8,64,256]{2,0,1:T(8,128)S(1)}) fusion(f32[8,64,256]{2,0,1:T(8,128)S(1)} %copy.177, f32[1,64,256]{2,0,1:T(1,128)S(1)} %copy.178, f32[1,64,256]{2,0,1:T(1,128)S(1)} %copy.176, ...), kind=kLoop, calls=%fused_computation.150 | loop fusion | flops 5373952 | bytes 9021440 | tf_op jit(solution)/shard_map/sub | solution.py:197
  130.2 2.1 %collective-permute-start.5 = (f32[4,64,256]{2,0,1:T(4,128)S(1)}, f32[4,64,256]{2,0,1:T(4,128)S(1)}, u32[]{:S(2)}, u32[]{:S(2)}) collective-permute-start(f32[4,64,256]{2,0,1:T(4,128)S(1)} %get-tuple-element.135), channel_id=1, source_target_pairs={{1,0},{2,1},{3,2},{4,3},{5,4},{6,5},{7,6},{8,7},{9,8},{10,9},{11,1... | collective-permute-start | bytes 786440 | tf_op jit(solution)/shard_map/ppermute | solution.py:22
  132.3 2.4 %collective-permute-start.4 = (f32[4,64,256]{2,0,1:T(4,128)S(1)}, f32[4,64,256]{2,0,1:T(4,128)S(1)}, u32[]{:S(2)}, u32[]{:S(2)}) collective-permute-start(f32[4,64,256]{2,0,1:T(4,128)S(1)} %get-tuple-element.134), channel_id=1, source_target_pairs={{0,1},{1,2},{2,3},{3,4},{4,5},{5,6},{6,7},{7,8},{8,9},{9,10},{10,1... | collective-permute-start | bytes 786440 | tf_op jit(solution)/shard_map/ppermute | solution.py:21
  137.7 9.3 %collective-permute-done.4 = f32[4,64,256]{2,0,1:T(4,128)S(1)} collective-permute-done((f32[4,64,256]{2,0,1:T(4,128)S(1)}, f32[4,64,256]{2,0,1:T(4,128)S(1)}, u32[]{:S(2)}, u32[]{:S(2)}) %collective-permute-start.4) | collective-permute-done | bytes 262176 | tf_op jit(solution)/shard_map/ppermute | solution.py:21
  147.0 2.0 %fusion.58 = (f32[16,64,256]{2,0,1:T(8,128)S(1)}, f32[16,64,256]{2,0,1:T(8,128)S(1)}) fusion(f32[18,64,256]{2,0,1:T(8,128)S(1)} %pad_maximum_fusion.2, f32[18,64,256]{2,0,1:T(8,128)S(1)} %pad_maximum_fusion.1, f32[16,64,255]{2,0,1:T(8,128)S(1)} %get-tuple-element.156, f32[16,64,255]{2,0,1:T(8,128)S(1)} %get-tuple-element.62, ...), kind=kLoop, calls=%fused_computation.80 | loop fusion | flops 9175040 | bytes 16695296 | tf_op jit(solution)/shard_map/jit(_where)/select_n | solution.py:102
  151.3 2.1 %fusion.48 = f32[14,64,256]{2,0,1:T(8,128)S(1)} fusion(f32[16,64,256]{2,0,1:T(8,128)S(1)} %get-tuple-element.88, f32[16,64,256]{2,0,1:T(8,128)S(1)} %get-tuple-element.87, f32[18,64,256]{2,0,1:T(8,128)S(1)} %pad_maximum_fusion.1, f32[14,64,255]{2,0,1:T(8,128)S(1)} %get-tuple-element.86, f32[14,64,255]{2,0,1:T(8,128)S(1)} %copy-done.8, ...), kind=kLoop, calls=%fused_computation.66 | loop fusion | flops 7569408 | bytes 13690880 | tf_op jit(solution)/shard_map/jit(_where)/select_n | solution.py:102
  155.8 2.1 %fusion.40 = f32[12,64,256]{2,0,1:T(8,128)S(1)} fusion(f32[16,64,256]{2,0,1:T(8,128)S(1)} %get-tuple-element.88, f32[14,64,256]{2,0,1:T(8,128)S(1)} %fusion.48, f32[18,64,256]{2,0,1:T(8,128)S(1)} %pad_maximum_fusion.1, f32[12,64,255]{2,0,1:T(8,128)S(1)} %get-tuple-element.82, f32[12,64,255]{2,0,1:T(8,128)S(1)} %copy-done.6, ...), kind=kLoop, calls=%fused_computation.54 | loop fusion | flops 6488064 | bytes 11735040 | tf_op jit(solution)/shard_map/jit(_where)/select_n | solution.py:102
  158.8 2.2 %fusion.31 = (f32[10,64,256]{2,0,1:T(8,128)S(1)}, pred[10,64,256]{2,0,1:T(8,128)(4,1)S(1)}) fusion(f32[16,64,256]{2,0,1:T(8,128)S(1)} %get-tuple-element.88, f32[12,64,256]{2,0,1:T(8,128)S(1)} %fusion.40, f32[8,64,256]{2,0,1:T(8,128)S(1)} %copy-done.4, f32[5,64,256]{2,0,1:T(8,128)S(1)} %copy.159, f32[5,64,256]{2,0,1:T(8,128)S(1)} %copy.161, ...), kind=kLoop, calls=%fused_computation.41 | loop fusion | flops 5570560 | bytes 9811968 | tf_op jit(solution)/shard_map/div | solution.py:102
  162.9 4.5 %collective-permute-done.13 = f32[8]{0:T(128)S(1)} collective-permute-done((f32[8]{0:T(128)S(1)}, f32[8]{0:T(128)S(1)}, u32[]{:S(2)}, u32[]{:S(2)}) %collective-permute-start.13) | collective-permute-done | bytes 64 | tf_op jit(solution)/shard_map/ppermute | solution.py:150
  (209 shorter events, 78.1 us)
Async XLA Ops:
  4.6 13.4 %copy-start.19 = (f32[8,64,256]{2,1,0:T(8,128)S(1)}, f32[8,64,256]{2,1,0:T(8,128)}, u32[]{:S(2)}) copy-start(f32[8,64,256]{2,1,0:T(8,128)} %param.14) | copy-start | bytes 1572868
  5.5 12.6 %copy-start.21 = (f32[8,64,256]{2,1,0:T(8,128)S(1)}, f32[8,64,256]{2,1,0:T(8,128)}, u32[]{:S(2)}) copy-start(f32[8,64,256]{2,1,0:T(8,128)} %param.15) | copy-start | bytes 1572868
  5.5 71.2 %collective-permute-start.3 = (f32[10,64,256]{2,1,0:T(8,128)}, f32[10,64,256]{2,1,0:T(8,128)}, u32[]{:S(2)}, u32[]{:S(2)}) collective-permute-start(f32[10,64,256]{2,1,0:T(8,128)} %pad_maximum_fusion.12), channel_id=1, source_target_pairs={{1,0},{2,1},{3,2},{4,3},{5,4},{6,5},{7,6},{8,7},{9,8},{10,9},{11,1... | collective-permute-start | bytes 1966088 | tf_op jit(solution)/shard_map/ppermute | solution.py:22
  16.1 57.7 %collective-permute-start.2 = (f32[10,64,256]{2,1,0:T(8,128)}, f32[10,64,256]{2,1,0:T(8,128)}, u32[]{:S(2)}, u32[]{:S(2)}) collective-permute-start(f32[10,64,256]{2,1,0:T(8,128)} %pad_maximum_fusion.11), channel_id=1, source_target_pairs={{0,1},{1,2},{2,3},{3,4},{4,5},{5,6},{6,7},{7,8},{8,9},{9,10},{10,1... | collective-permute-start | bytes 1966088 | tf_op jit(solution)/shard_map/ppermute | solution.py:21
  18.1 9.9 %copy-start.1 = (f32[8,64,256]{2,1,0:T(8,128)S(1)}, f32[8,64,256]{2,1,0:T(8,128)}, u32[]{:S(2)}) copy-start(f32[8,64,256]{2,1,0:T(8,128)} %param.13) | copy-start | bytes 1572868
  18.9 10.0 %copy-start.40 = (s32[8]{0:T(128)S(1)}, s32[8]{0:T(128)}, u32[]{:S(2)}) copy-start(s32[8]{0:T(128)} %param.18) | copy-start | bytes 100
  19.8 55.3 %collective-permute-start.1 = (f32[10,64,256]{2,1,0:T(8,128)}, f32[10,64,256]{2,1,0:T(8,128)}, u32[]{:S(2)}, u32[]{:S(2)}) collective-permute-start(f32[10,64,256]{2,1,0:T(8,128)} %pad_maximum_fusion.10), channel_id=1, source_target_pairs={{1,0},{2,1},{3,2},{4,3},{5,4},{6,5},{7,6},{8,7},{9,8},{10,9},{11,1... | collective-permute-start | bytes 1966088 | tf_op jit(solution)/shard_map/ppermute | solution.py:22
  31.0 21.8 %collective-permute-start.6 = (f32[8]{0:T(128)S(1)}, f32[8]{0:T(128)S(1)}, u32[]{:S(2)}, u32[]{:S(2)}) collective-permute-start(f32[8]{0:T(128)S(1)} %fusion.128), channel_id=1, source_target_pairs={{0,1},{1,0},{2,3},{3,2},{4,5},{5,4},{6,7},{7,6},{8,9},{9,8},{10,11... | collective-permute-start | bytes 104 | tf_op jit(solution)/shard_map/ppermute | solution.py:150
  32.3 18.6 %collective-permute-start.14 = (f32[8,2,8,256]{3,2,1,0:T(8,128)}, f32[8,2,8,256]{3,2,1,0:T(8,128)}, u32[]{:S(2)}, u32[]{:S(2)}) collective-permute-start(f32[8,2,8,256]{3,2,1,0:T(8,128)} %fusion.120), channel_id=1, source_target_pairs={{0,32},{32,0},{64,96},{96,64},{128,160},{160,128},{192,224},{224,1... | collective-permute-start | bytes 393224 | tf_op jit(solution)/shard_map/ppermute | solution.py:154
  52.3 5.8 %collective-permute-start.15 = (f32[8,2,8,256]{3,2,1,0:T(8,128)}, f32[8,2,8,256]{3,2,1,0:T(8,128)S(1)}, u32[]{:S(2)}, u32[]{:S(2)}) collective-permute-start(f32[8,2,8,256]{3,2,1,0:T(8,128)} %add_dynamic-update-slice_fusion), channel_id=1, source_target_pairs={{0,64},{32,96},{64,0},{96,32},{128,192},{160,224},{192,128},{224,1... | collective-permute-start | bytes 393224 | tf_op jit(solution)/shard_map/ppermute | solution.py:154
  53.4 7.8 %collective-permute-start.7 = (f32[8]{0:T(128)S(1)}, f32[8]{0:T(128)S(1)}, u32[]{:S(2)}, u32[]{:S(2)}) collective-permute-start(f32[8]{0:T(128)S(1)} %fusion.177), channel_id=1, source_target_pairs={{0,2},{1,3},{2,0},{3,1},{4,6},{5,7},{6,4},{7,5},{8,10},{9,11},{10,... | collective-permute-start | bytes 104 | tf_op jit(solution)/shard_map/ppermute | solution.py:150
  59.0 14.3 %collective-permute-start.16 = (f32[8,2,8,256]{3,2,1,0:T(8,128)S(1)}, f32[8,2,8,256]{3,2,1,0:T(8,128)S(1)}, u32[]{:S(2)}, u32[]{:S(2)}) collective-permute-start(f32[8,2,8,256]{3,2,1,0:T(8,128)S(1)} %add.638), channel_id=1, source_target_pairs={{0,128},{32,160},{64,192},{96,224},{128,0},{160,32},{192,64},{224,... | collective-permute-start | bytes 393224 | tf_op jit(solution)/shard_map/ppermute | solution.py:154
  61.8 5.2 %collective-permute-start.8 = (f32[8]{0:T(128)S(1)}, f32[8]{0:T(128)S(1)}, u32[]{:S(2)}, u32[]{:S(2)}) collective-permute-start(f32[8]{0:T(128)S(1)} %fusion.178), channel_id=1, source_target_pairs={{0,4},{1,5},{2,6},{3,7},{4,0},{5,1},{6,2},{7,3},{8,12},{9,13},{10,... | collective-permute-start | bytes 104 | tf_op jit(solution)/shard_map/ppermute | solution.py:150
  67.0 4.5 %collective-permute-start.9 = (f32[8]{0:T(128)S(1)}, f32[8]{0:T(128)S(1)}, u32[]{:S(2)}, u32[]{:S(2)}) collective-permute-start(f32[8]{0:T(128)S(1)} %add.630), channel_id=1, source_target_pairs={{0,8},{1,9},{2,10},{3,11},{4,12},{5,13},{6,14},{7,15},{8,0},{9,1},... | collective-permute-start | bytes 104 | tf_op jit(solution)/shard_map/ppermute | solution.py:150
  71.5 23.4 %collective-permute-start = (f32[10,64,256]{2,1,0:T(8,128)}, f32[10,64,256]{2,1,0:T(8,128)S(1)}, u32[]{:S(2)}, u32[]{:S(2)}) collective-permute-start(f32[10,64,256]{2,1,0:T(8,128)} %pad_maximum_fusion.9), channel_id=1, source_target_pairs={{0,1},{1,2},{2,3},{3,4},{4,5},{5,6},{6,7},{7,8},{8,9},{9,10},{10,1... | collective-permute-start | bytes 1966088 | tf_op jit(solution)/shard_map/ppermute | solution.py:21
  73.4 61.3 %collective-permute-start.10 = (f32[8]{0:T(128)S(1)}, f32[8]{0:T(128)S(1)}, u32[]{:S(2)}, u32[]{:S(2)}) collective-permute-start(f32[8]{0:T(128)S(1)} %add.631), channel_id=1, source_target_pairs={{0,16},{1,17},{2,18},{3,19},{4,20},{5,21},{6,22},{7,23},{8,24},{9,... | collective-permute-start | bytes 104 | tf_op jit(solution)/shard_map/ppermute | solution.py:150
  82.1 12.9 %copy-start.2 = (f32[8,64,256]{2,0,1:T(8,128)S(1)}, f32[8,64,256]{2,0,1:T(8,128)}, u32[]{:S(2)}) copy-start(f32[8,64,256]{2,0,1:T(8,128)} %copy.169) | copy-start | bytes 1572868
  128.1 43.2 %copy-start.24 = (f32[8,64,256]{2,0,1:T(8,128)}, f32[8,64,256]{2,0,1:T(8,128)S(1)}, u32[]{:S(2)}) copy-start(f32[8,64,256]{2,0,1:T(8,128)S(1)} %get-tuple-element.20) | copy-start | bytes 1572868
  130.2 7.4 %collective-permute-start.5 = (f32[4,64,256]{2,0,1:T(4,128)S(1)}, f32[4,64,256]{2,0,1:T(4,128)S(1)}, u32[]{:S(2)}, u32[]{:S(2)}) collective-permute-start(f32[4,64,256]{2,0,1:T(4,128)S(1)} %get-tuple-element.135), channel_id=1, source_target_pairs={{1,0},{2,1},{3,2},{4,3},{5,4},{6,5},{7,6},{8,7},{9,8},{10,9},{11,1... | collective-permute-start | bytes 786440 | tf_op jit(solution)/shard_map/ppermute | solution.py:22
  132.3 14.7 %collective-permute-start.4 = (f32[4,64,256]{2,0,1:T(4,128)S(1)}, f32[4,64,256]{2,0,1:T(4,128)S(1)}, u32[]{:S(2)}, u32[]{:S(2)}) collective-permute-start(f32[4,64,256]{2,0,1:T(4,128)S(1)} %get-tuple-element.134), channel_id=1, source_target_pairs={{0,1},{1,2},{2,3},{3,4},{4,5},{5,6},{6,7},{7,8},{8,9},{9,10},{10,1... | collective-permute-start | bytes 786440 | tf_op jit(solution)/shard_map/ppermute | solution.py:21
  134.7 23.7 %collective-permute-start.11 = (f32[8]{0:T(128)S(1)}, f32[8]{0:T(128)S(1)}, u32[]{:S(2)}, u32[]{:S(2)}) collective-permute-start(f32[8]{0:T(128)S(1)} %add.632), channel_id=1, source_target_pairs={{0,32},{1,33},{2,34},{3,35},{4,36},{5,37},{6,38},{7,39},{8,40},{9,... | collective-permute-start | bytes 104 | tf_op jit(solution)/shard_map/ppermute | solution.py:150
  137.3 9.7 %copy-start.18 = (f32[16,63,256]{2,0,1:T(8,128)S(1)}, f32[16,63,256]{2,0,1:T(8,128)}, u32[]{:S(2)}) copy-start(f32[16,63,256]{2,0,1:T(8,128)} %get-tuple-element.155) | copy-start | bytes 3096580
  158.5 3.9 %collective-permute-start.12 = (f32[8]{0:T(128)S(1)}, f32[8]{0:T(128)S(1)}, u32[]{:S(2)}, u32[]{:S(2)}) collective-permute-start(f32[8]{0:T(128)S(1)} %add.633), channel_id=1, source_target_pairs={{0,64},{1,65},{2,66},{3,67},{4,68},{5,69},{6,70},{7,71},{8,72},{9,... | collective-permute-start | bytes 104 | tf_op jit(solution)/shard_map/ppermute | solution.py:150
  162.4 5.1 %collective-permute-start.13 = (f32[8]{0:T(128)S(1)}, f32[8]{0:T(128)S(1)}, u32[]{:S(2)}, u32[]{:S(2)}) collective-permute-start(f32[8]{0:T(128)S(1)} %add.634), channel_id=1, source_target_pairs={{0,128},{1,129},{2,130},{3,131},{4,132},{5,133},{6,134},{7,135},{8... | collective-permute-start | bytes 104 | tf_op jit(solution)/shard_map/ppermute | solution.py:150
  (35 other events, 111.4 us)

commit v4 on v3

--- a/solution.py
+++ b/solution.py
@@ -124,40 +124,45 @@
     choose = (jnp.arange(nzones, dtype=jnp.int32) == zone_here).astype(jnp.float32)
     totals = choose * jnp.sum(solvent[:, -1, :])
     count = lax.axis_size(ALL)
-    zone_bits = []
-    bit = 1
-    while bit < count:
-        zone_bits.append(bit)
-        bit *= 2
+    rows = lax.axis_size("zone")
 
     planes = jnp.stack([enthalpy[:, -1, :], solvent[:, -1, :]])
-    rows = lax.axis_size("zone")
-    buffer = jnp.zeros((rows,) + planes.shape, jnp.float32)
+    buffer = jnp.zeros((rows + 1,) + planes.shape, jnp.float32)
     buffer = lax.dynamic_update_slice(
         buffer, planes[None], (lax.axis_index("zone"), 0, 0, 0)
     )
+    buffer = buffer.at[rows, 0, 0, :nzones].set(totals)
+    bricks = count // rows
     duct_bits = []
     bit = 1
     while bit < rows:
         duct_bits.append(bit)
         bit *= 2
-    state = {"totals": totals, "buffer": buffer}
+    zone_bits = []
+    bit = 1
+    while bit < bricks:
+        zone_bits.append(bit)
+        bit *= 2
+    state = {"buffer": buffer, "totals": None}
 
     def advance(anchor):
-        sent = {}
-        if zone_bits:
-            b = zone_bits.pop(0)
-            sent["totals"] = lax.ppermute(
-                state["totals"], ALL, [(i, i ^ b) for i in range(count)])
         if duct_bits:
             b = duct_bits.pop(0)
-            sent["buffer"] = lax.ppermute(
-                state["buffer"], "zone", [(i, i ^ b) for i in range(rows)])
-        if sent and anchor is not None:
+            key = "buffer"
+            sent = lax.ppermute(
+                state[key], "zone", [(i, i ^ b) for i in range(rows)])
+        elif zone_bits:
+            b = zone_bits.pop(0)
+            key = "totals"
+            if state[key] is None:
+                state[key] = state["buffer"][rows, 0, 0, :nzones]
+            sent = lax.ppermute(
+                state[key], "brick", [(i, i ^ b) for i in range(bricks)])
+        else:
+            return
+        if anchor is not None:
             sent, _ = lax.optimization_barrier((sent, anchor))
-        if sent:
-            for key, value in sent.items():
-                state[key] = state[key] + value
+        state[key] = state[key] + sent
 
     narrow_head = jnp.concatenate(
         [velocity[:, 0:2].reshape((6,) + enthalpy.shape[1:]), pressure[0:2],
@@ -207,7 +212,7 @@
     while zone_bits or duct_bits:
         advance(iterate)
     totals = state["totals"]
-    gathered = state["buffer"]
+    gathered = state["buffer"][:rows]
     iterate, heat_new, solv_new, totals, gathered = lax.optimization_barrier(
         (iterate, heat_new, solv_new, totals, gathered))
 

time: 183 us -> 159 us (0.87)
  waiting for transfers between devices: 41.6 us -> 13.9 us
  other arithmetic: 43.2 us -> 34.3 us
  starting transfers between devices: 33.1 us -> 40 us
  local copies, waits for them, and re-layouts: 57.8 us -> 63.6 us
    ppermute x3, waiting for transfers between devices: 22 us -> 0.01 us  [neighbours(): from_left = lax.ppermute(tail, ALL, [(i, i + 1) for i in range(count - 1)])]
    ppermute x3, starting transfers between devices: 19.6 us -> 28.4 us  [neighbours(): from_right = lax.ppermute(head, ALL, [(i + 1, i) for i in range(count - 1)])]
    ppermute x11 -> x8, waiting for transfers between devices: 19.6 us -> 13.9 us  [the longest x5 8.17 us: advance(): lax.ppermute(state[key], 'brick', [(i, i ^ b) for i in range(bricks)])]
    unnamed x89 -> x101, local copies, waits for them, and re-layouts: 12.9 us -> 17.3 us
    add x11 -> x8, other arithmetic: 3.43 us -> 0.08 us  [advance(): state[key] = state[key] + sent]
    slice x22 -> x23, local copies, waits for them, and re-layouts: 21.6 us -> 24.5 us  [shifted_down(): inner = lax.slice_in_dim(values, 0, values.shape[axis] - 1, axis=axis)]
    ppermute x11 -> x8, starting transfers between devices: 7.24 us -> 5.47 us  [the longest x3 3.4 us: advance(): sent = lax.ppermute(state[key], 'zone', [(i, i ^ b) for i in range(rows)])]
  transfers between devices with their start and end apart: 17 -> 14, of which waited for: 8 -> 5; matrix products, arithmetic and copies ran while one was open for 43% -> 46% of each run, Pallas kernels for 0% -> 0%
where the time goes in v4:
time: 159 us; the launch traced here: 158 us
  local copies, waits for them, and re-layouts  63.6 us (40%)
  starting transfers between devices  40 us (25%)
  other arithmetic  34.3 us (22%)
  waiting for transfers between devices  13.9 us (9%)
  between operations  6.11 us (4%)
    ppermute x3, starting transfers between devices, neighbours(): from_right = lax.ppermute(head, ALL, [(i + 1, i) for i in range(count - 1)])  28.4 us
    slice x23, local copies, waits for them, and re-layouts, shifted_down(): inner = lax.slice_in_dim(values, 0, values.shape[axis] - 1, axis=axis)  24.5 us
    unnamed x101, local copies, waits for them, and re-layouts  17.3 us
    ppermute x5, waiting for transfers between devices, advance(): lax.ppermute(state[key], 'brick', [(i, i ^ b) for i in range(bricks)])  8.17 us
    select_n x4, other arithmetic, sweep(): jnp.where(inside, numerator / jnp.where(inside, denominator, 1.0), 0.0)  6.69 us
    mul x3, other arithmetic, momentum(): parts.append(open_here * (centre + time_step * forcing))  6.57 us
    ppermute x3, starting transfers between devices, neighbours(): from_left = lax.ppermute(tail, ALL, [(i, i + 1) for i in range(count - 1)])  6.16 us
    ppermute x3, waiting for transfers between devices, advance(): sent = lax.ppermute(state[key], 'zone', [(i, i ^ b) for i in range(rows)])  5.71 us
  transfers between devices with their start and end apart: 14, of which 5 were waited for; matrix products, arithmetic and copies ran while one was open for 46% of the time, Pallas kernels for 0%

profile of v4, /device:TPU:2, one launch (start us, length us, event | category | flops | bytes accessed | tf_op | source)
XLA Modules:
  0.0 157.9 jit_solution(3666886231362365268)
XLA Ops:
  6.5 2.0 %collective-permute-start.6 = (f32[9,2,8,256]{3,2,1,0:T(8,128)S(1)}, f32[9,2,8,256]{3,2,1,0:T(8,128)S(1)}, u32[]{:S(2)}, u32[]{:S(2)}) collective-permute-start(f32[9,2,8,256]{3,2,1,0:T(8,128)S(1)} %scatter.4), channel_id=1, source_target_pairs={{0,32},{32,0},{64,96},{96,64},{128,160},{160,128},{192,224},{224,1... | collective-permute-start | bytes 442376 | tf_op jit(solution)/shard_map/ppermute | solution.py:152
  11.5 2.0 %collective-permute-start.2 = (f32[10,64,256]{2,1,0:T(8,128)}, f32[10,64,256]{2,1,0:T(8,128)}, u32[]{:S(2)}, u32[]{:S(2)}) collective-permute-start(f32[10,64,256]{2,1,0:T(8,128)} %pad_maximum_fusion.11), channel_id=1, source_target_pairs={{0,1},{1,2},{2,3},{3,4},{4,5},{5,6},{6,7},{7,8},{8,9},{9,10},{10,1... | collective-permute-start | bytes 1966088 | tf_op jit(solution)/shard_map/ppermute | solution.py:21
  14.4 8.4 %collective-permute-start.3 = (f32[10,64,256]{2,1,0:T(8,128)}, f32[10,64,256]{2,1,0:T(8,128)}, u32[]{:S(2)}, u32[]{:S(2)}) collective-permute-start(f32[10,64,256]{2,1,0:T(8,128)} %pad_maximum_fusion.12), channel_id=1, source_target_pairs={{1,0},{2,1},{3,2},{4,3},{5,4},{6,5},{7,6},{8,7},{9,8},{10,9},{11,1... | collective-permute-start | bytes 1966088 | tf_op jit(solution)/shard_map/ppermute | solution.py:22
  23.9 1.9 %collective-permute-start = (f32[10,64,256]{2,1,0:T(8,128)}, f32[10,64,256]{2,1,0:T(8,128)}, u32[]{:S(2)}, u32[]{:S(2)}) collective-permute-start(f32[10,64,256]{2,1,0:T(8,128)} %pad_maximum_fusion.9), channel_id=1, source_target_pairs={{0,1},{1,2},{2,3},{3,4},{4,5},{5,6},{6,7},{7,8},{8,9},{9,10},{10,1... | collective-permute-start | bytes 1966088 | tf_op jit(solution)/shard_map/ppermute | solution.py:21
  26.8 7.8 %collective-permute-start.1 = (f32[10,64,256]{2,1,0:T(8,128)}, f32[10,64,256]{2,1,0:T(8,128)}, u32[]{:S(2)}, u32[]{:S(2)}) collective-permute-start(f32[10,64,256]{2,1,0:T(8,128)} %pad_maximum_fusion.10), channel_id=1, source_target_pairs={{1,0},{2,1},{3,2},{4,3},{5,4},{6,5},{7,6},{8,7},{9,8},{10,9},{11,1... | collective-permute-start | bytes 1966088 | tf_op jit(solution)/shard_map/ppermute | solution.py:22
  34.7 2.1 %fusion.145 = (f32[3,8,64,256]{3,1,2,0:T(8,128)S(1)}, f32[3,10,64,256]{3,1,2,0:T(8,128)}) fusion(f32[3,8,64,256]{3,2,1,0:T(8,128)S(1)} %copy-done.27), kind=kLoop, calls=%fused_computation.227 | loop fusion | bytes 4718592 | tf_op args[0]
  38.1 1.7 %fusion.167 = (f32[8,64,255]{2,0,1:T(8,128)}, f32[8,64,255]{2,0,1:T(8,128)}, f32[8,64,255]{2,0,1:T(8,128)}, f32[8,64,255]{2,0,1:T(8,128)}) fusion(f32[8,64,256]{2,0,1:T(8,128)S(1)} %copy.211, f32[8,64,256]{2,0,1:T(8,128)S(1)} %copy.177), kind=kLoop, calls=%fused_computation.249 | loop fusion | bytes 4177920 | tf_op jit(solution)/shard_map/slice | solution.py:28
  43.8 5.3 %collective-permute-done.7 = f32[9,2,8,256]{3,2,1,0:T(8,128)S(1)} collective-permute-done((f32[9,2,8,256]{3,2,1,0:T(8,128)S(1)}, f32[9,2,8,256]{3,2,1,0:T(8,128)S(1)}, u32[]{:S(2)}, u32[]{:S(2)}) %collective-permute-start.7) | collective-permute-done | bytes 147488 | tf_op jit(solution)/shard_map/ppermute | solution.py:152
  52.9 2.0 %copy.183 = f32[8,64,256]{2,1,0:T(8,128)} copy(f32[8,64,256]{2,0,1:T(8,128)} %get-tuple-element.131) | data formatting | bytes 1048576 | tf_op jit(solution)/shard_map/mul | solution.py:243
  74.1 1.8 %fusion.140 = (f32[16,64,255]{2,0,1:T(8,128)S(1)}, f32[16,64,255]{2,0,1:T(8,128)S(1)}, f32[16,64,255]{2,0,1:T(8,128)S(1)}, f32[16,64,255]{2,0,1:T(8,128)}) fusion(f32[18,64,256]{2,0,1:T(8,128)S(1)} %pad_maximum_fusion.1, f32[18,64,256]{2,0,1:T(8,128)S(1)} %pad_maximum_fusion.2), kind=kLoop, calls=%fused_computation.222 | loop fusion | bytes 8355840 | tf_op jit(solution)/shard_map/slice | solution.py:28
  75.9 2.2 %fusion.138 = (f32[16,63,256]{2,0,1:T(8,128)}, f32[16,63,256]{2,0,1:T(8,128)}, f32[16,63,256]{2,0,1:T(8,128)}, f32[16,63,256]{2,0,1:T(8,128)}) fusion(f32[18,64,256]{2,0,1:T(8,128)S(1)} %pad_maximum_fusion.1, f32[18,64,256]{2,0,1:T(8,128)S(1)} %pad_maximum_fusion.2), kind=kLoop, calls=%fused_computation.220 | loop fusion | bytes 8257536 | tf_op jit(solution)/shard_map/slice | solution.py:28
  78.1 1.8 %fusion.137 = (f32[14,64,255]{2,0,1:T(8,128)}, f32[14,64,255]{2,0,1:T(8,128)}) fusion(f32[18,64,256]{2,0,1:T(8,128)S(1)} %pad_maximum_fusion.1), kind=kLoop, calls=%fused_computation.219 | loop fusion | bytes 3655680 | tf_op jit(solution)/shard_map/slice | solution.py:28
  81.5 1.7 %fusion.135 = (f32[12,64,255]{2,0,1:T(8,128)}, f32[12,64,255]{2,0,1:T(8,128)}) fusion(f32[18,64,256]{2,0,1:T(8,128)S(1)} %pad_maximum_fusion.1), kind=kLoop, calls=%fused_computation.217 | loop fusion | bytes 3133440 | tf_op jit(solution)/shard_map/slice | solution.py:28
  84.8 1.8 %fusion.133 = (f32[10,64,255]{2,0,1:T(8,128)}, f32[10,64,255]{2,0,1:T(8,128)}) fusion(f32[18,64,256]{2,0,1:T(8,128)S(1)} %pad_maximum_fusion.1), kind=kLoop, calls=%fused_computation.215 | loop fusion | bytes 2611200 | tf_op jit(solution)/shard_map/slice | solution.py:28
  87.5 2.8 %fusion.75 = f32[10,64,256]{2,0,1:T(8,128)S(1)} fusion(f32[3,10,64,256]{3,1,2,0:T(8,128)S(1)} %copy-done, f32[3,8,64,256]{3,1,2,0:T(8,128)S(1)} %get-tuple-element.83, f32[3,2,64,256]{3,1,2,0:T(2,128)S(1)} %copy.162, f32[10,64,255]{2,0,1:T(8,128)S(1)} %get-tuple-element.80, f32[10,64,255]{2,0,1:T(8,128)S(1)} %get-tuple-element.79, ...), kind=kLoop, calls=%fused_computation.104 | loop fusion | flops 2457600 | bytes 8488960 | tf_op jit(solution)/shard_map/mul | solution.py:56
  93.4 2.6 %fusion.13 = f32[10,64,256]{2,0,1:T(8,128)S(1)} fusion(f32[3,8,64,256]{3,1,2,0:T(8,128)S(1)} %get-tuple-element.83, f32[3,2,64,256]{3,1,2,0:T(2,128)S(1)} %copy.162, f32[3,10,64,256]{3,1,2,0:T(8,128)S(1)} %copy-done, f32[1,64,256]{2,0,1:T(1,128)S(1)} %copy.178, f32[8,64,256]{2,0,1:T(8,128)S(1)} %copy.177, f32[1,64,256]{2,0,1:T(1,128)S(1)} %copy.176, ...), kind=kLoop, calls=%fused_computation.22 | loop fusion | flops 3112960 | bytes 9128960 | tf_op jit(solution)/shard_map/mul | solution.py:56
  99.1 2.2 %collective-permute-start.4 = (f32[4,64,256]{2,0,1:T(4,128)S(1)}, f32[4,64,256]{2,0,1:T(4,128)S(1)}, u32[]{:S(2)}, u32[]{:S(2)}) collective-permute-start(f32[4,64,256]{2,0,1:T(4,128)S(1)} %get-tuple-element.146), channel_id=1, source_target_pairs={{0,1},{1,2},{2,3},{3,4},{4,5},{5,6},{6,7},{7,8},{8,9},{9,10},{10,1... | collective-permute-start | bytes 786440 | tf_op jit(solution)/shard_map/ppermute | solution.py:21
  101.3 12.1 %collective-permute-start.5 = (f32[4,64,256]{2,0,1:T(4,128)S(1)}, f32[4,64,256]{2,0,1:T(4,128)S(1)}, u32[]{:S(2)}, u32[]{:S(2)}) collective-permute-start(f32[4,64,256]{2,0,1:T(4,128)S(1)} %get-tuple-element.147), channel_id=1, source_target_pairs={{1,0},{2,1},{3,2},{4,3},{5,4},{6,5},{7,6},{8,7},{9,8},{10,9},{11,1... | collective-permute-start | bytes 786440 | tf_op jit(solution)/shard_map/ppermute | solution.py:22
  113.8 1.7 %fusion.104 = (f32[8,64,256]{2,0,1:T(8,128)S(1)}, f32[8,64,256]{2,0,1:T(8,128)S(1)}, f32[1,8,64,256]{3,1,2,0:T(8,128)S(1)}, f32[1,8,64,256]{3,1,2,0:T(8,128)S(1)}, f32[8,64,256]{2,0,1:T(8,128)S(1)}) fusion(f32[8,64,256]{2,0,1:T(8,128)S(1)} %copy.177, f32[1,64,256]{2,0,1:T(1,128)S(1)} %copy.178, f32[1,64,256]{2,0,1:T(1,128)S(1)} %copy.176, ...), kind=kLoop, calls=%fused_computation.150 | loop fusion | flops 5373952 | bytes 9021440 | tf_op jit(solution)/shard_map/sub | solution.py:202
  121.2 2.0 %fusion.58 = (f32[16,64,256]{2,0,1:T(8,128)S(1)}, f32[16,64,256]{2,0,1:T(8,128)S(1)}) fusion(f32[18,64,256]{2,0,1:T(8,128)S(1)} %pad_maximum_fusion.2, f32[18,64,256]{2,0,1:T(8,128)S(1)} %pad_maximum_fusion.1, f32[16,64,255]{2,0,1:T(8,128)S(1)} %get-tuple-element.166, f32[16,64,255]{2,0,1:T(8,128)S(1)} %get-tuple-element.74, ...), kind=kLoop, calls=%fused_computation.80 | loop fusion | flops 9175040 | bytes 16695296 | tf_op jit(solution)/shard_map/jit(_where)/select_n | solution.py:102
  125.6 2.1 %fusion.48 = f32[14,64,256]{2,0,1:T(8,128)S(1)} fusion(f32[16,64,256]{2,0,1:T(8,128)S(1)} %get-tuple-element.100, f32[16,64,256]{2,0,1:T(8,128)S(1)} %get-tuple-element.99, f32[18,64,256]{2,0,1:T(8,128)S(1)} %pad_maximum_fusion.1, f32[14,64,255]{2,0,1:T(8,128)S(1)} %get-tuple-element.98, f32[14,64,255]{2,0,1:T(8,128)S(1)} %copy-done.11, ...), kind=kLoop, calls=%fused_computation.66 | loop fusion | flops 7569408 | bytes 13690880 | tf_op jit(solution)/shard_map/jit(_where)/select_n | solution.py:102
  130.0 2.1 %fusion.40 = f32[12,64,256]{2,0,1:T(8,128)S(1)} fusion(f32[16,64,256]{2,0,1:T(8,128)S(1)} %get-tuple-element.100, f32[14,64,256]{2,0,1:T(8,128)S(1)} %fusion.48, f32[18,64,256]{2,0,1:T(8,128)S(1)} %pad_maximum_fusion.1, f32[12,64,255]{2,0,1:T(8,128)S(1)} %get-tuple-element.94, f32[12,64,255]{2,0,1:T(8,128)S(1)} %copy-done.9, ...), kind=kLoop, calls=%fused_computation.54 | loop fusion | flops 6488064 | bytes 11735040 | tf_op jit(solution)/shard_map/jit(_where)/select_n | solution.py:102
  134.1 2.2 %fusion.31 = (f32[10,64,256]{2,0,1:T(8,128)S(1)}, pred[10,64,256]{2,0,1:T(8,128)(4,1)S(1)}) fusion(f32[16,64,256]{2,0,1:T(8,128)S(1)} %get-tuple-element.100, f32[12,64,256]{2,0,1:T(8,128)S(1)} %fusion.40, f32[8,64,256]{2,0,1:T(8,128)S(1)} %copy-done.4, f32[5,64,256]{2,0,1:T(8,128)S(1)} %copy.159, f32[5,64,256]{2,0,1:T(8,128)S(1)} %copy.161, ...), kind=kLoop, calls=%fused_computation.41 | loop fusion | flops 5570560 | bytes 9811968 | tf_op jit(solution)/shard_map/div | solution.py:102
  139.0 6.2 %collective-permute-done.13 = f32[8]{0:T(128)S(1)} collective-permute-done((f32[8]{0:T(128)S(1)}, f32[8]{0:T(128)S(1)}, u32[]{:S(2)}, u32[]{:S(2)}) %collective-permute-start.13) | collective-permute-done | bytes 64 | tf_op jit(solution)/shard_map/ppermute | solution.py:159
  (215 shorter events, 73.1 us)
Async XLA Ops:
  2.1 8.5 %copy-start.25 = (f32[8,64,256]{2,1,0:T(8,128)S(1)}, f32[8,64,256]{2,1,0:T(8,128)}, u32[]{:S(2)}) copy-start(f32[8,64,256]{2,1,0:T(8,128)} %param.16) | copy-start | bytes 1572868
  6.5 36.2 %collective-permute-start.6 = (f32[9,2,8,256]{3,2,1,0:T(8,128)S(1)}, f32[9,2,8,256]{3,2,1,0:T(8,128)S(1)}, u32[]{:S(2)}, u32[]{:S(2)}) collective-permute-start(f32[9,2,8,256]{3,2,1,0:T(8,128)S(1)} %scatter.4), channel_id=1, source_target_pairs={{0,32},{32,0},{64,96},{96,64},{128,160},{160,128},{192,224},{224,1... | collective-permute-start | bytes 442376 | tf_op jit(solution)/shard_map/ppermute | solution.py:152
  11.5 11.4 %copy-start.28 = (f32[8,64,256]{2,1,0:T(8,128)S(1)}, f32[8,64,256]{2,1,0:T(8,128)}, u32[]{:S(2)}) copy-start(f32[8,64,256]{2,1,0:T(8,128)} %param.17) | copy-start | bytes 1572868
  11.5 45.7 %collective-permute-start.2 = (f32[10,64,256]{2,1,0:T(8,128)}, f32[10,64,256]{2,1,0:T(8,128)}, u32[]{:S(2)}, u32[]{:S(2)}) collective-permute-start(f32[10,64,256]{2,1,0:T(8,128)} %pad_maximum_fusion.11), channel_id=1, source_target_pairs={{0,1},{1,2},{2,3},{3,4},{4,5},{5,6},{6,7},{7,8},{8,9},{9,10},{10,1... | collective-permute-start | bytes 1966088 | tf_op jit(solution)/shard_map/ppermute | solution.py:21
  14.4 44.1 %collective-permute-start.3 = (f32[10,64,256]{2,1,0:T(8,128)}, f32[10,64,256]{2,1,0:T(8,128)}, u32[]{:S(2)}, u32[]{:S(2)}) collective-permute-start(f32[10,64,256]{2,1,0:T(8,128)} %pad_maximum_fusion.12), channel_id=1, source_target_pairs={{1,0},{2,1},{3,2},{4,3},{5,4},{6,5},{7,6},{8,7},{9,8},{10,9},{11,1... | collective-permute-start | bytes 1966088 | tf_op jit(solution)/shard_map/ppermute | solution.py:22
  23.0 11.6 %copy-start.27 = (f32[3,8,64,256]{3,2,1,0:T(8,128)S(1)}, f32[3,8,64,256]{3,2,1,0:T(8,128)}, u32[]{:S(2)}) copy-start(f32[3,8,64,256]{3,2,1,0:T(8,128)} %param.13) | copy-start | bytes 4718596
  23.9 43.1 %collective-permute-start = (f32[10,64,256]{2,1,0:T(8,128)}, f32[10,64,256]{2,1,0:T(8,128)}, u32[]{:S(2)}, u32[]{:S(2)}) collective-permute-start(f32[10,64,256]{2,1,0:T(8,128)} %pad_maximum_fusion.9), channel_id=1, source_target_pairs={{0,1},{1,2},{2,3},{3,4},{4,5},{5,6},{6,7},{7,8},{8,9},{9,10},{10,1... | collective-permute-start | bytes 1966088 | tf_op jit(solution)/shard_map/ppermute | solution.py:21
  26.8 38.1 %collective-permute-start.1 = (f32[10,64,256]{2,1,0:T(8,128)}, f32[10,64,256]{2,1,0:T(8,128)}, u32[]{:S(2)}, u32[]{:S(2)}) collective-permute-start(f32[10,64,256]{2,1,0:T(8,128)} %pad_maximum_fusion.10), channel_id=1, source_target_pairs={{1,0},{2,1},{3,2},{4,3},{5,4},{6,5},{7,6},{8,7},{9,8},{10,9},{11,1... | collective-permute-start | bytes 1966088 | tf_op jit(solution)/shard_map/ppermute | solution.py:22
  42.7 6.4 %collective-permute-start.7 = (f32[9,2,8,256]{3,2,1,0:T(8,128)S(1)}, f32[9,2,8,256]{3,2,1,0:T(8,128)S(1)}, u32[]{:S(2)}, u32[]{:S(2)}) collective-permute-start(f32[9,2,8,256]{3,2,1,0:T(8,128)S(1)} %add.621), channel_id=1, source_target_pairs={{0,64},{32,96},{64,0},{96,32},{128,192},{160,224},{192,128},{224,1... | collective-permute-start | bytes 442376 | tf_op jit(solution)/shard_map/ppermute | solution.py:152
  43.8 11.0 %copy-start.47 = (f32[8]{0:T(128)S(1)}, f32[8]{0:T(128)}, u32[]{:S(2)}) copy-start(f32[8]{0:T(128)} %param.21) | copy-start | bytes 100
  49.1 6.7 %collective-permute-start.8 = (f32[9,2,8,256]{3,2,1,0:T(8,128)S(1)}, f32[9,2,8,256]{3,2,1,0:T(8,128)S(1)}, u32[]{:S(2)}, u32[]{:S(2)}) collective-permute-start(f32[9,2,8,256]{3,2,1,0:T(8,128)S(1)} %add.622), channel_id=1, source_target_pairs={{0,128},{32,160},{64,192},{96,224},{128,0},{160,32},{192,64},{224,... | collective-permute-start | bytes 442376 | tf_op jit(solution)/shard_map/ppermute | solution.py:152
  55.9 1.2 collective-permute-start.9
  57.2 38.9 %collective-permute-start.10 = (f32[8]{0:T(128)S(1)}, f32[8]{0:T(128)S(1)}, u32[]{:S(2)}, u32[]{:S(2)}) collective-permute-start(f32[8]{0:T(128)S(1)} %fusion.130), channel_id=1, source_target_pairs={{0,2},{1,3},{2,0},{3,1},{4,6},{5,7},{6,4},{7,5},{8,10},{9,11},{10,... | collective-permute-start | bytes 104 | tf_op jit(solution)/shard_map/ppermute | solution.py:159
  96.1 36.7 %collective-permute-start.11 = (f32[8]{0:T(128)S(1)}, f32[8]{0:T(128)S(1)}, u32[]{:S(2)}, u32[]{:S(2)}) collective-permute-start(f32[8]{0:T(128)S(1)} %add.625), channel_id=1, source_target_pairs={{0,4},{1,5},{2,6},{3,7},{4,0},{5,1},{6,2},{7,3},{8,12},{9,13},{10,... | collective-permute-start | bytes 104 | tf_op jit(solution)/shard_map/ppermute | solution.py:159
  98.7 15.1 %copy-start.40 = (f32[8,63,256]{2,0,1:T(8,128)S(1)}, f32[8,63,256]{2,0,1:T(8,128)}, u32[]{:S(2)}) copy-start(f32[8,63,256]{2,0,1:T(8,128)} %get-tuple-element.143) | copy-start | bytes 1548292
  98.7 15.1 %copy-start.43 = (s32[8,64,256]{2,1,0:T(8,128)S(1)}, s32[8,64,256]{2,1,0:T(8,128)}, u32[]{:S(2)}) copy-start(s32[8,64,256]{2,1,0:T(8,128)} %param.18) | copy-start | bytes 1572868
  99.0 14.8 %copy-start.3 = (f32[8,64,255]{2,0,1:T(8,128)S(1)}, f32[8,64,255]{2,0,1:T(8,128)}, u32[]{:S(2)}) copy-start(f32[8,64,255]{2,0,1:T(8,128)} %get-tuple-element.139) | copy-start | bytes 1566724
  99.0 14.8 %copy-start.35 = (f32[8,64,255]{2,0,1:T(8,128)S(1)}, f32[8,64,255]{2,0,1:T(8,128)}, u32[]{:S(2)}) copy-start(f32[8,64,255]{2,0,1:T(8,128)} %get-tuple-element.168) | copy-start | bytes 1566724
  99.0 14.8 %copy-start.36 = (f32[8,64,255]{2,0,1:T(8,128)S(1)}, f32[8,64,255]{2,0,1:T(8,128)}, u32[]{:S(2)}) copy-start(f32[8,64,255]{2,0,1:T(8,128)} %get-tuple-element.169) | copy-start | bytes 1566724
  99.0 14.8 %copy-start.39 = (f32[8,63,256]{2,0,1:T(8,128)S(1)}, f32[8,63,256]{2,0,1:T(8,128)}, u32[]{:S(2)}) copy-start(f32[8,63,256]{2,0,1:T(8,128)} %get-tuple-element.142) | copy-start | bytes 1548292
  99.1 20.5 %collective-permute-start.4 = (f32[4,64,256]{2,0,1:T(4,128)S(1)}, f32[4,64,256]{2,0,1:T(4,128)S(1)}, u32[]{:S(2)}, u32[]{:S(2)}) collective-permute-start(f32[4,64,256]{2,0,1:T(4,128)S(1)} %get-tuple-element.146), channel_id=1, source_target_pairs={{0,1},{1,2},{2,3},{3,4},{4,5},{5,6},{6,7},{7,8},{8,9},{9,10},{10,1... | collective-permute-start | bytes 786440 | tf_op jit(solution)/shard_map/ppermute | solution.py:21
  101.3 18.3 %collective-permute-start.5 = (f32[4,64,256]{2,0,1:T(4,128)S(1)}, f32[4,64,256]{2,0,1:T(4,128)S(1)}, u32[]{:S(2)}, u32[]{:S(2)}) collective-permute-start(f32[4,64,256]{2,0,1:T(4,128)S(1)} %get-tuple-element.147), channel_id=1, source_target_pairs={{1,0},{2,1},{3,2},{4,3},{5,4},{6,5},{7,6},{8,7},{9,8},{10,9},{11,1... | collective-permute-start | bytes 786440 | tf_op jit(solution)/shard_map/ppermute | solution.py:22
  132.8 4.8 %collective-permute-start.12 = (f32[8]{0:T(128)S(1)}, f32[8]{0:T(128)S(1)}, u32[]{:S(2)}, u32[]{:S(2)}) collective-permute-start(f32[8]{0:T(128)S(1)} %add.626), channel_id=1, source_target_pairs={{0,8},{1,9},{2,10},{3,11},{4,12},{5,13},{6,14},{7,15},{8,0},{9,1},... | collective-permute-start | bytes 104 | tf_op jit(solution)/shard_map/ppermute | solution.py:159
  137.7 7.5 %collective-permute-start.13 = (f32[8]{0:T(128)S(1)}, f32[8]{0:T(128)S(1)}, u32[]{:S(2)}, u32[]{:S(2)}) collective-permute-start(f32[8]{0:T(128)S(1)} %add.627), channel_id=1, source_target_pairs={{0,16},{1,17},{2,18},{3,19},{4,20},{5,21},{6,22},{7,23},{8,24},{9,... | collective-permute-start | bytes 104 | tf_op jit(solution)/shard_map/ppermute | solution.py:159
  (38 other events, 76.1 us)

commit v5 on v4

v5 whole, which is shorter than its diff:
```python
import jax
import jax.numpy as jnp
from jax import lax
from jax.experimental import pallas as pl
from jax.experimental.pallas import tpu as pltpu
from jax.sharding import PartitionSpec as P

ITERS = 4
ALL = ("zone", "brick")


time_step = 0.2
viscosity = 0.1
diffusivity = 0.1
buoyancy = 0.5
evaporation = 0.5
latent_heat = 0.8
solvent_limit = 0.2


def neighbours(head, tail):
    count = lax.axis_size(ALL)
    from_left = lax.ppermute(tail, ALL, [(i, i + 1) for i in range(count - 1)])
    from_right = lax.ppermute(head, ALL, [(i + 1, i) for i in range(count - 1)])
    return from_left, from_right


def _down(v, axis):
    idx = lax.broadcasted_iota(jnp.int32, v.shape, axis)
    return jnp.where(idx == 0, 0.0, pltpu.roll(v, 1, axis))


def _up(v, axis):
    n = v.shape[axis]
    idx = lax.broadcasted_iota(jnp.int32, v.shape, axis)
    return jnp.where(idx == n - 1, 0.0, pltpu.roll(v, n - 1, axis))


def _laplacian_plane(back, centre, front):
    lap = back + front + _down(centre, 0) + _up(centre, 0)
    return lap + _down(centre, 1) + _up(centre, 1) - 6.0 * centre


def stage_one_kernel(vel2, pres5, heat1, poro5, solv1, solid,
                     star_out, source_out, heat_out, solv_out, star):
    wide = star.shape[1]
    cells = source_out.shape[0]

    def momentum_plane(j, carry):
        open_here = poro5[j + 4]
        pressure_mid = pres5[j + 4]
        for component in range(3):
            centre = vel2[component, j + 1]
            laplacian = _laplacian_plane(vel2[component, j], centre, vel2[component, j + 2])
            if component == 0:
                gradient = 0.5 * (pres5[j + 5] - pres5[j + 3])
            else:
                axis = component - 1
                gradient = 0.5 * (_up(pressure_mid, axis) - _down(pressure_mid, axis))
            forcing = viscosity * laplacian - gradient
            if component == 1:
                forcing = forcing + buoyancy * heat1[j]
            star[component, j] = open_here * (centre + time_step * forcing)
        return carry

    lax.fori_loop(0, wide, momentum_plane, 0)

    def cell_plane(x, carry):
        j = x + 1
        s0 = star[0, j]
        s1 = star[1, j]
        s2 = star[2, j]
        result = 0.5 * (star[0, j + 1] - star[0, j - 1])
        result = result + 0.5 * (_up(s1, 0) - _down(s1, 0))
        result = result + 0.5 * (_up(s2, 1) - _down(s2, 1))
        source_out[x] = result / time_step
        star_out[0, x] = s0
        star_out[1, x] = s1
        star_out[2, x] = s2
        drying = time_step * evaporation * solid[x].astype(jnp.float32) * solv1[j]
        for scalar, out, latent in ((heat1, heat_out, True), (solv1, solv_out, False)):
            back = scalar[x]
            centre = scalar[j]
            front = scalar[x + 2]
            laplacian = _laplacian_plane(back, centre, front)
            advect = jnp.maximum(s0, 0.0) * (centre - back) + jnp.minimum(s0, 0.0) * (front - centre)
            advect = advect + jnp.maximum(s1, 0.0) * (centre - _down(centre, 0))
            advect = advect + jnp.minimum(s1, 0.0) * (_up(centre, 0) - centre)
            advect = advect + jnp.maximum(s2, 0.0) * (centre - _down(centre, 1))
            advect = advect + jnp.minimum(s2, 0.0) * (_up(centre, 1) - centre)
            moved = centre + time_step * (diffusivity * laplacian - advect)
            if latent:
                out[x] = moved - latent_heat * drying
            else:
                out[x] = moved - drying
        return carry

    lax.fori_loop(0, cells, cell_plane, 0)


def stage_two_kernel(pres5, poro5, source4, star_in, vel_out, pres_out, even, odd):
    cells = pres_out.shape[0]
    buffers = (even, odd)
    prev = pres5
    for k in range(ITERS):
        out = buffers[k % 2]
        count = source4.shape[0] - 2 * k

        def body(j, carry, k=k, prev=prev, out=out):
            open_here = poro5[k + j + 1]
            pressure_mid = prev[j + 1]
            face_back = 0.5 * (open_here + poro5[k + j])
            face_front = 0.5 * (open_here + poro5[k + j + 2])
            numerator = face_back * prev[j] + face_front * prev[j + 2] - source4[k + j]
            denominator = face_back + face_front
            for axis in (0, 1):
                face_low = 0.5 * (open_here + _down(open_here, axis))
                face_high = 0.5 * (open_here + _up(open_here, axis))
                numerator = (
                    numerator
                    + face_low * _down(pressure_mid, axis)
                    + face_high * _up(pressure_mid, axis)
                )
                denominator = denominator + face_low + face_high
            inside = open_here > 0.0
            out[j] = jnp.where(inside, numerator / jnp.where(inside, denominator, 1.0), 0.0)
            return carry

        lax.fori_loop(0, count, body, 0)
        prev = out
    final = prev

    def finish(x, carry):
        here = final[x + 1]
        pres_out[x] = here
        scale = time_step * poro5[x + 5]
        vel_out[0, x] = star_in[0, x] - scale * (0.5 * (final[x + 2] - final[x]))
        vel_out[1, x] = star_in[1, x] - scale * (0.5 * (_up(here, 0) - _down(here, 0)))
        vel_out[2, x] = star_in[2, x] - scale * (0.5 * (_up(here, 1) - _down(here, 1)))
        return carry

    lax.fori_loop(0, cells, finish, 0)


def _params():
    return pltpu.CompilerParams(vmem_limit_bytes=48 * 1024 * 1024)


def stage_one(vel2, pres5, heat1, poro5, solv1, solid):
    cells = solid.shape[0]
    plane = solid.shape[1:]
    f32 = jnp.float32
    outs = (
        jax.ShapeDtypeStruct((3, cells) + plane, f32),
        jax.ShapeDtypeStruct((cells,) + plane, f32),
        jax.ShapeDtypeStruct((cells,) + plane, f32),
        jax.ShapeDtypeStruct((cells,) + plane, f32),
    )
    points = cells * plane[0] * plane[1]
    return pl.pallas_call(
        stage_one_kernel,
        out_shape=outs,
        scratch_shapes=[pltpu.VMEM((3, cells + 2) + plane, f32)],
        compiler_params=_params(),
        cost_estimate=pl.CostEstimate(
            flops=260 * points, transcendentals=0, bytes_accessed=4 * points * 19),
    )(vel2, pres5, heat1, poro5, solv1, solid)


def stage_two(pres5, poro5, source4, vel_star):
    cells = vel_star.shape[1]
    plane = vel_star.shape[2:]
    f32 = jnp.float32
    outs = (
        jax.ShapeDtypeStruct((3, cells) + plane, f32),
        jax.ShapeDtypeStruct((cells,) + plane, f32),
    )
    points = cells * plane[0] * plane[1]
    return pl.pallas_call(
        stage_two_kernel,
        out_shape=outs,
        scratch_shapes=[pltpu.VMEM((source4.shape[0],) + plane, f32)] * 2,
        compiler_params=_params(),
        cost_estimate=pl.CostEstimate(
            flops=200 * points, transcendentals=0, bytes_accessed=4 * points * 12),
    )(pres5, poro5, source4, vel_star)


def on_device_body(
    velocity,
    enthalpy,
    solvent,
    pressure,
    porosity,
    solid_mask,
    nozzle_mask,
    zone_sizes,
    zone_setpoint,
    duct_source,
    duct_span,
):
    cx = enthalpy.shape[0]
    device = lax.axis_index(ALL)

    starts = jnp.cumsum(zone_sizes) - zone_sizes
    zone_here = jnp.sum((device >= starts).astype(jnp.int32)) - 1
    nzones = zone_sizes.shape[0]
    choose = (jnp.arange(nzones, dtype=jnp.int32) == zone_here).astype(jnp.float32)
    totals = choose * jnp.sum(solvent[:, -1, :])
    count = lax.axis_size(ALL)
    rows = lax.axis_size("zone")

    planes = jnp.stack([enthalpy[:, -1, :], solvent[:, -1, :]])
    buffer = jnp.zeros((rows + 1,) + planes.shape, jnp.float32)
    buffer = lax.dynamic_update_slice(
        buffer, planes[None], (lax.axis_index("zone"), 0, 0, 0)
    )
    buffer = buffer.at[rows, 0, 0, :nzones].set(totals)
    bricks = count // rows
    duct_bits = []
    bit = 1
    while bit < rows:
        duct_bits.append(bit)
        bit *= 2
    zone_bits = []
    bit = 1
    while bit < bricks:
        zone_bits.append(bit)
        bit *= 2
    state = {"buffer": buffer, "totals": None}

    def advance(anchor):
        if duct_bits:
            b = duct_bits.pop(0)
            key = "buffer"
            sent = lax.ppermute(
                state[key], "zone", [(i, i ^ b) for i in range(rows)])
        elif zone_bits:
            b = zone_bits.pop(0)
            key = "totals"
            if state[key] is None:
                state[key] = state["buffer"][rows, 0, 0, :nzones]
            sent = lax.ppermute(
                state[key], "brick", [(i, i ^ b) for i in range(bricks)])
        else:
            return
        if anchor is not None:
            sent, _ = lax.optimization_barrier((sent, anchor))
        state[key] = state[key] + sent

    narrow_head = jnp.concatenate(
        [velocity[:, 0:2].reshape((6,) + enthalpy.shape[1:]), pressure[0:2],
         enthalpy[0:1], solvent[0:1]], axis=0)
    narrow_tail = jnp.concatenate(
        [velocity[:, cx - 2:].reshape((6,) + enthalpy.shape[1:]), pressure[cx - 2:],
         enthalpy[cx - 1:], solvent[cx - 1:]], axis=0)
    wide_head = jnp.concatenate([pressure[0:5], porosity[0:5]], axis=0)
    wide_tail = jnp.concatenate([pressure[cx - 5:], porosity[cx - 5:]], axis=0)
    n_left, n_right = neighbours(narrow_head, narrow_tail)
    w_left, w_right = neighbours(wide_head, wide_tail)

    vel2 = jnp.concatenate(
        [n_left[0:6].reshape((3, 2) + enthalpy.shape[1:]), velocity,
         n_right[0:6].reshape((3, 2) + enthalpy.shape[1:])], axis=1)
    pres5 = jnp.concatenate([w_left[0:5], pressure, w_right[0:5]], axis=0)
    poro5 = jnp.concatenate([w_left[5:10], porosity, w_right[5:10]], axis=0)
    heat1 = jnp.concatenate([n_left[8:9], enthalpy, n_right[8:9]], axis=0)
    solv1 = jnp.concatenate([n_left[9:10], solvent, n_right[9:10]], axis=0)

    advance(None)
    advance(None)
    advance(None)
    advance(None)
    vel_star, source, heat_new, solv_new = stage_one(vel2, pres5, heat1, poro5, solv1, solid_mask)
    advance(vel_star)

    s_left, s_right = neighbours(source[0:4], source[cx - 4:])
    source4 = jnp.concatenate([s_left, source, s_right], axis=0)
    advance(source4)

    velocity_new, final = stage_two(pres5, poro5, source4, vel_star)
    while zone_bits or duct_bits:
        advance(final)
    totals = state["totals"]
    gathered = state["buffer"][:rows]

    counts = zone_sizes.astype(jnp.float32) * (cx * enthalpy.shape[2])
    means = totals / counts
    fresh_all = means / (means + solvent_limit)
    fresh = jnp.sum(choose * fresh_all)
    target = jnp.sum(choose * zone_setpoint)
    arrived = lax.dynamic_index_in_dim(gathered, duct_source[0], axis=0, keepdims=False)
    supply_heat = (1.0 - fresh) * arrived[0] + fresh * target
    supply_solv = (1.0 - fresh) * arrived[1]
    column = jnp.arange(enthalpy.shape[2], dtype=jnp.int32)
    inside_box = (column >= duct_span[0, 0]) & (column < duct_span[0, 0] + duct_span[0, 1])
    jets = (nozzle_mask > 0) & inside_box[None, :]
    heat_layer = jnp.where(jets, supply_heat, heat_new[:, 0, :])
    solv_layer = jnp.where(jets, supply_solv, solv_new[:, 0, :])
    enthalpy_new = jnp.concatenate([heat_layer[:, None, :], heat_new[:, 1:, :]], axis=1)
    solvent_new = jnp.concatenate([solv_layer[:, None, :], solv_new[:, 1:, :]], axis=1)
    return (velocity_new, enthalpy_new, solvent_new, final)


def solution(mesh):
    placed = (
        P(None, ALL, None, None),
        P(ALL, None, None),
        P(ALL, None, None),
        P(ALL, None, None),
        P(ALL, None, None),
        P(ALL, None, None),
        P(ALL, None),
        P(),
        P(),
        P(ALL),
        P(ALL, None),
    )
    return jax.shard_map(
        on_device_body,
        mesh=mesh,
        in_specs=placed,
        out_specs=(
            P(None, ALL, None, None),
            P(ALL, None, None),
            P(ALL, None, None),
            P(ALL, None, None),
        ),
        check_vma=False,
    )
```

time: 159 us -> 114 us (0.72)
  the two profiles are of different devices: /device:TPU:2 before, /device:TPU:32 now
where the time goes in v5:
time: 114 us; the launch traced here: 112 us
  starting transfers between devices  41.5 us (36%)
  waiting for transfers between devices  21.7 us (19%)
  Pallas kernels  17.7 us (16%)
  other arithmetic  14.6 us (13%)
  local copies, waits for them, and re-layouts  10.3 us (9%)
  between operations  5.73 us (5%)
    ppermute x3, starting transfers between devices, neighbours(): from_right = lax.ppermute(head, ALL, [(i + 1, i) for i in range(count - 1)])  27.4 us
    ppermute x5, waiting for transfers between devices, advance(): lax.ppermute(state[key], 'brick', [(i, i ^ b) for i in range(bricks)])  11.9 us
    pallas_call x1, Pallas kernels, stage_two(): pl.pallas_call(stage_two_kernel, out_shape=outs, scratch_shapes=[pltpu.VM...  10.5 us
    ppermute x3, waiting for transfers between devices, neighbours(): from_left = lax.ppermute(tail, ALL, [(i, i + 1) for i in range(count - 1)])  8.23 us
    pallas_call x1, Pallas kernels, stage_one(): pl.pallas_call(stage_one_kernel, out_shape=outs, scratch_shapes=[pltpu.VM...  7.22 us
    ppermute x3, starting transfers between devices, neighbours(): from_left = lax.ppermute(tail, ALL, [(i, i + 1) for i in range(count - 1)])  5.74 us
    ppermute x3, starting transfers between devices, advance(): sent = lax.ppermute(state[key], 'zone', [(i, i ^ b) for i in range(rows)])  5.23 us
    ppermute x5, starting transfers between devices, advance(): lax.ppermute(state[key], 'brick', [(i, i ^ b) for i in range(bricks)])  3.13 us
  transfers between devices with their start and end apart: 14, of which 7 were waited for; matrix products, arithmetic and copies ran while one was open for 13% of the time, Pallas kernels for 9%

profile of v5, /device:TPU:32, one launch (start us, length us, event | category | flops | bytes accessed | tf_op | source)
XLA Modules:
  0.0 111.5 jit_solution(6063423955103112855)
XLA Ops:
  0.6 1.2 %fusion.21 = (f32[5,64,256]{2,1,0:T(8,128)S(1)}, f32[5,64,256]{2,1,0:T(8,128)S(1)}) fusion(f32[8,64,256]{2,1,0:T(8,128)} %param.17), kind=kLoop, calls=%fused_computation.52 | loop fusion | bytes 1310720 | tf_op jit(solution)/shard_map/slice | solution.py:258
  2.8 9.8 %collective-permute-start.1 = (f32[10,64,256]{2,1,0:T(8,128)}, f32[10,64,256]{2,1,0:T(8,128)}, u32[]{:S(2)}, u32[]{:S(2)}) collective-permute-start(f32[10,64,256]{2,1,0:T(8,128)} %pad_maximum_fusion.4), channel_id=1, source_target_pairs={{1,0},{2,1},{3,2},{4,3},{5,4},{6,5},{7,6},{8,7},{9,8},{10,9},{11,1... | collective-permute-start | bytes 1966088 | tf_op jit(solution)/shard_map/ppermute | solution.py:24
  13.5 1.9 %collective-permute-start = (f32[10,64,256]{2,1,0:T(8,128)}, f32[10,64,256]{2,1,0:T(8,128)}, u32[]{:S(2)}, u32[]{:S(2)}) collective-permute-start(f32[10,64,256]{2,1,0:T(8,128)} %pad_maximum_fusion.3), channel_id=1, source_target_pairs={{0,1},{1,2},{2,3},{3,4},{4,5},{5,6},{6,7},{7,8},{8,9},{9,10},{10,1... | collective-permute-start | bytes 1966088 | tf_op jit(solution)/shard_map/ppermute | solution.py:23
  15.4 1.5 %slice_reduce_fusion = (f32[]{:T(128)}, f32[8,1,256]{2,1,0:T(1,128)S(1)}) fusion(f32[8,64,256]{2,1,0:T(8,128)} %param.15), kind=kLoop, calls=%fused_computation.41 | loop fusion | flops 2047 | bytes 16388 | tf_op jit(solution)/shard_map/reduce_sum | solution.py:209
  21.4 8.9 %collective-permute-start.3 = (f32[10,64,256]{2,1,0:T(8,128)}, f32[10,64,256]{2,1,0:T(8,128)S(1)}, u32[]{:S(2)}, u32[]{:S(2)}) collective-permute-start(f32[10,64,256]{2,1,0:T(8,128)} %pad_maximum_fusion.6), channel_id=1, source_target_pairs={{1,0},{2,1},{3,2},{4,3},{5,4},{6,5},{7,6},{8,7},{9,8},{10,9},{11,1... | collective-permute-start | bytes 1966088 | tf_op jit(solution)/shard_map/ppermute | solution.py:24
  30.4 1.6 %collective-permute-start.7 = (f32[9,2,8,256]{3,2,1,0:T(8,128)S(1)}, f32[9,2,8,256]{3,2,1,0:T(8,128)}, u32[]{:S(2)}, u32[]{:S(2)}) collective-permute-start(f32[9,2,8,256]{3,2,1,0:T(8,128)S(1)} %add.55), channel_id=1, source_target_pairs={{0,64},{32,96},{64,0},{96,32},{128,192},{160,224},{192,128},{224,1... | collective-permute-start | bytes 442376 | tf_op jit(solution)/shard_map/ppermute | solution.py:236
  32.9 1.9 %collective-permute-start.2 = (f32[10,64,256]{2,1,0:T(8,128)}, f32[10,64,256]{2,1,0:T(8,128)}, u32[]{:S(2)}, u32[]{:S(2)}) collective-permute-start(f32[10,64,256]{2,1,0:T(8,128)} %pad_maximum_fusion.5), channel_id=1, source_target_pairs={{0,1},{1,2},{2,3},{3,4},{4,5},{5,6},{6,7},{7,8},{8,9},{9,10},{10,1... | collective-permute-start | bytes 1966088 | tf_op jit(solution)/shard_map/ppermute | solution.py:23
  36.7 1.6 %add.56 = f32[9,2,8,256]{3,2,1,0:T(8,128)} add(f32[9,2,8,256]{3,2,1,0:T(8,128)S(1)} %add.55, f32[9,2,8,256]{3,2,1,0:T(8,128)} %collective-permute-done.7) | non-fusion elementwise | flops 36864 | bytes 442368 | tf_op jit(solution)/shard_map/add | solution.py:249
  38.3 3.6 %collective-permute-start.8 = (f32[9,2,8,256]{3,2,1,0:T(8,128)}, f32[9,2,8,256]{3,2,1,0:T(8,128)S(1)}, u32[]{:S(2)}, u32[]{:S(2)}) collective-permute-start(f32[9,2,8,256]{3,2,1,0:T(8,128)} %add.56), channel_id=1, source_target_pairs={{0,128},{32,160},{64,192},{96,224},{128,0},{160,32},{192,64},{224,... | collective-permute-start | bytes 442376 | tf_op jit(solution)/shard_map/ppermute | solution.py:236
  43.8 1.4 %collective-permute-done.8 = f32[9,2,8,256]{3,2,1,0:T(8,128)S(1)} collective-permute-done((f32[9,2,8,256]{3,2,1,0:T(8,128)}, f32[9,2,8,256]{3,2,1,0:T(8,128)S(1)}, u32[]{:S(2)}, u32[]{:S(2)}) %collective-permute-start.8) | collective-permute-done | bytes 147488 | tf_op jit(solution)/shard_map/ppermute | solution.py:236
  46.2 1.1 %fusion.15 = (f32[5,64,256]{2,1,0:T(8,128)S(1)}, f32[5,64,256]{2,1,0:T(8,128)S(1)}) fusion(f32[10,64,256]{2,1,0:T(8,128)} %collective-permute-done.1), kind=kLoop, calls=%fused_computation.46 | loop fusion | bytes 1310720 | tf_op jit(solution)/shard_map/slice | solution.py:266
  47.3 1.4 %fusion.14 = (f32[5,64,256]{2,1,0:T(8,128)S(1)}, f32[5,64,256]{2,1,0:T(8,128)S(1)}) fusion(f32[10,64,256]{2,1,0:T(8,128)} %collective-permute-done), kind=kLoop, calls=%fused_computation.45 | loop fusion | bytes 1310720 | tf_op jit(solution)/shard_map/slice | solution.py:266
  49.8 7.0 %collective-permute-done.2 = f32[10,64,256]{2,1,0:T(8,128)} collective-permute-done((f32[10,64,256]{2,1,0:T(8,128)}, f32[10,64,256]{2,1,0:T(8,128)}, u32[]{:S(2)}, u32[]{:S(2)}) %collective-permute-start.2) | collective-permute-done | bytes 655392 | tf_op jit(solution)/shard_map/ppermute | solution.py:23
  56.9 1.0 slice.182
  57.9 1.6 %pad_maximum_fusion.vel2 = f32[3,12,64,256]{3,2,1,0:T(8,128)} fusion(f32[3,2,64,256]{3,2,1,0:T(8,128)S(1)} %bitcast.49, f32[3,8,64,256]{3,2,1,0:T(8,128)S(1)} %copy-done.3, f32[3,2,64,256]{3,2,1,0:T(8,128)S(1)} %bitcast.50), kind=kLoop, calls=%fused_computation | loop fusion | flops 1179648 | bytes 4718592 | tf_op jit(solution)/shard_map/concatenate | solution.py:262
  61.6 7.2 %shard_map.138 = (f32[3,8,64,256]{3,2,1,0:T(8,128)}, f32[8,64,256]{2,1,0:T(8,128)S(1)}, f32[8,64,256]{2,1,0:T(8,128)S(1)}, f32[8,64,256]{2,1,0:T(8,128)S(1)}) custom-call(f32[3,12,64,256]{3,2,1,0:T(8,128)} %pad_maximum_fusion.vel2, f32[18,64,256]{2,1,0:T(8,128)S(1)} %pad_maximum_fusion.1.pres5, f32[10,64,256]{2,1,0:T(8,128)S(1)} %pad_maximum_fusion.7.heat1, ...), custom_call_target="tpu_custom_call" | custom-call | flops 34078720 | bytes 9961472 | tf_op jit(solution)/shard_map/pallas_call | solution.py:160
  68.8 1.9 %collective-permute-start.4 = (f32[4,64,256]{2,1,0:T(8,128)S(1)}, f32[4,64,256]{2,1,0:T(8,128)S(1)}, u32[]{:S(2)}, u32[]{:S(2)}) collective-permute-start(f32[4,64,256]{2,1,0:T(8,128)S(1)} %get-tuple-element.51), channel_id=1, source_target_pairs={{0,1},{1,2},{2,3},{3,4},{4,5},{5,6},{6,7},{7,8},{8,9},{9,10},{10,1... | collective-permute-start | bytes 786440 | tf_op jit(solution)/shard_map/ppermute | solution.py:23
  70.9 8.8 %collective-permute-start.5 = (f32[4,64,256]{2,1,0:T(8,128)S(1)}, f32[4,64,256]{2,1,0:T(8,128)S(1)}, u32[]{:S(2)}, u32[]{:S(2)}) collective-permute-start(f32[4,64,256]{2,1,0:T(8,128)S(1)} %get-tuple-element.50), channel_id=1, source_target_pairs={{1,0},{2,1},{3,2},{4,3},{5,4},{6,5},{7,6},{8,7},{9,8},{10,9},{11,1... | collective-permute-start | bytes 786440 | tf_op jit(solution)/shard_map/ppermute | solution.py:24
  80.5 2.8 %collective-permute-done.10 = f32[8]{0:T(128)S(1)} collective-permute-done((f32[8]{0:T(128)S(1)}, f32[8]{0:T(128)S(1)}, u32[]{:S(2)}, u32[]{:S(2)}) %collective-permute-start.10) | collective-permute-done | bytes 64 | tf_op jit(solution)/shard_map/ppermute | solution.py:243
  83.3 1.2 %collective-permute-done.4 = f32[4,64,256]{2,1,0:T(8,128)S(1)} collective-permute-done((f32[4,64,256]{2,1,0:T(8,128)S(1)}, f32[4,64,256]{2,1,0:T(8,128)S(1)}, u32[]{:S(2)}, u32[]{:S(2)}) %collective-permute-start.4) | collective-permute-done | bytes 262176 | tf_op jit(solution)/shard_map/ppermute | solution.py:23
  84.7 10.5 %shard_map.139 = (f32[3,8,64,256]{3,2,1,0:T(8,128)}, f32[8,64,256]{2,1,0:T(8,128)}) custom-call(f32[18,64,256]{2,1,0:T(8,128)S(1)} %pad_maximum_fusion.1.pres5, f32[18,64,256]{2,1,0:T(8,128)S(1)} %pad_maximum_fusion.2.poro5, f32[16,64,256]{2,1,0:T(8,128)S(1)} %constant_dynamic-update-slice_fusion.source4, f32[3,8,64,256]{3,2,1,0:T(8,128)S(1)} %copy-done), custom_call_target="tpu_custom_call" | custom-call | flops 26214400 | bytes 6291456 | tf_op jit(solution)/shard_map/pallas_call | solution.py:179
  95.8 3.9 %collective-permute-done.12 = f32[8]{0:T(128)S(1)} collective-permute-done((f32[8]{0:T(128)S(1)}, f32[8]{0:T(128)S(1)}, u32[]{:S(2)}, u32[]{:S(2)}) %collective-permute-start.12) | collective-permute-done | bytes 64 | tf_op jit(solution)/shard_map/ppermute | solution.py:243
  99.7 2.3 %collective-permute-start.13 = (f32[8]{0:T(128)S(1)}, f32[8]{0:T(128)S(1)}, u32[]{:S(2)}, u32[]{:S(2)}) collective-permute-start(f32[8]{0:T(128)S(1)} %add.61), channel_id=1, source_target_pairs={{0,16},{1,17},{2,18},{3,19},{4,20},{5,21},{6,22},{7,23},{8,24},{9,... | collective-permute-start | bytes 104 | tf_op jit(solution)/shard_map/ppermute | solution.py:243
  102.0 5.2 %collective-permute-done.13 = f32[8]{0:T(128)S(1)} collective-permute-done((f32[8]{0:T(128)S(1)}, f32[8]{0:T(128)S(1)}, u32[]{:S(2)}, u32[]{:S(2)}) %collective-permute-start.13) | collective-permute-done | bytes 64 | tf_op jit(solution)/shard_map/ppermute | solution.py:243
  (94 shorter events, 16.7 us)
Async XLA Ops:
  1.9 14.9 %copy-start.7 = (f32[8,64,256]{2,1,0:T(8,128)S(1)}, f32[8,64,256]{2,1,0:T(8,128)}, u32[]{:S(2)}) copy-start(f32[8,64,256]{2,1,0:T(8,128)} %param.14) | copy-start | bytes 1572868
  1.9 15.0 %copy-start.13 = (s32[8]{0:T(128)S(1)}, s32[8]{0:T(128)}, u32[]{:S(2)}) copy-start(s32[8]{0:T(128)} %param.20) | copy-start | bytes 100
  2.8 17.5 %copy-start.3 = (f32[3,8,64,256]{3,2,1,0:T(8,128)S(1)}, f32[3,8,64,256]{3,2,1,0:T(8,128)}, u32[]{:S(2)}) copy-start(f32[3,8,64,256]{3,2,1,0:T(8,128)} %param.13) | copy-start | bytes 4718596
  2.8 43.3 %collective-permute-start.1 = (f32[10,64,256]{2,1,0:T(8,128)}, f32[10,64,256]{2,1,0:T(8,128)}, u32[]{:S(2)}, u32[]{:S(2)}) collective-permute-start(f32[10,64,256]{2,1,0:T(8,128)} %pad_maximum_fusion.4), channel_id=1, source_target_pairs={{1,0},{2,1},{3,2},{4,3},{5,4},{6,5},{7,6},{8,7},{9,8},{10,9},{11,1... | collective-permute-start | bytes 1966088 | tf_op jit(solution)/shard_map/ppermute | solution.py:24
  13.5 33.8 %collective-permute-start = (f32[10,64,256]{2,1,0:T(8,128)}, f32[10,64,256]{2,1,0:T(8,128)}, u32[]{:S(2)}, u32[]{:S(2)}) collective-permute-start(f32[10,64,256]{2,1,0:T(8,128)} %pad_maximum_fusion.3), channel_id=1, source_target_pairs={{0,1},{1,2},{2,3},{3,4},{4,5},{5,6},{6,7},{7,8},{8,9},{9,10},{10,1... | collective-permute-start | bytes 1966088 | tf_op jit(solution)/shard_map/ppermute | solution.py:23
  19.3 11.1 %collective-permute-start.6 = (f32[9,2,8,256]{3,2,1,0:T(8,128)S(1)}, f32[9,2,8,256]{3,2,1,0:T(8,128)S(1)}, u32[]{:S(2)}, u32[]{:S(2)}) collective-permute-start(f32[9,2,8,256]{3,2,1,0:T(8,128)S(1)} %scatter.4), channel_id=1, source_target_pairs={{0,32},{32,0},{64,96},{96,64},{128,160},{160,128},{192,224},{224,1... | collective-permute-start | bytes 442376 | tf_op jit(solution)/shard_map/ppermute | solution.py:236
  20.5 9.9 %copy-start.10 = (f32[9,2,8,256]{3,2,1,0:T(8,128)S(1)}, f32[9,2,8,256]{3,2,1,0:T(8,128)}, u32[]{:S(2)}) copy-start(f32[9,2,8,256]{3,2,1,0:T(8,128)} %copy-done.9) | copy-start | bytes 442372
  21.4 13.5 %copy-start.12 = (s32[1,2]{1,0:T(1,128)S(1)}, s32[1,2]{1,0:T(1,128)}, u32[]{:S(2)}) copy-start(s32[1,2]{1,0:T(1,128)} %param.23) | copy-start | bytes 28
  21.4 21.8 %copy-start.14 = (f32[8]{0:T(128)S(1)}, f32[8]{0:T(128)}, u32[]{:S(2)}) copy-start(f32[8]{0:T(128)} %param.21) | copy-start | bytes 100
  21.4 25.9 %collective-permute-start.3 = (f32[10,64,256]{2,1,0:T(8,128)}, f32[10,64,256]{2,1,0:T(8,128)S(1)}, u32[]{:S(2)}, u32[]{:S(2)}) collective-permute-start(f32[10,64,256]{2,1,0:T(8,128)} %pad_maximum_fusion.6), channel_id=1, source_target_pairs={{1,0},{2,1},{3,2},{4,3},{5,4},{6,5},{7,6},{8,7},{9,8},{10,9},{11,1... | collective-permute-start | bytes 1966088 | tf_op jit(solution)/shard_map/ppermute | solution.py:24
  30.4 6.3 %collective-permute-start.7 = (f32[9,2,8,256]{3,2,1,0:T(8,128)S(1)}, f32[9,2,8,256]{3,2,1,0:T(8,128)}, u32[]{:S(2)}, u32[]{:S(2)}) collective-permute-start(f32[9,2,8,256]{3,2,1,0:T(8,128)S(1)} %add.55), channel_id=1, source_target_pairs={{0,64},{32,96},{64,0},{96,32},{128,192},{160,224},{192,128},{224,1... | collective-permute-start | bytes 442376 | tf_op jit(solution)/shard_map/ppermute | solution.py:236
  32.9 24.0 %collective-permute-start.2 = (f32[10,64,256]{2,1,0:T(8,128)}, f32[10,64,256]{2,1,0:T(8,128)}, u32[]{:S(2)}, u32[]{:S(2)}) collective-permute-start(f32[10,64,256]{2,1,0:T(8,128)} %pad_maximum_fusion.5), channel_id=1, source_target_pairs={{0,1},{1,2},{2,3},{3,4},{4,5},{5,6},{6,7},{7,8},{8,9},{9,10},{10,1... | collective-permute-start | bytes 1966088 | tf_op jit(solution)/shard_map/ppermute | solution.py:23
  38.3 6.9 %collective-permute-start.8 = (f32[9,2,8,256]{3,2,1,0:T(8,128)}, f32[9,2,8,256]{3,2,1,0:T(8,128)S(1)}, u32[]{:S(2)}, u32[]{:S(2)}) collective-permute-start(f32[9,2,8,256]{3,2,1,0:T(8,128)} %add.56), channel_id=1, source_target_pairs={{0,128},{32,160},{64,192},{96,224},{128,0},{160,32},{192,64},{224,... | collective-permute-start | bytes 442376 | tf_op jit(solution)/shard_map/ppermute | solution.py:236
  49.7 8.2 %slice-start = ((f32[10,64,256]{2,1,0:T(8,128)}), f32[6,64,256]{2,1,0:T(8,128)S(1)}, s32[]{:S(2)}) async-start(f32[10,64,256]{2,1,0:T(8,128)} %copy-done.5), calls=%async_computation | async-start | bytes 786432 | tf_op jit(solution)/shard_map/slice | solution.py:264
  57.9 1.6 %copy-start.6 = (f32[10,64,256]{2,1,0:T(8,128)S(1)}, f32[10,64,256]{2,1,0:T(8,128)}, u32[]{:S(2)}) copy-start(f32[10,64,256]{2,1,0:T(8,128)} %copy-done.5) | copy-start | bytes 1966084
  68.8 15.7 %collective-permute-start.4 = (f32[4,64,256]{2,1,0:T(8,128)S(1)}, f32[4,64,256]{2,1,0:T(8,128)S(1)}, u32[]{:S(2)}, u32[]{:S(2)}) collective-permute-start(f32[4,64,256]{2,1,0:T(8,128)S(1)} %get-tuple-element.51), channel_id=1, source_target_pairs={{0,1},{1,2},{2,3},{3,4},{4,5},{5,6},{6,7},{7,8},{8,9},{9,10},{10,1... | collective-permute-start | bytes 786440 | tf_op jit(solution)/shard_map/ppermute | solution.py:23
  70.8 8.9 %collective-permute-start.9 = (f32[8]{0:T(128)S(1)}, f32[8]{0:T(128)S(1)}, u32[]{:S(2)}, u32[]{:S(2)}) collective-permute-start(f32[8]{0:T(128)S(1)} %slice_bitcast_fusion.2), channel_id=1, source_target_pairs={{0,1},{1,0},{2,3},{3,2},{4,5},{5,4},{6,7},{7,6},{8,9},{9,8},{10,11... | collective-permute-start | bytes 104 | tf_op jit(solution)/shard_map/ppermute | solution.py:243
  70.9 13.7 %collective-permute-start.5 = (f32[4,64,256]{2,1,0:T(8,128)S(1)}, f32[4,64,256]{2,1,0:T(8,128)S(1)}, u32[]{:S(2)}, u32[]{:S(2)}) collective-permute-start(f32[4,64,256]{2,1,0:T(8,128)S(1)} %get-tuple-element.50), channel_id=1, source_target_pairs={{1,0},{2,1},{3,2},{4,3},{5,4},{6,5},{7,6},{8,7},{9,8},{10,9},{11,1... | collective-permute-start | bytes 786440 | tf_op jit(solution)/shard_map/ppermute | solution.py:24
  79.7 3.7 %collective-permute-start.10 = (f32[8]{0:T(128)S(1)}, f32[8]{0:T(128)S(1)}, u32[]{:S(2)}, u32[]{:S(2)}) collective-permute-start(f32[8]{0:T(128)S(1)} %fusion.10), channel_id=1, source_target_pairs={{0,2},{1,3},{2,0},{3,1},{4,6},{5,7},{6,4},{7,5},{8,10},{9,11},{10,... | collective-permute-start | bytes 104 | tf_op jit(solution)/shard_map/ppermute | solution.py:243
  80.5 4.1 %copy-start = (f32[3,8,64,256]{3,2,1,0:T(8,128)S(1)}, f32[3,8,64,256]{3,2,1,0:T(8,128)}, u32[]{:S(2)}) copy-start(f32[3,8,64,256]{3,2,1,0:T(8,128)} %get-tuple-element.27.star_in) | copy-start | bytes 4718596
  83.3 11.8 %collective-permute-start.11 = (f32[8]{0:T(128)S(1)}, f32[8]{0:T(128)S(1)}, u32[]{:S(2)}, u32[]{:S(2)}) collective-permute-start(f32[8]{0:T(128)S(1)} %add.59), channel_id=1, source_target_pairs={{0,4},{1,5},{2,6},{3,7},{4,0},{5,1},{6,2},{7,3},{8,12},{9,13},{10,... | collective-permute-start | bytes 104 | tf_op jit(solution)/shard_map/ppermute | solution.py:243
  84.6 25.1 %copy-start.11 = (s32[8,256]{1,0:T(8,128)S(1)}, s32[8,256]{1,0:T(8,128)}, u32[]{:S(2)}) copy-start(s32[8,256]{1,0:T(8,128)} %param.19) | copy-start | bytes 24580
  95.1 4.5 %collective-permute-start.12 = (f32[8]{0:T(128)S(1)}, f32[8]{0:T(128)S(1)}, u32[]{:S(2)}, u32[]{:S(2)}) collective-permute-start(f32[8]{0:T(128)S(1)} %add.60), channel_id=1, source_target_pairs={{0,8},{1,9},{2,10},{3,11},{4,12},{5,13},{6,14},{7,15},{8,0},{9,1},... | collective-permute-start | bytes 104 | tf_op jit(solution)/shard_map/ppermute | solution.py:243
  99.7 7.5 %collective-permute-start.13 = (f32[8]{0:T(128)S(1)}, f32[8]{0:T(128)S(1)}, u32[]{:S(2)}, u32[]{:S(2)}) collective-permute-start(f32[8]{0:T(128)S(1)} %add.61), channel_id=1, source_target_pairs={{0,16},{1,17},{2,18},{3,19},{4,20},{5,21},{6,22},{7,23},{8,24},{9,... | collective-permute-start | bytes 104 | tf_op jit(solution)/shard_map/ppermute | solution.py:243
  (6 other events, 7.1 us)

commit v6 on v5

--- a/solution.py
+++ b/solution.py
@@ -41,19 +41,31 @@
     return lap + _down(centre, 1) + _up(centre, 1) - 6.0 * centre
 
 
-def stage_one_kernel(vel2, pres5, heat1, poro5, solv1, solid,
-                     star_out, source_out, heat_out, solv_out, star):
+def stage_one_kernel(velocity, pressure, enthalpy, solvent, porosity, solid, left, right,
+                     star_out, source_out, heat_out, solv_out,
+                     vel2, pres2, heat1, solv1, poro1, star):
     wide = star.shape[1]
     cells = source_out.shape[0]
+    for component in range(3):
+        vel2[component, 0:2] = left[2 * component:2 * component + 2]
+        vel2[component, 2:cells + 2] = velocity[component]
+        vel2[component, cells + 2:cells + 4] = right[2 * component:2 * component + 2]
+    pres2[0:2] = left[6:8]
+    pres2[2:cells + 2] = pressure[...]
+    pres2[cells + 2:cells + 4] = right[6:8]
+    for layer, (target, local) in enumerate(((heat1, enthalpy), (solv1, solvent), (poro1, porosity))):
+        target[0:1] = left[8 + layer:9 + layer]
+        target[1:cells + 1] = local[...]
+        target[cells + 1:cells + 2] = right[8 + layer:9 + layer]
 
     def momentum_plane(j, carry):
-        open_here = poro5[j + 4]
-        pressure_mid = pres5[j + 4]
+        open_here = poro1[j]
+        pressure_mid = pres2[j + 1]
         for component in range(3):
             centre = vel2[component, j + 1]
             laplacian = _laplacian_plane(vel2[component, j], centre, vel2[component, j + 2])
             if component == 0:
-                gradient = 0.5 * (pres5[j + 5] - pres5[j + 3])
+                gradient = 0.5 * (pres2[j + 2] - pres2[j])
             else:
                 axis = component - 1
                 gradient = 0.5 * (_up(pressure_mid, axis) - _down(pressure_mid, axis))
@@ -98,8 +110,19 @@
     lax.fori_loop(0, cells, cell_plane, 0)
 
 
-def stage_two_kernel(pres5, poro5, source4, star_in, vel_out, pres_out, even, odd):
+def stage_two_kernel(pressure, porosity, source, star_in, wide_left, wide_right,
+                     source_left, source_right, vel_out, pres_out,
+                     pres5, poro5, source4, even, odd):
     cells = pres_out.shape[0]
+    pres5[0:5] = wide_left[0:5]
+    pres5[5:cells + 5] = pressure[...]
+    pres5[cells + 5:cells + 10] = wide_right[0:5]
+    poro5[0:5] = wide_left[5:10]
+    poro5[5:cells + 5] = porosity[...]
+    poro5[cells + 5:cells + 10] = wide_right[5:10]
+    source4[0:4] = source_left[...]
+    source4[4:cells + 4] = source[...]
+    source4[cells + 4:cells + 8] = source_right[...]
     buffers = (even, odd)
     prev = pres5
     for k in range(ITERS):
@@ -146,7 +169,7 @@
     return pltpu.CompilerParams(vmem_limit_bytes=48 * 1024 * 1024)
 
 
-def stage_one(vel2, pres5, heat1, poro5, solv1, solid):
+def stage_one(velocity, pressure, enthalpy, solvent, porosity, solid, left, right):
     cells = solid.shape[0]
     plane = solid.shape[1:]
     f32 = jnp.float32
@@ -160,14 +183,22 @@
     return pl.pallas_call(
         stage_one_kernel,
         out_shape=outs,
-        scratch_shapes=[pltpu.VMEM((3, cells + 2) + plane, f32)],
+        scratch_shapes=[
+            pltpu.VMEM((3, cells + 4) + plane, f32),
+            pltpu.VMEM((cells + 4,) + plane, f32),
+            pltpu.VMEM((cells + 2,) + plane, f32),
+            pltpu.VMEM((cells + 2,) + plane, f32),
+            pltpu.VMEM((cells + 2,) + plane, f32),
+            pltpu.VMEM((3, cells + 2) + plane, f32),
+        ],
         compiler_params=_params(),
         cost_estimate=pl.CostEstimate(
             flops=260 * points, transcendentals=0, bytes_accessed=4 * points * 19),
-    )(vel2, pres5, heat1, poro5, solv1, solid)
-
-
-def stage_two(pres5, poro5, source4, vel_star):
+    )(velocity, pressure, enthalpy, solvent, porosity, solid, left, right)
+
+
+def stage_two(pressure, porosity, source, vel_star, wide_left, wide_right, source_left,
+              source_right):
     cells = vel_star.shape[1]
     plane = vel_star.shape[2:]
     f32 = jnp.float32
@@ -179,11 +210,17 @@
     return pl.pallas_call(
         stage_two_kernel,
         out_shape=outs,
-        scratch_shapes=[pltpu.VMEM((source4.shape[0],) + plane, f32)] * 2,
+        scratch_shapes=[
+            pltpu.VMEM((cells + 10,) + plane, f32),
+            pltpu.VMEM((cells + 10,) + plane, f32),
+            pltpu.VMEM((cells + 8,) + plane, f32),
+            pltpu.VMEM((cells + 8,) + plane, f32),
+            pltpu.VMEM((cells + 8,) + plane, f32),
+        ],
         compiler_params=_params(),
         cost_estimate=pl.CostEstimate(
             flops=200 * points, transcendentals=0, bytes_accessed=4 * points * 12),
-    )(pres5, poro5, source4, vel_star)
+    )(pressure, porosity, source, vel_star, wide_left, wide_right, source_left, source_right)
 
 
 def on_device_body(
@@ -248,37 +285,31 @@
             sent, _ = lax.optimization_barrier((sent, anchor))
         state[key] = state[key] + sent
 
+    plane = enthalpy.shape[1:]
     narrow_head = jnp.concatenate(
-        [velocity[:, 0:2].reshape((6,) + enthalpy.shape[1:]), pressure[0:2],
-         enthalpy[0:1], solvent[0:1]], axis=0)
+        [velocity[:, 0:2].reshape((6,) + plane), pressure[0:2],
+         enthalpy[0:1], solvent[0:1], porosity[0:1]], axis=0)
     narrow_tail = jnp.concatenate(
-        [velocity[:, cx - 2:].reshape((6,) + enthalpy.shape[1:]), pressure[cx - 2:],
-         enthalpy[cx - 1:], solvent[cx - 1:]], axis=0)
+        [velocity[:, cx - 2:].reshape((6,) + plane), pressure[cx - 2:],
+         enthalpy[cx - 1:], solvent[cx - 1:], porosity[cx - 1:]], axis=0)
     wide_head = jnp.concatenate([pressure[0:5], porosity[0:5]], axis=0)
     wide_tail = jnp.concatenate([pressure[cx - 5:], porosity[cx - 5:]], axis=0)
     n_left, n_right = neighbours(narrow_head, narrow_tail)
     w_left, w_right = neighbours(wide_head, wide_tail)
 
-    vel2 = jnp.concatenate(
-        [n_left[0:6].reshape((3, 2) + enthalpy.shape[1:]), velocity,
-         n_right[0:6].reshape((3, 2) + enthalpy.shape[1:])], axis=1)
-    pres5 = jnp.concatenate([w_left[0:5], pressure, w_right[0:5]], axis=0)
-    poro5 = jnp.concatenate([w_left[5:10], porosity, w_right[5:10]], axis=0)
-    heat1 = jnp.concatenate([n_left[8:9], enthalpy, n_right[8:9]], axis=0)
-    solv1 = jnp.concatenate([n_left[9:10], solvent, n_right[9:10]], axis=0)
-
     advance(None)
     advance(None)
     advance(None)
     advance(None)
-    vel_star, source, heat_new, solv_new = stage_one(vel2, pres5, heat1, poro5, solv1, solid_mask)
+    vel_star, source, heat_new, solv_new = stage_one(
+        velocity, pressure, enthalpy, solvent, porosity, solid_mask, n_left, n_right)
     advance(vel_star)
 
     s_left, s_right = neighbours(source[0:4], source[cx - 4:])
-    source4 = jnp.concatenate([s_left, source, s_right], axis=0)
-    advance(source4)
-
-    velocity_new, final = stage_two(pres5, poro5, source4, vel_star)
+    advance(s_left)
+
+    velocity_new, final = stage_two(
+        pressure, porosity, source, vel_star, w_left, w_right, s_left, s_right)
     while zone_bits or duct_bits:
         advance(final)
     totals = state["totals"]

time: 114 us -> 112 us (0.982)
  the two profiles are of different devices: /device:TPU:32 before, /device:TPU:38 now
where the time goes in v6:
time: 112 us
  starting transfers between devices  39.9 us (36%)
  waiting for transfers between devices  22 us (20%)
  Pallas kernels  19.2 us (17%)
  other arithmetic  15.1 us (13%)
  local copies, waits for them, and re-layouts  10 us (9%)
  between operations  5.52 us (5%)
    ppermute x3, starting transfers between devices, neighbours(): from_right = lax.ppermute(head, ALL, [(i + 1, i) for i in range(count - 1)])  20.3 us
    pallas_call x1, Pallas kernels, stage_two(): pl.pallas_call(stage_two_kernel, out_shape=outs, scratch_shapes=[pltpu.VM...  12.1 us
    ppermute x3, waiting for transfers between devices, advance(): sent = lax.ppermute(state[key], 'zone', [(i, i ^ b) for i in range(rows)])  11.4 us
    ppermute x5, starting transfers between devices, advance(): lax.ppermute(state[key], 'brick', [(i, i ^ b) for i in range(bricks)])  11.3 us
    ppermute x5, waiting for transfers between devices, advance(): lax.ppermute(state[key], 'brick', [(i, i ^ b) for i in range(bricks)])  10.6 us
    pallas_call x1, Pallas kernels, stage_one(): pl.pallas_call(stage_one_kernel, out_shape=outs, scratch_shapes=[pltpu.VM...  7.1 us
    ppermute x3, starting transfers between devices, neighbours(): from_left = lax.ppermute(tail, ALL, [(i, i + 1) for i in range(count - 1)])  5.74 us
    add x7, other arithmetic, advance(): state[key] = state[key] + sent  4.27 us
  transfers between devices with their start and end apart: 14, of which 6 were waited for; matrix products, arithmetic and copies ran while one was open for 15% of the time, Pallas kernels for 17%

profile of v6, /device:TPU:38, one launch (start us, length us, event | category | flops | bytes accessed | tf_op | source)
XLA Modules:
  0.0 111.7 jit_solution(16173317702816069314)
XLA Ops:
  0.7 1.3 %fusion.11 = (f32[3,2,64,256]{3,2,1,0:T(8,128)S(1)}, f32[3,2,64,256]{3,2,1,0:T(8,128)S(1)}) fusion(f32[3,8,64,256]{3,2,1,0:T(8,128)} %velocity.1), kind=kLoop, calls=%fused_computation.42 | loop fusion | bytes 1572864 | tf_op jit(solution)/shard_map/slice | solution.py:290
  5.6 1.9 %collective-permute-start = (f32[11,64,256]{2,1,0:T(8,128)}, f32[11,64,256]{2,1,0:T(8,128)S(1)}, u32[]{:S(2)}, u32[]{:S(2)}) collective-permute-start(f32[11,64,256]{2,1,0:T(8,128)} %get-tuple-element.49), channel_id=1, source_target_pairs={{0,1},{1,2},{2,3},{3,4},{4,5},{5,6},{6,7},{7,8},{8,9},{9,10},{10,1... | collective-permute-start | bytes 2162696 | tf_op jit(solution)/shard_map/ppermute | solution.py:23
  7.5 9.6 %collective-permute-start.1 = (f32[11,64,256]{2,1,0:T(8,128)}, f32[11,64,256]{2,1,0:T(8,128)S(1)}, u32[]{:S(2)}, u32[]{:S(2)}) collective-permute-start(f32[11,64,256]{2,1,0:T(8,128)} %get-tuple-element.48), channel_id=1, source_target_pairs={{1,0},{2,1},{3,2},{4,3},{5,4},{6,5},{7,6},{8,7},{9,8},{10,9},{11,1... | collective-permute-start | bytes 2162696 | tf_op jit(solution)/shard_map/ppermute | solution.py:24
  17.8 1.4 %reduce-window.9 = s32[8,1]{0,1:T(1,128)} reduce-window(s32[8,1]{0,1:T(1,128)} %bitcast.47, s32[]{:T(128)} %constant.58.clone.1), window={size=8x1 pad=7_0x0_0}, to_apply=%region_0.0 | reduce-window | flops 56 | bytes 68 | tf_op jit(solution)/shard_map/reduce-window.4
  19.8 1.4 %fusion.9 = s32[]{:T(128)} fusion(s32[8]{0:T(128)} %param.20, s32[8,1]{0,1:T(1,128)} %reduce-window.9, s32[]{:T(128)S(6)} %add.53), kind=kLoop, calls=%fused_computation.36 | loop fusion | flops 31 | bytes 72 | tf_op jit(solution)/shard_map/reduce_sum | solution.py:243
  23.1 1.3 %fusion = f32[9,2,8,256]{3,2,1,0:T(8,128)} fusion(f32[9,2,8,256]{3,2,1,0:T(8,128)} %broadcast_in_dim.13, s32[]{:T(128)S(6)} %select_n.14, f32[1,8,256]{2,1,0:T(8,128)} %get-tuple-element.60, f32[1,8,256]{2,1,0:T(8,128)} %get-tuple-element.61), kind=kLoop, calls=%fused_computation.15 | loop fusion | flops 4096 | bytes 32772 | tf_op jit(solution)/shard_map/dynamic_update_slice | solution.py:252
  24.4 1.3 %scatter.4 = f32[9,2,8,256]{3,2,1,0:T(8,128)} dynamic-update-slice(f32[9,2,8,256]{3,2,1,0:T(8,128)} %fusion, f32[1,1,1,8]{3,2,1,0:T(1,128)S(1)} %compare_select_fusion, s32[]{:T(128)} %constant.67.clone.1, s32[]{:T(128)} %constant.58.clone.1, s32[]{:T(128)} %constant.58.clone.1, s32[]{:T(128)} %constant.58.clone.1) | dynamic-update-slice | bytes 68 | tf_op jit(solution)/shard_map/scatter | solution.py:255
  27.2 1.9 %collective-permute-start.2 = (f32[10,64,256]{2,1,0:T(8,128)}, f32[10,64,256]{2,1,0:T(8,128)}, u32[]{:S(2)}, u32[]{:S(2)}) collective-permute-start(f32[10,64,256]{2,1,0:T(8,128)} %pad_maximum_fusion), channel_id=1, source_target_pairs={{0,1},{1,2},{2,3},{3,4},{4,5},{5,6},{6,7},{7,8},{8,9},{9,10},{10,1... | collective-permute-start | bytes 1966088 | tf_op jit(solution)/shard_map/ppermute | solution.py:23
  29.1 6.6 %collective-permute-done.6 = f32[9,2,8,256]{3,2,1,0:T(8,128)S(1)} collective-permute-done((f32[9,2,8,256]{3,2,1,0:T(8,128)}, f32[9,2,8,256]{3,2,1,0:T(8,128)S(1)}, u32[]{:S(2)}, u32[]{:S(2)}) %collective-permute-start.6) | collective-permute-done | bytes 147488 | tf_op jit(solution)/shard_map/ppermute | solution.py:273
  35.7 1.6 %add.55 = f32[9,2,8,256]{3,2,1,0:T(8,128)} add(f32[9,2,8,256]{3,2,1,0:T(8,128)} %scatter.4, f32[9,2,8,256]{3,2,1,0:T(8,128)S(1)} %collective-permute-done.6) | non-fusion elementwise | flops 36864 | bytes 442368 | tf_op jit(solution)/shard_map/add | solution.py:286
  39.0 1.9 %collective-permute-start.3 = (f32[10,64,256]{2,1,0:T(8,128)}, f32[10,64,256]{2,1,0:T(8,128)}, u32[]{:S(2)}, u32[]{:S(2)}) collective-permute-start(f32[10,64,256]{2,1,0:T(8,128)} %pad_maximum_fusion.1), channel_id=1, source_target_pairs={{1,0},{2,1},{3,2},{4,3},{5,4},{6,5},{7,6},{8,7},{9,8},{10,9},{11,1... | collective-permute-start | bytes 1966088 | tf_op jit(solution)/shard_map/ppermute | solution.py:24
  42.8 1.7 %add.56 = f32[9,2,8,256]{3,2,1,0:T(8,128)} add(f32[9,2,8,256]{3,2,1,0:T(8,128)} %add.55, f32[9,2,8,256]{3,2,1,0:T(8,128)} %collective-permute-done.7) | non-fusion elementwise | flops 36864 | bytes 442368 | tf_op jit(solution)/shard_map/add | solution.py:286
  44.5 1.3 %collective-permute-start.8 = (f32[9,2,8,256]{3,2,1,0:T(8,128)}, f32[9,2,8,256]{3,2,1,0:T(8,128)}, u32[]{:S(2)}, u32[]{:S(2)}) collective-permute-start(f32[9,2,8,256]{3,2,1,0:T(8,128)} %add.56), channel_id=1, source_target_pairs={{0,128},{32,160},{64,192},{96,224},{128,0},{160,32},{192,64},{224,... | collective-permute-start | bytes 442376 | tf_op jit(solution)/shard_map/ppermute | solution.py:273
  47.8 4.8 %collective-permute-done.8 = f32[9,2,8,256]{3,2,1,0:T(8,128)} collective-permute-done((f32[9,2,8,256]{3,2,1,0:T(8,128)}, f32[9,2,8,256]{3,2,1,0:T(8,128)}, u32[]{:S(2)}, u32[]{:S(2)}) %collective-permute-start.8) | collective-permute-done | bytes 147488 | tf_op jit(solution)/shard_map/ppermute | solution.py:273
  53.6 1.0 copy-done.5
  54.7 7.1 %shard_map.138 = (f32[3,8,64,256]{3,2,1,0:T(8,128)}, f32[8,64,256]{2,1,0:T(8,128)S(1)}, f32[8,64,256]{2,1,0:T(8,128)S(1)}, f32[8,64,256]{2,1,0:T(8,128)S(1)}) custom-call(f32[3,8,64,256]{3,2,1,0:T(8,128)} %velocity.1, f32[8,64,256]{2,1,0:T(8,128)S(1)} %copy-done, f32[8,64,256]{2,1,0:T(8,128)S(1)} %copy-done.3, f32[8,64,256]{2,1,0:T(8,128)S(1)} %copy-done.4, ...), custom_call_target="tpu_custom_call" | custom-call | flops 34078720 | bytes 9961472 | tf_op jit(solution)/shard_map/pallas_call | solution.py:183
  61.8 1.9 %collective-permute-start.4 = (f32[4,64,256]{2,1,0:T(8,128)S(1)}, f32[4,64,256]{2,1,0:T(8,128)S(1)}, u32[]{:S(2)}, u32[]{:S(2)}) collective-permute-start(f32[4,64,256]{2,1,0:T(8,128)S(1)} %get-tuple-element.43), channel_id=1, source_target_pairs={{0,1},{1,2},{2,3},{3,4},{4,5},{5,6},{6,7},{7,8},{8,9},{9,10},{10,1... | collective-permute-start | bytes 786440 | tf_op jit(solution)/shard_map/ppermute | solution.py:23
  63.7 8.8 %collective-permute-start.5 = (f32[4,64,256]{2,1,0:T(8,128)S(1)}, f32[4,64,256]{2,1,0:T(8,128)S(1)}, u32[]{:S(2)}, u32[]{:S(2)}) collective-permute-start(f32[4,64,256]{2,1,0:T(8,128)S(1)} %get-tuple-element.42), channel_id=1, source_target_pairs={{1,0},{2,1},{3,2},{4,3},{5,4},{6,5},{7,6},{8,7},{9,8},{10,9},{11,1... | collective-permute-start | bytes 786440 | tf_op jit(solution)/shard_map/ppermute | solution.py:24
  72.6 1.1 %collective-permute-done.9 = f32[8]{0:T(128)S(1)} collective-permute-done((f32[8]{0:T(128)S(1)}, f32[8]{0:T(128)S(1)}, u32[]{:S(2)}, u32[]{:S(2)}) %collective-permute-start.9) | collective-permute-done | bytes 64 | tf_op jit(solution)/shard_map/ppermute | solution.py:280
  74.5 2.8 %collective-permute-done.10 = f32[8]{0:T(128)S(1)} collective-permute-done((f32[8]{0:T(128)S(1)}, f32[8]{0:T(128)S(1)}, u32[]{:S(2)}, u32[]{:S(2)}) %collective-permute-start.10) | collective-permute-done | bytes 64 | tf_op jit(solution)/shard_map/ppermute | solution.py:280
  77.4 5.1 %collective-permute-done.11 = f32[8]{0:T(128)S(1)} collective-permute-done((f32[8]{0:T(128)S(1)}, f32[8]{0:T(128)S(1)}, u32[]{:S(2)}, u32[]{:S(2)}) %collective-permute-start.11) | collective-permute-done | bytes 64 | tf_op jit(solution)/shard_map/ppermute | solution.py:280
  82.6 12.1 %shard_map.139 = (f32[3,8,64,256]{3,2,1,0:T(8,128)}, f32[8,64,256]{2,1,0:T(8,128)}) custom-call(f32[8,64,256]{2,1,0:T(8,128)S(1)} %copy-done, f32[8,64,256]{2,1,0:T(8,128)S(1)} %copy-done.1, f32[8,64,256]{2,1,0:T(8,128)S(1)} %get-tuple-element.26.source, f32[3,8,64,256]{3,2,1,0:T(8,128)S(1)} %copy-done.2, f32[10,64,256]{2,1,0:T(8,128)} %collective-permute-done.2.wide_left, ...), custom_call_target="tpu_custom_call" | custom-call | flops 26214400 | bytes 6291456 | tf_op jit(solution)/shard_map/pallas_call | solution.py:210
  94.7 11.1 %collective-permute-start.13 = (f32[8]{0:T(128)S(1)}, f32[8]{0:T(128)S(1)}, u32[]{:S(2)}, u32[]{:S(2)}) collective-permute-start(f32[8]{0:T(128)S(1)} %add.61), channel_id=1, source_target_pairs={{0,16},{1,17},{2,18},{3,19},{4,20},{5,21},{6,22},{7,23},{8,24},{9,... | collective-permute-start | bytes 104 | tf_op jit(solution)/shard_map/ppermute | solution.py:280
  105.7 1.5 %collective-permute-done.13 = f32[8]{0:T(128)S(1)} collective-permute-done((f32[8]{0:T(128)S(1)}, f32[8]{0:T(128)S(1)}, u32[]{:S(2)}, u32[]{:S(2)}) %collective-permute-start.13) | collective-permute-done | bytes 64 | tf_op jit(solution)/shard_map/ppermute | solution.py:280
  (69 shorter events, 15.5 us)
Async XLA Ops:
  0.6 2.2 %copy-start = (f32[8,64,256]{2,1,0:T(8,128)S(1)}, f32[8,64,256]{2,1,0:T(8,128)}, u32[]{:S(2)}) copy-start(f32[8,64,256]{2,1,0:T(8,128)} %pressure.3) | copy-start | bytes 1572868
  0.6 2.9 %copy-start.3 = (f32[8,64,256]{2,1,0:T(8,128)S(1)}, f32[8,64,256]{2,1,0:T(8,128)}, u32[]{:S(2)}) copy-start(f32[8,64,256]{2,1,0:T(8,128)} %enthalpy.1) | copy-start | bytes 1572868
  1.9 2.3 %copy-start.4 = (f32[8,64,256]{2,1,0:T(8,128)S(1)}, f32[8,64,256]{2,1,0:T(8,128)}, u32[]{:S(2)}) copy-start(f32[8,64,256]{2,1,0:T(8,128)} %solvent.1) | copy-start | bytes 1572868
  1.9 3.0 %copy-start.1 = (f32[8,64,256]{2,1,0:T(8,128)S(1)}, f32[8,64,256]{2,1,0:T(8,128)}, u32[]{:S(2)}) copy-start(f32[8,64,256]{2,1,0:T(8,128)} %porosity.3) | copy-start | bytes 1572868
  5.6 48.0 %collective-permute-start = (f32[11,64,256]{2,1,0:T(8,128)}, f32[11,64,256]{2,1,0:T(8,128)S(1)}, u32[]{:S(2)}, u32[]{:S(2)}) collective-permute-start(f32[11,64,256]{2,1,0:T(8,128)} %get-tuple-element.49), channel_id=1, source_target_pairs={{0,1},{1,2},{2,3},{3,4},{4,5},{5,6},{6,7},{7,8},{8,9},{9,10},{10,1... | collective-permute-start | bytes 2162696 | tf_op jit(solution)/shard_map/ppermute | solution.py:23
  7.5 46.1 %collective-permute-start.1 = (f32[11,64,256]{2,1,0:T(8,128)}, f32[11,64,256]{2,1,0:T(8,128)S(1)}, u32[]{:S(2)}, u32[]{:S(2)}) collective-permute-start(f32[11,64,256]{2,1,0:T(8,128)} %get-tuple-element.48), channel_id=1, source_target_pairs={{1,0},{2,1},{3,2},{4,3},{5,4},{6,5},{7,6},{8,7},{9,8},{10,9},{11,1... | collective-permute-start | bytes 2162696 | tf_op jit(solution)/shard_map/ppermute | solution.py:24
  25.8 10.0 %collective-permute-start.6 = (f32[9,2,8,256]{3,2,1,0:T(8,128)}, f32[9,2,8,256]{3,2,1,0:T(8,128)S(1)}, u32[]{:S(2)}, u32[]{:S(2)}) collective-permute-start(f32[9,2,8,256]{3,2,1,0:T(8,128)} %scatter.4), channel_id=1, source_target_pairs={{0,32},{32,0},{64,96},{96,64},{128,160},{160,128},{192,224},{224,1... | collective-permute-start | bytes 442376 | tf_op jit(solution)/shard_map/ppermute | solution.py:273
  26.3 14.7 %copy-start.7 = (s32[1,2]{1,0:T(1,128)S(1)}, s32[1,2]{1,0:T(1,128)}, u32[]{:S(2)}) copy-start(s32[1,2]{1,0:T(1,128)} %param.23) | copy-start | bytes 28
  26.3 20.9 %copy-start.9 = (f32[8]{0:T(128)S(1)}, f32[8]{0:T(128)}, u32[]{:S(2)}) copy-start(f32[8]{0:T(128)} %param.21) | copy-start | bytes 100
  27.2 55.4 %collective-permute-start.2 = (f32[10,64,256]{2,1,0:T(8,128)}, f32[10,64,256]{2,1,0:T(8,128)}, u32[]{:S(2)}, u32[]{:S(2)}) collective-permute-start(f32[10,64,256]{2,1,0:T(8,128)} %pad_maximum_fusion), channel_id=1, source_target_pairs={{0,1},{1,2},{2,3},{3,4},{4,5},{5,6},{6,7},{7,8},{8,9},{9,10},{10,1... | collective-permute-start | bytes 1966088 | tf_op jit(solution)/shard_map/ppermute | solution.py:23
  37.3 5.5 %collective-permute-start.7 = (f32[9,2,8,256]{3,2,1,0:T(8,128)}, f32[9,2,8,256]{3,2,1,0:T(8,128)}, u32[]{:S(2)}, u32[]{:S(2)}) collective-permute-start(f32[9,2,8,256]{3,2,1,0:T(8,128)} %add.55), channel_id=1, source_target_pairs={{0,64},{32,96},{64,0},{96,32},{128,192},{160,224},{192,128},{224,1... | collective-permute-start | bytes 442376 | tf_op jit(solution)/shard_map/ppermute | solution.py:273
  39.0 43.5 %collective-permute-start.3 = (f32[10,64,256]{2,1,0:T(8,128)}, f32[10,64,256]{2,1,0:T(8,128)}, u32[]{:S(2)}, u32[]{:S(2)}) collective-permute-start(f32[10,64,256]{2,1,0:T(8,128)} %pad_maximum_fusion.1), channel_id=1, source_target_pairs={{1,0},{2,1},{3,2},{4,3},{5,4},{6,5},{7,6},{8,7},{9,8},{10,9},{11,1... | collective-permute-start | bytes 1966088 | tf_op jit(solution)/shard_map/ppermute | solution.py:24
  44.5 8.1 %collective-permute-start.8 = (f32[9,2,8,256]{3,2,1,0:T(8,128)}, f32[9,2,8,256]{3,2,1,0:T(8,128)}, u32[]{:S(2)}, u32[]{:S(2)}) collective-permute-start(f32[9,2,8,256]{3,2,1,0:T(8,128)} %add.56), channel_id=1, source_target_pairs={{0,128},{32,160},{64,192},{96,224},{128,0},{160,32},{192,64},{224,... | collective-permute-start | bytes 442376 | tf_op jit(solution)/shard_map/ppermute | solution.py:273
  53.6 1.0 copy-start.5
  61.8 20.6 %collective-permute-start.4 = (f32[4,64,256]{2,1,0:T(8,128)S(1)}, f32[4,64,256]{2,1,0:T(8,128)S(1)}, u32[]{:S(2)}, u32[]{:S(2)}) collective-permute-start(f32[4,64,256]{2,1,0:T(8,128)S(1)} %get-tuple-element.43), channel_id=1, source_target_pairs={{0,1},{1,2},{2,3},{3,4},{4,5},{5,6},{6,7},{7,8},{8,9},{9,10},{10,1... | collective-permute-start | bytes 786440 | tf_op jit(solution)/shard_map/ppermute | solution.py:23
  63.7 18.8 %collective-permute-start.5 = (f32[4,64,256]{2,1,0:T(8,128)S(1)}, f32[4,64,256]{2,1,0:T(8,128)S(1)}, u32[]{:S(2)}, u32[]{:S(2)}) collective-permute-start(f32[4,64,256]{2,1,0:T(8,128)S(1)} %get-tuple-element.42), channel_id=1, source_target_pairs={{1,0},{2,1},{3,2},{4,3},{5,4},{6,5},{7,6},{8,7},{9,8},{10,9},{11,1... | collective-permute-start | bytes 786440 | tf_op jit(solution)/shard_map/ppermute | solution.py:24
  72.5 1.2 %collective-permute-start.9 = (f32[8]{0:T(128)S(1)}, f32[8]{0:T(128)S(1)}, u32[]{:S(2)}, u32[]{:S(2)}) collective-permute-start(f32[8]{0:T(128)S(1)} %slice_bitcast_fusion.2), channel_id=1, source_target_pairs={{0,1},{1,0},{2,3},{3,2},{4,5},{5,4},{6,7},{7,6},{8,9},{9,8},{10,11... | collective-permute-start | bytes 104 | tf_op jit(solution)/shard_map/ppermute | solution.py:280
  73.8 3.6 %collective-permute-start.10 = (f32[8]{0:T(128)S(1)}, f32[8]{0:T(128)S(1)}, u32[]{:S(2)}, u32[]{:S(2)}) collective-permute-start(f32[8]{0:T(128)S(1)} %fusion.10), channel_id=1, source_target_pairs={{0,2},{1,3},{2,0},{3,1},{4,6},{5,7},{6,4},{7,5},{8,10},{9,11},{10,... | collective-permute-start | bytes 104 | tf_op jit(solution)/shard_map/ppermute | solution.py:280
  73.8 8.7 %copy-start.2 = (f32[3,8,64,256]{3,2,1,0:T(8,128)S(1)}, f32[3,8,64,256]{3,2,1,0:T(8,128)}, u32[]{:S(2)}) copy-start(f32[3,8,64,256]{3,2,1,0:T(8,128)} %get-tuple-element.27.star_in) | copy-start | bytes 4718596
  77.4 5.1 %collective-permute-start.11 = (f32[8]{0:T(128)S(1)}, f32[8]{0:T(128)S(1)}, u32[]{:S(2)}, u32[]{:S(2)}) collective-permute-start(f32[8]{0:T(128)S(1)} %add.59), channel_id=1, source_target_pairs={{0,4},{1,5},{2,6},{3,7},{4,0},{5,1},{6,2},{7,3},{8,12},{9,13},{10,... | collective-permute-start | bytes 104 | tf_op jit(solution)/shard_map/ppermute | solution.py:280
  82.4 24.9 %copy-start.8 = (s32[8]{0:T(128)S(1)}, s32[8]{0:T(128)}, u32[]{:S(2)}) copy-start(s32[8]{0:T(128)} %param.20) | copy-start | bytes 100
  82.4 27.4 %copy-start.6 = (s32[8,256]{1,0:T(8,128)S(1)}, s32[8,256]{1,0:T(8,128)}, u32[]{:S(2)}) copy-start(s32[8,256]{1,0:T(8,128)} %param.19) | copy-start | bytes 24580
  82.5 12.2 %collective-permute-start.12 = (f32[8]{0:T(128)S(1)}, f32[8]{0:T(128)S(1)}, u32[]{:S(2)}, u32[]{:S(2)}) collective-permute-start(f32[8]{0:T(128)S(1)} %add.60), channel_id=1, source_target_pairs={{0,8},{1,9},{2,10},{3,11},{4,12},{5,13},{6,14},{7,15},{8,0},{9,1},... | collective-permute-start | bytes 104 | tf_op jit(solution)/shard_map/ppermute | solution.py:280
  94.7 12.6 %collective-permute-start.13 = (f32[8]{0:T(128)S(1)}, f32[8]{0:T(128)S(1)}, u32[]{:S(2)}, u32[]{:S(2)}) collective-permute-start(f32[8]{0:T(128)S(1)} %add.61), channel_id=1, source_target_pairs={{0,16},{1,17},{2,18},{3,19},{4,20},{5,21},{6,22},{7,23},{8,24},{9,... | collective-permute-start | bytes 104 | tf_op jit(solution)/shard_map/ppermute | solution.py:280

commit v7 on v6

--- a/solution.py
+++ b/solution.py
@@ -248,42 +248,39 @@
     rows = lax.axis_size("zone")
 
     planes = jnp.stack([enthalpy[:, -1, :], solvent[:, -1, :]])
-    buffer = jnp.zeros((rows + 1,) + planes.shape, jnp.float32)
-    buffer = lax.dynamic_update_slice(
-        buffer, planes[None], (lax.axis_index("zone"), 0, 0, 0)
-    )
-    buffer = buffer.at[rows, 0, 0, :nzones].set(totals)
+    message = jnp.concatenate(
+        [planes, jnp.zeros((1,) + planes.shape[1:], jnp.float32).at[0, 0, :nzones].set(totals)],
+        axis=0)
     bricks = count // rows
-    duct_bits = []
-    bit = 1
-    while bit < rows:
-        duct_bits.append(bit)
-        bit *= 2
-    zone_bits = []
-    bit = 1
-    while bit < bricks:
-        zone_bits.append(bit)
-        bit *= 2
-    state = {"buffer": buffer, "totals": None}
+    rounds = [("zone", rows, 1, rows)]
+    stride = 1
+    while stride < bricks:
+        radix = 4 if stride * 4 <= bricks else bricks // stride
+        rounds.append(("brick", bricks, stride, radix))
+        stride *= radix
+    state = {"totals": None, "arrived": None}
 
     def advance(anchor):
-        if duct_bits:
-            b = duct_bits.pop(0)
-            key = "buffer"
-            sent = lax.ppermute(
-                state[key], "zone", [(i, i ^ b) for i in range(rows)])
-        elif zone_bits:
-            b = zone_bits.pop(0)
-            key = "totals"
-            if state[key] is None:
-                state[key] = state["buffer"][rows, 0, 0, :nzones]
-            sent = lax.ppermute(
-                state[key], "brick", [(i, i ^ b) for i in range(bricks)])
-        else:
+        if not rounds:
             return
+        axis, size, stride, radix = rounds.pop(0)
+        value = message if axis == "zone" else state["totals"]
+        sent = [
+            lax.ppermute(value, axis, [(i, i ^ (k * stride)) for i in range(size)])
+            for k in range(1, radix)
+        ]
         if anchor is not None:
             sent, _ = lax.optimization_barrier((sent, anchor))
-        state[key] = state[key] + sent
+        if axis == "zone":
+            received = jnp.stack([message] + sent)
+            pick = jnp.bitwise_xor(duct_source[0], lax.axis_index("zone"))
+            state["arrived"] = lax.dynamic_index_in_dim(received, pick, axis=0, keepdims=False)
+            state["totals"] = jnp.sum(received[:, 2, 0, :nzones], axis=0)
+        else:
+            total = state["totals"]
+            for part in sent:
+                total = total + part
+            state["totals"] = total
 
     plane = enthalpy.shape[1:]
     narrow_head = jnp.concatenate(
@@ -298,29 +295,26 @@
     w_left, w_right = neighbours(wide_head, wide_tail)
 
     advance(None)
-    advance(None)
-    advance(None)
-    advance(None)
     vel_star, source, heat_new, solv_new = stage_one(
         velocity, pressure, enthalpy, solvent, porosity, solid_mask, n_left, n_right)
     advance(vel_star)
 
     s_left, s_right = neighbours(source[0:4], source[cx - 4:])
     advance(s_left)
+    advance(s_left)
 
     velocity_new, final = stage_two(
         pressure, porosity, source, vel_star, w_left, w_right, s_left, s_right)
-    while zone_bits or duct_bits:
+    while rounds:
         advance(final)
     totals = state["totals"]
-    gathered = state["buffer"][:rows]
+    arrived = state["arrived"]
 
     counts = zone_sizes.astype(jnp.float32) * (cx * enthalpy.shape[2])
     means = totals / counts
     fresh_all = means / (means + solvent_limit)
     fresh = jnp.sum(choose * fresh_all)
     target = jnp.sum(choose * zone_setpoint)
-    arrived = lax.dynamic_index_in_dim(gathered, duct_source[0], axis=0, keepdims=False)
     supply_heat = (1.0 - fresh) * arrived[0] + fresh * target
     supply_solv = (1.0 - fresh) * arrived[1]
     column = jnp.arange(enthalpy.shape[2], dtype=jnp.int32)

time: 112 us -> 126 us (1.12)
  the two profiles are of different devices: /device:TPU:38 before, /device:TPU:32 now
where the time goes in v7:
time: 126 us; the launch traced here: 125 us
  starting transfers between devices  61.1 us (48%)
  Pallas kernels  17.9 us (14%)
  other arithmetic  13.8 us (11%)
  waiting for transfers between devices  13.8 us (11%)
  local copies, waits for them, and re-layouts  12.8 us (10%)
  between operations  5.56 us (4%)
    ppermute x14, starting transfers between devices, advance(): lax.ppermute(value, axis, [(i, i ^ k * stride) for i in range(size)])  28.8 us
    ppermute x3, starting transfers between devices, neighbours(): from_right = lax.ppermute(head, ALL, [(i + 1, i) for i in range(count - 1)])  26.6 us
    ppermute x14, waiting for transfers between devices, advance(): lax.ppermute(value, axis, [(i, i ^ k * stride) for i in range(size)])  11.8 us
    pallas_call x1, Pallas kernels, stage_two(): pl.pallas_call(stage_two_kernel, out_shape=outs, scratch_shapes=[pltpu.VM...  10.8 us
    pallas_call x1, Pallas kernels, stage_one(): pl.pallas_call(stage_one_kernel, out_shape=outs, scratch_shapes=[pltpu.VM...  7.1 us
    unnamed x30, local copies, waits for them, and re-layouts  6.64 us
    ppermute x3, starting transfers between devices, neighbours(): from_left = lax.ppermute(tail, ALL, [(i, i + 1) for i in range(count - 1)])  5.74 us
  transfers between devices with their start and end apart: 20, of which 7 were waited for; matrix products, arithmetic and copies ran while one was open for 14% of the time, Pallas kernels for 14%

profile of v7, /device:TPU:32, one launch (start us, length us, event | category | flops | bytes accessed | tf_op | source)
XLA Modules:
  0.0 125.0 jit_solution(17297882671775832019)
XLA Ops:
  0.7 1.6 %fusion.10 = (f32[8,1,256]{2,1,0:T(1,128)S(1)}, f32[]{:T(128)}) fusion(f32[8,64,256]{2,1,0:T(8,128)} %solvent.1), kind=kLoop, calls=%fused_computation.52 | loop fusion | flops 2047 | bytes 16388 | tf_op jit(solution)/shard_map/slice | solution.py:250
  3.9 1.3 %fusion.8 = s32[]{:T(128)} fusion(s32[8]{0:T(128)} %param.20, s32[8,1]{0,1:T(1,128)S(1)} %reduce-window.9, s32[]{:T(128)S(6)} %add.49), kind=kLoop, calls=%fused_computation.45 | loop fusion | flops 31 | bytes 72 | tf_op jit(solution)/shard_map/reduce_sum | solution.py:243
  6.5 1.9 %collective-permute-start.6 = (f32[3,8,256]{2,1,0:T(8,128)S(1)}, f32[3,8,256]{2,1,0:T(8,128)S(1)}, u32[]{:S(2)}, u32[]{:S(2)}) collective-permute-start(f32[3,8,256]{2,1,0:T(8,128)S(1)} %select_maximum_fusion), channel_id=1, source_target_pairs={{0,32},{32,0},{64,96},{96,64},{128,160},{160,128},{192,224},{224,1... | collective-permute-start | bytes 73736 | tf_op jit(solution)/shard_map/ppermute | solution.py:269
  8.4 1.7 %collective-permute-start.8 = (f32[3,8,256]{2,1,0:T(8,128)S(1)}, f32[3,8,256]{2,1,0:T(8,128)S(1)}, u32[]{:S(2)}, u32[]{:S(2)}) collective-permute-start(f32[3,8,256]{2,1,0:T(8,128)S(1)} %select_maximum_fusion), channel_id=1, source_target_pairs={{0,96},{32,64},{64,32},{96,0},{128,224},{160,192},{192,160},{224,1... | collective-permute-start | bytes 73736 | tf_op jit(solution)/shard_map/ppermute | solution.py:269
  10.1 3.0 %collective-permute-start.9 = (f32[3,8,256]{2,1,0:T(8,128)S(1)}, f32[3,8,256]{2,1,0:T(8,128)S(1)}, u32[]{:S(2)}, u32[]{:S(2)}) collective-permute-start(f32[3,8,256]{2,1,0:T(8,128)S(1)} %select_maximum_fusion), channel_id=1, source_target_pairs={{0,128},{32,160},{64,192},{96,224},{128,0},{160,32},{192,64},{224,... | collective-permute-start | bytes 73736 | tf_op jit(solution)/shard_map/ppermute | solution.py:269
  13.1 1.8 %collective-permute-start.10 = (f32[3,8,256]{2,1,0:T(8,128)S(1)}, f32[3,8,256]{2,1,0:T(8,128)S(1)}, u32[]{:S(2)}, u32[]{:S(2)}) collective-permute-start(f32[3,8,256]{2,1,0:T(8,128)S(1)} %select_maximum_fusion), channel_id=1, source_target_pairs={{0,160},{32,128},{64,224},{96,192},{128,32},{160,0},{192,96},{224,... | collective-permute-start | bytes 73736 | tf_op jit(solution)/shard_map/ppermute | solution.py:269
  24.5 2.0 %pad_maximum_fusion = f32[10,64,256]{2,1,0:T(8,128)} fusion(f32[5,64,256]{2,1,0:T(8,128)} %get-tuple-element.53, f32[5,64,256]{2,1,0:T(8,128)} %get-tuple-element.51), kind=kLoop, calls=%fused_computation | loop fusion | flops 163840 | bytes 1310720 | tf_op jit(solution)/shard_map/concatenate | solution.py:293
  30.6 1.8 %collective-permute-start.12 = (f32[3,8,256]{2,1,0:T(8,128)S(1)}, f32[3,8,256]{2,1,0:T(8,128)S(1)}, u32[]{:S(2)}, u32[]{:S(2)}) collective-permute-start(f32[3,8,256]{2,1,0:T(8,128)S(1)} %select_maximum_fusion), channel_id=1, source_target_pairs={{0,224},{32,192},{64,160},{96,128},{128,96},{160,64},{192,32},{224... | collective-permute-start | bytes 73736 | tf_op jit(solution)/shard_map/ppermute | solution.py:269
  33.0 1.9 %collective-permute-start = (f32[11,64,256]{2,1,0:T(8,128)}, f32[11,64,256]{2,1,0:T(8,128)S(1)}, u32[]{:S(2)}, u32[]{:S(2)}) collective-permute-start(f32[11,64,256]{2,1,0:T(8,128)} %get-tuple-element.55), channel_id=1, source_target_pairs={{0,1},{1,2},{2,3},{3,4},{4,5},{5,6},{6,7},{7,8},{8,9},{9,10},{10,1... | collective-permute-start | bytes 2162696 | tf_op jit(solution)/shard_map/ppermute | solution.py:23
  35.5 8.7 %collective-permute-start.1 = (f32[11,64,256]{2,1,0:T(8,128)}, f32[11,64,256]{2,1,0:T(8,128)S(1)}, u32[]{:S(2)}, u32[]{:S(2)}) collective-permute-start(f32[11,64,256]{2,1,0:T(8,128)} %get-tuple-element.54), channel_id=1, source_target_pairs={{1,0},{2,1},{3,2},{4,3},{5,4},{6,5},{7,6},{8,7},{9,8},{10,9},{11,1... | collective-permute-start | bytes 2162696 | tf_op jit(solution)/shard_map/ppermute | solution.py:24
  44.9 1.9 %collective-permute-start.2 = (f32[10,64,256]{2,1,0:T(8,128)}, f32[10,64,256]{2,1,0:T(8,128)S(1)}, u32[]{:S(2)}, u32[]{:S(2)}) collective-permute-start(f32[10,64,256]{2,1,0:T(8,128)} %pad_maximum_fusion), channel_id=1, source_target_pairs={{0,1},{1,2},{2,3},{3,4},{4,5},{5,6},{6,7},{7,8},{8,9},{9,10},{10,1... | collective-permute-start | bytes 1966088 | tf_op jit(solution)/shard_map/ppermute | solution.py:23
  47.4 8.7 %collective-permute-start.3 = (f32[10,64,256]{2,1,0:T(8,128)}, f32[10,64,256]{2,1,0:T(8,128)S(1)}, u32[]{:S(2)}, u32[]{:S(2)}) collective-permute-start(f32[10,64,256]{2,1,0:T(8,128)} %pad_maximum_fusion.1), channel_id=1, source_target_pairs={{1,0},{2,1},{3,2},{4,3},{5,4},{6,5},{7,6},{8,7},{9,8},{10,9},{11,1... | collective-permute-start | bytes 1966088 | tf_op jit(solution)/shard_map/ppermute | solution.py:24
  57.4 2.0 %collective-permute-done.1.right = f32[11,64,256]{2,1,0:T(8,128)S(1)} collective-permute-done((f32[11,64,256]{2,1,0:T(8,128)}, f32[11,64,256]{2,1,0:T(8,128)S(1)}, u32[]{:S(2)}, u32[]{:S(2)}) %collective-permute-start.1) | collective-permute-done | bytes 720928 | tf_op jit(solution)/shard_map/ppermute | solution.py:24
  59.4 7.1 %shard_map.138 = (f32[3,8,64,256]{3,2,1,0:T(8,128)}, f32[8,64,256]{2,1,0:T(8,128)S(1)}, f32[8,64,256]{2,1,0:T(8,128)S(1)}, f32[8,64,256]{2,1,0:T(8,128)S(1)}) custom-call(f32[3,8,64,256]{3,2,1,0:T(8,128)} %velocity.1, f32[8,64,256]{2,1,0:T(8,128)S(1)} %copy-done, f32[8,64,256]{2,1,0:T(8,128)S(1)} %copy-done.3, f32[8,64,256]{2,1,0:T(8,128)S(1)} %copy-done.4, ...), custom_call_target="tpu_custom_call" | custom-call | flops 34078720 | bytes 9961472 | tf_op jit(solution)/shard_map/pallas_call | solution.py:183
  66.5 1.9 %collective-permute-start.4 = (f32[4,64,256]{2,1,0:T(8,128)S(1)}, f32[4,64,256]{2,1,0:T(8,128)S(1)}, u32[]{:S(2)}, u32[]{:S(2)}) collective-permute-start(f32[4,64,256]{2,1,0:T(8,128)S(1)} %get-tuple-element.49), channel_id=1, source_target_pairs={{0,1},{1,2},{2,3},{3,4},{4,5},{5,6},{6,7},{7,8},{8,9},{9,10},{10,1... | collective-permute-start | bytes 786440 | tf_op jit(solution)/shard_map/ppermute | solution.py:23
  71.2 1.8 %collective-permute-done.14 = f32[8]{0:T(128)S(1)} collective-permute-done((f32[8]{0:T(128)S(1)}, f32[8]{0:T(128)S(1)}, u32[]{:S(2)}, u32[]{:S(2)}) %collective-permute-start.14) | collective-permute-done | bytes 64 | tf_op jit(solution)/shard_map/ppermute | solution.py:269
  73.4 9.1 %collective-permute-start.5 = (f32[4,64,256]{2,1,0:T(8,128)S(1)}, f32[4,64,256]{2,1,0:T(8,128)S(1)}, u32[]{:S(2)}, u32[]{:S(2)}) collective-permute-start(f32[4,64,256]{2,1,0:T(8,128)S(1)} %get-tuple-element.48), channel_id=1, source_target_pairs={{1,0},{2,1},{3,2},{4,3},{5,4},{6,5},{7,6},{8,7},{9,8},{10,9},{11,1... | collective-permute-start | bytes 786440 | tf_op jit(solution)/shard_map/ppermute | solution.py:24
  83.4 5.1 %collective-permute-done.16 = f32[8]{0:T(128)S(1)} collective-permute-done((f32[8]{0:T(128)S(1)}, f32[8]{0:T(128)S(1)}, u32[]{:S(2)}, u32[]{:S(2)}) %collective-permute-start.16) | collective-permute-done | bytes 64 | tf_op jit(solution)/shard_map/ppermute | solution.py:269
  88.4 2.6 %collective-permute-start.17 = (f32[8]{0:T(128)S(1)}, f32[8]{0:T(128)S(1)}, u32[]{:S(2)}, u32[]{:S(2)}) collective-permute-start(f32[8]{0:T(128)S(1)} %add_add_fusion.1), channel_id=1, source_target_pairs={{0,8},{1,9},{2,10},{3,11},{4,12},{5,13},{6,14},{7,15},{8,0},{9,1},... | collective-permute-start | bytes 104 | tf_op jit(solution)/shard_map/ppermute | solution.py:269
  91.1 1.8 %collective-permute-done.17 = f32[8]{0:T(128)S(1)} collective-permute-done((f32[8]{0:T(128)S(1)}, f32[8]{0:T(128)S(1)}, u32[]{:S(2)}, u32[]{:S(2)}) %collective-permute-start.17) | collective-permute-done | bytes 64 | tf_op jit(solution)/shard_map/ppermute | solution.py:269
  92.9 5.6 %collective-permute-start.18 = (f32[8]{0:T(128)S(1)}, f32[8]{0:T(128)S(1)}, u32[]{:S(2)}, u32[]{:S(2)}) collective-permute-start(f32[8]{0:T(128)S(1)} %add_add_fusion.1), channel_id=1, source_target_pairs={{0,12},{1,13},{2,14},{3,15},{4,8},{5,9},{6,10},{7,11},{8,4},{9,5},... | collective-permute-start | bytes 104 | tf_op jit(solution)/shard_map/ppermute | solution.py:269
  98.5 1.5 %collective-permute-done.18 = f32[8]{0:T(128)S(1)} collective-permute-done((f32[8]{0:T(128)S(1)}, f32[8]{0:T(128)S(1)}, u32[]{:S(2)}, u32[]{:S(2)}) %collective-permute-start.18) | collective-permute-done | bytes 64 | tf_op jit(solution)/shard_map/ppermute | solution.py:269
  100.1 8.3 %collective-permute-start.19 = (f32[8]{0:T(128)S(1)}, f32[8]{0:T(128)S(1)}, u32[]{:S(2)}, u32[]{:S(2)}) collective-permute-start(f32[8]{0:T(128)S(1)} %add_add_fusion), channel_id=1, source_target_pairs={{0,16},{1,17},{2,18},{3,19},{4,20},{5,21},{6,22},{7,23},{8,24},{9,... | collective-permute-start | bytes 104 | tf_op jit(solution)/shard_map/ppermute | solution.py:269
  108.4 10.8 %shard_map.139 = (f32[3,8,64,256]{3,2,1,0:T(8,128)}, f32[8,64,256]{2,1,0:T(8,128)}) custom-call(f32[8,64,256]{2,1,0:T(8,128)S(1)} %copy-done, f32[8,64,256]{2,1,0:T(8,128)S(1)} %copy-done.1, f32[8,64,256]{2,1,0:T(8,128)S(1)} %get-tuple-element.29.source, f32[3,8,64,256]{3,2,1,0:T(8,128)S(1)} %copy-done.2, ...), custom_call_target="tpu_custom_call" | custom-call | flops 26214400 | bytes 6291456 | tf_op jit(solution)/shard_map/pallas_call | solution.py:210
  (81 shorter events, 25.4 us)
Async XLA Ops:
  6.5 22.3 %collective-permute-start.6 = (f32[3,8,256]{2,1,0:T(8,128)S(1)}, f32[3,8,256]{2,1,0:T(8,128)S(1)}, u32[]{:S(2)}, u32[]{:S(2)}) collective-permute-start(f32[3,8,256]{2,1,0:T(8,128)S(1)} %select_maximum_fusion), channel_id=1, source_target_pairs={{0,32},{32,0},{64,96},{96,64},{128,160},{160,128},{192,224},{224,1... | collective-permute-start | bytes 73736 | tf_op jit(solution)/shard_map/ppermute | solution.py:269
  8.4 22.1 %collective-permute-start.7 = (f32[3,8,256]{2,1,0:T(8,128)S(1)}, f32[3,8,256]{2,1,0:T(8,128)S(1)}, u32[]{:S(2)}, u32[]{:S(2)}) collective-permute-start(f32[3,8,256]{2,1,0:T(8,128)S(1)} %select_maximum_fusion), channel_id=1, source_target_pairs={{0,64},{32,96},{64,0},{96,32},{128,192},{160,224},{192,128},{224,1... | collective-permute-start | bytes 73736 | tf_op jit(solution)/shard_map/ppermute | solution.py:269
  8.4 24.5 %collective-permute-start.8 = (f32[3,8,256]{2,1,0:T(8,128)S(1)}, f32[3,8,256]{2,1,0:T(8,128)S(1)}, u32[]{:S(2)}, u32[]{:S(2)}) collective-permute-start(f32[3,8,256]{2,1,0:T(8,128)S(1)} %select_maximum_fusion), channel_id=1, source_target_pairs={{0,96},{32,64},{64,32},{96,0},{128,224},{160,192},{192,160},{224,1... | collective-permute-start | bytes 73736 | tf_op jit(solution)/shard_map/ppermute | solution.py:269
  10.1 25.4 %collective-permute-start.9 = (f32[3,8,256]{2,1,0:T(8,128)S(1)}, f32[3,8,256]{2,1,0:T(8,128)S(1)}, u32[]{:S(2)}, u32[]{:S(2)}) collective-permute-start(f32[3,8,256]{2,1,0:T(8,128)S(1)} %select_maximum_fusion), channel_id=1, source_target_pairs={{0,128},{32,160},{64,192},{96,224},{128,0},{160,32},{192,64},{224,... | collective-permute-start | bytes 73736 | tf_op jit(solution)/shard_map/ppermute | solution.py:269
  13.1 31.7 %collective-permute-start.10 = (f32[3,8,256]{2,1,0:T(8,128)S(1)}, f32[3,8,256]{2,1,0:T(8,128)S(1)}, u32[]{:S(2)}, u32[]{:S(2)}) collective-permute-start(f32[3,8,256]{2,1,0:T(8,128)S(1)} %select_maximum_fusion), channel_id=1, source_target_pairs={{0,160},{32,128},{64,224},{96,192},{128,32},{160,0},{192,96},{224,... | collective-permute-start | bytes 73736 | tf_op jit(solution)/shard_map/ppermute | solution.py:269
  22.5 36.8 %copy-start.5 = (s32[8,64,256]{2,1,0:T(8,128)S(1)}, s32[8,64,256]{2,1,0:T(8,128)}, u32[]{:S(2)}) copy-start(s32[8,64,256]{2,1,0:T(8,128)} %solid.1) | copy-start | bytes 1572868
  28.8 18.6 %collective-permute-start.11 = (f32[3,8,256]{2,1,0:T(8,128)S(1)}, f32[3,8,256]{2,1,0:T(8,128)S(1)}, u32[]{:S(2)}, u32[]{:S(2)}) collective-permute-start(f32[3,8,256]{2,1,0:T(8,128)S(1)} %select_maximum_fusion), channel_id=1, source_target_pairs={{0,192},{32,224},{64,128},{96,160},{128,64},{160,96},{192,0},{224,... | collective-permute-start | bytes 73736 | tf_op jit(solution)/shard_map/ppermute | solution.py:269
  30.6 26.2 %collective-permute-start.12 = (f32[3,8,256]{2,1,0:T(8,128)S(1)}, f32[3,8,256]{2,1,0:T(8,128)S(1)}, u32[]{:S(2)}, u32[]{:S(2)}) collective-permute-start(f32[3,8,256]{2,1,0:T(8,128)S(1)} %select_maximum_fusion), channel_id=1, source_target_pairs={{0,224},{32,192},{64,160},{96,128},{128,96},{160,64},{192,32},{224... | collective-permute-start | bytes 73736 | tf_op jit(solution)/shard_map/ppermute | solution.py:269
  33.0 24.4 %collective-permute-start = (f32[11,64,256]{2,1,0:T(8,128)}, f32[11,64,256]{2,1,0:T(8,128)S(1)}, u32[]{:S(2)}, u32[]{:S(2)}) collective-permute-start(f32[11,64,256]{2,1,0:T(8,128)} %get-tuple-element.55), channel_id=1, source_target_pairs={{0,1},{1,2},{2,3},{3,4},{4,5},{5,6},{6,7},{7,8},{8,9},{9,10},{10,1... | collective-permute-start | bytes 2162696 | tf_op jit(solution)/shard_map/ppermute | solution.py:23
  35.5 23.8 %collective-permute-start.1 = (f32[11,64,256]{2,1,0:T(8,128)}, f32[11,64,256]{2,1,0:T(8,128)S(1)}, u32[]{:S(2)}, u32[]{:S(2)}) collective-permute-start(f32[11,64,256]{2,1,0:T(8,128)} %get-tuple-element.54), channel_id=1, source_target_pairs={{1,0},{2,1},{3,2},{4,3},{5,4},{6,5},{7,6},{8,7},{9,8},{10,9},{11,1... | collective-permute-start | bytes 2162696 | tf_op jit(solution)/shard_map/ppermute | solution.py:24
  44.9 63.5 %collective-permute-start.2 = (f32[10,64,256]{2,1,0:T(8,128)}, f32[10,64,256]{2,1,0:T(8,128)S(1)}, u32[]{:S(2)}, u32[]{:S(2)}) collective-permute-start(f32[10,64,256]{2,1,0:T(8,128)} %pad_maximum_fusion), channel_id=1, source_target_pairs={{0,1},{1,2},{2,3},{3,4},{4,5},{5,6},{6,7},{7,8},{8,9},{9,10},{10,1... | collective-permute-start | bytes 1966088 | tf_op jit(solution)/shard_map/ppermute | solution.py:23
  47.4 61.0 %collective-permute-start.3 = (f32[10,64,256]{2,1,0:T(8,128)}, f32[10,64,256]{2,1,0:T(8,128)S(1)}, u32[]{:S(2)}, u32[]{:S(2)}) collective-permute-start(f32[10,64,256]{2,1,0:T(8,128)} %pad_maximum_fusion.1), channel_id=1, source_target_pairs={{1,0},{2,1},{3,2},{4,3},{5,4},{6,5},{7,6},{8,7},{9,8},{10,9},{11,1... | collective-permute-start | bytes 1966088 | tf_op jit(solution)/shard_map/ppermute | solution.py:24
  66.5 33.5 %collective-permute-start.4 = (f32[4,64,256]{2,1,0:T(8,128)S(1)}, f32[4,64,256]{2,1,0:T(8,128)S(1)}, u32[]{:S(2)}, u32[]{:S(2)}) collective-permute-start(f32[4,64,256]{2,1,0:T(8,128)S(1)} %get-tuple-element.49), channel_id=1, source_target_pairs={{0,1},{1,2},{2,3},{3,4},{4,5},{5,6},{6,7},{7,8},{8,9},{9,10},{10,1... | collective-permute-start | bytes 786440 | tf_op jit(solution)/shard_map/ppermute | solution.py:23
  69.2 1.2 collective-permute-start.13
  69.3 3.7 %collective-permute-start.14 = (f32[8]{0:T(128)S(1)}, f32[8]{0:T(128)S(1)}, u32[]{:S(2)}, u32[]{:S(2)}) collective-permute-start(f32[8]{0:T(128)S(1)} %slice_reduce_fusion), channel_id=1, source_target_pairs={{0,2},{1,3},{2,0},{3,1},{4,6},{5,7},{6,4},{7,5},{8,10},{9,11},{10,... | collective-permute-start | bytes 104 | tf_op jit(solution)/shard_map/ppermute | solution.py:269
  70.4 3.0 %collective-permute-start.15 = (f32[8]{0:T(128)S(1)}, f32[8]{0:T(128)S(1)}, u32[]{:S(2)}, u32[]{:S(2)}) collective-permute-start(f32[8]{0:T(128)S(1)} %slice_reduce_fusion), channel_id=1, source_target_pairs={{0,3},{1,2},{2,1},{3,0},{4,7},{5,6},{6,5},{7,4},{8,11},{9,10},{10,... | collective-permute-start | bytes 104 | tf_op jit(solution)/shard_map/ppermute | solution.py:269
  73.4 35.0 %collective-permute-start.5 = (f32[4,64,256]{2,1,0:T(8,128)S(1)}, f32[4,64,256]{2,1,0:T(8,128)S(1)}, u32[]{:S(2)}, u32[]{:S(2)}) collective-permute-start(f32[4,64,256]{2,1,0:T(8,128)S(1)} %get-tuple-element.48), channel_id=1, source_target_pairs={{1,0},{2,1},{3,2},{4,3},{5,4},{6,5},{7,6},{8,7},{9,8},{10,9},{11,1... | collective-permute-start | bytes 786440 | tf_op jit(solution)/shard_map/ppermute | solution.py:24
  82.9 25.6 %copy-start.2 = (f32[3,8,64,256]{3,2,1,0:T(8,128)S(1)}, f32[3,8,64,256]{3,2,1,0:T(8,128)}, u32[]{:S(2)}) copy-start(f32[3,8,64,256]{3,2,1,0:T(8,128)} %get-tuple-element.30.star_in) | copy-start | bytes 4718596
  83.3 5.2 %collective-permute-start.16 = (f32[8]{0:T(128)S(1)}, f32[8]{0:T(128)S(1)}, u32[]{:S(2)}, u32[]{:S(2)}) collective-permute-start(f32[8]{0:T(128)S(1)} %add_add_fusion.1), channel_id=1, source_target_pairs={{0,4},{1,5},{2,6},{3,7},{4,0},{5,1},{6,2},{7,3},{8,12},{9,13},{10,... | collective-permute-start | bytes 104 | tf_op jit(solution)/shard_map/ppermute | solution.py:269
  88.4 4.5 %collective-permute-start.17 = (f32[8]{0:T(128)S(1)}, f32[8]{0:T(128)S(1)}, u32[]{:S(2)}, u32[]{:S(2)}) collective-permute-start(f32[8]{0:T(128)S(1)} %add_add_fusion.1), channel_id=1, source_target_pairs={{0,8},{1,9},{2,10},{3,11},{4,12},{5,13},{6,14},{7,15},{8,0},{9,1},... | collective-permute-start | bytes 104 | tf_op jit(solution)/shard_map/ppermute | solution.py:269
  92.9 7.1 %collective-permute-start.18 = (f32[8]{0:T(128)S(1)}, f32[8]{0:T(128)S(1)}, u32[]{:S(2)}, u32[]{:S(2)}) collective-permute-start(f32[8]{0:T(128)S(1)} %add_add_fusion.1), channel_id=1, source_target_pairs={{0,12},{1,13},{2,14},{3,15},{4,8},{5,9},{6,10},{7,11},{8,4},{9,5},... | collective-permute-start | bytes 104 | tf_op jit(solution)/shard_map/ppermute | solution.py:269
  100.0 19.2 %copy-start.8 = (s32[8]{0:T(128)S(1)}, s32[8]{0:T(128)}, u32[]{:S(2)}) copy-start(s32[8]{0:T(128)} %param.20) | copy-start | bytes 100
  100.1 20.4 %copy-start.6 = (s32[8,256]{1,0:T(8,128)S(1)}, s32[8,256]{1,0:T(8,128)}, u32[]{:S(2)}) copy-start(s32[8,256]{1,0:T(8,128)} %param.19) | copy-start | bytes 24580
  100.1 19.1 %collective-permute-start.19 = (f32[8]{0:T(128)S(1)}, f32[8]{0:T(128)S(1)}, u32[]{:S(2)}, u32[]{:S(2)}) collective-permute-start(f32[8]{0:T(128)S(1)} %add_add_fusion), channel_id=1, source_target_pairs={{0,16},{1,17},{2,18},{3,19},{4,20},{5,21},{6,22},{7,23},{8,24},{9,... | collective-permute-start | bytes 104 | tf_op jit(solution)/shard_map/ppermute | solution.py:269
  (6 other events, 73.6 us)

commit v8 on v7

--- a/solution.py
+++ b/solution.py
@@ -272,10 +272,14 @@
         if anchor is not None:
             sent, _ = lax.optimization_barrier((sent, anchor))
         if axis == "zone":
-            received = jnp.stack([message] + sent)
             pick = jnp.bitwise_xor(duct_source[0], lax.axis_index("zone"))
-            state["arrived"] = lax.dynamic_index_in_dim(received, pick, axis=0, keepdims=False)
-            state["totals"] = jnp.sum(received[:, 2, 0, :nzones], axis=0)
+            arrived = message[0:2]
+            total = message[2, 0, :nzones]
+            for k, part in enumerate(sent, start=1):
+                arrived = jnp.where(pick == k, part[0:2], arrived)
+                total = total + part[2, 0, :nzones]
+            state["arrived"] = arrived
+            state["totals"] = total
         else:
             total = state["totals"]
             for part in sent:
@@ -292,6 +296,7 @@
     wide_head = jnp.concatenate([pressure[0:5], porosity[0:5]], axis=0)
     wide_tail = jnp.concatenate([pressure[cx - 5:], porosity[cx - 5:]], axis=0)
     n_left, n_right = neighbours(narrow_head, narrow_tail)
+    wide_head, wide_tail, _ = lax.optimization_barrier((wide_head, wide_tail, (n_left, n_right)))
     w_left, w_right = neighbours(wide_head, wide_tail)
 
     advance(None)

time: 126 us -> 125 us (level)
  starting transfers between devices: 61.1 us -> 49.6 us
  waiting for transfers between devices: 13.8 us -> 23.5 us
  Pallas kernels: 17.9 us -> 19.4 us
    ppermute x14, waiting for transfers between devices: 11.8 us -> 23.5 us  [advance(): lax.ppermute(value, axis, [(i, i ^ k * stride) for i in range(size)])]
    ppermute x14, starting transfers between devices: 28.8 us -> 21 us  [advance(): lax.ppermute(value, axis, [(i, i ^ k * stride) for i in range(size)])]
    ppermute x3, starting transfers between devices: 26.6 us -> 22.5 us  [neighbours(): from_right = lax.ppermute(head, ALL, [(i + 1, i) for i in range(count - 1)])]
    unnamed x30 -> x34, local copies, waits for them, and re-layouts: 6.64 us -> 4.1 us
    concatenate x1 -> x0, other arithmetic: 2.01 us -> none  [on_device_body(): wide_tail = jnp.concatenate([pressure[cx - 5:], porosity[cx - 5:]], axis=0)]
    ppermute x3, waiting for transfers between devices: 1.98 us -> 0.01 us  [neighbours(): from_right = lax.ppermute(head, ALL, [(i + 1, i) for i in range(count - 1)])]
    pallas_call x2, local copies, waits for them, and re-layouts: 0.62 us -> 2.2 us  [stage_one(): pl.pallas_call(stage_one_kernel, out_shape=outs, scratch_shapes=[pltpu.VM...]
    slice x2, local copies, waits for them, and re-layouts: 1.58 us -> 0.1 us  [on_device_body(): wide_tail = jnp.concatenate([pressure[cx - 5:], porosity[cx - 5:]], axis=0)]
  transfers between devices with their start and end apart: 20 -> 20, of which waited for: 7 -> 3; matrix products, arithmetic and copies ran while one was open for 14% -> 16% of each run, Pallas kernels for 14% -> 6%
where the time goes in v8:
time: 125 us; the launch traced here: 124 us
  starting transfers between devices  49.6 us (40%)
  waiting for transfers between devices  23.5 us (19%)
  Pallas kernels  19.4 us (16%)
  other arithmetic  14 us (11%)
  local copies, waits for them, and re-layouts  12.1 us (10%)
  between operations  5.52 us (4%)
    ppermute x14, waiting for transfers between devices, advance(): lax.ppermute(value, axis, [(i, i ^ k * stride) for i in range(size)])  23.5 us
    ppermute x3, starting transfers between devices, neighbours(): from_right = lax.ppermute(head, ALL, [(i + 1, i) for i in range(count - 1)])  22.5 us
    ppermute x14, starting transfers between devices, advance(): lax.ppermute(value, axis, [(i, i ^ k * stride) for i in range(size)])  21 us
    pallas_call x1, Pallas kernels, stage_two(): pl.pallas_call(stage_two_kernel, out_shape=outs, scratch_shapes=[pltpu.VM...  12.1 us
    pallas_call x1, Pallas kernels, stage_one(): pl.pallas_call(stage_one_kernel, out_shape=outs, scratch_shapes=[pltpu.VM...  7.29 us
    ppermute x3, starting transfers between devices, neighbours(): from_left = lax.ppermute(tail, ALL, [(i, i + 1) for i in range(count - 1)])  6.09 us
    unnamed x34, local copies, waits for them, and re-layouts  4.1 us
  transfers between devices with their start and end apart: 20, of which 3 were waited for; matrix products, arithmetic and copies ran while one was open for 16% of the time, Pallas kernels for 6%

profile of v8, /device:TPU:32, one launch (start us, length us, event | category | flops | bytes accessed | tf_op | source)
XLA Modules:
  0.0 124.2 jit_solution(7496455725294569472)
XLA Ops:
  0.6 1.5 %fusion.21 = (f32[8,1,256]{2,1,0:T(1,128)S(1)}, f32[]{:T(128)}) fusion(f32[8,64,256]{2,1,0:T(8,128)} %solvent.1), kind=kLoop, calls=%fused_computation.63 | loop fusion | flops 2047 | bytes 16388 | tf_op jit(solution)/shard_map/slice | solution.py:246
  3.8 1.3 %fusion.12 = s32[]{:T(128)} fusion(s32[8]{0:T(128)} %param.20, s32[8,1]{0,1:T(1,128)S(1)} %reduce-window.9, s32[]{:T(128)S(6)} %add.66), kind=kLoop, calls=%fused_computation.39 | loop fusion | flops 31 | bytes 72 | tf_op jit(solution)/shard_map/reduce_sum | solution.py:243
  6.5 1.9 %collective-permute-start.6 = (f32[3,8,256]{2,1,0:T(8,128)S(1)}, f32[3,8,256]{2,1,0:T(8,128)S(1)}, u32[]{:S(2)}, u32[]{:S(2)}) collective-permute-start(f32[3,8,256]{2,1,0:T(8,128)S(1)} %select_maximum_fusion), channel_id=1, source_target_pairs={{0,32},{32,0},{64,96},{96,64},{128,160},{160,128},{192,224},{224,1... | collective-permute-start | bytes 73736 | tf_op jit(solution)/shard_map/ppermute | solution.py:269
  8.4 1.7 %collective-permute-start.8 = (f32[3,8,256]{2,1,0:T(8,128)S(1)}, f32[3,8,256]{2,1,0:T(8,128)S(1)}, u32[]{:S(2)}, u32[]{:S(2)}) collective-permute-start(f32[3,8,256]{2,1,0:T(8,128)S(1)} %select_maximum_fusion), channel_id=1, source_target_pairs={{0,96},{32,64},{64,32},{96,0},{128,224},{160,192},{192,160},{224,1... | collective-permute-start | bytes 73736 | tf_op jit(solution)/shard_map/ppermute | solution.py:269
  14.9 1.9 %collective-permute-start = (f32[11,64,256]{2,1,0:T(8,128)}, f32[11,64,256]{2,1,0:T(8,128)S(1)}, u32[]{:S(2)}, u32[]{:S(2)}) collective-permute-start(f32[11,64,256]{2,1,0:T(8,128)} %get-tuple-element.59), channel_id=1, source_target_pairs={{0,1},{1,2},{2,3},{3,4},{4,5},{5,6},{6,7},{7,8},{8,9},{9,10},{10,1... | collective-permute-start | bytes 2162696 | tf_op jit(solution)/shard_map/ppermute | solution.py:23
  16.8 8.8 %collective-permute-start.1 = (f32[11,64,256]{2,1,0:T(8,128)}, f32[11,64,256]{2,1,0:T(8,128)}, u32[]{:S(2)}, u32[]{:S(2)}) collective-permute-start(f32[11,64,256]{2,1,0:T(8,128)} %get-tuple-element.58), channel_id=1, source_target_pairs={{1,0},{2,1},{3,2},{4,3},{5,4},{6,5},{7,6},{8,7},{9,8},{10,9},{11,1... | collective-permute-start | bytes 2162696 | tf_op jit(solution)/shard_map/ppermute | solution.py:24
  25.8 1.2 pad_maximum_fusion
  27.5 3.0 %collective-permute-start.9 = (f32[3,8,256]{2,1,0:T(8,128)S(1)}, f32[3,8,256]{2,1,0:T(8,128)S(1)}, u32[]{:S(2)}, u32[]{:S(2)}) collective-permute-start(f32[3,8,256]{2,1,0:T(8,128)S(1)} %select_maximum_fusion), channel_id=1, source_target_pairs={{0,128},{32,160},{64,192},{96,224},{128,0},{160,32},{192,64},{224,... | collective-permute-start | bytes 73736 | tf_op jit(solution)/shard_map/ppermute | solution.py:269
  32.7 3.1 %collective-permute-start.11 = (f32[3,8,256]{2,1,0:T(8,128)S(1)}, f32[3,8,256]{2,1,0:T(8,128)S(1)}, u32[]{:S(2)}, u32[]{:S(2)}) collective-permute-start(f32[3,8,256]{2,1,0:T(8,128)S(1)} %select_maximum_fusion), channel_id=1, source_target_pairs={{0,192},{32,224},{64,128},{96,160},{128,64},{160,96},{192,0},{224,... | collective-permute-start | bytes 73736 | tf_op jit(solution)/shard_map/ppermute | solution.py:269
  35.7 1.6 %collective-permute-start.12 = (f32[3,8,256]{2,1,0:T(8,128)S(1)}, f32[3,8,256]{2,1,0:T(8,128)S(1)}, u32[]{:S(2)}, u32[]{:S(2)}) collective-permute-start(f32[3,8,256]{2,1,0:T(8,128)S(1)} %select_maximum_fusion), channel_id=1, source_target_pairs={{0,224},{32,192},{64,160},{96,128},{128,96},{160,64},{192,32},{224... | collective-permute-start | bytes 73736 | tf_op jit(solution)/shard_map/ppermute | solution.py:269
  38.6 3.7 %collective-permute-done.10 = f32[3,8,256]{2,1,0:T(8,128)S(1)} collective-permute-done((f32[3,8,256]{2,1,0:T(8,128)S(1)}, f32[3,8,256]{2,1,0:T(8,128)S(1)}, u32[]{:S(2)}, u32[]{:S(2)}) %collective-permute-start.10) | collective-permute-done | bytes 24608 | tf_op jit(solution)/shard_map/ppermute | solution.py:269
  43.5 1.7 %collective-permute-start.15 = (f32[8]{0:T(128)S(1)}, f32[8]{0:T(128)S(1)}, u32[]{:S(2)}, u32[]{:S(2)}) collective-permute-start(f32[8]{0:T(128)S(1)} %fusion.13), channel_id=1, source_target_pairs={{0,3},{1,2},{2,1},{3,0},{4,7},{5,6},{6,5},{7,4},{8,11},{9,10},{10,... | collective-permute-start | bytes 104 | tf_op jit(solution)/shard_map/ppermute | solution.py:269
  46.3 7.3 %shard_map.138 = (f32[3,8,64,256]{3,2,1,0:T(8,128)}, f32[8,64,256]{2,1,0:T(8,128)S(1)}, f32[8,64,256]{2,1,0:T(8,128)S(1)}, f32[8,64,256]{2,1,0:T(8,128)S(1)}) custom-call(f32[3,8,64,256]{3,2,1,0:T(8,128)} %velocity.1, f32[8,64,256]{2,1,0:T(8,128)S(1)} %copy-done, f32[8,64,256]{2,1,0:T(8,128)S(1)} %copy-done.3, f32[8,64,256]{2,1,0:T(8,128)S(1)} %copy-done.4, ...), custom_call_target="tpu_custom_call" | custom-call | flops 34078720 | bytes 9961472 | tf_op jit(solution)/shard_map/pallas_call | solution.py:183
  54.3 2.3 %collective-permute-start.4 = (f32[4,64,256]{2,1,0:T(8,128)S(1)}, f32[4,64,256]{2,1,0:T(8,128)S(1)}, u32[]{:S(2)}, u32[]{:S(2)}) collective-permute-start(f32[4,64,256]{2,1,0:T(8,128)S(1)} %get-tuple-element.53), channel_id=1, source_target_pairs={{0,1},{1,2},{2,3},{3,4},{4,5},{5,6},{6,7},{7,8},{8,9},{9,10},{10,1... | collective-permute-start | bytes 786440 | tf_op jit(solution)/shard_map/ppermute | solution.py:23
  57.5 3.8 %collective-permute-start.17 = (f32[8]{0:T(128)S(1)}, f32[8]{0:T(128)S(1)}, u32[]{:S(2)}, u32[]{:S(2)}) collective-permute-start(f32[8]{0:T(128)S(1)} %add_add_fusion.1), channel_id=1, source_target_pairs={{0,8},{1,9},{2,10},{3,11},{4,12},{5,13},{6,14},{7,15},{8,0},{9,1},... | collective-permute-start | bytes 104 | tf_op jit(solution)/shard_map/ppermute | solution.py:269
  61.3 2.1 %collective-permute-start.18 = (f32[8]{0:T(128)S(1)}, f32[8]{0:T(128)S(1)}, u32[]{:S(2)}, u32[]{:S(2)}) collective-permute-start(f32[8]{0:T(128)S(1)} %add_add_fusion.1), channel_id=1, source_target_pairs={{0,12},{1,13},{2,14},{3,15},{4,8},{5,9},{6,10},{7,11},{8,4},{9,5},... | collective-permute-start | bytes 104 | tf_op jit(solution)/shard_map/ppermute | solution.py:269
  67.3 1.9 %collective-permute-start.2 = (f32[10,64,256]{2,1,0:T(8,128)}, f32[10,64,256]{2,1,0:T(8,128)}, u32[]{:S(2)}, u32[]{:S(2)}) collective-permute-start(f32[10,64,256]{2,1,0:T(8,128)} %get-tuple-element.33), channel_id=1, source_target_pairs={{0,1},{1,2},{2,3},{3,4},{4,5},{5,6},{6,7},{7,8},{8,9},{9,10},{10,1... | collective-permute-start | bytes 1966088 | tf_op jit(solution)/shard_map/ppermute | solution.py:23
  69.2 11.3 %collective-permute-start.3 = (f32[10,64,256]{2,1,0:T(8,128)}, f32[10,64,256]{2,1,0:T(8,128)}, u32[]{:S(2)}, u32[]{:S(2)}) collective-permute-start(f32[10,64,256]{2,1,0:T(8,128)} %get-tuple-element.34), channel_id=1, source_target_pairs={{1,0},{2,1},{3,2},{4,3},{5,4},{6,5},{7,6},{8,7},{9,8},{10,9},{11,1... | collective-permute-start | bytes 1966088 | tf_op jit(solution)/shard_map/ppermute | solution.py:24
  80.5 2.4 %collective-permute-start.5 = (f32[4,64,256]{2,1,0:T(8,128)}, f32[4,64,256]{2,1,0:T(8,128)}, u32[]{:S(2)}, u32[]{:S(2)}) collective-permute-start(f32[4,64,256]{2,1,0:T(8,128)} %get-tuple-element.52), channel_id=1, source_target_pairs={{1,0},{2,1},{3,2},{4,3},{5,4},{6,5},{7,6},{8,7},{9,8},{10,9},{11,1... | collective-permute-start | bytes 786440 | tf_op jit(solution)/shard_map/ppermute | solution.py:24
  83.0 1.8 %collective-permute-start.19 = (f32[8]{0:T(128)S(1)}, f32[8]{0:T(128)S(1)}, u32[]{:S(2)}, u32[]{:S(2)}) collective-permute-start(f32[8]{0:T(128)S(1)} %add_add_fusion), channel_id=1, source_target_pairs={{0,16},{1,17},{2,18},{3,19},{4,20},{5,21},{6,22},{7,23},{8,24},{9,... | collective-permute-start | bytes 104 | tf_op jit(solution)/shard_map/ppermute | solution.py:269
  84.8 19.5 %collective-permute-done.19 = f32[8]{0:T(128)S(1)} collective-permute-done((f32[8]{0:T(128)S(1)}, f32[8]{0:T(128)S(1)}, u32[]{:S(2)}, u32[]{:S(2)}) %collective-permute-start.19) | collective-permute-done | bytes 64 | tf_op jit(solution)/shard_map/ppermute | solution.py:269
  108.3 1.9 %pad_maximum_fusion.2 = f32[8,64,256]{2,1,0:T(8,128)} fusion(f32[8,63,256]{2,1,0:T(8,128)} %slice.180, f32[8,1,256]{2,1,0:T(1,128)S(1)} %copy.18), kind=kLoop, calls=%fused_computation.2 | loop fusion | flops 131072 | bytes 1048576 | tf_op jit(solution)/shard_map/concatenate | solution.py:330
  110.2 1.9 %pad_maximum_fusion.3 = f32[8,64,256]{2,1,0:T(8,128)} fusion(f32[8,63,256]{2,1,0:T(8,128)} %slice.183, f32[8,1,256]{2,1,0:T(1,128)S(1)} %broadcast_in_dim.9), kind=kLoop, calls=%fused_computation.3 | loop fusion | flops 131072 | bytes 1048576 | tf_op jit(solution)/shard_map/concatenate | solution.py:331
  112.1 12.1 %shard_map.139 = (f32[3,8,64,256]{3,2,1,0:T(8,128)}, f32[8,64,256]{2,1,0:T(8,128)}) custom-call(f32[8,64,256]{2,1,0:T(8,128)S(1)} %copy-done, f32[8,64,256]{2,1,0:T(8,128)S(1)} %copy-done.1, f32[8,64,256]{2,1,0:T(8,128)S(1)} %get-tuple-element.31.source, f32[3,8,64,256]{3,2,1,0:T(8,128)S(1)} %copy-done.2, f32[10,64,256]{2,1,0:T(8,128)} %collective-permute-done.2.wide_left, ...), custom_call_target="tpu_custom_call" | custom-call | flops 26214400 | bytes 6291456 | tf_op jit(solution)/shard_map/pallas_call | solution.py:210
  (83 shorter events, 19.0 us)
Async XLA Ops:
  6.5 21.1 %collective-permute-start.6 = (f32[3,8,256]{2,1,0:T(8,128)S(1)}, f32[3,8,256]{2,1,0:T(8,128)S(1)}, u32[]{:S(2)}, u32[]{:S(2)}) collective-permute-start(f32[3,8,256]{2,1,0:T(8,128)S(1)} %select_maximum_fusion), channel_id=1, source_target_pairs={{0,32},{32,0},{64,96},{96,64},{128,160},{160,128},{192,224},{224,1... | collective-permute-start | bytes 73736 | tf_op jit(solution)/shard_map/ppermute | solution.py:269
  8.4 24.2 %collective-permute-start.7 = (f32[3,8,256]{2,1,0:T(8,128)S(1)}, f32[3,8,256]{2,1,0:T(8,128)S(1)}, u32[]{:S(2)}, u32[]{:S(2)}) collective-permute-start(f32[3,8,256]{2,1,0:T(8,128)S(1)} %select_maximum_fusion), channel_id=1, source_target_pairs={{0,64},{32,96},{64,0},{96,32},{128,192},{160,224},{192,128},{224,1... | collective-permute-start | bytes 73736 | tf_op jit(solution)/shard_map/ppermute | solution.py:269
  8.4 24.3 %collective-permute-start.8 = (f32[3,8,256]{2,1,0:T(8,128)S(1)}, f32[3,8,256]{2,1,0:T(8,128)S(1)}, u32[]{:S(2)}, u32[]{:S(2)}) collective-permute-start(f32[3,8,256]{2,1,0:T(8,128)S(1)} %select_maximum_fusion), channel_id=1, source_target_pairs={{0,96},{32,64},{64,32},{96,0},{128,224},{160,192},{192,160},{224,1... | collective-permute-start | bytes 73736 | tf_op jit(solution)/shard_map/ppermute | solution.py:269
  14.9 30.3 %collective-permute-start = (f32[11,64,256]{2,1,0:T(8,128)}, f32[11,64,256]{2,1,0:T(8,128)S(1)}, u32[]{:S(2)}, u32[]{:S(2)}) collective-permute-start(f32[11,64,256]{2,1,0:T(8,128)} %get-tuple-element.59), channel_id=1, source_target_pairs={{0,1},{1,2},{2,3},{3,4},{4,5},{5,6},{6,7},{7,8},{8,9},{9,10},{10,1... | collective-permute-start | bytes 2162696 | tf_op jit(solution)/shard_map/ppermute | solution.py:23
  16.8 28.4 %collective-permute-start.1 = (f32[11,64,256]{2,1,0:T(8,128)}, f32[11,64,256]{2,1,0:T(8,128)}, u32[]{:S(2)}, u32[]{:S(2)}) collective-permute-start(f32[11,64,256]{2,1,0:T(8,128)} %get-tuple-element.58), channel_id=1, source_target_pairs={{1,0},{2,1},{3,2},{4,3},{5,4},{6,5},{7,6},{8,7},{9,8},{10,9},{11,1... | collective-permute-start | bytes 2162696 | tf_op jit(solution)/shard_map/ppermute | solution.py:24
  27.5 8.2 %collective-permute-start.9 = (f32[3,8,256]{2,1,0:T(8,128)S(1)}, f32[3,8,256]{2,1,0:T(8,128)S(1)}, u32[]{:S(2)}, u32[]{:S(2)}) collective-permute-start(f32[3,8,256]{2,1,0:T(8,128)S(1)} %select_maximum_fusion), channel_id=1, source_target_pairs={{0,128},{32,160},{64,192},{96,224},{128,0},{160,32},{192,64},{224,... | collective-permute-start | bytes 73736 | tf_op jit(solution)/shard_map/ppermute | solution.py:269
  32.6 9.8 %collective-permute-start.10 = (f32[3,8,256]{2,1,0:T(8,128)S(1)}, f32[3,8,256]{2,1,0:T(8,128)S(1)}, u32[]{:S(2)}, u32[]{:S(2)}) collective-permute-start(f32[3,8,256]{2,1,0:T(8,128)S(1)} %select_maximum_fusion), channel_id=1, source_target_pairs={{0,160},{32,128},{64,224},{96,192},{128,32},{160,0},{192,96},{224,... | collective-permute-start | bytes 73736 | tf_op jit(solution)/shard_map/ppermute | solution.py:269
  32.7 9.7 %collective-permute-start.11 = (f32[3,8,256]{2,1,0:T(8,128)S(1)}, f32[3,8,256]{2,1,0:T(8,128)S(1)}, u32[]{:S(2)}, u32[]{:S(2)}) collective-permute-start(f32[3,8,256]{2,1,0:T(8,128)S(1)} %select_maximum_fusion), channel_id=1, source_target_pairs={{0,192},{32,224},{64,128},{96,160},{128,64},{160,96},{192,0},{224,... | collective-permute-start | bytes 73736 | tf_op jit(solution)/shard_map/ppermute | solution.py:269
  35.7 6.9 %collective-permute-start.12 = (f32[3,8,256]{2,1,0:T(8,128)S(1)}, f32[3,8,256]{2,1,0:T(8,128)S(1)}, u32[]{:S(2)}, u32[]{:S(2)}) collective-permute-start(f32[3,8,256]{2,1,0:T(8,128)S(1)} %select_maximum_fusion), channel_id=1, source_target_pairs={{0,224},{32,192},{64,160},{96,128},{128,96},{160,64},{192,32},{224... | collective-permute-start | bytes 73736 | tf_op jit(solution)/shard_map/ppermute | solution.py:269
  42.4 11.2 %copy-start.6 = (f32[3,8,256]{2,1,0:T(8,128)}, f32[3,8,256]{2,1,0:T(8,128)S(1)}, u32[]{:S(2)}) copy-start(f32[3,8,256]{2,1,0:T(8,128)S(1)} %collective-permute-done.10) | copy-start | bytes 73732
  43.3 14.1 %collective-permute-start.13 = (f32[8]{0:T(128)S(1)}, f32[8]{0:T(128)S(1)}, u32[]{:S(2)}, u32[]{:S(2)}) collective-permute-start(f32[8]{0:T(128)S(1)} %fusion.13), channel_id=1, source_target_pairs={{0,1},{1,0},{2,3},{3,2},{4,5},{5,4},{6,7},{7,6},{8,9},{9,8},{10,11... | collective-permute-start | bytes 104 | tf_op jit(solution)/shard_map/ppermute | solution.py:269
  43.4 14.0 %collective-permute-start.14 = (f32[8]{0:T(128)S(1)}, f32[8]{0:T(128)S(1)}, u32[]{:S(2)}, u32[]{:S(2)}) collective-permute-start(f32[8]{0:T(128)S(1)} %fusion.13), channel_id=1, source_target_pairs={{0,2},{1,3},{2,0},{3,1},{4,6},{5,7},{6,4},{7,5},{8,10},{9,11},{10,... | collective-permute-start | bytes 104 | tf_op jit(solution)/shard_map/ppermute | solution.py:269
  43.5 13.9 %collective-permute-start.15 = (f32[8]{0:T(128)S(1)}, f32[8]{0:T(128)S(1)}, u32[]{:S(2)}, u32[]{:S(2)}) collective-permute-start(f32[8]{0:T(128)S(1)} %fusion.13), channel_id=1, source_target_pairs={{0,3},{1,2},{2,1},{3,0},{4,7},{5,6},{6,5},{7,4},{8,11},{9,10},{10,... | collective-permute-start | bytes 104 | tf_op jit(solution)/shard_map/ppermute | solution.py:269
  54.3 28.6 %collective-permute-start.4 = (f32[4,64,256]{2,1,0:T(8,128)S(1)}, f32[4,64,256]{2,1,0:T(8,128)S(1)}, u32[]{:S(2)}, u32[]{:S(2)}) collective-permute-start(f32[4,64,256]{2,1,0:T(8,128)S(1)} %get-tuple-element.53), channel_id=1, source_target_pairs={{0,1},{1,2},{2,3},{3,4},{4,5},{5,6},{6,7},{7,8},{8,9},{9,10},{10,1... | collective-permute-start | bytes 786440 | tf_op jit(solution)/shard_map/ppermute | solution.py:23
  57.4 11.8 %collective-permute-start.16 = (f32[8]{0:T(128)S(1)}, f32[8]{0:T(128)S(1)}, u32[]{:S(2)}, u32[]{:S(2)}) collective-permute-start(f32[8]{0:T(128)S(1)} %add_add_fusion.1), channel_id=1, source_target_pairs={{0,4},{1,5},{2,6},{3,7},{4,0},{5,1},{6,2},{7,3},{8,12},{9,13},{10,... | collective-permute-start | bytes 104 | tf_op jit(solution)/shard_map/ppermute | solution.py:269
  57.5 23.0 %collective-permute-start.17 = (f32[8]{0:T(128)S(1)}, f32[8]{0:T(128)S(1)}, u32[]{:S(2)}, u32[]{:S(2)}) collective-permute-start(f32[8]{0:T(128)S(1)} %add_add_fusion.1), channel_id=1, source_target_pairs={{0,8},{1,9},{2,10},{3,11},{4,12},{5,13},{6,14},{7,15},{8,0},{9,1},... | collective-permute-start | bytes 104 | tf_op jit(solution)/shard_map/ppermute | solution.py:269
  61.3 21.7 %collective-permute-start.18 = (f32[8]{0:T(128)S(1)}, f32[8]{0:T(128)S(1)}, u32[]{:S(2)}, u32[]{:S(2)}) collective-permute-start(f32[8]{0:T(128)S(1)} %add_add_fusion.1), channel_id=1, source_target_pairs={{0,12},{1,13},{2,14},{3,15},{4,8},{5,9},{6,10},{7,11},{8,4},{9,5},... | collective-permute-start | bytes 104 | tf_op jit(solution)/shard_map/ppermute | solution.py:269
  64.2 40.0 %copy-start.13 = (s32[8]{0:T(128)S(1)}, s32[8]{0:T(128)}, u32[]{:S(2)}) copy-start(s32[8]{0:T(128)} %param.20) | copy-start | bytes 100
  64.2 42.6 %copy-start.11 = (s32[8,256]{1,0:T(8,128)S(1)}, s32[8,256]{1,0:T(8,128)}, u32[]{:S(2)}) copy-start(s32[8,256]{1,0:T(8,128)} %param.19) | copy-start | bytes 24580
  66.5 45.6 %copy-start.2 = (f32[3,8,64,256]{3,2,1,0:T(8,128)S(1)}, f32[3,8,64,256]{3,2,1,0:T(8,128)}, u32[]{:S(2)}) copy-start(f32[3,8,64,256]{3,2,1,0:T(8,128)} %get-tuple-element.32.star_in) | copy-start | bytes 4718596
  67.3 44.8 %collective-permute-start.2 = (f32[10,64,256]{2,1,0:T(8,128)}, f32[10,64,256]{2,1,0:T(8,128)}, u32[]{:S(2)}, u32[]{:S(2)}) collective-permute-start(f32[10,64,256]{2,1,0:T(8,128)} %get-tuple-element.33), channel_id=1, source_target_pairs={{0,1},{1,2},{2,3},{3,4},{4,5},{5,6},{6,7},{7,8},{8,9},{9,10},{10,1... | collective-permute-start | bytes 1966088 | tf_op jit(solution)/shard_map/ppermute | solution.py:23
  69.2 42.8 %collective-permute-start.3 = (f32[10,64,256]{2,1,0:T(8,128)}, f32[10,64,256]{2,1,0:T(8,128)}, u32[]{:S(2)}, u32[]{:S(2)}) collective-permute-start(f32[10,64,256]{2,1,0:T(8,128)} %get-tuple-element.34), channel_id=1, source_target_pairs={{1,0},{2,1},{3,2},{4,3},{5,4},{6,5},{7,6},{8,7},{9,8},{10,9},{11,1... | collective-permute-start | bytes 1966088 | tf_op jit(solution)/shard_map/ppermute | solution.py:24
  80.5 31.5 %collective-permute-start.5 = (f32[4,64,256]{2,1,0:T(8,128)}, f32[4,64,256]{2,1,0:T(8,128)}, u32[]{:S(2)}, u32[]{:S(2)}) collective-permute-start(f32[4,64,256]{2,1,0:T(8,128)} %get-tuple-element.52), channel_id=1, source_target_pairs={{1,0},{2,1},{3,2},{4,3},{5,4},{6,5},{7,6},{8,7},{9,8},{10,9},{11,1... | collective-permute-start | bytes 786440 | tf_op jit(solution)/shard_map/ppermute | solution.py:24
  83.0 21.3 %collective-permute-start.19 = (f32[8]{0:T(128)S(1)}, f32[8]{0:T(128)S(1)}, u32[]{:S(2)}, u32[]{:S(2)}) collective-permute-start(f32[8]{0:T(128)S(1)} %add_add_fusion), channel_id=1, source_target_pairs={{0,16},{1,17},{2,18},{3,19},{4,20},{5,21},{6,22},{7,23},{8,24},{9,... | collective-permute-start | bytes 104 | tf_op jit(solution)/shard_map/ppermute | solution.py:269
  (11 other events, 50.8 us)

commit v9 on v8

--- a/solution.py
+++ b/solution.py
@@ -255,7 +255,7 @@
     rounds = [("zone", rows, 1, rows)]
     stride = 1
     while stride < bricks:
-        radix = 4 if stride * 4 <= bricks else bricks // stride
+        radix = min(8 if stride == 1 else 4, bricks // stride)
         rounds.append(("brick", bricks, stride, radix))
         stride *= radix
     state = {"totals": None, "arrived": None}
@@ -299,14 +299,11 @@
     wide_head, wide_tail, _ = lax.optimization_barrier((wide_head, wide_tail, (n_left, n_right)))
     w_left, w_right = neighbours(wide_head, wide_tail)
 
-    advance(None)
     vel_star, source, heat_new, solv_new = stage_one(
         velocity, pressure, enthalpy, solvent, porosity, solid_mask, n_left, n_right)
     advance(vel_star)
 
     s_left, s_right = neighbours(source[0:4], source[cx - 4:])
-    advance(s_left)
-    advance(s_left)
 
     velocity_new, final = stage_two(
         pressure, porosity, source, vel_star, w_left, w_right, s_left, s_right)

time: 125 us -> 129 us (1.032)
  starting transfers between devices: 49.6 us -> 61.3 us
  local copies, waits for them, and re-layouts: 12.1 us -> 8.23 us
  waiting for transfers between devices: 23.5 us -> 21.3 us
  Pallas kernels: 19.4 us -> 18 us
    ppermute x14 -> x17, waiting for transfers between devices: 23.5 us -> 6.33 us  [advance(): lax.ppermute(value, axis, [(i, i ^ k * stride) for i in range(size)])]
    ppermute x3, waiting for transfers between devices: 0.01 us -> 13.4 us  [neighbours(): from_left = lax.ppermute(tail, ALL, [(i, i + 1) for i in range(count - 1)])]
    ppermute x14 -> x17, starting transfers between devices: 21 us -> 29.2 us  [advance(): lax.ppermute(value, axis, [(i, i ^ k * stride) for i in range(size)])]
    ppermute x3, starting transfers between devices: 22.5 us -> 26.3 us  [neighbours(): from_right = lax.ppermute(head, ALL, [(i + 1, i) for i in range(count - 1)])]
    pallas_call x2, local copies, waits for them, and re-layouts: 2.2 us -> 0.62 us  [stage_one(): pl.pallas_call(stage_one_kernel, out_shape=outs, scratch_shapes=[pltpu.VM...]
    slice x1 -> x0, other arithmetic: 1.53 us -> none  [on_device_body(): totals = choose * jnp.sum(solvent[:, -1, :])]
    ppermute x3, waiting for transfers between devices: 0.01 us -> 1.54 us  [neighbours(): from_right = lax.ppermute(head, ALL, [(i + 1, i) for i in range(count - 1)])]
    reduce_sum x0 -> x1, other arithmetic: none -> 1.46 us  [on_device_body(): totals = choose * jnp.sum(solvent[:, -1, :])]
  transfers between devices with their start and end apart: 20 -> 23, of which waited for: 3 -> 6; matrix products, arithmetic and copies ran while one was open for 16% -> 9% of each run, Pallas kernels for 6% -> 14%
where the time goes in v9:
time: 129 us; the launch traced here: 127 us
  starting transfers between devices  61.3 us (48%)
  waiting for transfers between devices  21.3 us (17%)
  Pallas kernels  18 us (14%)
  other arithmetic  13 us (10%)
  local copies, waits for them, and re-layouts  8.23 us (6%)
  between operations  5.39 us (4%)
    ppermute x17, starting transfers between devices, advance(): lax.ppermute(value, axis, [(i, i ^ k * stride) for i in range(size)])  29.2 us
    ppermute x3, starting transfers between devices, neighbours(): from_right = lax.ppermute(head, ALL, [(i + 1, i) for i in range(count - 1)])  26.3 us
    ppermute x3, waiting for transfers between devices, neighbours(): from_left = lax.ppermute(tail, ALL, [(i, i + 1) for i in range(count - 1)])  13.4 us
    pallas_call x1, Pallas kernels, stage_two(): pl.pallas_call(stage_two_kernel, out_shape=outs, scratch_shapes=[pltpu.VM...  10.8 us
    pallas_call x1, Pallas kernels, stage_one(): pl.pallas_call(stage_one_kernel, out_shape=outs, scratch_shapes=[pltpu.VM...  7.21 us
    ppermute x17, waiting for transfers between devices, advance(): lax.ppermute(value, axis, [(i, i ^ k * stride) for i in range(size)])  6.33 us
    ppermute x3, starting transfers between devices, neighbours(): from_left = lax.ppermute(tail, ALL, [(i, i + 1) for i in range(count - 1)])  5.75 us
    unnamed x28, local copies, waits for them, and re-layouts  4.08 us
  transfers between devices with their start and end apart: 23, of which 6 were waited for; matrix products, arithmetic and copies ran while one was open for 9% of the time, Pallas kernels for 14%

profile of v9, /device:TPU:32, one launch (start us, length us, event | category | flops | bytes accessed | tf_op | source)
XLA Modules:
  0.0 127.2 jit_solution(10002976374876132061)
XLA Ops:
  1.5 1.5 %slice_reduce_fusion = (f32[]{:T(128)}, f32[8,1,256]{2,1,0:T(1,128)S(1)}) fusion(f32[8,64,256]{2,1,0:T(8,128)} %solvent.1), kind=kLoop, calls=%fused_computation.54 | loop fusion | flops 2047 | bytes 16388 | tf_op jit(solution)/shard_map/reduce_sum | solution.py:246
  7.0 1.8 %collective-permute-start.6 = (f32[3,8,256]{2,1,0:T(8,128)}, f32[3,8,256]{2,1,0:T(8,128)}, u32[]{:S(2)}, u32[]{:S(2)}) collective-permute-start(f32[3,8,256]{2,1,0:T(8,128)} %select_maximum_fusion), channel_id=1, source_target_pairs={{0,32},{32,0},{64,96},{96,64},{128,160},{160,128},{192,224},{224,1... | collective-permute-start | bytes 73736 | tf_op jit(solution)/shard_map/ppermute | solution.py:269
  8.8 1.7 %collective-permute-start.8 = (f32[3,8,256]{2,1,0:T(8,128)}, f32[3,8,256]{2,1,0:T(8,128)}, u32[]{:S(2)}, u32[]{:S(2)}) collective-permute-start(f32[3,8,256]{2,1,0:T(8,128)} %select_maximum_fusion), channel_id=1, source_target_pairs={{0,96},{32,64},{64,32},{96,0},{128,224},{160,192},{192,160},{224,1... | collective-permute-start | bytes 73736 | tf_op jit(solution)/shard_map/ppermute | solution.py:269
  15.4 1.9 %collective-permute-start = (f32[11,64,256]{2,1,0:T(8,128)}, f32[11,64,256]{2,1,0:T(8,128)S(1)}, u32[]{:S(2)}, u32[]{:S(2)}) collective-permute-start(f32[11,64,256]{2,1,0:T(8,128)} %get-tuple-element.79), channel_id=1, source_target_pairs={{0,1},{1,2},{2,3},{3,4},{4,5},{5,6},{6,7},{7,8},{8,9},{9,10},{10,1... | collective-permute-start | bytes 2162696 | tf_op jit(solution)/shard_map/ppermute | solution.py:23
  17.3 8.8 %collective-permute-start.1 = (f32[11,64,256]{2,1,0:T(8,128)}, f32[11,64,256]{2,1,0:T(8,128)S(1)}, u32[]{:S(2)}, u32[]{:S(2)}) collective-permute-start(f32[11,64,256]{2,1,0:T(8,128)} %get-tuple-element.78), channel_id=1, source_target_pairs={{1,0},{2,1},{3,2},{4,3},{5,4},{6,5},{7,6},{8,7},{9,8},{10,9},{11,1... | collective-permute-start | bytes 2162696 | tf_op jit(solution)/shard_map/ppermute | solution.py:24
  30.5 8.1 %collective-permute-done.left = f32[11,64,256]{2,1,0:T(8,128)S(1)} collective-permute-done((f32[11,64,256]{2,1,0:T(8,128)}, f32[11,64,256]{2,1,0:T(8,128)S(1)}, u32[]{:S(2)}, u32[]{:S(2)}) %collective-permute-start) | collective-permute-done | bytes 720928 | tf_op jit(solution)/shard_map/ppermute | solution.py:23
  38.6 3.0 %collective-permute-start.9 = (f32[3,8,256]{2,1,0:T(8,128)}, f32[3,8,256]{2,1,0:T(8,128)}, u32[]{:S(2)}, u32[]{:S(2)}) collective-permute-start(f32[3,8,256]{2,1,0:T(8,128)} %select_maximum_fusion), channel_id=1, source_target_pairs={{0,128},{32,160},{64,192},{96,224},{128,0},{160,32},{192,64},{224,... | collective-permute-start | bytes 73736 | tf_op jit(solution)/shard_map/ppermute | solution.py:269
  43.5 2.3 %collective-permute-start.10 = (f32[3,8,256]{2,1,0:T(8,128)}, f32[3,8,256]{2,1,0:T(8,128)S(1)}, u32[]{:S(2)}, u32[]{:S(2)}) collective-permute-start(f32[3,8,256]{2,1,0:T(8,128)} %select_maximum_fusion), channel_id=1, source_target_pairs={{0,160},{32,128},{64,224},{96,192},{128,32},{160,0},{192,96},{224,... | collective-permute-start | bytes 73736 | tf_op jit(solution)/shard_map/ppermute | solution.py:269
  46.9 7.2 %shard_map.138 = (f32[3,8,64,256]{3,2,1,0:T(8,128)}, f32[8,64,256]{2,1,0:T(8,128)S(1)}, f32[8,64,256]{2,1,0:T(8,128)S(1)}, f32[8,64,256]{2,1,0:T(8,128)S(1)}) custom-call(f32[3,8,64,256]{3,2,1,0:T(8,128)} %velocity.1, f32[8,64,256]{2,1,0:T(8,128)S(1)} %copy-done, f32[8,64,256]{2,1,0:T(8,128)S(1)} %copy-done.3, f32[8,64,256]{2,1,0:T(8,128)S(1)} %copy-done.4, ...), custom_call_target="tpu_custom_call" | custom-call | flops 34078720 | bytes 9961472 | tf_op jit(solution)/shard_map/pallas_call | solution.py:183
  54.1 3.6 %collective-permute-start.11 = (f32[3,8,256]{2,1,0:T(8,128)}, f32[3,8,256]{2,1,0:T(8,128)S(1)}, u32[]{:S(2)}, u32[]{:S(2)}) collective-permute-start(f32[3,8,256]{2,1,0:T(8,128)} %select_maximum_fusion), channel_id=1, source_target_pairs={{0,192},{32,224},{64,128},{96,160},{128,64},{160,96},{192,0},{224,... | collective-permute-start | bytes 73736 | tf_op jit(solution)/shard_map/ppermute | solution.py:269
  57.7 1.9 %collective-permute-start.2 = (f32[10,64,256]{2,1,0:T(8,128)S(1)}, f32[10,64,256]{2,1,0:T(8,128)S(1)}, u32[]{:S(2)}, u32[]{:S(2)}) collective-permute-start(f32[10,64,256]{2,1,0:T(8,128)S(1)} %copy-done.7), channel_id=1, source_target_pairs={{0,1},{1,2},{2,3},{3,4},{4,5},{5,6},{6,7},{7,8},{8,9},{9,10},{10,1... | collective-permute-start | bytes 1966088 | tf_op jit(solution)/shard_map/ppermute | solution.py:23
  59.6 8.8 %collective-permute-start.3 = (f32[10,64,256]{2,1,0:T(8,128)S(1)}, f32[10,64,256]{2,1,0:T(8,128)S(1)}, u32[]{:S(2)}, u32[]{:S(2)}) collective-permute-start(f32[10,64,256]{2,1,0:T(8,128)S(1)} %copy-done.6), channel_id=1, source_target_pairs={{1,0},{2,1},{3,2},{4,3},{5,4},{6,5},{7,6},{8,7},{9,8},{10,9},{11,1... | collective-permute-start | bytes 1966088 | tf_op jit(solution)/shard_map/ppermute | solution.py:24
  68.5 1.9 %collective-permute-start.4 = (f32[4,64,256]{2,1,0:T(8,128)S(1)}, f32[4,64,256]{2,1,0:T(8,128)S(1)}, u32[]{:S(2)}, u32[]{:S(2)}) collective-permute-start(f32[4,64,256]{2,1,0:T(8,128)S(1)} %get-tuple-element.73), channel_id=1, source_target_pairs={{0,1},{1,2},{2,3},{3,4},{4,5},{5,6},{6,7},{7,8},{8,9},{9,10},{10,1... | collective-permute-start | bytes 786440 | tf_op jit(solution)/shard_map/ppermute | solution.py:23
  70.4 8.8 %collective-permute-start.5 = (f32[4,64,256]{2,1,0:T(8,128)S(1)}, f32[4,64,256]{2,1,0:T(8,128)S(1)}, u32[]{:S(2)}, u32[]{:S(2)}) collective-permute-start(f32[4,64,256]{2,1,0:T(8,128)S(1)} %get-tuple-element.72), channel_id=1, source_target_pairs={{1,0},{2,1},{3,2},{4,3},{5,4},{6,5},{7,6},{8,7},{9,8},{10,9},{11,1... | collective-permute-start | bytes 786440 | tf_op jit(solution)/shard_map/ppermute | solution.py:24
  79.2 1.4 %bitcast_add_fusion = f32[8]{0:T(128)S(1)} fusion(f32[3,8,256]{2,1,0:T(8,128)S(1)} %collective-permute-done.12, f32[3,8,256]{2,1,0:T(8,128)S(1)} %collective-permute-done.11, f32[3,8,256]{2,1,0:T(8,128)S(1)} %collective-permute-done.10, f32[3,8,256]{2,1,0:T(8,128)} %collective-permute-done.9, f32[3,8,256]{2,1,0:T(8,128)} %collective-permute-done.8, ...), kind=kLoop, calls=%fused_computation.40 | loop fusion | flops 72 | bytes 264 | tf_op jit(solution)/shard_map/add | solution.py:280
  82.2 5.3 %collective-permute-done.4.source_left = f32[4,64,256]{2,1,0:T(8,128)S(1)} collective-permute-done((f32[4,64,256]{2,1,0:T(8,128)S(1)}, f32[4,64,256]{2,1,0:T(8,128)S(1)}, u32[]{:S(2)}, u32[]{:S(2)}) %collective-permute-start.4) | collective-permute-done | bytes 262176 | tf_op jit(solution)/shard_map/ppermute | solution.py:23
  87.5 1.5 %collective-permute-done.5.source_right = f32[4,64,256]{2,1,0:T(8,128)S(1)} collective-permute-done((f32[4,64,256]{2,1,0:T(8,128)S(1)}, f32[4,64,256]{2,1,0:T(8,128)S(1)}, u32[]{:S(2)}, u32[]{:S(2)}) %collective-permute-start.5) | collective-permute-done | bytes 262176 | tf_op jit(solution)/shard_map/ppermute | solution.py:24
  89.0 3.4 %collective-permute-start.17 = (f32[8]{0:T(128)S(1)}, f32[8]{0:T(128)S(1)}, u32[]{:S(2)}, u32[]{:S(2)}) collective-permute-start(f32[8]{0:T(128)S(1)} %bitcast_add_fusion), channel_id=1, source_target_pairs={{0,5},{1,4},{2,7},{3,6},{4,1},{5,0},{6,3},{7,2},{8,13},{9,12},{10,... | collective-permute-start | bytes 104 | tf_op jit(solution)/shard_map/ppermute | solution.py:269
  92.5 10.8 %shard_map.139 = (f32[3,8,64,256]{3,2,1,0:T(8,128)}, f32[8,64,256]{2,1,0:T(8,128)}) custom-call(f32[8,64,256]{2,1,0:T(8,128)S(1)} %copy-done, f32[8,64,256]{2,1,0:T(8,128)S(1)} %copy-done.1, f32[8,64,256]{2,1,0:T(8,128)S(1)} %get-tuple-element.41.source, f32[3,8,64,256]{3,2,1,0:T(8,128)S(1)} %copy-done.2, ...), custom_call_target="tpu_custom_call" | custom-call | flops 26214400 | bytes 6291456 | tf_op jit(solution)/shard_map/pallas_call | solution.py:210
  104.3 1.7 %collective-permute-start.19 = (f32[8]{0:T(128)S(1)}, f32[8]{0:T(128)S(1)}, u32[]{:S(2)}, u32[]{:S(2)}) collective-permute-start(f32[8]{0:T(128)S(1)} %bitcast_add_fusion), channel_id=1, source_target_pairs={{0,7},{1,6},{2,5},{3,4},{4,3},{5,2},{6,1},{7,0},{8,15},{9,14},{10,... | collective-permute-start | bytes 104 | tf_op jit(solution)/shard_map/ppermute | solution.py:269
  106.0 2.0 %collective-permute-done.18 = f32[8]{0:T(128)S(1)} collective-permute-done((f32[8]{0:T(128)S(1)}, f32[8]{0:T(128)S(1)}, u32[]{:S(2)}, u32[]{:S(2)}) %collective-permute-start.18) | collective-permute-done | bytes 64 | tf_op jit(solution)/shard_map/ppermute | solution.py:269
  108.5 6.8 %collective-permute-start.20 = (f32[8]{0:T(128)S(1)}, f32[8]{0:T(128)S(1)}, u32[]{:S(2)}, u32[]{:S(2)}) collective-permute-start(f32[8]{0:T(128)S(1)} %add_add_fusion.1), channel_id=1, source_target_pairs={{0,8},{1,9},{2,10},{3,11},{4,12},{5,13},{6,14},{7,15},{8,0},{9,1},... | collective-permute-start | bytes 104 | tf_op jit(solution)/shard_map/ppermute | solution.py:269
  115.4 3.7 %collective-permute-start.22 = (f32[8]{0:T(128)S(1)}, f32[8]{0:T(128)S(1)}, u32[]{:S(2)}, u32[]{:S(2)}) collective-permute-start(f32[8]{0:T(128)S(1)} %add_add_fusion.1), channel_id=1, source_target_pairs={{0,24},{1,25},{2,26},{3,27},{4,28},{5,29},{6,30},{7,31},{8,16},{9,... | collective-permute-start | bytes 104 | tf_op jit(solution)/shard_map/ppermute | solution.py:269
  119.1 3.8 %collective-permute-done.21 = f32[8]{0:T(128)S(1)} collective-permute-done((f32[8]{0:T(128)S(1)}, f32[8]{0:T(128)S(1)}, u32[]{:S(2)}, u32[]{:S(2)}) %collective-permute-start.21) | collective-permute-done | bytes 64 | tf_op jit(solution)/shard_map/ppermute | solution.py:269
  (82 shorter events, 20.1 us)
Async XLA Ops:
  7.0 47.1 %collective-permute-start.6 = (f32[3,8,256]{2,1,0:T(8,128)}, f32[3,8,256]{2,1,0:T(8,128)}, u32[]{:S(2)}, u32[]{:S(2)}) collective-permute-start(f32[3,8,256]{2,1,0:T(8,128)} %select_maximum_fusion), channel_id=1, source_target_pairs={{0,32},{32,0},{64,96},{96,64},{128,160},{160,128},{192,224},{224,1... | collective-permute-start | bytes 73736 | tf_op jit(solution)/shard_map/ppermute | solution.py:269
  8.8 48.8 %collective-permute-start.7 = (f32[3,8,256]{2,1,0:T(8,128)}, f32[3,8,256]{2,1,0:T(8,128)}, u32[]{:S(2)}, u32[]{:S(2)}) collective-permute-start(f32[3,8,256]{2,1,0:T(8,128)} %select_maximum_fusion), channel_id=1, source_target_pairs={{0,64},{32,96},{64,0},{96,32},{128,192},{160,224},{192,128},{224,1... | collective-permute-start | bytes 73736 | tf_op jit(solution)/shard_map/ppermute | solution.py:269
  8.8 48.9 %collective-permute-start.8 = (f32[3,8,256]{2,1,0:T(8,128)}, f32[3,8,256]{2,1,0:T(8,128)}, u32[]{:S(2)}, u32[]{:S(2)}) collective-permute-start(f32[3,8,256]{2,1,0:T(8,128)} %select_maximum_fusion), channel_id=1, source_target_pairs={{0,96},{32,64},{64,32},{96,0},{128,224},{160,192},{192,160},{224,1... | collective-permute-start | bytes 73736 | tf_op jit(solution)/shard_map/ppermute | solution.py:269
  15.4 23.3 %collective-permute-start = (f32[11,64,256]{2,1,0:T(8,128)}, f32[11,64,256]{2,1,0:T(8,128)S(1)}, u32[]{:S(2)}, u32[]{:S(2)}) collective-permute-start(f32[11,64,256]{2,1,0:T(8,128)} %get-tuple-element.79), channel_id=1, source_target_pairs={{0,1},{1,2},{2,3},{3,4},{4,5},{5,6},{6,7},{7,8},{8,9},{9,10},{10,1... | collective-permute-start | bytes 2162696 | tf_op jit(solution)/shard_map/ppermute | solution.py:23
  17.3 26.2 %collective-permute-start.1 = (f32[11,64,256]{2,1,0:T(8,128)}, f32[11,64,256]{2,1,0:T(8,128)S(1)}, u32[]{:S(2)}, u32[]{:S(2)}) collective-permute-start(f32[11,64,256]{2,1,0:T(8,128)} %get-tuple-element.78), channel_id=1, source_target_pairs={{1,0},{2,1},{3,2},{4,3},{5,4},{6,5},{7,6},{8,7},{9,8},{10,9},{11,1... | collective-permute-start | bytes 2162696 | tf_op jit(solution)/shard_map/ppermute | solution.py:24
  38.6 21.0 %collective-permute-start.9 = (f32[3,8,256]{2,1,0:T(8,128)}, f32[3,8,256]{2,1,0:T(8,128)}, u32[]{:S(2)}, u32[]{:S(2)}) collective-permute-start(f32[3,8,256]{2,1,0:T(8,128)} %select_maximum_fusion), channel_id=1, source_target_pairs={{0,128},{32,160},{64,192},{96,224},{128,0},{160,32},{192,64},{224,... | collective-permute-start | bytes 73736 | tf_op jit(solution)/shard_map/ppermute | solution.py:269
  43.5 24.9 %collective-permute-start.10 = (f32[3,8,256]{2,1,0:T(8,128)}, f32[3,8,256]{2,1,0:T(8,128)S(1)}, u32[]{:S(2)}, u32[]{:S(2)}) collective-permute-start(f32[3,8,256]{2,1,0:T(8,128)} %select_maximum_fusion), channel_id=1, source_target_pairs={{0,160},{32,128},{64,224},{96,192},{128,32},{160,0},{192,96},{224,... | collective-permute-start | bytes 73736 | tf_op jit(solution)/shard_map/ppermute | solution.py:269
  54.1 16.3 %collective-permute-start.11 = (f32[3,8,256]{2,1,0:T(8,128)}, f32[3,8,256]{2,1,0:T(8,128)S(1)}, u32[]{:S(2)}, u32[]{:S(2)}) collective-permute-start(f32[3,8,256]{2,1,0:T(8,128)} %select_maximum_fusion), channel_id=1, source_target_pairs={{0,192},{32,224},{64,128},{96,160},{128,64},{160,96},{192,0},{224,... | collective-permute-start | bytes 73736 | tf_op jit(solution)/shard_map/ppermute | solution.py:269
  57.7 21.5 %collective-permute-start.12 = (f32[3,8,256]{2,1,0:T(8,128)}, f32[3,8,256]{2,1,0:T(8,128)S(1)}, u32[]{:S(2)}, u32[]{:S(2)}) collective-permute-start(f32[3,8,256]{2,1,0:T(8,128)} %select_maximum_fusion), channel_id=1, source_target_pairs={{0,224},{32,192},{64,160},{96,128},{128,96},{160,64},{192,32},{224... | collective-permute-start | bytes 73736 | tf_op jit(solution)/shard_map/ppermute | solution.py:269
  57.7 31.3 %collective-permute-start.2 = (f32[10,64,256]{2,1,0:T(8,128)S(1)}, f32[10,64,256]{2,1,0:T(8,128)S(1)}, u32[]{:S(2)}, u32[]{:S(2)}) collective-permute-start(f32[10,64,256]{2,1,0:T(8,128)S(1)} %copy-done.7), channel_id=1, source_target_pairs={{0,1},{1,2},{2,3},{3,4},{4,5},{5,6},{6,7},{7,8},{8,9},{9,10},{10,1... | collective-permute-start | bytes 1966088 | tf_op jit(solution)/shard_map/ppermute | solution.py:23
  59.6 29.4 %collective-permute-start.3 = (f32[10,64,256]{2,1,0:T(8,128)S(1)}, f32[10,64,256]{2,1,0:T(8,128)S(1)}, u32[]{:S(2)}, u32[]{:S(2)}) collective-permute-start(f32[10,64,256]{2,1,0:T(8,128)S(1)} %copy-done.6), channel_id=1, source_target_pairs={{1,0},{2,1},{3,2},{4,3},{5,4},{6,5},{7,6},{8,7},{9,8},{10,9},{11,1... | collective-permute-start | bytes 1966088 | tf_op jit(solution)/shard_map/ppermute | solution.py:24
  68.5 19.0 %collective-permute-start.4 = (f32[4,64,256]{2,1,0:T(8,128)S(1)}, f32[4,64,256]{2,1,0:T(8,128)S(1)}, u32[]{:S(2)}, u32[]{:S(2)}) collective-permute-start(f32[4,64,256]{2,1,0:T(8,128)S(1)} %get-tuple-element.73), channel_id=1, source_target_pairs={{0,1},{1,2},{2,3},{3,4},{4,5},{5,6},{6,7},{7,8},{8,9},{9,10},{10,1... | collective-permute-start | bytes 786440 | tf_op jit(solution)/shard_map/ppermute | solution.py:23
  70.4 18.6 %collective-permute-start.5 = (f32[4,64,256]{2,1,0:T(8,128)S(1)}, f32[4,64,256]{2,1,0:T(8,128)S(1)}, u32[]{:S(2)}, u32[]{:S(2)}) collective-permute-start(f32[4,64,256]{2,1,0:T(8,128)S(1)} %get-tuple-element.72), channel_id=1, source_target_pairs={{1,0},{2,1},{3,2},{4,3},{5,4},{6,5},{7,6},{8,7},{9,8},{10,9},{11,1... | collective-permute-start | bytes 786440 | tf_op jit(solution)/shard_map/ppermute | solution.py:24
  81.3 22.0 %collective-permute-start.13 = (f32[8]{0:T(128)S(1)}, f32[8]{0:T(128)S(1)}, u32[]{:S(2)}, u32[]{:S(2)}) collective-permute-start(f32[8]{0:T(128)S(1)} %bitcast_add_fusion), channel_id=1, source_target_pairs={{0,1},{1,0},{2,3},{3,2},{4,5},{5,4},{6,7},{7,6},{8,9},{9,8},{10,11... | collective-permute-start | bytes 104 | tf_op jit(solution)/shard_map/ppermute | solution.py:269
  82.2 43.2 %copy-start.8 = (s32[8,256]{1,0:T(8,128)S(1)}, s32[8,256]{1,0:T(8,128)}, u32[]{:S(2)}) copy-start(s32[8,256]{1,0:T(8,128)} %param.19) | copy-start | bytes 24580
  87.5 16.9 %collective-permute-start.14 = (f32[8]{0:T(128)S(1)}, f32[8]{0:T(128)S(1)}, u32[]{:S(2)}, u32[]{:S(2)}) collective-permute-start(f32[8]{0:T(128)S(1)} %bitcast_add_fusion), channel_id=1, source_target_pairs={{0,2},{1,3},{2,0},{3,1},{4,6},{5,7},{6,4},{7,5},{8,10},{9,11},{10,... | collective-permute-start | bytes 104 | tf_op jit(solution)/shard_map/ppermute | solution.py:269
  89.0 17.0 %collective-permute-start.15 = (f32[8]{0:T(128)S(1)}, f32[8]{0:T(128)S(1)}, u32[]{:S(2)}, u32[]{:S(2)}) collective-permute-start(f32[8]{0:T(128)S(1)} %bitcast_add_fusion), channel_id=1, source_target_pairs={{0,3},{1,2},{2,1},{3,0},{4,7},{5,6},{6,5},{7,4},{8,11},{9,10},{10,... | collective-permute-start | bytes 104 | tf_op jit(solution)/shard_map/ppermute | solution.py:269
  89.0 17.0 %collective-permute-start.16 = (f32[8]{0:T(128)S(1)}, f32[8]{0:T(128)S(1)}, u32[]{:S(2)}, u32[]{:S(2)}) collective-permute-start(f32[8]{0:T(128)S(1)} %bitcast_add_fusion), channel_id=1, source_target_pairs={{0,4},{1,5},{2,6},{3,7},{4,0},{5,1},{6,2},{7,3},{8,12},{9,13},{10,... | collective-permute-start | bytes 104 | tf_op jit(solution)/shard_map/ppermute | solution.py:269
  89.0 17.0 %collective-permute-start.17 = (f32[8]{0:T(128)S(1)}, f32[8]{0:T(128)S(1)}, u32[]{:S(2)}, u32[]{:S(2)}) collective-permute-start(f32[8]{0:T(128)S(1)} %bitcast_add_fusion), channel_id=1, source_target_pairs={{0,5},{1,4},{2,7},{3,6},{4,1},{5,0},{6,3},{7,2},{8,13},{9,12},{10,... | collective-permute-start | bytes 104 | tf_op jit(solution)/shard_map/ppermute | solution.py:269
  103.3 4.8 %collective-permute-start.18 = (f32[8]{0:T(128)S(1)}, f32[8]{0:T(128)S(1)}, u32[]{:S(2)}, u32[]{:S(2)}) collective-permute-start(f32[8]{0:T(128)S(1)} %bitcast_add_fusion), channel_id=1, source_target_pairs={{0,6},{1,7},{2,4},{3,5},{4,2},{5,3},{6,0},{7,1},{8,14},{9,15},{10,... | collective-permute-start | bytes 104 | tf_op jit(solution)/shard_map/ppermute | solution.py:269
  104.3 4.2 %collective-permute-start.19 = (f32[8]{0:T(128)S(1)}, f32[8]{0:T(128)S(1)}, u32[]{:S(2)}, u32[]{:S(2)}) collective-permute-start(f32[8]{0:T(128)S(1)} %bitcast_add_fusion), channel_id=1, source_target_pairs={{0,7},{1,6},{2,5},{3,4},{4,3},{5,2},{6,1},{7,0},{8,15},{9,14},{10,... | collective-permute-start | bytes 104 | tf_op jit(solution)/shard_map/ppermute | solution.py:269
  108.5 10.5 %collective-permute-start.20 = (f32[8]{0:T(128)S(1)}, f32[8]{0:T(128)S(1)}, u32[]{:S(2)}, u32[]{:S(2)}) collective-permute-start(f32[8]{0:T(128)S(1)} %add_add_fusion.1), channel_id=1, source_target_pairs={{0,8},{1,9},{2,10},{3,11},{4,12},{5,13},{6,14},{7,15},{8,0},{9,1},... | collective-permute-start | bytes 104 | tf_op jit(solution)/shard_map/ppermute | solution.py:269
  115.4 7.5 %collective-permute-start.21 = (f32[8]{0:T(128)S(1)}, f32[8]{0:T(128)S(1)}, u32[]{:S(2)}, u32[]{:S(2)}) collective-permute-start(f32[8]{0:T(128)S(1)} %add_add_fusion.1), channel_id=1, source_target_pairs={{0,16},{1,17},{2,18},{3,19},{4,20},{5,21},{6,22},{7,23},{8,24},{9,... | collective-permute-start | bytes 104 | tf_op jit(solution)/shard_map/ppermute | solution.py:269
  115.4 7.5 %collective-permute-start.22 = (f32[8]{0:T(128)S(1)}, f32[8]{0:T(128)S(1)}, u32[]{:S(2)}, u32[]{:S(2)}) collective-permute-start(f32[8]{0:T(128)S(1)} %add_add_fusion.1), channel_id=1, source_target_pairs={{0,24},{1,25},{2,26},{3,27},{4,28},{5,29},{6,30},{7,31},{8,16},{9,... | collective-permute-start | bytes 104 | tf_op jit(solution)/shard_map/ppermute | solution.py:269
  (11 other events, 152.3 us)

commit v10 on v9

--- a/solution.py
+++ b/solution.py
@@ -248,23 +248,27 @@
     rows = lax.axis_size("zone")
 
     planes = jnp.stack([enthalpy[:, -1, :], solvent[:, -1, :]])
-    message = jnp.concatenate(
-        [planes, jnp.zeros((1,) + planes.shape[1:], jnp.float32).at[0, 0, :nzones].set(totals)],
-        axis=0)
     bricks = count // rows
-    rounds = [("zone", rows, 1, rows)]
+    rounds = []
     stride = 1
     while stride < bricks:
         radix = min(8 if stride == 1 else 4, bricks // stride)
         rounds.append(("brick", bricks, stride, radix))
         stride *= radix
-    state = {"totals": None, "arrived": None}
+    rounds.append(("zone", rows, 1, rows))
+    state = {"totals": totals, "arrived": None}
 
     def advance(anchor):
         if not rounds:
             return
         axis, size, stride, radix = rounds.pop(0)
-        value = message if axis == "zone" else state["totals"]
+        if axis == "zone":
+            carried = jnp.zeros((1,) + planes.shape[1:], jnp.float32)
+            carried = carried.at[0, 0, :nzones].set(state["totals"])
+            message = jnp.concatenate([planes, carried], axis=0)
+            value = message
+        else:
+            value = state["totals"]
         sent = [
             lax.ppermute(value, axis, [(i, i ^ (k * stride)) for i in range(size)])
             for k in range(1, radix)
@@ -286,6 +290,10 @@
                 total = total + part
             state["totals"] = total
 
+    advance(None)
+    advance(None)
+    advance(None)
+
     plane = enthalpy.shape[1:]
     narrow_head = jnp.concatenate(
         [velocity[:, 0:2].reshape((6,) + plane), pressure[0:2],
@@ -301,7 +309,6 @@
 
     vel_star, source, heat_new, solv_new = stage_one(
         velocity, pressure, enthalpy, solvent, porosity, solid_mask, n_left, n_right)
-    advance(vel_star)
 
     s_left, s_right = neighbours(source[0:4], source[cx - 4:])
 

time: 129 us -> 118 us (0.915)
  starting transfers between devices: 61.3 us -> 53.7 us
  waiting for transfers between devices: 21.3 us -> 18.8 us
    ppermute x3, waiting for transfers between devices: 13.4 us -> 5.55 us  [neighbours(): from_left = lax.ppermute(tail, ALL, [(i, i + 1) for i in range(count - 1)])]
    ppermute x3, starting transfers between devices: 26.3 us -> 20.7 us  [neighbours(): from_right = lax.ppermute(head, ALL, [(i + 1, i) for i in range(count - 1)])]
    ppermute x3, waiting for transfers between devices: 1.54 us -> 5.67 us  [neighbours(): from_right = lax.ppermute(head, ALL, [(i + 1, i) for i in range(count - 1)])]
    ppermute x17, starting transfers between devices: 29.2 us -> 26.8 us  [advance(): lax.ppermute(value, axis, [(i, i ^ k * stride) for i in range(size)])]
    slice x0 -> x1, other arithmetic: none -> 1.61 us  [on_device_body(): totals = choose * jnp.sum(solvent[:, -1, :])]
    reduce_sum x1 -> x0, other arithmetic: 1.46 us -> none  [on_device_body(): totals = choose * jnp.sum(solvent[:, -1, :])]
    add x1 -> x0, other arithmetic: 1.35 us -> none  [advance(): total = total + part[2, 0, :nzones]]
    unnamed x28 -> x30, local copies, waits for them, and re-layouts: 4.08 us -> 4.57 us
  transfers between devices with their start and end apart: 23 -> 23, of which waited for: 6 -> 6; matrix products, arithmetic and copies ran while one was open for 9% -> 13% of each run, Pallas kernels for 14% -> 6%
where the time goes in v10:
time: 118 us; the launch traced here: 117 us
  starting transfers between devices  53.7 us (46%)
  waiting for transfers between devices  18.8 us (16%)
  Pallas kernels  17.9 us (15%)
  other arithmetic  12.5 us (11%)
  local copies, waits for them, and re-layouts  8.65 us (7%)
  between operations  5.55 us (5%)
    ppermute x17, starting transfers between devices, advance(): lax.ppermute(value, axis, [(i, i ^ k * stride) for i in range(size)])  26.8 us
    ppermute x3, starting transfers between devices, neighbours(): from_right = lax.ppermute(head, ALL, [(i + 1, i) for i in range(count - 1)])  20.7 us
    pallas_call x1, Pallas kernels, stage_two(): pl.pallas_call(stage_two_kernel, out_shape=outs, scratch_shapes=[pltpu.VM...  10.8 us
    ppermute x17, waiting for transfers between devices, advance(): lax.ppermute(value, axis, [(i, i ^ k * stride) for i in range(size)])  7.53 us
    pallas_call x1, Pallas kernels, stage_one(): pl.pallas_call(stage_one_kernel, out_shape=outs, scratch_shapes=[pltpu.VM...  7.1 us
    ppermute x3, starting transfers between devices, neighbours(): from_left = lax.ppermute(tail, ALL, [(i, i + 1) for i in range(count - 1)])  6.25 us
    ppermute x3, waiting for transfers between devices, neighbours(): from_right = lax.ppermute(head, ALL, [(i + 1, i) for i in range(count - 1)])  5.67 us
    ppermute x3, waiting for transfers between devices, neighbours(): from_left = lax.ppermute(tail, ALL, [(i, i + 1) for i in range(count - 1)])  5.55 us
  transfers between devices with their start and end apart: 23, of which 6 were waited for; matrix products, arithmetic and copies ran while one was open for 13% of the time, Pallas kernels for 6%

profile of v10, /device:TPU:32, one launch (start us, length us, event | category | flops | bytes accessed | tf_op | source)
XLA Modules:
  0.0 117.0 jit_solution(14870728932173665838)
XLA Ops:
  0.7 1.6 %fusion.22 = (f32[8,1,256]{2,1,0:T(1,128)S(1)}, f32[]{:T(128)}) fusion(f32[8,64,256]{2,1,0:T(8,128)} %solvent.1), kind=kLoop, calls=%fused_computation.63 | loop fusion | flops 2047 | bytes 16388 | tf_op jit(solution)/shard_map/slice | solution.py:246
  3.1 1.3 %fusion.12 = s32[]{:T(128)} fusion(s32[8]{0:T(128)} %param.20, s32[8,1]{0,1:T(1,128)S(1)} %reduce-window.9, s32[]{:T(128)S(6)} %add.75), kind=kLoop, calls=%fused_computation.38 | loop fusion | flops 31 | bytes 72 | tf_op jit(solution)/shard_map/reduce_sum | solution.py:243
  5.7 3.1 %collective-permute-start.11 = (f32[8]{0:T(128)S(1)}, f32[8]{0:T(128)S(1)}, u32[]{:S(2)}, u32[]{:S(2)}) collective-permute-start(f32[8]{0:T(128)S(1)} %fusion.20), channel_id=1, source_target_pairs={{0,6},{1,7},{2,4},{3,5},{4,2},{5,3},{6,0},{7,1},{8,14},{9,15},{10,... | collective-permute-start | bytes 104 | tf_op jit(solution)/shard_map/ppermute | solution.py:273
  8.8 2.7 %collective-permute-start.9 = (f32[8]{0:T(128)S(1)}, f32[8]{0:T(128)S(1)}, u32[]{:S(2)}, u32[]{:S(2)}) collective-permute-start(f32[8]{0:T(128)S(1)} %fusion.20), channel_id=1, source_target_pairs={{0,4},{1,5},{2,6},{3,7},{4,0},{5,1},{6,2},{7,3},{8,12},{9,13},{10,... | collective-permute-start | bytes 104 | tf_op jit(solution)/shard_map/ppermute | solution.py:273
  11.9 1.9 %collective-permute-start.7 = (f32[8]{0:T(128)S(1)}, f32[8]{0:T(128)S(1)}, u32[]{:S(2)}, u32[]{:S(2)}) collective-permute-start(f32[8]{0:T(128)S(1)} %fusion.20), channel_id=1, source_target_pairs={{0,2},{1,3},{2,0},{3,1},{4,6},{5,7},{6,4},{7,5},{8,10},{9,11},{10,... | collective-permute-start | bytes 104 | tf_op jit(solution)/shard_map/ppermute | solution.py:273
  19.6 1.2 pad_maximum_fusion
  21.1 9.8 %collective-permute-start.1 = (f32[11,64,256]{2,1,0:T(8,128)}, f32[11,64,256]{2,1,0:T(8,128)S(1)}, u32[]{:S(2)}, u32[]{:S(2)}) collective-permute-start(f32[11,64,256]{2,1,0:T(8,128)} %get-tuple-element.44), channel_id=1, source_target_pairs={{1,0},{2,1},{3,2},{4,3},{5,4},{6,5},{7,6},{8,7},{9,8},{10,9},{11,1... | collective-permute-start | bytes 2162696 | tf_op jit(solution)/shard_map/ppermute | solution.py:24
  31.0 1.9 %collective-permute-start = (f32[11,64,256]{2,1,0:T(8,128)}, f32[11,64,256]{2,1,0:T(8,128)S(1)}, u32[]{:S(2)}, u32[]{:S(2)}) collective-permute-start(f32[11,64,256]{2,1,0:T(8,128)} %get-tuple-element.45), channel_id=1, source_target_pairs={{0,1},{1,2},{2,3},{3,4},{4,5},{5,6},{6,7},{7,8},{8,9},{9,10},{10,1... | collective-permute-start | bytes 2162696 | tf_op jit(solution)/shard_map/ppermute | solution.py:23
  34.8 5.4 %collective-permute-start.13 = (f32[8]{0:T(128)S(1)}, f32[8]{0:T(128)S(1)}, u32[]{:S(2)}, u32[]{:S(2)}) collective-permute-start(f32[8]{0:T(128)S(1)} %add_add_fusion.1), channel_id=1, source_target_pairs={{0,8},{1,9},{2,10},{3,11},{4,12},{5,13},{6,14},{7,15},{8,0},{9,1},... | collective-permute-start | bytes 104 | tf_op jit(solution)/shard_map/ppermute | solution.py:273
  40.2 5.7 %collective-permute-done.15 = f32[8]{0:T(128)S(1)} collective-permute-done((f32[8]{0:T(128)S(1)}, f32[8]{0:T(128)S(1)}, u32[]{:S(2)}, u32[]{:S(2)}) %collective-permute-start.15) | collective-permute-done | bytes 64 | tf_op jit(solution)/shard_map/ppermute | solution.py:273
  48.0 3.6 %collective-permute-start.22 = (f32[3,8,256]{2,1,0:T(8,128)}, f32[3,8,256]{2,1,0:T(8,128)}, u32[]{:S(2)}, u32[]{:S(2)}) collective-permute-start(f32[3,8,256]{2,1,0:T(8,128)} %select_maximum_fusion), channel_id=1, source_target_pairs={{0,224},{32,192},{64,160},{96,128},{128,96},{160,64},{192,32},{224... | collective-permute-start | bytes 73736 | tf_op jit(solution)/shard_map/ppermute | solution.py:273
  52.2 2.9 %collective-permute-start.20 = (f32[3,8,256]{2,1,0:T(8,128)}, f32[3,8,256]{2,1,0:T(8,128)}, u32[]{:S(2)}, u32[]{:S(2)}) collective-permute-start(f32[3,8,256]{2,1,0:T(8,128)} %select_maximum_fusion), channel_id=1, source_target_pairs={{0,160},{32,128},{64,224},{96,192},{128,32},{160,0},{192,96},{224,... | collective-permute-start | bytes 73736 | tf_op jit(solution)/shard_map/ppermute | solution.py:273
  55.1 1.7 %collective-permute-start.19 = (f32[3,8,256]{2,1,0:T(8,128)}, f32[3,8,256]{2,1,0:T(8,128)}, u32[]{:S(2)}, u32[]{:S(2)}) collective-permute-start(f32[3,8,256]{2,1,0:T(8,128)} %select_maximum_fusion), channel_id=1, source_target_pairs={{0,128},{32,160},{64,192},{96,224},{128,0},{160,32},{192,64},{224,... | collective-permute-start | bytes 73736 | tf_op jit(solution)/shard_map/ppermute | solution.py:273
  58.7 2.0 %collective-permute-start.18 = (f32[3,8,256]{2,1,0:T(8,128)}, f32[3,8,256]{2,1,0:T(8,128)}, u32[]{:S(2)}, u32[]{:S(2)}) collective-permute-start(f32[3,8,256]{2,1,0:T(8,128)} %select_maximum_fusion), channel_id=1, source_target_pairs={{0,96},{32,64},{64,32},{96,0},{128,224},{160,192},{192,160},{224,1... | collective-permute-start | bytes 73736 | tf_op jit(solution)/shard_map/ppermute | solution.py:273
  60.7 1.6 %collective-permute-start.16 = (f32[3,8,256]{2,1,0:T(8,128)}, f32[3,8,256]{2,1,0:T(8,128)}, u32[]{:S(2)}, u32[]{:S(2)}) collective-permute-start(f32[3,8,256]{2,1,0:T(8,128)} %select_maximum_fusion), channel_id=1, source_target_pairs={{0,32},{32,0},{64,96},{96,64},{128,160},{160,128},{192,224},{224,1... | collective-permute-start | bytes 73736 | tf_op jit(solution)/shard_map/ppermute | solution.py:273
  64.9 1.4 %select_reduce_fusion.1 = f32[]{:T(128)} fusion(s32[8]{0:T(128)} %param.20, f32[3,8,256]{2,1,0:T(8,128)} %collective-permute-done.22, f32[3,8,256]{2,1,0:T(8,128)} %collective-permute-done.21, f32[3,8,256]{2,1,0:T(8,128)} %collective-permute-done.20, f32[3,8,256]{2,1,0:T(8,128)} %collective-permute-done.19, f32[3,8,256]{2,1,0:T(8,128)} %collective-permute-done.18, ...), kind=kLoop, calls=%fused_computation.55 | loop fusion | flops 127 | bytes 296 | tf_op jit(solution)/shard_map/reduce_sum | solution.py:325
  69.1 1.9 %collective-permute-start.2 = (f32[10,64,256]{2,1,0:T(8,128)}, f32[10,64,256]{2,1,0:T(8,128)S(1)}, u32[]{:S(2)}, u32[]{:S(2)}) collective-permute-start(f32[10,64,256]{2,1,0:T(8,128)} %get-tuple-element.26), channel_id=1, source_target_pairs={{0,1},{1,2},{2,3},{3,4},{4,5},{5,6},{6,7},{7,8},{8,9},{9,10},{10,1... | collective-permute-start | bytes 1966088 | tf_op jit(solution)/shard_map/ppermute | solution.py:23
  71.0 8.9 %collective-permute-start.3 = (f32[10,64,256]{2,1,0:T(8,128)}, f32[10,64,256]{2,1,0:T(8,128)S(1)}, u32[]{:S(2)}, u32[]{:S(2)}) collective-permute-start(f32[10,64,256]{2,1,0:T(8,128)} %get-tuple-element.27), channel_id=1, source_target_pairs={{1,0},{2,1},{3,2},{4,3},{5,4},{6,5},{7,6},{8,7},{9,8},{10,9},{11,1... | collective-permute-start | bytes 1966088 | tf_op jit(solution)/shard_map/ppermute | solution.py:24
  81.0 7.1 %shard_map.138 = (f32[3,8,64,256]{3,2,1,0:T(8,128)}, f32[8,64,256]{2,1,0:T(8,128)S(1)}, f32[8,64,256]{2,1,0:T(8,128)S(1)}, f32[8,64,256]{2,1,0:T(8,128)S(1)}) custom-call(f32[3,8,64,256]{3,2,1,0:T(8,128)} %velocity.1, f32[8,64,256]{2,1,0:T(8,128)S(1)} %copy-done, f32[8,64,256]{2,1,0:T(8,128)S(1)} %copy-done.3, f32[8,64,256]{2,1,0:T(8,128)S(1)} %copy-done.4, ...), custom_call_target="tpu_custom_call" | custom-call | flops 34078720 | bytes 9961472 | tf_op jit(solution)/shard_map/pallas_call | solution.py:183
  88.8 1.9 %collective-permute-start.5 = (f32[4,64,256]{2,1,0:T(8,128)S(1)}, f32[4,64,256]{2,1,0:T(8,128)S(1)}, u32[]{:S(2)}, u32[]{:S(2)}) collective-permute-start(f32[4,64,256]{2,1,0:T(8,128)S(1)} %get-tuple-element.38), channel_id=1, source_target_pairs={{1,0},{2,1},{3,2},{4,3},{5,4},{6,5},{7,6},{8,7},{9,8},{10,9},{11,1... | collective-permute-start | bytes 786440 | tf_op jit(solution)/shard_map/ppermute | solution.py:24
  90.7 2.4 %collective-permute-start.4 = (f32[4,64,256]{2,1,0:T(8,128)S(1)}, f32[4,64,256]{2,1,0:T(8,128)S(1)}, u32[]{:S(2)}, u32[]{:S(2)}) collective-permute-start(f32[4,64,256]{2,1,0:T(8,128)S(1)} %get-tuple-element.39), channel_id=1, source_target_pairs={{0,1},{1,2},{2,3},{3,4},{4,5},{5,6},{6,7},{7,8},{8,9},{9,10},{10,1... | collective-permute-start | bytes 786440 | tf_op jit(solution)/shard_map/ppermute | solution.py:23
  95.0 5.7 %collective-permute-done.5.source_right = f32[4,64,256]{2,1,0:T(8,128)S(1)} collective-permute-done((f32[4,64,256]{2,1,0:T(8,128)S(1)}, f32[4,64,256]{2,1,0:T(8,128)S(1)}, u32[]{:S(2)}, u32[]{:S(2)}) %collective-permute-start.5) | collective-permute-done | bytes 262176 | tf_op jit(solution)/shard_map/ppermute | solution.py:24
  100.7 5.5 %collective-permute-done.4.source_left = f32[4,64,256]{2,1,0:T(8,128)S(1)} collective-permute-done((f32[4,64,256]{2,1,0:T(8,128)S(1)}, f32[4,64,256]{2,1,0:T(8,128)S(1)}, u32[]{:S(2)}, u32[]{:S(2)}) %collective-permute-start.4) | collective-permute-done | bytes 262176 | tf_op jit(solution)/shard_map/ppermute | solution.py:23
  106.2 10.8 %shard_map.139 = (f32[3,8,64,256]{3,2,1,0:T(8,128)}, f32[8,64,256]{2,1,0:T(8,128)}) custom-call(f32[8,64,256]{2,1,0:T(8,128)S(1)} %copy-done, f32[8,64,256]{2,1,0:T(8,128)S(1)} %copy-done.1, f32[8,64,256]{2,1,0:T(8,128)S(1)} %get-tuple-element.24.source, f32[3,8,64,256]{3,2,1,0:T(8,128)S(1)} %copy-done.2, ...), custom_call_target="tpu_custom_call" | custom-call | flops 26214400 | bytes 6291456 | tf_op jit(solution)/shard_map/pallas_call | solution.py:210
  (83 shorter events, 19.5 us)
Async XLA Ops:
  5.7 15.1 %collective-permute-start.11 = (f32[8]{0:T(128)S(1)}, f32[8]{0:T(128)S(1)}, u32[]{:S(2)}, u32[]{:S(2)}) collective-permute-start(f32[8]{0:T(128)S(1)} %fusion.20), channel_id=1, source_target_pairs={{0,6},{1,7},{2,4},{3,5},{4,2},{5,3},{6,0},{7,1},{8,14},{9,15},{10,... | collective-permute-start | bytes 104 | tf_op jit(solution)/shard_map/ppermute | solution.py:273
  8.8 12.0 %collective-permute-start.10 = (f32[8]{0:T(128)S(1)}, f32[8]{0:T(128)S(1)}, u32[]{:S(2)}, u32[]{:S(2)}) collective-permute-start(f32[8]{0:T(128)S(1)} %fusion.20), channel_id=1, source_target_pairs={{0,5},{1,4},{2,7},{3,6},{4,1},{5,0},{6,3},{7,2},{8,13},{9,12},{10,... | collective-permute-start | bytes 104 | tf_op jit(solution)/shard_map/ppermute | solution.py:273
  8.8 12.3 %collective-permute-start.9 = (f32[8]{0:T(128)S(1)}, f32[8]{0:T(128)S(1)}, u32[]{:S(2)}, u32[]{:S(2)}) collective-permute-start(f32[8]{0:T(128)S(1)} %fusion.20), channel_id=1, source_target_pairs={{0,4},{1,5},{2,6},{3,7},{4,0},{5,1},{6,2},{7,3},{8,12},{9,13},{10,... | collective-permute-start | bytes 104 | tf_op jit(solution)/shard_map/ppermute | solution.py:273
  11.5 19.5 %collective-permute-start.8 = (f32[8]{0:T(128)S(1)}, f32[8]{0:T(128)S(1)}, u32[]{:S(2)}, u32[]{:S(2)}) collective-permute-start(f32[8]{0:T(128)S(1)} %fusion.20), channel_id=1, source_target_pairs={{0,3},{1,2},{2,1},{3,0},{4,7},{5,6},{6,5},{7,4},{8,11},{9,10},{10,... | collective-permute-start | bytes 104 | tf_op jit(solution)/shard_map/ppermute | solution.py:273
  11.9 21.0 %collective-permute-start.7 = (f32[8]{0:T(128)S(1)}, f32[8]{0:T(128)S(1)}, u32[]{:S(2)}, u32[]{:S(2)}) collective-permute-start(f32[8]{0:T(128)S(1)} %fusion.20), channel_id=1, source_target_pairs={{0,2},{1,3},{2,0},{3,1},{4,6},{5,7},{6,4},{7,5},{8,10},{9,11},{10,... | collective-permute-start | bytes 104 | tf_op jit(solution)/shard_map/ppermute | solution.py:273
  18.3 38.5 %copy-start.9 = (s32[1,2]{1,0:T(1,128)S(1)}, s32[1,2]{1,0:T(1,128)}, u32[]{:S(2)}) copy-start(s32[1,2]{1,0:T(1,128)} %param.23) | copy-start | bytes 28
  20.8 12.1 %collective-permute-start.12 = (f32[8]{0:T(128)S(1)}, f32[8]{0:T(128)S(1)}, u32[]{:S(2)}, u32[]{:S(2)}) collective-permute-start(f32[8]{0:T(128)S(1)} %fusion.20), channel_id=1, source_target_pairs={{0,7},{1,6},{2,5},{3,4},{4,3},{5,2},{6,1},{7,0},{8,15},{9,14},{10,... | collective-permute-start | bytes 104 | tf_op jit(solution)/shard_map/ppermute | solution.py:273
  20.8 12.1 %collective-permute-start.6 = (f32[8]{0:T(128)S(1)}, f32[8]{0:T(128)S(1)}, u32[]{:S(2)}, u32[]{:S(2)}) collective-permute-start(f32[8]{0:T(128)S(1)} %fusion.20), channel_id=1, source_target_pairs={{0,1},{1,0},{2,3},{3,2},{4,5},{5,4},{6,7},{7,6},{8,9},{9,8},{10,11... | collective-permute-start | bytes 104 | tf_op jit(solution)/shard_map/ppermute | solution.py:273
  21.1 47.9 %collective-permute-start.1 = (f32[11,64,256]{2,1,0:T(8,128)}, f32[11,64,256]{2,1,0:T(8,128)S(1)}, u32[]{:S(2)}, u32[]{:S(2)}) collective-permute-start(f32[11,64,256]{2,1,0:T(8,128)} %get-tuple-element.44), channel_id=1, source_target_pairs={{1,0},{2,1},{3,2},{4,3},{5,4},{6,5},{7,6},{8,7},{9,8},{10,9},{11,1... | collective-permute-start | bytes 2162696 | tf_op jit(solution)/shard_map/ppermute | solution.py:24
  31.0 38.1 %collective-permute-start = (f32[11,64,256]{2,1,0:T(8,128)}, f32[11,64,256]{2,1,0:T(8,128)S(1)}, u32[]{:S(2)}, u32[]{:S(2)}) collective-permute-start(f32[11,64,256]{2,1,0:T(8,128)} %get-tuple-element.45), channel_id=1, source_target_pairs={{0,1},{1,2},{2,3},{3,4},{4,5},{5,6},{6,7},{7,8},{8,9},{9,10},{10,1... | collective-permute-start | bytes 2162696 | tf_op jit(solution)/shard_map/ppermute | solution.py:23
  33.6 12.3 %collective-permute-start.15 = (f32[8]{0:T(128)S(1)}, f32[8]{0:T(128)S(1)}, u32[]{:S(2)}, u32[]{:S(2)}) collective-permute-start(f32[8]{0:T(128)S(1)} %add_add_fusion.1), channel_id=1, source_target_pairs={{0,24},{1,25},{2,26},{3,27},{4,28},{5,29},{6,30},{7,31},{8,16},{9,... | collective-permute-start | bytes 104 | tf_op jit(solution)/shard_map/ppermute | solution.py:273
  34.7 12.2 %collective-permute-start.14 = (f32[8]{0:T(128)S(1)}, f32[8]{0:T(128)S(1)}, u32[]{:S(2)}, u32[]{:S(2)}) collective-permute-start(f32[8]{0:T(128)S(1)} %add_add_fusion.1), channel_id=1, source_target_pairs={{0,16},{1,17},{2,18},{3,19},{4,20},{5,21},{6,22},{7,23},{8,24},{9,... | collective-permute-start | bytes 104 | tf_op jit(solution)/shard_map/ppermute | solution.py:273
  34.8 12.1 %collective-permute-start.13 = (f32[8]{0:T(128)S(1)}, f32[8]{0:T(128)S(1)}, u32[]{:S(2)}, u32[]{:S(2)}) collective-permute-start(f32[8]{0:T(128)S(1)} %add_add_fusion.1), channel_id=1, source_target_pairs={{0,8},{1,9},{2,10},{3,11},{4,12},{5,13},{6,14},{7,15},{8,0},{9,1},... | collective-permute-start | bytes 104 | tf_op jit(solution)/shard_map/ppermute | solution.py:273
  48.0 7.1 %collective-permute-start.22 = (f32[3,8,256]{2,1,0:T(8,128)}, f32[3,8,256]{2,1,0:T(8,128)}, u32[]{:S(2)}, u32[]{:S(2)}) collective-permute-start(f32[3,8,256]{2,1,0:T(8,128)} %select_maximum_fusion), channel_id=1, source_target_pairs={{0,224},{32,192},{64,160},{96,128},{128,96},{160,64},{192,32},{224... | collective-permute-start | bytes 73736 | tf_op jit(solution)/shard_map/ppermute | solution.py:273
  52.2 6.5 %collective-permute-start.21 = (f32[3,8,256]{2,1,0:T(8,128)}, f32[3,8,256]{2,1,0:T(8,128)}, u32[]{:S(2)}, u32[]{:S(2)}) collective-permute-start(f32[3,8,256]{2,1,0:T(8,128)} %select_maximum_fusion), channel_id=1, source_target_pairs={{0,192},{32,224},{64,128},{96,160},{128,64},{160,96},{192,0},{224,... | collective-permute-start | bytes 73736 | tf_op jit(solution)/shard_map/ppermute | solution.py:273
  52.2 8.5 %collective-permute-start.20 = (f32[3,8,256]{2,1,0:T(8,128)}, f32[3,8,256]{2,1,0:T(8,128)}, u32[]{:S(2)}, u32[]{:S(2)}) collective-permute-start(f32[3,8,256]{2,1,0:T(8,128)} %select_maximum_fusion), channel_id=1, source_target_pairs={{0,160},{32,128},{64,224},{96,192},{128,32},{160,0},{192,96},{224,... | collective-permute-start | bytes 73736 | tf_op jit(solution)/shard_map/ppermute | solution.py:273
  55.1 5.6 %collective-permute-start.19 = (f32[3,8,256]{2,1,0:T(8,128)}, f32[3,8,256]{2,1,0:T(8,128)}, u32[]{:S(2)}, u32[]{:S(2)}) collective-permute-start(f32[3,8,256]{2,1,0:T(8,128)} %select_maximum_fusion), channel_id=1, source_target_pairs={{0,128},{32,160},{64,192},{96,224},{128,0},{160,32},{192,64},{224,... | collective-permute-start | bytes 73736 | tf_op jit(solution)/shard_map/ppermute | solution.py:273
  58.7 5.4 %collective-permute-start.18 = (f32[3,8,256]{2,1,0:T(8,128)}, f32[3,8,256]{2,1,0:T(8,128)}, u32[]{:S(2)}, u32[]{:S(2)}) collective-permute-start(f32[3,8,256]{2,1,0:T(8,128)} %select_maximum_fusion), channel_id=1, source_target_pairs={{0,96},{32,64},{64,32},{96,0},{128,224},{160,192},{192,160},{224,1... | collective-permute-start | bytes 73736 | tf_op jit(solution)/shard_map/ppermute | solution.py:273
  60.7 4.1 %collective-permute-start.17 = (f32[3,8,256]{2,1,0:T(8,128)}, f32[3,8,256]{2,1,0:T(8,128)}, u32[]{:S(2)}, u32[]{:S(2)}) collective-permute-start(f32[3,8,256]{2,1,0:T(8,128)} %select_maximum_fusion), channel_id=1, source_target_pairs={{0,64},{32,96},{64,0},{96,32},{128,192},{160,224},{192,128},{224,1... | collective-permute-start | bytes 73736 | tf_op jit(solution)/shard_map/ppermute | solution.py:273
  60.7 4.2 %collective-permute-start.16 = (f32[3,8,256]{2,1,0:T(8,128)}, f32[3,8,256]{2,1,0:T(8,128)}, u32[]{:S(2)}, u32[]{:S(2)}) collective-permute-start(f32[3,8,256]{2,1,0:T(8,128)} %select_maximum_fusion), channel_id=1, source_target_pairs={{0,32},{32,0},{64,96},{96,64},{128,160},{160,128},{192,224},{224,1... | collective-permute-start | bytes 73736 | tf_op jit(solution)/shard_map/ppermute | solution.py:273
  69.1 37.2 %collective-permute-start.2 = (f32[10,64,256]{2,1,0:T(8,128)}, f32[10,64,256]{2,1,0:T(8,128)S(1)}, u32[]{:S(2)}, u32[]{:S(2)}) collective-permute-start(f32[10,64,256]{2,1,0:T(8,128)} %get-tuple-element.26), channel_id=1, source_target_pairs={{0,1},{1,2},{2,3},{3,4},{4,5},{5,6},{6,7},{7,8},{8,9},{9,10},{10,1... | collective-permute-start | bytes 1966088 | tf_op jit(solution)/shard_map/ppermute | solution.py:23
  71.0 35.2 %collective-permute-start.3 = (f32[10,64,256]{2,1,0:T(8,128)}, f32[10,64,256]{2,1,0:T(8,128)S(1)}, u32[]{:S(2)}, u32[]{:S(2)}) collective-permute-start(f32[10,64,256]{2,1,0:T(8,128)} %get-tuple-element.27), channel_id=1, source_target_pairs={{1,0},{2,1},{3,2},{4,3},{5,4},{6,5},{7,6},{8,7},{9,8},{10,9},{11,1... | collective-permute-start | bytes 1966088 | tf_op jit(solution)/shard_map/ppermute | solution.py:24
  88.8 11.9 %collective-permute-start.5 = (f32[4,64,256]{2,1,0:T(8,128)S(1)}, f32[4,64,256]{2,1,0:T(8,128)S(1)}, u32[]{:S(2)}, u32[]{:S(2)}) collective-permute-start(f32[4,64,256]{2,1,0:T(8,128)S(1)} %get-tuple-element.38), channel_id=1, source_target_pairs={{1,0},{2,1},{3,2},{4,3},{5,4},{6,5},{7,6},{8,7},{9,8},{10,9},{11,1... | collective-permute-start | bytes 786440 | tf_op jit(solution)/shard_map/ppermute | solution.py:24
  90.7 15.5 %collective-permute-start.4 = (f32[4,64,256]{2,1,0:T(8,128)S(1)}, f32[4,64,256]{2,1,0:T(8,128)S(1)}, u32[]{:S(2)}, u32[]{:S(2)}) collective-permute-start(f32[4,64,256]{2,1,0:T(8,128)S(1)} %get-tuple-element.39), channel_id=1, source_target_pairs={{0,1},{1,2},{2,3},{3,4},{4,5},{5,6},{6,7},{7,8},{8,9},{9,10},{10,1... | collective-permute-start | bytes 786440 | tf_op jit(solution)/shard_map/ppermute | solution.py:23
  (11 other events, 93.4 us)

commit v11 on v8

--- a/solution.py
+++ b/solution.py
@@ -111,15 +111,19 @@
 
 
 def stage_two_kernel(pressure, porosity, source, star_in, wide_left, wide_right,
-                     source_left, source_right, vel_out, pres_out,
+                     source_left, source_right, left, right, vel_out, pres_out,
                      pres5, poro5, source4, even, odd):
     cells = pres_out.shape[0]
-    pres5[0:5] = wide_left[0:5]
+    pres5[0:3] = wide_left[0:3]
+    pres5[3:5] = left[6:8]
     pres5[5:cells + 5] = pressure[...]
-    pres5[cells + 5:cells + 10] = wide_right[0:5]
-    poro5[0:5] = wide_left[5:10]
+    pres5[cells + 5:cells + 7] = right[6:8]
+    pres5[cells + 7:cells + 10] = wide_right[0:3]
+    poro5[0:4] = wide_left[3:7]
+    poro5[4:5] = left[10:11]
     poro5[5:cells + 5] = porosity[...]
-    poro5[cells + 5:cells + 10] = wide_right[5:10]
+    poro5[cells + 5:cells + 6] = right[10:11]
+    poro5[cells + 6:cells + 10] = wide_right[3:7]
     source4[0:4] = source_left[...]
     source4[4:cells + 4] = source[...]
     source4[cells + 4:cells + 8] = source_right[...]
@@ -198,7 +202,7 @@
 
 
 def stage_two(pressure, porosity, source, vel_star, wide_left, wide_right, source_left,
-              source_right):
+              source_right, left, right):
     cells = vel_star.shape[1]
     plane = vel_star.shape[2:]
     f32 = jnp.float32
@@ -220,7 +224,8 @@
         compiler_params=_params(),
         cost_estimate=pl.CostEstimate(
             flops=200 * points, transcendentals=0, bytes_accessed=4 * points * 12),
-    )(pressure, porosity, source, vel_star, wide_left, wide_right, source_left, source_right)
+    )(pressure, porosity, source, vel_star, wide_left, wide_right, source_left, source_right,
+      left, right)
 
 
 def on_device_body(
@@ -293,8 +298,8 @@
     narrow_tail = jnp.concatenate(
         [velocity[:, cx - 2:].reshape((6,) + plane), pressure[cx - 2:],
          enthalpy[cx - 1:], solvent[cx - 1:], porosity[cx - 1:]], axis=0)
-    wide_head = jnp.concatenate([pressure[0:5], porosity[0:5]], axis=0)
-    wide_tail = jnp.concatenate([pressure[cx - 5:], porosity[cx - 5:]], axis=0)
+    wide_head = jnp.concatenate([pressure[2:5], porosity[1:5]], axis=0)
+    wide_tail = jnp.concatenate([pressure[cx - 5:cx - 2], porosity[cx - 5:cx - 1]], axis=0)
     n_left, n_right = neighbours(narrow_head, narrow_tail)
     wide_head, wide_tail, _ = lax.optimization_barrier((wide_head, wide_tail, (n_left, n_right)))
     w_left, w_right = neighbours(wide_head, wide_tail)
@@ -309,7 +314,8 @@
     advance(s_left)
 
     velocity_new, final = stage_two(
-        pressure, porosity, source, vel_star, w_left, w_right, s_left, s_right)
+        pressure, porosity, source, vel_star, w_left, w_right, s_left, s_right,
+        n_left, n_right)
     while rounds:
         advance(final)
     totals = state["totals"]

time: 125 us -> 132 us (1.056)
  waiting for transfers between devices: 23.5 us -> 27.5 us
  local copies, waits for them, and re-layouts: 12.1 us -> 14.7 us
  other arithmetic: 14 us -> 16 us
    ppermute x14, waiting for transfers between devices: 23.5 us -> 27.4 us  [advance(): lax.ppermute(value, axis, [(i, i ^ k * stride) for i in range(size)])]
    unnamed x34 -> x46, local copies, waits for them, and re-layouts: 4.1 us -> 6.68 us
    ppermute x3, starting transfers between devices: 22.5 us -> 20 us  [neighbours(): from_right = lax.ppermute(head, ALL, [(i + 1, i) for i in range(count - 1)])]
    ppermute x14, starting transfers between devices: 21 us -> 22.8 us  [advance(): lax.ppermute(value, axis, [(i, i ^ k * stride) for i in range(size)])]
  transfers between devices with their start and end apart: 20 -> 20, of which waited for: 3 -> 3; matrix products, arithmetic and copies ran while one was open for 16% -> 17% of each run, Pallas kernels for 6% -> 5%
where the time goes in v11:
time: 132 us; the launch traced here: 131 us
  starting transfers between devices  48.8 us (37%)
  waiting for transfers between devices  27.5 us (21%)
  Pallas kernels  19 us (14%)
  other arithmetic  16 us (12%)
  local copies, waits for them, and re-layouts  14.7 us (11%)
  between operations  5.55 us (4%)
    ppermute x14, waiting for transfers between devices, advance(): lax.ppermute(value, axis, [(i, i ^ k * stride) for i in range(size)])  27.4 us
    ppermute x14, starting transfers between devices, advance(): lax.ppermute(value, axis, [(i, i ^ k * stride) for i in range(size)])  22.8 us
    ppermute x3, starting transfers between devices, neighbours(): from_right = lax.ppermute(head, ALL, [(i + 1, i) for i in range(count - 1)])  20 us
    pallas_call x1, Pallas kernels, stage_two(): pl.pallas_call(stage_two_kernel, out_shape=outs, scratch_shapes=[pltpu.VM...  11.9 us
    pallas_call x1, Pallas kernels, stage_one(): pl.pallas_call(stage_one_kernel, out_shape=outs, scratch_shapes=[pltpu.VM...  7.15 us
    unnamed x46, local copies, waits for them, and re-layouts  6.68 us
    ppermute x3, starting transfers between devices, neighbours(): from_left = lax.ppermute(tail, ALL, [(i, i + 1) for i in range(count - 1)])  6.08 us
  transfers between devices with their start and end apart: 20, of which 3 were waited for; matrix products, arithmetic and copies ran while one was open for 17% of the time, Pallas kernels for 5%

profile of v11, /device:TPU:32, one launch (start us, length us, event | category | flops | bytes accessed | tf_op | source)
XLA Modules:
  0.0 131.5 jit_solution(10636054905189577460)
XLA Ops:
  0.6 1.5 %fusion.21 = (f32[8,1,256]{2,1,0:T(1,128)S(1)}, f32[]{:T(128)}) fusion(f32[8,64,256]{2,1,0:T(8,128)} %solvent.1), kind=kLoop, calls=%fused_computation.63 | loop fusion | flops 2047 | bytes 16388 | tf_op jit(solution)/shard_map/slice | solution.py:251
  3.8 1.3 fusion.12
  7.1 2.6 %collective-permute-start.10 = (f32[3,8,256]{2,1,0:T(8,128)}, f32[3,8,256]{2,1,0:T(8,128)}, u32[]{:S(2)}, u32[]{:S(2)}) collective-permute-start(f32[3,8,256]{2,1,0:T(8,128)} %select_maximum_fusion), channel_id=1, source_target_pairs={{0,160},{32,128},{64,224},{96,192},{128,32},{160,0},{192,96},{224,... | collective-permute-start | bytes 73736 | tf_op jit(solution)/shard_map/ppermute | solution.py:274
  10.8 3.4 %collective-permute-start.12 = (f32[3,8,256]{2,1,0:T(8,128)}, f32[3,8,256]{2,1,0:T(8,128)}, u32[]{:S(2)}, u32[]{:S(2)}) collective-permute-start(f32[3,8,256]{2,1,0:T(8,128)} %select_maximum_fusion), channel_id=1, source_target_pairs={{0,224},{32,192},{64,160},{96,128},{128,96},{160,64},{192,32},{224... | collective-permute-start | bytes 73736 | tf_op jit(solution)/shard_map/ppermute | solution.py:274
  17.7 1.5 %slice_dynamic-update-slice_fusion.3 = (f32[11,64,256]{2,1,0:T(8,128)}, f32[11,64,256]{2,1,0:T(8,128)}) fusion(f32[11,64,256]{2,1,0:T(8,128)} %get-tuple-element.62, f32[8,64,256]{2,1,0:T(8,128)} %solvent.1, f32[11,64,256]{2,1,0:T(8,128)} %get-tuple-element.63), kind=kLoop, calls=%fused_computation.7 | loop fusion | bytes 262144
  19.9 1.9 %collective-permute-start = (f32[11,64,256]{2,1,0:T(8,128)}, f32[11,64,256]{2,1,0:T(8,128)S(1)}, u32[]{:S(2)}, u32[]{:S(2)}) collective-permute-start(f32[11,64,256]{2,1,0:T(8,128)} %get-tuple-element.59), channel_id=1, source_target_pairs={{0,1},{1,2},{2,3},{3,4},{4,5},{5,6},{6,7},{7,8},{8,9},{9,10},{10,1... | collective-permute-start | bytes 2162696 | tf_op jit(solution)/shard_map/ppermute | solution.py:23
  21.9 8.8 %collective-permute-start.1 = (f32[11,64,256]{2,1,0:T(8,128)}, f32[11,64,256]{2,1,0:T(8,128)S(1)}, u32[]{:S(2)}, u32[]{:S(2)}) collective-permute-start(f32[11,64,256]{2,1,0:T(8,128)} %get-tuple-element.58), channel_id=1, source_target_pairs={{1,0},{2,1},{3,2},{4,3},{5,4},{6,5},{7,6},{8,7},{9,8},{10,9},{11,1... | collective-permute-start | bytes 2162696 | tf_op jit(solution)/shard_map/ppermute | solution.py:24
  34.3 1.7 %collective-permute-start.7 = (f32[3,8,256]{2,1,0:T(8,128)}, f32[3,8,256]{2,1,0:T(8,128)S(1)}, u32[]{:S(2)}, u32[]{:S(2)}) collective-permute-start(f32[3,8,256]{2,1,0:T(8,128)} %select_maximum_fusion), channel_id=1, source_target_pairs={{0,64},{32,96},{64,0},{96,32},{128,192},{160,224},{192,128},{224,1... | collective-permute-start | bytes 73736 | tf_op jit(solution)/shard_map/ppermute | solution.py:274
  36.0 1.9 %collective-permute-start.8 = (f32[3,8,256]{2,1,0:T(8,128)}, f32[3,8,256]{2,1,0:T(8,128)S(1)}, u32[]{:S(2)}, u32[]{:S(2)}) collective-permute-start(f32[3,8,256]{2,1,0:T(8,128)} %select_maximum_fusion), channel_id=1, source_target_pairs={{0,96},{32,64},{64,32},{96,0},{128,224},{160,192},{192,160},{224,1... | collective-permute-start | bytes 73736 | tf_op jit(solution)/shard_map/ppermute | solution.py:274
  37.9 9.3 %collective-permute-done.6 = f32[3,8,256]{2,1,0:T(8,128)S(1)} collective-permute-done((f32[3,8,256]{2,1,0:T(8,128)}, f32[3,8,256]{2,1,0:T(8,128)S(1)}, u32[]{:S(2)}, u32[]{:S(2)}) %collective-permute-start.6) | collective-permute-done | bytes 24608 | tf_op jit(solution)/shard_map/ppermute | solution.py:274
  49.1 3.6 %collective-permute-done.9 = f32[3,8,256]{2,1,0:T(8,128)S(1)} collective-permute-done((f32[3,8,256]{2,1,0:T(8,128)}, f32[3,8,256]{2,1,0:T(8,128)S(1)}, u32[]{:S(2)}, u32[]{:S(2)}) %collective-permute-start.9) | collective-permute-done | bytes 24608 | tf_op jit(solution)/shard_map/ppermute | solution.py:274
  52.7 1.4 %fusion.13 = f32[8]{0:T(128)S(1)} fusion(f32[3,8,256]{2,1,0:T(8,128)} %collective-permute-done.12, f32[3,8,256]{2,1,0:T(8,128)} %collective-permute-done.11, f32[3,8,256]{2,1,0:T(8,128)} %collective-permute-done.10, f32[3,8,256]{2,1,0:T(8,128)S(1)} %collective-permute-done.9, f32[3,8,256]{2,1,0:T(8,128)S(1)} %collective-permute-done.8, ...), kind=kLoop, calls=%fused_computation.41 | loop fusion | flops 72 | bytes 264 | tf_op jit(solution)/shard_map/add | solution.py:285
  54.2 1.8 %collective-permute-start.15 = (f32[8]{0:T(128)S(1)}, f32[8]{0:T(128)S(1)}, u32[]{:S(2)}, u32[]{:S(2)}) collective-permute-start(f32[8]{0:T(128)S(1)} %fusion.13), channel_id=1, source_target_pairs={{0,3},{1,2},{2,1},{3,0},{4,7},{5,6},{6,5},{7,4},{8,11},{9,10},{10,... | collective-permute-start | bytes 104 | tf_op jit(solution)/shard_map/ppermute | solution.py:274
  58.1 7.1 %shard_map.138 = (f32[3,8,64,256]{3,2,1,0:T(8,128)}, f32[8,64,256]{2,1,0:T(8,128)S(1)}, f32[8,64,256]{2,1,0:T(8,128)S(1)}, f32[8,64,256]{2,1,0:T(8,128)S(1)}) custom-call(f32[3,8,64,256]{3,2,1,0:T(8,128)} %velocity.1, f32[8,64,256]{2,1,0:T(8,128)S(1)} %copy-done, f32[8,64,256]{2,1,0:T(8,128)S(1)} %copy-done.3, f32[8,64,256]{2,1,0:T(8,128)S(1)} %copy-done.4, ...), custom_call_target="tpu_custom_call" | custom-call | flops 34078720 | bytes 9961472 | tf_op jit(solution)/shard_map/pallas_call | solution.py:187
  66.0 2.3 %collective-permute-start.4 = (f32[4,64,256]{2,1,0:T(8,128)S(1)}, f32[4,64,256]{2,1,0:T(8,128)S(1)}, u32[]{:S(2)}, u32[]{:S(2)}) collective-permute-start(f32[4,64,256]{2,1,0:T(8,128)S(1)} %get-tuple-element.53), channel_id=1, source_target_pairs={{0,1},{1,2},{2,3},{3,4},{4,5},{5,6},{6,7},{7,8},{8,9},{9,10},{10,1... | collective-permute-start | bytes 786440 | tf_op jit(solution)/shard_map/ppermute | solution.py:23
  69.5 5.6 %collective-permute-start.18 = (f32[8]{0:T(128)S(1)}, f32[8]{0:T(128)S(1)}, u32[]{:S(2)}, u32[]{:S(2)}) collective-permute-start(f32[8]{0:T(128)S(1)} %add_add_fusion.1), channel_id=1, source_target_pairs={{0,12},{1,13},{2,14},{3,15},{4,8},{5,9},{6,10},{7,11},{8,4},{9,5},... | collective-permute-start | bytes 104 | tf_op jit(solution)/shard_map/ppermute | solution.py:274
  79.0 1.9 %collective-permute-start.2 = (f32[7,64,256]{2,1,0:T(8,128)}, f32[7,64,256]{2,1,0:T(8,128)S(1)}, u32[]{:S(2)}, u32[]{:S(2)}) collective-permute-start(f32[7,64,256]{2,1,0:T(8,128)} %get-tuple-element.33), channel_id=1, source_target_pairs={{0,1},{1,2},{2,3},{3,4},{4,5},{5,6},{6,7},{7,8},{8,9},{9,10},{10,1... | collective-permute-start | bytes 1376264 | tf_op jit(solution)/shard_map/ppermute | solution.py:23
  80.9 8.8 %collective-permute-start.3 = (f32[7,64,256]{2,1,0:T(8,128)}, f32[7,64,256]{2,1,0:T(8,128)}, u32[]{:S(2)}, u32[]{:S(2)}) collective-permute-start(f32[7,64,256]{2,1,0:T(8,128)} %get-tuple-element.34), channel_id=1, source_target_pairs={{1,0},{2,1},{3,2},{4,3},{5,4},{6,5},{7,6},{8,7},{9,8},{10,9},{11,1... | collective-permute-start | bytes 1376264 | tf_op jit(solution)/shard_map/ppermute | solution.py:24
  89.7 2.4 %collective-permute-start.5 = (f32[4,64,256]{2,1,0:T(8,128)}, f32[4,64,256]{2,1,0:T(8,128)}, u32[]{:S(2)}, u32[]{:S(2)}) collective-permute-start(f32[4,64,256]{2,1,0:T(8,128)} %get-tuple-element.52), channel_id=1, source_target_pairs={{1,0},{2,1},{3,2},{4,3},{5,4},{6,5},{7,6},{8,7},{9,8},{10,9},{11,1... | collective-permute-start | bytes 786440 | tf_op jit(solution)/shard_map/ppermute | solution.py:24
  92.8 4.2 %collective-permute-start.19 = (f32[8]{0:T(128)S(1)}, f32[8]{0:T(128)S(1)}, u32[]{:S(2)}, u32[]{:S(2)}) collective-permute-start(f32[8]{0:T(128)S(1)} %add_add_fusion), channel_id=1, source_target_pairs={{0,16},{1,17},{2,18},{3,19},{4,20},{5,21},{6,22},{7,23},{8,24},{9,... | collective-permute-start | bytes 104 | tf_op jit(solution)/shard_map/ppermute | solution.py:274
  97.0 14.6 %collective-permute-done.19 = f32[8]{0:T(128)S(1)} collective-permute-done((f32[8]{0:T(128)S(1)}, f32[8]{0:T(128)S(1)}, u32[]{:S(2)}, u32[]{:S(2)}) %collective-permute-start.19) | collective-permute-done | bytes 64 | tf_op jit(solution)/shard_map/ppermute | solution.py:274
  115.8 1.9 %pad_maximum_fusion.1 = f32[8,64,256]{2,1,0:T(8,128)} fusion(f32[8,63,256]{2,1,0:T(8,128)} %slice.183, f32[8,1,256]{2,1,0:T(1,128)S(1)} %broadcast_in_dim.9), kind=kLoop, calls=%fused_computation.1 | loop fusion | flops 131072 | bytes 1048576 | tf_op jit(solution)/shard_map/concatenate | solution.py:337
  117.7 1.9 %pad_maximum_fusion = f32[8,64,256]{2,1,0:T(8,128)} fusion(f32[8,63,256]{2,1,0:T(8,128)} %slice.180, f32[8,1,256]{2,1,0:T(1,128)S(1)} %copy.18), kind=kLoop, calls=%fused_computation | loop fusion | flops 131072 | bytes 1048576 | tf_op jit(solution)/shard_map/concatenate | solution.py:336
  119.6 11.9 %shard_map.139 = (f32[3,8,64,256]{3,2,1,0:T(8,128)}, f32[8,64,256]{2,1,0:T(8,128)}) custom-call(f32[8,64,256]{2,1,0:T(8,128)S(1)} %copy-done, f32[8,64,256]{2,1,0:T(8,128)S(1)} %copy-done.1, f32[8,64,256]{2,1,0:T(8,128)S(1)} %get-tuple-element.31.source, f32[3,8,64,256]{3,2,1,0:T(8,128)S(1)} %copy-done.2, ...), custom_call_target="tpu_custom_call" | custom-call | flops 26214400 | bytes 6291456 | tf_op jit(solution)/shard_map/pallas_call | solution.py:214
  (95 shorter events, 22.8 us)
Async XLA Ops:
  7.1 25.3 %collective-permute-start.10 = (f32[3,8,256]{2,1,0:T(8,128)}, f32[3,8,256]{2,1,0:T(8,128)}, u32[]{:S(2)}, u32[]{:S(2)}) collective-permute-start(f32[3,8,256]{2,1,0:T(8,128)} %select_maximum_fusion), channel_id=1, source_target_pairs={{0,160},{32,128},{64,224},{96,192},{128,32},{160,0},{192,96},{224,... | collective-permute-start | bytes 73736 | tf_op jit(solution)/shard_map/ppermute | solution.py:274
  9.7 24.6 %collective-permute-start.11 = (f32[3,8,256]{2,1,0:T(8,128)}, f32[3,8,256]{2,1,0:T(8,128)}, u32[]{:S(2)}, u32[]{:S(2)}) collective-permute-start(f32[3,8,256]{2,1,0:T(8,128)} %select_maximum_fusion), channel_id=1, source_target_pairs={{0,192},{32,224},{64,128},{96,160},{128,64},{160,96},{192,0},{224,... | collective-permute-start | bytes 73736 | tf_op jit(solution)/shard_map/ppermute | solution.py:274
  10.8 25.2 %collective-permute-start.12 = (f32[3,8,256]{2,1,0:T(8,128)}, f32[3,8,256]{2,1,0:T(8,128)}, u32[]{:S(2)}, u32[]{:S(2)}) collective-permute-start(f32[3,8,256]{2,1,0:T(8,128)} %select_maximum_fusion), channel_id=1, source_target_pairs={{0,224},{32,192},{64,160},{96,128},{128,96},{160,64},{192,32},{224... | collective-permute-start | bytes 73736 | tf_op jit(solution)/shard_map/ppermute | solution.py:274
  19.9 36.0 %collective-permute-start = (f32[11,64,256]{2,1,0:T(8,128)}, f32[11,64,256]{2,1,0:T(8,128)S(1)}, u32[]{:S(2)}, u32[]{:S(2)}) collective-permute-start(f32[11,64,256]{2,1,0:T(8,128)} %get-tuple-element.59), channel_id=1, source_target_pairs={{0,1},{1,2},{2,3},{3,4},{4,5},{5,6},{6,7},{7,8},{8,9},{9,10},{10,1... | collective-permute-start | bytes 2162696 | tf_op jit(solution)/shard_map/ppermute | solution.py:23
  21.9 34.1 %collective-permute-start.1 = (f32[11,64,256]{2,1,0:T(8,128)}, f32[11,64,256]{2,1,0:T(8,128)S(1)}, u32[]{:S(2)}, u32[]{:S(2)}) collective-permute-start(f32[11,64,256]{2,1,0:T(8,128)} %get-tuple-element.58), channel_id=1, source_target_pairs={{1,0},{2,1},{3,2},{4,3},{5,4},{6,5},{7,6},{8,7},{9,8},{10,9},{11,1... | collective-permute-start | bytes 2162696 | tf_op jit(solution)/shard_map/ppermute | solution.py:24
  32.4 14.8 %collective-permute-start.6 = (f32[3,8,256]{2,1,0:T(8,128)}, f32[3,8,256]{2,1,0:T(8,128)S(1)}, u32[]{:S(2)}, u32[]{:S(2)}) collective-permute-start(f32[3,8,256]{2,1,0:T(8,128)} %select_maximum_fusion), channel_id=1, source_target_pairs={{0,32},{32,0},{64,96},{96,64},{128,160},{160,128},{192,224},{224,1... | collective-permute-start | bytes 73736 | tf_op jit(solution)/shard_map/ppermute | solution.py:274
  34.3 14.7 %collective-permute-start.7 = (f32[3,8,256]{2,1,0:T(8,128)}, f32[3,8,256]{2,1,0:T(8,128)S(1)}, u32[]{:S(2)}, u32[]{:S(2)}) collective-permute-start(f32[3,8,256]{2,1,0:T(8,128)} %select_maximum_fusion), channel_id=1, source_target_pairs={{0,64},{32,96},{64,0},{96,32},{128,192},{160,224},{192,128},{224,1... | collective-permute-start | bytes 73736 | tf_op jit(solution)/shard_map/ppermute | solution.py:274
  36.0 13.1 %collective-permute-start.8 = (f32[3,8,256]{2,1,0:T(8,128)}, f32[3,8,256]{2,1,0:T(8,128)S(1)}, u32[]{:S(2)}, u32[]{:S(2)}) collective-permute-start(f32[3,8,256]{2,1,0:T(8,128)} %select_maximum_fusion), channel_id=1, source_target_pairs={{0,96},{32,64},{64,32},{96,0},{128,224},{160,192},{192,160},{224,1... | collective-permute-start | bytes 73736 | tf_op jit(solution)/shard_map/ppermute | solution.py:274
  47.1 5.5 %collective-permute-start.9 = (f32[3,8,256]{2,1,0:T(8,128)}, f32[3,8,256]{2,1,0:T(8,128)S(1)}, u32[]{:S(2)}, u32[]{:S(2)}) collective-permute-start(f32[3,8,256]{2,1,0:T(8,128)} %select_maximum_fusion), channel_id=1, source_target_pairs={{0,128},{32,160},{64,192},{96,224},{128,0},{160,32},{192,64},{224,... | collective-permute-start | bytes 73736 | tf_op jit(solution)/shard_map/ppermute | solution.py:274
  54.1 15.0 %collective-permute-start.13 = (f32[8]{0:T(128)S(1)}, f32[8]{0:T(128)S(1)}, u32[]{:S(2)}, u32[]{:S(2)}) collective-permute-start(f32[8]{0:T(128)S(1)} %fusion.13), channel_id=1, source_target_pairs={{0,1},{1,0},{2,3},{3,2},{4,5},{5,4},{6,7},{7,6},{8,9},{9,8},{10,11... | collective-permute-start | bytes 104 | tf_op jit(solution)/shard_map/ppermute | solution.py:274
  54.1 15.0 %collective-permute-start.14 = (f32[8]{0:T(128)S(1)}, f32[8]{0:T(128)S(1)}, u32[]{:S(2)}, u32[]{:S(2)}) collective-permute-start(f32[8]{0:T(128)S(1)} %fusion.13), channel_id=1, source_target_pairs={{0,2},{1,3},{2,0},{3,1},{4,6},{5,7},{6,4},{7,5},{8,10},{9,11},{10,... | collective-permute-start | bytes 104 | tf_op jit(solution)/shard_map/ppermute | solution.py:274
  54.2 14.9 %collective-permute-start.15 = (f32[8]{0:T(128)S(1)}, f32[8]{0:T(128)S(1)}, u32[]{:S(2)}, u32[]{:S(2)}) collective-permute-start(f32[8]{0:T(128)S(1)} %fusion.13), channel_id=1, source_target_pairs={{0,3},{1,2},{2,1},{3,0},{4,7},{5,6},{6,5},{7,4},{8,11},{9,10},{10,... | collective-permute-start | bytes 104 | tf_op jit(solution)/shard_map/ppermute | solution.py:274
  58.1 10.2 %copy-start.15 = (f32[3,8,256]{2,1,0:T(8,128)S(1)}, f32[3,8,256]{2,1,0:T(8,128)}, u32[]{:S(2)}) copy-start(f32[3,8,256]{2,1,0:T(8,128)} %copy-done.14) | copy-start | bytes 73732
  66.0 26.1 %collective-permute-start.4 = (f32[4,64,256]{2,1,0:T(8,128)S(1)}, f32[4,64,256]{2,1,0:T(8,128)S(1)}, u32[]{:S(2)}, u32[]{:S(2)}) collective-permute-start(f32[4,64,256]{2,1,0:T(8,128)S(1)} %get-tuple-element.53), channel_id=1, source_target_pairs={{0,1},{1,2},{2,3},{3,4},{4,5},{5,6},{6,7},{7,8},{8,9},{9,10},{10,1... | collective-permute-start | bytes 786440 | tf_op jit(solution)/shard_map/ppermute | solution.py:23
  69.1 11.8 %collective-permute-start.16 = (f32[8]{0:T(128)S(1)}, f32[8]{0:T(128)S(1)}, u32[]{:S(2)}, u32[]{:S(2)}) collective-permute-start(f32[8]{0:T(128)S(1)} %add_add_fusion.1), channel_id=1, source_target_pairs={{0,4},{1,5},{2,6},{3,7},{4,0},{5,1},{6,2},{7,3},{8,12},{9,13},{10,... | collective-permute-start | bytes 104 | tf_op jit(solution)/shard_map/ppermute | solution.py:274
  69.2 20.5 %collective-permute-start.17 = (f32[8]{0:T(128)S(1)}, f32[8]{0:T(128)S(1)}, u32[]{:S(2)}, u32[]{:S(2)}) collective-permute-start(f32[8]{0:T(128)S(1)} %add_add_fusion.1), channel_id=1, source_target_pairs={{0,8},{1,9},{2,10},{3,11},{4,12},{5,13},{6,14},{7,15},{8,0},{9,1},... | collective-permute-start | bytes 104 | tf_op jit(solution)/shard_map/ppermute | solution.py:274
  69.5 22.6 %collective-permute-start.18 = (f32[8]{0:T(128)S(1)}, f32[8]{0:T(128)S(1)}, u32[]{:S(2)}, u32[]{:S(2)}) collective-permute-start(f32[8]{0:T(128)S(1)} %add_add_fusion.1), channel_id=1, source_target_pairs={{0,12},{1,13},{2,14},{3,15},{4,8},{5,9},{6,10},{7,11},{8,4},{9,5},... | collective-permute-start | bytes 104 | tf_op jit(solution)/shard_map/ppermute | solution.py:274
  76.2 35.4 %copy-start.18 = (s32[8]{0:T(128)S(1)}, s32[8]{0:T(128)}, u32[]{:S(2)}) copy-start(s32[8]{0:T(128)} %param.20) | copy-start | bytes 100
  76.2 38.0 %copy-start.16 = (s32[8,256]{1,0:T(8,128)S(1)}, s32[8,256]{1,0:T(8,128)}, u32[]{:S(2)}) copy-start(s32[8,256]{1,0:T(8,128)} %param.19) | copy-start | bytes 24580
  76.2 38.0 %copy-start.19 = (pred[256]{0:T(512)(128)(4,1)S(1)}, pred[256]{0:T(512)(128)(4,1)}, u32[]{:S(2)}) copy-start(pred[256]{0:T(512)(128)(4,1)} %compare_and_fusion.1) | copy-start | bytes 772
  79.0 40.6 %collective-permute-start.2 = (f32[7,64,256]{2,1,0:T(8,128)}, f32[7,64,256]{2,1,0:T(8,128)S(1)}, u32[]{:S(2)}, u32[]{:S(2)}) collective-permute-start(f32[7,64,256]{2,1,0:T(8,128)} %get-tuple-element.33), channel_id=1, source_target_pairs={{0,1},{1,2},{2,3},{3,4},{4,5},{5,6},{6,7},{7,8},{8,9},{9,10},{10,1... | collective-permute-start | bytes 1376264 | tf_op jit(solution)/shard_map/ppermute | solution.py:23
  80.9 38.7 %collective-permute-start.3 = (f32[7,64,256]{2,1,0:T(8,128)}, f32[7,64,256]{2,1,0:T(8,128)}, u32[]{:S(2)}, u32[]{:S(2)}) collective-permute-start(f32[7,64,256]{2,1,0:T(8,128)} %get-tuple-element.34), channel_id=1, source_target_pairs={{1,0},{2,1},{3,2},{4,3},{5,4},{6,5},{7,6},{8,7},{9,8},{10,9},{11,1... | collective-permute-start | bytes 1376264 | tf_op jit(solution)/shard_map/ppermute | solution.py:24
  89.7 29.9 %collective-permute-start.5 = (f32[4,64,256]{2,1,0:T(8,128)}, f32[4,64,256]{2,1,0:T(8,128)}, u32[]{:S(2)}, u32[]{:S(2)}) collective-permute-start(f32[4,64,256]{2,1,0:T(8,128)} %get-tuple-element.52), channel_id=1, source_target_pairs={{1,0},{2,1},{3,2},{4,3},{5,4},{6,5},{7,6},{8,7},{9,8},{10,9},{11,1... | collective-permute-start | bytes 786440 | tf_op jit(solution)/shard_map/ppermute | solution.py:24
  92.8 18.8 %collective-permute-start.19 = (f32[8]{0:T(128)S(1)}, f32[8]{0:T(128)S(1)}, u32[]{:S(2)}, u32[]{:S(2)}) collective-permute-start(f32[8]{0:T(128)S(1)} %add_add_fusion), channel_id=1, source_target_pairs={{0,16},{1,17},{2,18},{3,19},{4,20},{5,21},{6,22},{7,23},{8,24},{9,... | collective-permute-start | bytes 104 | tf_op jit(solution)/shard_map/ppermute | solution.py:274
  (17 other events, 95.8 us)

commit v12 on v8

--- a/solution.py
+++ b/solution.py
@@ -112,7 +112,7 @@
 
 def stage_two_kernel(pressure, porosity, source, star_in, wide_left, wide_right,
                      source_left, source_right, vel_out, pres_out,
-                     pres5, poro5, source4, even, odd):
+                     pres5, poro5, source4, even, odd, coef):
     cells = pres_out.shape[0]
     pres5[0:5] = wide_left[0:5]
     pres5[5:cells + 5] = pressure[...]
@@ -123,6 +123,24 @@
     source4[0:4] = source_left[...]
     source4[4:cells + 4] = source[...]
     source4[cells + 4:cells + 8] = source_right[...]
+
+    def faces(j, carry):
+        open_here = poro5[j + 1]
+        face_back = 0.5 * (open_here + poro5[j])
+        face_front = 0.5 * (open_here + poro5[j + 2])
+        coef[0, j] = face_back
+        coef[1, j] = face_front
+        denominator = face_back + face_front
+        for axis in (0, 1):
+            face_low = 0.5 * (open_here + _down(open_here, axis))
+            face_high = 0.5 * (open_here + _up(open_here, axis))
+            coef[2 + 2 * axis, j] = face_low
+            coef[3 + 2 * axis, j] = face_high
+            denominator = denominator + face_low + face_high
+        coef[6, j] = denominator
+        return carry
+
+    lax.fori_loop(0, source4.shape[0], faces, 0)
     buffers = (even, odd)
     prev = pres5
     for k in range(ITERS):
@@ -130,23 +148,18 @@
         count = source4.shape[0] - 2 * k
 
         def body(j, carry, k=k, prev=prev, out=out):
-            open_here = poro5[k + j + 1]
+            c = k + j
+            open_here = poro5[c + 1]
             pressure_mid = prev[j + 1]
-            face_back = 0.5 * (open_here + poro5[k + j])
-            face_front = 0.5 * (open_here + poro5[k + j + 2])
-            numerator = face_back * prev[j] + face_front * prev[j + 2] - source4[k + j]
-            denominator = face_back + face_front
+            numerator = coef[0, c] * prev[j] + coef[1, c] * prev[j + 2] - source4[c]
             for axis in (0, 1):
-                face_low = 0.5 * (open_here + _down(open_here, axis))
-                face_high = 0.5 * (open_here + _up(open_here, axis))
                 numerator = (
                     numerator
-                    + face_low * _down(pressure_mid, axis)
-                    + face_high * _up(pressure_mid, axis)
+                    + coef[2 + 2 * axis, c] * _down(pressure_mid, axis)
+                    + coef[3 + 2 * axis, c] * _up(pressure_mid, axis)
                 )
-                denominator = denominator + face_low + face_high
             inside = open_here > 0.0
-            out[j] = jnp.where(inside, numerator / jnp.where(inside, denominator, 1.0), 0.0)
+            out[j] = jnp.where(inside, numerator / jnp.where(inside, coef[6, c], 1.0), 0.0)
             return carry
 
         lax.fori_loop(0, count, body, 0)
@@ -216,6 +229,7 @@
             pltpu.VMEM((cells + 8,) + plane, f32),
             pltpu.VMEM((cells + 8,) + plane, f32),
             pltpu.VMEM((cells + 8,) + plane, f32),
+            pltpu.VMEM((7, cells + 8) + plane, f32),
         ],
         compiler_params=_params(),
         cost_estimate=pl.CostEstimate(
@@ -327,8 +341,8 @@
     jets = (nozzle_mask > 0) & inside_box[None, :]
     heat_layer = jnp.where(jets, supply_heat, heat_new[:, 0, :])
     solv_layer = jnp.where(jets, supply_solv, solv_new[:, 0, :])
-    enthalpy_new = jnp.concatenate([heat_layer[:, None, :], heat_new[:, 1:, :]], axis=1)
-    solvent_new = jnp.concatenate([solv_layer[:, None, :], solv_new[:, 1:, :]], axis=1)
+    enthalpy_new = heat_new.at[:, 0, :].set(heat_layer)
+    solvent_new = solv_new.at[:, 0, :].set(solv_layer)
     return (velocity_new, enthalpy_new, solvent_new, final)
 
 

time: 125 us -> 129 us (1.032)
  local copies, waits for them, and re-layouts: 12.1 us -> 20.9 us
  other arithmetic: 14 us -> 10.2 us
    unnamed x34 -> x40, local copies, waits for them, and re-layouts: 4.1 us -> 11.6 us
    concatenate x2 -> x0, other arithmetic: 3.79 us -> none  [the longest x1 1.9 us: on_device_body(): jnp.concatenate([heat_layer[:, None, :], heat_new[:, 1:, :]], axis=1)]
    scatter x0 -> x2, local copies, waits for them, and re-layouts: none -> 3 us  [the longest x1 1.51 us: on_device_body(): enthalpy_new = heat_new.at[:, 0, :].set(heat_layer)]
    slice x2 -> x0, local copies, waits for them, and re-layouts: 1.7 us -> none  [the longest x1 0.85 us: on_device_body(): solv_new[:, 1:, :]]
  transfers between devices with their start and end apart: 20 -> 20, of which waited for: 3 -> 3; matrix products, arithmetic and copies ran while one was open for 16% -> 15% of each run, Pallas kernels for 6% -> 6%
where the time goes in v12:
time: 129 us; the launch traced here: 128 us
  starting transfers between devices  49.6 us (38%)
  waiting for transfers between devices  23.6 us (18%)
  local copies, waits for them, and re-layouts  20.9 us (16%)
  Pallas kernels  18.4 us (14%)
  other arithmetic  10.2 us (8%)
  between operations  5.43 us (4%)
    ppermute x14, waiting for transfers between devices, advance(): lax.ppermute(value, axis, [(i, i ^ k * stride) for i in range(size)])  23.6 us
    ppermute x3, starting transfers between devices, neighbours(): from_right = lax.ppermute(head, ALL, [(i + 1, i) for i in range(count - 1)])  22.4 us
    ppermute x14, starting transfers between devices, advance(): lax.ppermute(value, axis, [(i, i ^ k * stride) for i in range(size)])  21 us
    unnamed x40, local copies, waits for them, and re-layouts  11.6 us
    pallas_call x1, Pallas kernels, stage_two(): pl.pallas_call(stage_two_kernel, out_shape=outs, scratch_shapes=[pltpu.VM...  11.3 us
    pallas_call x1, Pallas kernels, stage_one(): pl.pallas_call(stage_one_kernel, out_shape=outs, scratch_shapes=[pltpu.VM...  7.1 us
    ppermute x3, starting transfers between devices, neighbours(): from_left = lax.ppermute(tail, ALL, [(i, i + 1) for i in range(count - 1)])  6.1 us
  transfers between devices with their start and end apart: 20, of which 3 were waited for; matrix products, arithmetic and copies ran while one was open for 15% of the time, Pallas kernels for 6%

profile of v12, /device:TPU:32, one launch (start us, length us, event | category | flops | bytes accessed | tf_op | source)
XLA Modules:
  0.0 128.1 jit_solution(4164998708669819233)
XLA Ops:
  0.6 1.5 %fusion.21 = (f32[8,1,256]{2,1,0:T(1,128)S(1)}, f32[]{:T(128)}) fusion(f32[8,64,256]{2,1,0:T(8,128)} %solvent.1), kind=kLoop, calls=%fused_computation.61 | loop fusion | flops 2047 | bytes 16388 | tf_op jit(solution)/shard_map/slice | solution.py:260
  6.4 1.9 %collective-permute-start.6 = (f32[3,8,256]{2,1,0:T(8,128)S(1)}, f32[3,8,256]{2,1,0:T(8,128)S(1)}, u32[]{:S(2)}, u32[]{:S(2)}) collective-permute-start(f32[3,8,256]{2,1,0:T(8,128)S(1)} %select_maximum_fusion), channel_id=1, source_target_pairs={{0,32},{32,0},{64,96},{96,64},{128,160},{160,128},{192,224},{224,1... | collective-permute-start | bytes 73736 | tf_op jit(solution)/shard_map/ppermute | solution.py:283
  8.3 1.7 %collective-permute-start.8 = (f32[3,8,256]{2,1,0:T(8,128)S(1)}, f32[3,8,256]{2,1,0:T(8,128)S(1)}, u32[]{:S(2)}, u32[]{:S(2)}) collective-permute-start(f32[3,8,256]{2,1,0:T(8,128)S(1)} %select_maximum_fusion), channel_id=1, source_target_pairs={{0,96},{32,64},{64,32},{96,0},{128,224},{160,192},{192,160},{224,1... | collective-permute-start | bytes 73736 | tf_op jit(solution)/shard_map/ppermute | solution.py:283
  12.7 1.5 %slice_dynamic-update-slice_fusion.4 = (f32[11,64,256]{2,1,0:T(8,128)}, f32[11,64,256]{2,1,0:T(8,128)S(1)}) fusion(f32[11,64,256]{2,1,0:T(8,128)} %get-tuple-element.88, f32[8,64,256]{2,1,0:T(8,128)} %enthalpy.1, f32[11,64,256]{2,1,0:T(8,128)S(1)} %get-tuple-element.89), kind=kLoop, calls=%fused_computation.6 | loop fusion | bytes 262144
  14.2 1.5 %slice_dynamic-update-slice_fusion.3 = (f32[11,64,256]{2,1,0:T(8,128)}, f32[11,64,256]{2,1,0:T(8,128)S(1)}) fusion(f32[11,64,256]{2,1,0:T(8,128)} %get-tuple-element.86, f32[8,64,256]{2,1,0:T(8,128)} %solvent.1, f32[11,64,256]{2,1,0:T(8,128)S(1)} %get-tuple-element.87), kind=kLoop, calls=%fused_computation.5 | loop fusion | bytes 262144
  16.3 1.9 %collective-permute-start = (f32[11,64,256]{2,1,0:T(8,128)S(1)}, f32[11,64,256]{2,1,0:T(8,128)S(1)}, u32[]{:S(2)}, u32[]{:S(2)}) collective-permute-start(f32[11,64,256]{2,1,0:T(8,128)S(1)} %get-tuple-element.83), channel_id=1, source_target_pairs={{0,1},{1,2},{2,3},{3,4},{4,5},{5,6},{6,7},{7,8},{8,9},{9,10},{10,1... | collective-permute-start | bytes 2162696 | tf_op jit(solution)/shard_map/ppermute | solution.py:23
  18.2 8.8 %collective-permute-start.1 = (f32[11,64,256]{2,1,0:T(8,128)}, f32[11,64,256]{2,1,0:T(8,128)S(1)}, u32[]{:S(2)}, u32[]{:S(2)}) collective-permute-start(f32[11,64,256]{2,1,0:T(8,128)} %get-tuple-element.82), channel_id=1, source_target_pairs={{1,0},{2,1},{3,2},{4,3},{5,4},{6,5},{7,6},{8,7},{9,8},{10,9},{11,1... | collective-permute-start | bytes 2162696 | tf_op jit(solution)/shard_map/ppermute | solution.py:24
  29.0 3.0 %collective-permute-start.9 = (f32[3,8,256]{2,1,0:T(8,128)S(1)}, f32[3,8,256]{2,1,0:T(8,128)S(1)}, u32[]{:S(2)}, u32[]{:S(2)}) collective-permute-start(f32[3,8,256]{2,1,0:T(8,128)S(1)} %select_maximum_fusion), channel_id=1, source_target_pairs={{0,128},{32,160},{64,192},{96,224},{128,0},{160,32},{192,64},{224,... | collective-permute-start | bytes 73736 | tf_op jit(solution)/shard_map/ppermute | solution.py:283
  34.0 3.1 %collective-permute-start.11 = (f32[3,8,256]{2,1,0:T(8,128)S(1)}, f32[3,8,256]{2,1,0:T(8,128)S(1)}, u32[]{:S(2)}, u32[]{:S(2)}) collective-permute-start(f32[3,8,256]{2,1,0:T(8,128)S(1)} %select_maximum_fusion), channel_id=1, source_target_pairs={{0,192},{32,224},{64,128},{96,160},{128,64},{160,96},{192,0},{224,... | collective-permute-start | bytes 73736 | tf_op jit(solution)/shard_map/ppermute | solution.py:283
  37.1 1.6 %collective-permute-start.12 = (f32[3,8,256]{2,1,0:T(8,128)S(1)}, f32[3,8,256]{2,1,0:T(8,128)S(1)}, u32[]{:S(2)}, u32[]{:S(2)}) collective-permute-start(f32[3,8,256]{2,1,0:T(8,128)S(1)} %select_maximum_fusion), channel_id=1, source_target_pairs={{0,224},{32,192},{64,160},{96,128},{128,96},{160,64},{192,32},{224... | collective-permute-start | bytes 73736 | tf_op jit(solution)/shard_map/ppermute | solution.py:283
  40.0 3.8 %collective-permute-done.10 = f32[3,8,256]{2,1,0:T(8,128)S(1)} collective-permute-done((f32[3,8,256]{2,1,0:T(8,128)S(1)}, f32[3,8,256]{2,1,0:T(8,128)S(1)}, u32[]{:S(2)}, u32[]{:S(2)}) %collective-permute-start.10) | collective-permute-done | bytes 24608 | tf_op jit(solution)/shard_map/ppermute | solution.py:283
  44.9 1.7 %collective-permute-start.15 = (f32[8]{0:T(128)S(1)}, f32[8]{0:T(128)S(1)}, u32[]{:S(2)}, u32[]{:S(2)}) collective-permute-start(f32[8]{0:T(128)S(1)} %fusion.13), channel_id=1, source_target_pairs={{0,3},{1,2},{2,1},{3,0},{4,7},{5,6},{6,5},{7,4},{8,11},{9,10},{10,... | collective-permute-start | bytes 104 | tf_op jit(solution)/shard_map/ppermute | solution.py:283
  53.7 7.1 %shard_map.138 = (f32[3,8,64,256]{3,2,1,0:T(8,128)S(1)}, f32[8,64,256]{2,1,0:T(8,128)S(1)}, f32[8,64,256]{2,1,0:T(8,128)}, f32[8,64,256]{2,1,0:T(8,128)}) custom-call(f32[3,8,64,256]{3,2,1,0:T(8,128)} %velocity.1, f32[8,64,256]{2,1,0:T(8,128)S(1)} %copy-done, f32[8,64,256]{2,1,0:T(8,128)S(1)} %copy-done.2, f32[8,64,256]{2,1,0:T(8,128)S(1)} %copy-done.3, ...), custom_call_target="tpu_custom_call" | custom-call | flops 34078720 | bytes 9961472 | tf_op jit(solution)/shard_map/pallas_call | solution.py:196
  61.6 2.3 %collective-permute-start.4 = (f32[4,64,256]{2,1,0:T(8,128)S(1)}, f32[4,64,256]{2,1,0:T(8,128)S(1)}, u32[]{:S(2)}, u32[]{:S(2)}) collective-permute-start(f32[4,64,256]{2,1,0:T(8,128)S(1)} %get-tuple-element.77), channel_id=1, source_target_pairs={{0,1},{1,2},{2,3},{3,4},{4,5},{5,6},{6,7},{7,8},{8,9},{9,10},{10,1... | collective-permute-start | bytes 786440 | tf_op jit(solution)/shard_map/ppermute | solution.py:23
  64.8 3.5 %collective-permute-start.17 = (f32[8]{0:T(128)S(1)}, f32[8]{0:T(128)S(1)}, u32[]{:S(2)}, u32[]{:S(2)}) collective-permute-start(f32[8]{0:T(128)S(1)} %add_add_fusion.1), channel_id=1, source_target_pairs={{0,8},{1,9},{2,10},{3,11},{4,12},{5,13},{6,14},{7,15},{8,0},{9,1},... | collective-permute-start | bytes 104 | tf_op jit(solution)/shard_map/ppermute | solution.py:283
  68.4 2.3 %collective-permute-start.18 = (f32[8]{0:T(128)S(1)}, f32[8]{0:T(128)S(1)}, u32[]{:S(2)}, u32[]{:S(2)}) collective-permute-start(f32[8]{0:T(128)S(1)} %add_add_fusion.1), channel_id=1, source_target_pairs={{0,12},{1,13},{2,14},{3,15},{4,8},{5,9},{6,10},{7,11},{8,4},{9,5},... | collective-permute-start | bytes 104 | tf_op jit(solution)/shard_map/ppermute | solution.py:283
  70.7 1.9 %collective-permute-start.2 = (f32[10,64,256]{2,1,0:T(8,128)}, f32[10,64,256]{2,1,0:T(8,128)}, u32[]{:S(2)}, u32[]{:S(2)}) collective-permute-start(f32[10,64,256]{2,1,0:T(8,128)} %get-tuple-element.57), channel_id=1, source_target_pairs={{0,1},{1,2},{2,3},{3,4},{4,5},{5,6},{6,7},{7,8},{8,9},{9,10},{10,1... | collective-permute-start | bytes 1966088 | tf_op jit(solution)/shard_map/ppermute | solution.py:23
  74.8 11.2 %collective-permute-start.3 = (f32[10,64,256]{2,1,0:T(8,128)}, f32[10,64,256]{2,1,0:T(8,128)}, u32[]{:S(2)}, u32[]{:S(2)}) collective-permute-start(f32[10,64,256]{2,1,0:T(8,128)} %get-tuple-element.58), channel_id=1, source_target_pairs={{1,0},{2,1},{3,2},{4,3},{5,4},{6,5},{7,6},{8,7},{9,8},{10,9},{11,1... | collective-permute-start | bytes 1966088 | tf_op jit(solution)/shard_map/ppermute | solution.py:24
  86.1 2.4 %collective-permute-start.5 = (f32[4,64,256]{2,1,0:T(8,128)}, f32[4,64,256]{2,1,0:T(8,128)}, u32[]{:S(2)}, u32[]{:S(2)}) collective-permute-start(f32[4,64,256]{2,1,0:T(8,128)} %get-tuple-element.76), channel_id=1, source_target_pairs={{1,0},{2,1},{3,2},{4,3},{5,4},{6,5},{7,6},{8,7},{9,8},{10,9},{11,1... | collective-permute-start | bytes 786440 | tf_op jit(solution)/shard_map/ppermute | solution.py:24
  88.5 1.8 %collective-permute-start.19 = (f32[8]{0:T(128)S(1)}, f32[8]{0:T(128)S(1)}, u32[]{:S(2)}, u32[]{:S(2)}) collective-permute-start(f32[8]{0:T(128)S(1)} %add_add_fusion), channel_id=1, source_target_pairs={{0,16},{1,17},{2,18},{3,19},{4,20},{5,21},{6,22},{7,23},{8,24},{9,... | collective-permute-start | bytes 104 | tf_op jit(solution)/shard_map/ppermute | solution.py:283
  90.3 19.5 %collective-permute-done.19 = f32[8]{0:T(128)S(1)} collective-permute-done((f32[8]{0:T(128)S(1)}, f32[8]{0:T(128)S(1)}, u32[]{:S(2)}, u32[]{:S(2)}) %collective-permute-start.19) | collective-permute-done | bytes 64 | tf_op jit(solution)/shard_map/ppermute | solution.py:283
  113.8 1.5 %scatter.11 = f32[8,64,256]{2,1,0:T(8,128)} dynamic-update-slice(f32[8,64,256]{2,1,0:T(8,128)} %get-tuple-element.60, f32[8,1,256]{2,1,0:T(1,128)S(1)} %copy.18, s32[]{:T(128)} %constant.102.clone.1, s32[]{:T(128)} %constant.102.clone.1, s32[]{:T(128)} %constant.102.clone.1) | dynamic-update-slice | bytes 16388 | tf_op jit(solution)/shard_map/scatter | solution.py:344
  115.3 1.5 %scatter.14 = f32[8,64,256]{2,1,0:T(8,128)} dynamic-update-slice(f32[8,64,256]{2,1,0:T(8,128)} %get-tuple-element.68, f32[8,1,256]{2,1,0:T(1,128)S(1)} %reshape.159, s32[]{:T(128)} %constant.102.clone.1, s32[]{:T(128)} %constant.102.clone.1, s32[]{:T(128)} %constant.102.clone.1) | dynamic-update-slice | bytes 16388 | tf_op jit(solution)/shard_map/scatter | solution.py:345
  116.8 11.3 %shard_map.139 = (f32[3,8,64,256]{3,2,1,0:T(8,128)}, f32[8,64,256]{2,1,0:T(8,128)}) custom-call(f32[8,64,256]{2,1,0:T(8,128)S(1)} %copy-done, f32[8,64,256]{2,1,0:T(8,128)S(1)} %copy-done.1, f32[8,64,256]{2,1,0:T(8,128)S(1)} %get-tuple-element.55.source, f32[3,8,64,256]{3,2,1,0:T(8,128)S(1)} %get-tuple-element.56.star_in, ...), custom_call_target="tpu_custom_call" | custom-call | flops 26214400 | bytes 6291456 | tf_op jit(solution)/shard_map/pallas_call | solution.py:223
  (87 shorter events, 24.3 us)
Async XLA Ops:
  6.4 22.5 %collective-permute-start.6 = (f32[3,8,256]{2,1,0:T(8,128)S(1)}, f32[3,8,256]{2,1,0:T(8,128)S(1)}, u32[]{:S(2)}, u32[]{:S(2)}) collective-permute-start(f32[3,8,256]{2,1,0:T(8,128)S(1)} %select_maximum_fusion), channel_id=1, source_target_pairs={{0,32},{32,0},{64,96},{96,64},{128,160},{160,128},{192,224},{224,1... | collective-permute-start | bytes 73736 | tf_op jit(solution)/shard_map/ppermute | solution.py:283
  8.3 25.6 %collective-permute-start.7 = (f32[3,8,256]{2,1,0:T(8,128)S(1)}, f32[3,8,256]{2,1,0:T(8,128)S(1)}, u32[]{:S(2)}, u32[]{:S(2)}) collective-permute-start(f32[3,8,256]{2,1,0:T(8,128)S(1)} %select_maximum_fusion), channel_id=1, source_target_pairs={{0,64},{32,96},{64,0},{96,32},{128,192},{160,224},{192,128},{224,1... | collective-permute-start | bytes 73736 | tf_op jit(solution)/shard_map/ppermute | solution.py:283
  8.3 25.7 %collective-permute-start.8 = (f32[3,8,256]{2,1,0:T(8,128)S(1)}, f32[3,8,256]{2,1,0:T(8,128)S(1)}, u32[]{:S(2)}, u32[]{:S(2)}) collective-permute-start(f32[3,8,256]{2,1,0:T(8,128)S(1)} %select_maximum_fusion), channel_id=1, source_target_pairs={{0,96},{32,64},{64,32},{96,0},{128,224},{160,192},{192,160},{224,1... | collective-permute-start | bytes 73736 | tf_op jit(solution)/shard_map/ppermute | solution.py:283
  16.3 30.3 %collective-permute-start = (f32[11,64,256]{2,1,0:T(8,128)S(1)}, f32[11,64,256]{2,1,0:T(8,128)S(1)}, u32[]{:S(2)}, u32[]{:S(2)}) collective-permute-start(f32[11,64,256]{2,1,0:T(8,128)S(1)} %get-tuple-element.83), channel_id=1, source_target_pairs={{0,1},{1,2},{2,3},{3,4},{4,5},{5,6},{6,7},{7,8},{8,9},{9,10},{10,1... | collective-permute-start | bytes 2162696 | tf_op jit(solution)/shard_map/ppermute | solution.py:23
  18.2 29.3 %collective-permute-start.1 = (f32[11,64,256]{2,1,0:T(8,128)}, f32[11,64,256]{2,1,0:T(8,128)S(1)}, u32[]{:S(2)}, u32[]{:S(2)}) collective-permute-start(f32[11,64,256]{2,1,0:T(8,128)} %get-tuple-element.82), channel_id=1, source_target_pairs={{1,0},{2,1},{3,2},{4,3},{5,4},{6,5},{7,6},{8,7},{9,8},{10,9},{11,1... | collective-permute-start | bytes 2162696 | tf_op jit(solution)/shard_map/ppermute | solution.py:24
  29.0 8.1 %collective-permute-start.9 = (f32[3,8,256]{2,1,0:T(8,128)S(1)}, f32[3,8,256]{2,1,0:T(8,128)S(1)}, u32[]{:S(2)}, u32[]{:S(2)}) collective-permute-start(f32[3,8,256]{2,1,0:T(8,128)S(1)} %select_maximum_fusion), channel_id=1, source_target_pairs={{0,128},{32,160},{64,192},{96,224},{128,0},{160,32},{192,64},{224,... | collective-permute-start | bytes 73736 | tf_op jit(solution)/shard_map/ppermute | solution.py:283
  33.9 9.8 %collective-permute-start.10 = (f32[3,8,256]{2,1,0:T(8,128)S(1)}, f32[3,8,256]{2,1,0:T(8,128)S(1)}, u32[]{:S(2)}, u32[]{:S(2)}) collective-permute-start(f32[3,8,256]{2,1,0:T(8,128)S(1)} %select_maximum_fusion), channel_id=1, source_target_pairs={{0,160},{32,128},{64,224},{96,192},{128,32},{160,0},{192,96},{224,... | collective-permute-start | bytes 73736 | tf_op jit(solution)/shard_map/ppermute | solution.py:283
  34.0 9.7 %collective-permute-start.11 = (f32[3,8,256]{2,1,0:T(8,128)S(1)}, f32[3,8,256]{2,1,0:T(8,128)S(1)}, u32[]{:S(2)}, u32[]{:S(2)}) collective-permute-start(f32[3,8,256]{2,1,0:T(8,128)S(1)} %select_maximum_fusion), channel_id=1, source_target_pairs={{0,192},{32,224},{64,128},{96,160},{128,64},{160,96},{192,0},{224,... | collective-permute-start | bytes 73736 | tf_op jit(solution)/shard_map/ppermute | solution.py:283
  37.1 6.9 %collective-permute-start.12 = (f32[3,8,256]{2,1,0:T(8,128)S(1)}, f32[3,8,256]{2,1,0:T(8,128)S(1)}, u32[]{:S(2)}, u32[]{:S(2)}) collective-permute-start(f32[3,8,256]{2,1,0:T(8,128)S(1)} %select_maximum_fusion), channel_id=1, source_target_pairs={{0,224},{32,192},{64,160},{96,128},{128,96},{160,64},{192,32},{224... | collective-permute-start | bytes 73736 | tf_op jit(solution)/shard_map/ppermute | solution.py:283
  43.8 17.8 %copy-start.11 = (f32[3,8,256]{2,1,0:T(8,128)}, f32[3,8,256]{2,1,0:T(8,128)S(1)}, u32[]{:S(2)}) copy-start(f32[3,8,256]{2,1,0:T(8,128)S(1)} %collective-permute-done.10) | copy-start | bytes 73732
  43.8 17.8 %copy-start.12 = (f32[3,8,256]{2,1,0:T(8,128)}, f32[3,8,256]{2,1,0:T(8,128)S(1)}, u32[]{:S(2)}) copy-start(f32[3,8,256]{2,1,0:T(8,128)S(1)} %collective-permute-done.11) | copy-start | bytes 73732
  44.7 20.0 %collective-permute-start.13 = (f32[8]{0:T(128)S(1)}, f32[8]{0:T(128)S(1)}, u32[]{:S(2)}, u32[]{:S(2)}) collective-permute-start(f32[8]{0:T(128)S(1)} %fusion.13), channel_id=1, source_target_pairs={{0,1},{1,0},{2,3},{3,2},{4,5},{5,4},{6,7},{7,6},{8,9},{9,8},{10,11... | collective-permute-start | bytes 104 | tf_op jit(solution)/shard_map/ppermute | solution.py:283
  44.8 19.9 %collective-permute-start.14 = (f32[8]{0:T(128)S(1)}, f32[8]{0:T(128)S(1)}, u32[]{:S(2)}, u32[]{:S(2)}) collective-permute-start(f32[8]{0:T(128)S(1)} %fusion.13), channel_id=1, source_target_pairs={{0,2},{1,3},{2,0},{3,1},{4,6},{5,7},{6,4},{7,5},{8,10},{9,11},{10,... | collective-permute-start | bytes 104 | tf_op jit(solution)/shard_map/ppermute | solution.py:283
  44.9 19.8 %collective-permute-start.15 = (f32[8]{0:T(128)S(1)}, f32[8]{0:T(128)S(1)}, u32[]{:S(2)}, u32[]{:S(2)}) collective-permute-start(f32[8]{0:T(128)S(1)} %fusion.13), channel_id=1, source_target_pairs={{0,3},{1,2},{2,1},{3,0},{4,7},{5,6},{6,5},{7,4},{8,11},{9,10},{10,... | collective-permute-start | bytes 104 | tf_op jit(solution)/shard_map/ppermute | solution.py:283
  60.8 49.0 %copy-start.16 = (s32[8]{0:T(128)S(1)}, s32[8]{0:T(128)}, u32[]{:S(2)}) copy-start(s32[8]{0:T(128)} %param.24) | copy-start | bytes 100
  60.8 50.2 %copy-start.14 = (s32[8,256]{1,0:T(8,128)S(1)}, s32[8,256]{1,0:T(8,128)}, u32[]{:S(2)}) copy-start(s32[8,256]{1,0:T(8,128)} %param.23) | copy-start | bytes 24580
  61.6 26.9 %collective-permute-start.4 = (f32[4,64,256]{2,1,0:T(8,128)S(1)}, f32[4,64,256]{2,1,0:T(8,128)S(1)}, u32[]{:S(2)}, u32[]{:S(2)}) collective-permute-start(f32[4,64,256]{2,1,0:T(8,128)S(1)} %get-tuple-element.77), channel_id=1, source_target_pairs={{0,1},{1,2},{2,3},{3,4},{4,5},{5,6},{6,7},{7,8},{8,9},{9,10},{10,1... | collective-permute-start | bytes 786440 | tf_op jit(solution)/shard_map/ppermute | solution.py:23
  64.7 10.1 %collective-permute-start.16 = (f32[8]{0:T(128)S(1)}, f32[8]{0:T(128)S(1)}, u32[]{:S(2)}, u32[]{:S(2)}) collective-permute-start(f32[8]{0:T(128)S(1)} %add_add_fusion.1), channel_id=1, source_target_pairs={{0,4},{1,5},{2,6},{3,7},{4,0},{5,1},{6,2},{7,3},{8,12},{9,13},{10,... | collective-permute-start | bytes 104 | tf_op jit(solution)/shard_map/ppermute | solution.py:283
  64.8 21.2 %collective-permute-start.17 = (f32[8]{0:T(128)S(1)}, f32[8]{0:T(128)S(1)}, u32[]{:S(2)}, u32[]{:S(2)}) collective-permute-start(f32[8]{0:T(128)S(1)} %add_add_fusion.1), channel_id=1, source_target_pairs={{0,8},{1,9},{2,10},{3,11},{4,12},{5,13},{6,14},{7,15},{8,0},{9,1},... | collective-permute-start | bytes 104 | tf_op jit(solution)/shard_map/ppermute | solution.py:283
  68.4 20.1 %collective-permute-start.18 = (f32[8]{0:T(128)S(1)}, f32[8]{0:T(128)S(1)}, u32[]{:S(2)}, u32[]{:S(2)}) collective-permute-start(f32[8]{0:T(128)S(1)} %add_add_fusion.1), channel_id=1, source_target_pairs={{0,12},{1,13},{2,14},{3,15},{4,8},{5,9},{6,10},{7,11},{8,4},{9,5},... | collective-permute-start | bytes 104 | tf_op jit(solution)/shard_map/ppermute | solution.py:283
  70.7 46.1 %collective-permute-start.2 = (f32[10,64,256]{2,1,0:T(8,128)}, f32[10,64,256]{2,1,0:T(8,128)}, u32[]{:S(2)}, u32[]{:S(2)}) collective-permute-start(f32[10,64,256]{2,1,0:T(8,128)} %get-tuple-element.57), channel_id=1, source_target_pairs={{0,1},{1,2},{2,3},{3,4},{4,5},{5,6},{6,7},{7,8},{8,9},{9,10},{10,1... | collective-permute-start | bytes 1966088 | tf_op jit(solution)/shard_map/ppermute | solution.py:23
  74.8 42.0 %collective-permute-start.3 = (f32[10,64,256]{2,1,0:T(8,128)}, f32[10,64,256]{2,1,0:T(8,128)}, u32[]{:S(2)}, u32[]{:S(2)}) collective-permute-start(f32[10,64,256]{2,1,0:T(8,128)} %get-tuple-element.58), channel_id=1, source_target_pairs={{1,0},{2,1},{3,2},{4,3},{5,4},{6,5},{7,6},{8,7},{9,8},{10,9},{11,1... | collective-permute-start | bytes 1966088 | tf_op jit(solution)/shard_map/ppermute | solution.py:24
  86.1 30.7 %collective-permute-start.5 = (f32[4,64,256]{2,1,0:T(8,128)}, f32[4,64,256]{2,1,0:T(8,128)}, u32[]{:S(2)}, u32[]{:S(2)}) collective-permute-start(f32[4,64,256]{2,1,0:T(8,128)} %get-tuple-element.76), channel_id=1, source_target_pairs={{1,0},{2,1},{3,2},{4,3},{5,4},{6,5},{7,6},{8,7},{9,8},{10,9},{11,1... | collective-permute-start | bytes 786440 | tf_op jit(solution)/shard_map/ppermute | solution.py:24
  88.5 21.3 %collective-permute-start.19 = (f32[8]{0:T(128)S(1)}, f32[8]{0:T(128)S(1)}, u32[]{:S(2)}, u32[]{:S(2)}) collective-permute-start(f32[8]{0:T(128)S(1)} %add_add_fusion), channel_id=1, source_target_pairs={{0,16},{1,17},{2,18},{3,19},{4,20},{5,21},{6,22},{7,23},{8,24},{9,... | collective-permute-start | bytes 104 | tf_op jit(solution)/shard_map/ppermute | solution.py:283
  (14 other events, 65.4 us)
